TPU v7x, 32 devices: a whole 2x2x4 slice. The times are simulated.
32 devices in a mesh: freq: 4 (over x, core), tile: 8 (over z, y).
Axes of the slice: x: 2, y: 2, z: 4, core: 2. Of those that a mesh axis runs over, the one named last changes fastest.
Arguments:
- travel_time: float32 [512, 8, 512], P('tile', None, 'freq'), may hold values from 0 to 4
- crossing: int32 [8, 512], P('tile'), may hold values from 0 to 63
- bins: int32 [4], P('freq'), may hold values from 8 to 71
- transmission: float32 [4, 2, 64], P('freq'), may hold values from -1 to 1
- capture: bfloat16 [4, 2, 512, 512], P('freq', None, 'tile'), may hold values from -0.01171875 to 0.01171875
Outputs:
- image: float32 [2, 8, 512], P(None, 'tile')
All inputs are finite; a program needn't handle non-finite values.
Results may differ from a plain program's by a relative error of at most 0.0033.
Values may be sent and summed in bfloat16 or wider, within the bound.
No kernel may reach another device: no remote copies, remote signals or barrier semaphores. Data moves between devices by JAX's collectives and lax.ppermute only.
A program may use at most 64 MiB of HBM per device.

v0:
```python
import math

import jax
import jax.numpy as jnp
from jax import lax
from jax.sharding import PartitionSpec as P

TWO_PI = 2.0 * math.pi


def make_fields(times, bin_values):
    scaled = (TWO_PI * bin_values.astype(jnp.float32)).reshape((-1,) + (1,) * times.ndim)
    angle = scaled * times[None]
    return jnp.stack(
        [jnp.cos(angle).astype(jnp.bfloat16), (-jnp.sin(angle)).astype(jnp.bfloat16)], axis=1
    )


def body(travel_time, crossing, bins, transmission, capture):
    group = 1
    senders = lax.axis_size("freq")
    sub = lax.axis_index("freq") % group
    regrouped = lax.all_to_all(travel_time, "tile", split_axis=1, concat_axis=0, tiled=True)
    tile_view = lax.all_gather(regrouped, "freq", axis=2, tiled=True)
    fields = make_fields(tile_view, bins)
    count = fields.shape[0]
    elements = fields.shape[2]
    voxels = fields.shape[3] * fields.shape[4]
    flat = fields.reshape(count, 2, elements, voxels)
    stacked = flat.reshape(count, 2 * elements, voxels)
    piece = lax.all_gather(capture, "tile", axis=2, tiled=True)
    rows = piece.shape[2]
    cap_real = piece[0, 0]
    cap_imag = piece[0, 1]
    block = jnp.concatenate(
        [
            jnp.concatenate([cap_real, -cap_imag], axis=1),
            jnp.concatenate([cap_imag, cap_real], axis=1),
        ],
        axis=0,
    )
    product = jnp.dot(block, stacked[0], preferred_element_type=jnp.float32)
    w_real = product[:rows]
    w_imag = product[rows:]
    g_real = flat[0, 0].astype(jnp.float32)
    g_imag = flat[0, 1].astype(jnp.float32)
    sums_real = [jnp.sum(g_real * w_real - g_imag * w_imag, axis=0)]
    sums_imag = [jnp.sum(g_real * w_imag + g_imag * w_real, axis=0)]
    focus_real = jnp.stack(sums_real)
    focus_imag = jnp.stack(sums_imag)
    row_count = crossing.shape[0]
    columns = crossing.shape[1]
    width = columns // (senders * group)
    cross_view = crossing.reshape(row_count, senders, group, width)
    flat_cross = lax.dynamic_index_in_dim(cross_view, sub, 2, keepdims=False).reshape(-1)
    cells = transmission.shape[2]
    match = flat_cross[None, :] == lax.broadcasted_iota(jnp.int32, (cells, 1), 0)
    coeff_real = jnp.sum(
        jnp.where(match[None], transmission[:, 0][:, :, None], jnp.float32(0.0)), axis=1
    )
    coeff_imag = jnp.sum(
        jnp.where(match[None], transmission[:, 1][:, :, None], jnp.float32(0.0)), axis=1
    )
    square_real = coeff_real * coeff_real - coeff_imag * coeff_imag
    square_imag = 2.0 * coeff_real * coeff_imag
    part_real = jnp.sum(square_real * focus_real - square_imag * focus_imag, axis=0)
    part_imag = jnp.sum(square_real * focus_imag + square_imag * focus_real, axis=0)
    local_part = jnp.stack([part_real, part_imag]).reshape(2, row_count, senders, 1, width)
    selector = (lax.broadcasted_iota(jnp.int32, (1, 1, 1, group, 1), 3) == sub).astype(jnp.float32)
    partial_image = (local_part * selector).reshape(2, row_count, columns)
    image = lax.psum(partial_image, "freq")
    return image


def solution(mesh):
    in_specs = (
        P("tile", None, "freq"),
        P("tile", None),
        P("freq"),
        P("freq", None, None),
        P("freq", None, "tile", None),
    )
    out_specs = P(None, "tile", None)
    return jax.shard_map(body, mesh=mesh, in_specs=in_specs, out_specs=out_specs, check_vma=False)
```

profile of v0, /device:TPU:0, one launch (start us, length us, event | category | flops | bytes accessed | tf_op | source)
XLA Modules:
  0.0 89.6 jit_solution(9563920641388800474)
XLA Ops:
  6.5 0.0 all-gather.5.cloned.1.call-start
  6.5 0.7 all-gather.5.cloned.1.call-update
  7.3 0.0 all-gather.3.cloned.1.call-start
  7.3 1.0 %copy.10 = f32[64,8,128]{2,0,1:T(8,128)S(1)} copy(f32[64,8,128]{2,1,0:T(8,128)} %param.5) | data formatting | bytes 524288 | tf_op args[0]
  8.3 17.1 %all_to_all.18 = f32[64,8,128]{2,0,1:T(8,128)} all-to-all(f32[64,8,128]{2,0,1:T(8,128)S(1)} %copy.10), channel_id=1, replica_groups=mesh['freq'=4,'tile'=8] {'tile'}, dimensions={1} | all-to-all | bytes 524288 | tf_op jit(solution)/shard_map/all_to_all | solution.py:23
  25.4 0.0 all-gather.3.cloned.1.call-update
  26.1 0.8 slice_bitcast_fusion.4
  26.8 0.8 select_reduce_fusion.1
  27.6 24.9 %all-gather.5.cloned.1.call-done = bf16[1,2,512,512]{3,2,1,0:T(8,128)(2,1)} async-done(((bf16[1,2,64,512]{3,2,1,0:T(8,128)(2,1)}), bf16[1,2,512,512]{3,2,1,0:T(8,128)(2,1)}) %all-gather.5.cloned.1.call-update) | async-done | bytes 1048592 | tf_op jit(solution)/shard_map/all_gather | solution.py:31
  52.6 1.1 %fusion.15 = bf16[512,512]{1,0:T(8,128)(2,1)S(1)} fusion(bf16[1,2,512,512]{3,2,1,0:T(8,128)(2,1)} %all-gather.5.cloned.1.call-done), kind=kLoop, calls=%fused_computation.36 | loop fusion | flops 262144 | bytes 1048576 | tf_op jit(solution)/shard_map/neg | solution.py:37
  53.7 1.3 %slice_bitcast_fusion.1 = (bf16[512,512]{1,0:T(8,128)(2,1)S(1)}, bf16[512,512]{1,0:T(8,128)(2,1)S(1)}) fusion(bf16[1,2,512,512]{3,2,1,0:T(8,128)(2,1)} %all-gather.5.cloned.1.call-done), kind=kLoop, calls=%fused_computation.22 | loop fusion | bytes 2097152 | tf_op jit(solution)/shard_map/squeeze | solution.py:34
  54.9 14.8 %all-gather.3.cloned.1.call-done = f32[512,1,512]{2,0,1:T(8,128)} async-done(((f32[512,1,128]{2,0,1:T(8,128)}), f32[512,1,512]{2,0,1:T(8,128)}) %all-gather.3.cloned.1.call-update) | async-done | bytes 1048592 | tf_op jit(solution)/shard_map/all_gather | solution.py:24
  69.7 4.7 %fusion.12 = (bf16[1,1,512,1,512]{4,2,1,3,0:T(8,128)(2,1)S(1)}, bf16[1,1,512,1,512]{4,2,1,3,0:T(8,128)(2,1)S(1)}) fusion(f32[512,1,512]{2,0,1:T(8,128)} %all-gather.3.cloned.1.call-done, f32[]{:T(128)} %bitcast.3), kind=kLoop, calls=%fused_computation.19 | loop fusion | flops 1048576 | bytes 2097156 | tf_op jit(solution)/shard_map/convert_element_type | solution.py:15
  74.5 0.1 fusion.16
  74.6 1.2 %fusion = f32[1024,512]{1,0:T(8,128)S(1)} fusion(bf16[1024,512]{1,0:T(8,128)(2,1)S(1)} %bitcast.43, bf16[512,512]{1,0:T(8,128)(2,1)S(1)} %get-tuple-element.12, bf16[512,512]{1,0:T(8,128)(2,1)S(1)} %get-tuple-element.11, bf16[512,512]{1,0:T(8,128)(2,1)S(1)} %fusion.15), kind=kOutput, calls=%fused_computation | convolution fusion | flops 1082130432 | bytes 4718592 | tf_op jit(solution)/shard_map/dot_general | solution.py:42
  75.9 0.4 fusion.11
  76.3 6.5 %psum.7 = f32[2,1,512]{2,1,0:T(1,128)} all-reduce(f32[2,1,512]{2,1,0:T(1,128)S(1)} %pad_maximum_fusion.1), channel_id=1, replica_groups=mesh['freq'=4,'tile'=8] {'freq'}, use_global_device_ids=true, to_apply=%region_4.5 | all-reduce | flops 1024 | bytes 8192 | tf_op jit(solution)/shard_map/psum | solution.py:71
  (2 shorter events, 0.0 us)
Async XLA Ops:
  6.5 46.0 %all-gather.5.cloned.1.call-start = ((), (), s32[]{:S(2)}) async-start(), calls=%async_computation.2 | async-start | bytes 1179648 | tf_op jit(solution)/shard_map/all_gather | solution.py:31
  7.3 62.5 %all-gather.3.cloned.1.call-start = ((), (), s32[]{:S(2)}) async-start(), calls=%async_computation.1 | async-start | bytes 1310720 | tf_op jit(solution)/shard_map/all_gather | solution.py:24
Sparse Core Ops, SparseCore 0:
  9.5 42.9 all-gather.4
  54.1 15.5 all-gather.2
where the time goes:
time: 90 us; the launch traced here: 89.6 us
  waiting for transfers between devices  40.5 us (45%)
  blocking collectives  23.6 us (26%)
  between operations  14.1 us (16%)
  other arithmetic  7.14 us (8%)
  local copies, waits for them, and re-layouts  3.03 us (3%)
  matrix products  1.24 us (1%)
    all_gather x1, waiting for transfers between devices, body(): piece = lax.all_gather(capture, 'tile', axis=2, tiled=True)  24.9 us
    all_to_all x1, blocking collectives, body(): lax.all_to_all(travel_time, 'tile', split_axis=1, concat_axis=0, tiled=True)  17.1 us
    all_gather x1, waiting for transfers between devices, body(): tile_view = lax.all_gather(regrouped, 'freq', axis=2, tiled=True)  14.8 us
    psum x1, blocking collectives, body(): image = lax.psum(partial_image, 'freq')  6.49 us
    convert_element_type x1, other arithmetic, make_fields(): jnp.cos(angle).astype(jnp.bfloat16)  4.75 us
  transfers between devices with their start and end apart: 2, of which 2 were waited for; matrix products, arithmetic and copies ran while one was open for 5% of the time, Pallas kernels for 0%

commit v1 on v0

v1 whole, which is shorter than its diff:
```python
import math

import jax
import jax.numpy as jnp
from jax import lax
from jax.sharding import PartitionSpec as P

TWO_PI = 2.0 * math.pi


def gather_shifted(block, axis_name, size):
    pieces = [block]
    for s in range(1, size):
        pairs = [(i, (i - s) % size) for i in range(size)]
        pieces.append(lax.ppermute(block, axis_name, pairs))
    return pieces


def all_sum(value, axis_name, size):
    step = 1
    while step < size:
        pairs = [(i, i ^ step) for i in range(size)]
        value = value + lax.ppermute(value, axis_name, pairs)
        step *= 2
    return value


def body(travel_time, crossing, bins, transmission, capture):
    tiles = lax.axis_size("tile")
    freqs = lax.axis_size("freq")
    k = lax.axis_index("tile")
    f = lax.axis_index("freq")

    cap_pieces = gather_shifted(capture[0], "tile", tiles)
    cap_perm = jnp.concatenate(cap_pieces, axis=1)
    rows = cap_perm.shape[1]
    own = capture.shape[2]
    cap_real = cap_perm[0]
    cap_imag = cap_perm[1]

    regrouped = lax.all_to_all(travel_time, "tile", split_axis=1, concat_axis=0, tiled=True)
    col_pieces = gather_shifted(regrouped, "freq", freqs)
    view = jnp.stack(col_pieces, axis=2)
    elements, row_count, _, width = view.shape
    voxels = row_count * freqs * width

    scaled = TWO_PI * bins[0].astype(jnp.float32)
    angle = scaled * view.reshape(elements, voxels)
    field_real = jnp.cos(angle).astype(jnp.bfloat16)
    field_imag = (-jnp.sin(angle)).astype(jnp.bfloat16)
    stacked = jnp.concatenate([field_real, field_imag], axis=0)

    block = jnp.concatenate(
        [
            jnp.concatenate([cap_real, -cap_imag], axis=1),
            jnp.concatenate([cap_imag, cap_real], axis=1),
        ],
        axis=0,
    )
    product = jnp.dot(block, stacked, preferred_element_type=jnp.float32)
    w_real = product[:rows]
    w_imag = product[rows:]

    start = k * own
    g_real = lax.dynamic_slice_in_dim(jnp.concatenate([field_real, field_real], axis=0), start, rows, 0)
    g_imag = lax.dynamic_slice_in_dim(jnp.concatenate([field_imag, field_imag], axis=0), start, rows, 0)
    g_real = g_real.astype(jnp.float32)
    g_imag = g_imag.astype(jnp.float32)
    focus_real = jnp.sum(g_real * w_real - g_imag * w_imag, axis=0)
    focus_imag = jnp.sum(g_real * w_imag + g_imag * w_real, axis=0)

    focus = jnp.stack([focus_real, focus_imag]).reshape(2, row_count, freqs, width)
    focus = jnp.roll(focus, f, axis=2).reshape(2, row_count, freqs * width)
    focus_real = focus[0]
    focus_imag = focus[1]

    cells = transmission.shape[2]
    match = crossing[None] == lax.broadcasted_iota(jnp.int32, (cells, 1, 1), 0)
    coeff_real = jnp.sum(jnp.where(match, transmission[0, 0][:, None, None], jnp.float32(0.0)), axis=0)
    coeff_imag = jnp.sum(jnp.where(match, transmission[0, 1][:, None, None], jnp.float32(0.0)), axis=0)
    square_real = coeff_real * coeff_real - coeff_imag * coeff_imag
    square_imag = 2.0 * coeff_real * coeff_imag
    part_real = square_real * focus_real - square_imag * focus_imag
    part_imag = square_real * focus_imag + square_imag * focus_real
    partial_image = jnp.stack([part_real, part_imag])
    return all_sum(partial_image, "freq", freqs)


def solution(mesh):
    in_specs = (
        P("tile", None, "freq"),
        P("tile", None),
        P("freq"),
        P("freq", None, None),
        P("freq", None, "tile", None),
    )
    out_specs = P(None, "tile", None)
    return jax.shard_map(body, mesh=mesh, in_specs=in_specs, out_specs=out_specs, check_vma=False)
```

time: 90 us -> 62.1 us (0.69)
  the two profiles are of different devices: /device:TPU:0 before, /device:TPU:16 now
where the time goes in v1:
time: 62.1 us; the launch traced here: 61.1 us
  waiting for transfers between devices  27.3 us (44%)
  starting transfers between devices  20.8 us (33%)
  other arithmetic  6.42 us (10%)
  local copies, waits for them, and re-layouts  4.5 us (7%)
  matrix products  1.24 us (2%)
  between operations  0.85 us (1%)
    ppermute x10, waiting for transfers between devices, gather_shifted(): pieces.append(lax.ppermute(block, axis_name, pairs))  24 us
    ppermute x10, starting transfers between devices, gather_shifted(): pieces.append(lax.ppermute(block, axis_name, pairs))  13.1 us
    all_to_all x1, starting transfers between devices, body(): lax.all_to_all(travel_time, 'tile', split_axis=1, concat_axis=0, tiled=True)  6.11 us
    convert_element_type x1, other arithmetic, body(): field_imag = (-jnp.sin(angle)).astype(jnp.bfloat16)  3.92 us
    ppermute x2, waiting for transfers between devices, all_sum(): value = value + lax.ppermute(value, axis_name, pairs)  3.27 us
    unnamed x10, local copies, waits for them, and re-layouts  2.84 us
    ppermute x2, starting transfers between devices, all_sum(): value = value + lax.ppermute(value, axis_name, pairs)  1.62 us
  transfers between devices with their start and end apart: 13, of which 8 were waited for; matrix products, arithmetic and copies ran while one was open for 7% of the time, Pallas kernels for 0%

profile of v1, /device:TPU:16, one launch (start us, length us, event | category | flops | bytes accessed | tf_op | source)
XLA Modules:
  0.0 61.1 jit_solution(4718005493482643300)
XLA Ops:
  0.0 1.4 %collective-permute-start.3 = (bf16[2,64,512]{2,1,0:T(8,128)(2,1)}, bf16[2,64,512]{2,1,0:T(8,128)(2,1)S(1)}, u32[]{:S(2)}, u32[]{:S(2)}) collective-permute-start(bf16[2,64,512]{2,1,0:T(8,128)(2,1)} %bitcast.55), channel_id=1, source_target_pairs={{0,7},{1,0},{2,1},{3,2},{4,3},{5,4},{6,5},{7,6},{8,15},{9,8},{10,9... | collective-permute-start | bytes 393224 | tf_op jit(solution)/shard_map/ppermute | solution.py:15
  1.4 0.4 collective-permute-start.4
  1.9 3.5 %collective-permute-start.5 = (bf16[2,64,512]{2,1,0:T(8,128)(2,1)}, bf16[2,64,512]{2,1,0:T(8,128)(2,1)S(1)}, u32[]{:S(2)}, u32[]{:S(2)}) collective-permute-start(bf16[2,64,512]{2,1,0:T(8,128)(2,1)} %bitcast.57), channel_id=1, source_target_pairs={{0,5},{1,6},{2,7},{3,0},{4,1},{5,2},{6,3},{7,4},{8,13},{9,14},{10,... | collective-permute-start | bytes 393224 | tf_op jit(solution)/shard_map/ppermute | solution.py:15
  5.4 0.0 collective-permute-start.6
  5.4 2.9 %collective-permute-start.7 = (bf16[2,64,512]{2,1,0:T(8,128)(2,1)}, bf16[2,64,512]{2,1,0:T(8,128)(2,1)S(1)}, u32[]{:S(2)}, u32[]{:S(2)}) collective-permute-start(bf16[2,64,512]{2,1,0:T(8,128)(2,1)} %bitcast.59), channel_id=1, source_target_pairs={{0,3},{1,4},{2,5},{3,6},{4,7},{5,0},{6,1},{7,2},{8,11},{9,12},{10,... | collective-permute-start | bytes 393224 | tf_op jit(solution)/shard_map/ppermute | solution.py:15
  8.3 1.7 %copy.11 = f32[64,8,128]{2,0,1:T(8,128)} copy(f32[64,8,128]{2,1,0:T(8,128)} %param.5) | data formatting | bytes 524288 | tf_op args[0]
  10.0 6.1 %all-to-all-start = ((f32[64,8,128]{2,0,1:T(8,128)}), f32[64,8,128]{2,0,1:T(8,128)S(1)}, u32[]{:S(2)}, u32[]{:S(2)}) async-start(f32[64,8,128]{2,0,1:T(8,128)} %copy.11), calls=%async_computation | async-start | bytes 524288 | tf_op jit(solution)/shard_map/all_to_all | solution.py:41
  16.1 0.9 %constant_dynamic-update-slice_fusion.7 = bf16[2,512,512]{2,1,0:T(8,128)(2,1)S(1)} fusion(bf16[1,2,64,512]{3,2,1,0:T(8,128)(2,1)} %param.9), kind=kLoop, calls=%fused_computation.40 | loop fusion | bytes 262144
  17.0 0.8 %slice_bitcast_fusion.2 = (f32[64]{0:T(128)S(1)}, f32[64]{0:T(128)S(1)}) fusion(f32[1,2,64]{2,1,0:T(2,128)} %param.8), kind=kLoop, calls=%fused_computation.53 | loop fusion | bytes 1024 | tf_op jit(solution)/shard_map/jit(_where)/broadcast_in_dim | solution.py:80
  17.8 0.8 %select_reduce_fusion.1 = (f32[512]{0:T(512)S(1)}, f32[512]{0:T(512)S(1)}) fusion(f32[64]{0:T(128)S(1)} %get-tuple-element.20, s32[512]{0:T(512)} %bitcast.68, f32[64]{0:T(128)S(1)} %get-tuple-element.19), kind=kLoop, calls=%fused_computation.31 | loop fusion | flops 162816 | bytes 6656 | tf_op jit(solution)/shard_map/reduce_sum | solution.py:79
  19.2 0.0 collective-permute-done.3
  19.2 1.5 %collective-permute-start.8 = (bf16[2,64,512]{2,1,0:T(8,128)(2,1)}, bf16[2,64,512]{2,1,0:T(8,128)(2,1)S(1)}, u32[]{:S(2)}, u32[]{:S(2)}) collective-permute-start(bf16[2,64,512]{2,1,0:T(8,128)(2,1)} %bitcast.60), channel_id=1, source_target_pairs={{0,2},{1,3},{2,4},{3,5},{4,6},{5,7},{6,0},{7,1},{8,10},{9,11},{10,... | collective-permute-start | bytes 393224 | tf_op jit(solution)/shard_map/ppermute | solution.py:15
  20.8 0.0 collective-permute-done.4
  20.8 1.5 %collective-permute-start.9 = (bf16[2,64,512]{2,1,0:T(8,128)(2,1)}, bf16[2,64,512]{2,1,0:T(8,128)(2,1)S(1)}, u32[]{:S(2)}, u32[]{:S(2)}) collective-permute-start(bf16[2,64,512]{2,1,0:T(8,128)(2,1)} %bitcast.61), channel_id=1, source_target_pairs={{0,1},{1,2},{2,3},{3,4},{4,5},{5,6},{6,7},{7,0},{8,9},{9,10},{10,1... | collective-permute-start | bytes 393224 | tf_op jit(solution)/shard_map/ppermute | solution.py:15
  22.3 3.0 %collective-permute-done.5 = bf16[2,64,512]{2,1,0:T(8,128)(2,1)S(1)} collective-permute-done((bf16[2,64,512]{2,1,0:T(8,128)(2,1)}, bf16[2,64,512]{2,1,0:T(8,128)(2,1)S(1)}, u32[]{:S(2)}, u32[]{:S(2)}) %collective-permute-start.5) | collective-permute-done | bytes 131104 | tf_op jit(solution)/shard_map/ppermute | solution.py:15
  25.3 2.8 %collective-permute-done.6 = bf16[2,64,512]{2,1,0:T(8,128)(2,1)S(1)} collective-permute-done((bf16[2,64,512]{2,1,0:T(8,128)(2,1)}, bf16[2,64,512]{2,1,0:T(8,128)(2,1)S(1)}, u32[]{:S(2)}, u32[]{:S(2)}) %collective-permute-start.6) | collective-permute-done | bytes 131104 | tf_op jit(solution)/shard_map/ppermute | solution.py:15
  28.2 0.0 collective-permute-done.7
  28.2 5.5 %collective-permute-done.8 = bf16[2,64,512]{2,1,0:T(8,128)(2,1)S(1)} collective-permute-done((bf16[2,64,512]{2,1,0:T(8,128)(2,1)}, bf16[2,64,512]{2,1,0:T(8,128)(2,1)S(1)}, u32[]{:S(2)}, u32[]{:S(2)}) %collective-permute-start.8) | collective-permute-done | bytes 131104 | tf_op jit(solution)/shard_map/ppermute | solution.py:15
  33.7 0.1 collective-permute-done.9
  33.9 0.0 all-to-all-done
  33.9 1.2 %collective-permute-start = (f32[512,1,128]{2,0,1:T(8,128)S(1)}, f32[512,1,128]{2,0,1:T(8,128)S(1)}, u32[]{:S(2)}, u32[]{:S(2)}) collective-permute-start(f32[512,1,128]{2,0,1:T(8,128)S(1)} %bitcast.48), channel_id=1, source_target_pairs={{0,24},{8,0},{16,8},{24,16},{1,25},{9,1},{17,9},{25,17},{2,26},{10... | collective-permute-start | bytes 786440 | tf_op jit(solution)/shard_map/ppermute | solution.py:15
  35.1 0.5 collective-permute-start.1
  35.6 0.1 collective-permute-start.2
  35.7 0.1 slice_bitcast_fusion
  35.8 6.0 %collective-permute-done = f32[512,1,128]{2,0,1:T(8,128)S(1)} collective-permute-done((f32[512,1,128]{2,0,1:T(8,128)S(1)}, f32[512,1,128]{2,0,1:T(8,128)S(1)}, u32[]{:S(2)}, u32[]{:S(2)}) %collective-permute-start) | collective-permute-done | bytes 262176 | tf_op jit(solution)/shard_map/ppermute | solution.py:15
  41.8 6.5 %collective-permute-done.1 = f32[512,1,128]{2,0,1:T(8,128)S(1)} collective-permute-done((f32[512,1,128]{2,0,1:T(8,128)S(1)}, f32[512,1,128]{2,0,1:T(8,128)S(1)}, u32[]{:S(2)}, u32[]{:S(2)}) %collective-permute-start.1) | collective-permute-done | bytes 262176 | tf_op jit(solution)/shard_map/ppermute | solution.py:15
  48.3 0.0 collective-permute-done.2
  48.3 3.9 %negate_convert_fusion = (bf16[512,1,4,128]{3,0,2,1:T(8,128)(2,1)S(1)}, bf16[512,1,4,128]{3,0,2,1:T(8,128)(2,1)S(1)}) fusion(f32[512,1,1,128]{3,0,2,1:T(8,128)S(1)} %bitcast.54, f32[512,1,1,128]{3,0,2,1:T(8,128)S(1)} %bitcast.53, f32[512,1,1,128]{3,0,2,1:T(8,128)S(1)} %bitcast.52, f32[512,1,1,128]{3,0,2,1:T(8,128)S(1)} %bitcast.51, f32[]{:T(128)} %bitcast.4), kind=kLoop, calls=%fused_computation.22 | loop fusion | flops 1835008 | bytes 2097156 | tf_op jit(solution)/shard_map/convert_element_type | solution.py:50
  52.3 0.4 copy.13
  52.7 0.1 copy.18
  52.8 0.4 copy.12
  53.2 0.1 copy.19
  53.3 1.2 %fusion = f32[1024,512]{1,0:T(8,128)S(1)} fusion(bf16[512,512]{1,0:T(8,128)(2,1)S(1)} %get-tuple-element.12, bf16[512,512]{1,0:T(8,128)(2,1)S(1)} %get-tuple-element.11, bf16[512,512]{1,0:T(8,128)(2,1)S(1)} %fusion.19, bf16[512,512]{1,0:T(8,128)(2,1)S(1)} %bitcast.46, bf16[512,512]{1,0:T(8,128)(2,1)S(1)} %bitcast.44), kind=kOutput, calls=%fused_computation | convolution fusion | flops 1084227584 | bytes 4718592 | tf_op jit(solution)/shard_map/dot_general | solution.py:60
  54.5 1.0 %fusion.11 = (f32[512]{0:T(512)S(1)}, f32[512]{0:T(512)S(1)}) fusion(f32[1024,512]{1,0:T(8,128)S(1)} %fusion, s32[]{:T(128)S(6)} %select_n.42, bf16[512,512]{1,0:T(8,128)(2,1)S(1)} %bitcast.47, bf16[512,512]{1,0:T(8,128)(2,1)S(1)} %bitcast.45), kind=kLoop, calls=%fused_computation.18 | loop fusion | flops 6290432 | bytes 3149828 | tf_op jit(solution)/shard_map/reduce_sum | solution.py:70
  55.6 0.1 collective-permute-start.10
  55.7 1.2 %collective-permute-done.10 = f32[2,1,512]{2,1,0:T(1,128)S(1)} collective-permute-done((f32[2,1,512]{2,1,0:T(1,128)S(1)}, f32[2,1,512]{2,1,0:T(1,128)S(1)}, u32[]{:S(2)}, u32[]{:S(2)}) %collective-permute-start.10) | collective-permute-done | bytes 4128 | tf_op jit(solution)/shard_map/ppermute | solution.py:23
  56.9 1.6 %collective-permute-start.11 = (f32[2,1,512]{2,1,0:T(1,128)S(1)}, f32[2,1,512]{2,1,0:T(1,128)S(1)}, u32[]{:S(2)}, u32[]{:S(2)}) collective-permute-start(f32[2,1,512]{2,1,0:T(1,128)S(1)} %fusion.18), channel_id=1, source_target_pairs={{0,16},{8,24},{16,0},{24,8},{1,17},{9,25},{17,1},{25,9},{2,18},{10... | collective-permute-start | bytes 12296 | tf_op jit(solution)/shard_map/ppermute | solution.py:23
  58.4 2.1 %collective-permute-done.11 = f32[2,1,512]{2,1,0:T(1,128)S(1)} collective-permute-done((f32[2,1,512]{2,1,0:T(1,128)S(1)}, f32[2,1,512]{2,1,0:T(1,128)S(1)}, u32[]{:S(2)}, u32[]{:S(2)}) %collective-permute-start.11) | collective-permute-done | bytes 4128 | tf_op jit(solution)/shard_map/ppermute | solution.py:23
  60.5 0.6 fusion.21
  (14 shorter events, 0.2 us)
Async XLA Ops:
  0.0 19.2 %collective-permute-start.3 = (bf16[2,64,512]{2,1,0:T(8,128)(2,1)}, bf16[2,64,512]{2,1,0:T(8,128)(2,1)S(1)}, u32[]{:S(2)}, u32[]{:S(2)}) collective-permute-start(bf16[2,64,512]{2,1,0:T(8,128)(2,1)} %bitcast.55), channel_id=1, source_target_pairs={{0,7},{1,0},{2,1},{3,2},{4,3},{5,4},{6,5},{7,6},{8,15},{9,8},{10,9... | collective-permute-start | bytes 393224 | tf_op jit(solution)/shard_map/ppermute | solution.py:15
  1.4 19.4 %collective-permute-start.4 = (bf16[2,64,512]{2,1,0:T(8,128)(2,1)}, bf16[2,64,512]{2,1,0:T(8,128)(2,1)S(1)}, u32[]{:S(2)}, u32[]{:S(2)}) collective-permute-start(bf16[2,64,512]{2,1,0:T(8,128)(2,1)} %bitcast.56), channel_id=1, source_target_pairs={{0,6},{1,7},{2,0},{3,1},{4,2},{5,3},{6,4},{7,5},{8,14},{9,15},{10,... | collective-permute-start | bytes 393224 | tf_op jit(solution)/shard_map/ppermute | solution.py:15
  1.9 23.5 %collective-permute-start.5 = (bf16[2,64,512]{2,1,0:T(8,128)(2,1)}, bf16[2,64,512]{2,1,0:T(8,128)(2,1)S(1)}, u32[]{:S(2)}, u32[]{:S(2)}) collective-permute-start(bf16[2,64,512]{2,1,0:T(8,128)(2,1)} %bitcast.57), channel_id=1, source_target_pairs={{0,5},{1,6},{2,7},{3,0},{4,1},{5,2},{6,3},{7,4},{8,13},{9,14},{10,... | collective-permute-start | bytes 393224 | tf_op jit(solution)/shard_map/ppermute | solution.py:15
  5.4 22.7 %collective-permute-start.6 = (bf16[2,64,512]{2,1,0:T(8,128)(2,1)}, bf16[2,64,512]{2,1,0:T(8,128)(2,1)S(1)}, u32[]{:S(2)}, u32[]{:S(2)}) collective-permute-start(bf16[2,64,512]{2,1,0:T(8,128)(2,1)} %bitcast.58), channel_id=1, source_target_pairs={{0,4},{1,5},{2,6},{3,7},{4,0},{5,1},{6,2},{7,3},{8,12},{9,13},{10,... | collective-permute-start | bytes 393224 | tf_op jit(solution)/shard_map/ppermute | solution.py:15
  5.4 22.7 %collective-permute-start.7 = (bf16[2,64,512]{2,1,0:T(8,128)(2,1)}, bf16[2,64,512]{2,1,0:T(8,128)(2,1)S(1)}, u32[]{:S(2)}, u32[]{:S(2)}) collective-permute-start(bf16[2,64,512]{2,1,0:T(8,128)(2,1)} %bitcast.59), channel_id=1, source_target_pairs={{0,3},{1,4},{2,5},{3,6},{4,7},{5,0},{6,1},{7,2},{8,11},{9,12},{10,... | collective-permute-start | bytes 393224 | tf_op jit(solution)/shard_map/ppermute | solution.py:15
  10.0 23.9 %all-to-all-start = ((f32[64,8,128]{2,0,1:T(8,128)}), f32[64,8,128]{2,0,1:T(8,128)S(1)}, u32[]{:S(2)}, u32[]{:S(2)}) async-start(f32[64,8,128]{2,0,1:T(8,128)} %copy.11), calls=%async_computation | async-start | bytes 524288 | tf_op jit(solution)/shard_map/all_to_all | solution.py:41
  19.2 14.5 %collective-permute-start.8 = (bf16[2,64,512]{2,1,0:T(8,128)(2,1)}, bf16[2,64,512]{2,1,0:T(8,128)(2,1)S(1)}, u32[]{:S(2)}, u32[]{:S(2)}) collective-permute-start(bf16[2,64,512]{2,1,0:T(8,128)(2,1)} %bitcast.60), channel_id=1, source_target_pairs={{0,2},{1,3},{2,4},{3,5},{4,6},{5,7},{6,0},{7,1},{8,10},{9,11},{10,... | collective-permute-start | bytes 393224 | tf_op jit(solution)/shard_map/ppermute | solution.py:15
  20.8 13.1 %collective-permute-start.9 = (bf16[2,64,512]{2,1,0:T(8,128)(2,1)}, bf16[2,64,512]{2,1,0:T(8,128)(2,1)S(1)}, u32[]{:S(2)}, u32[]{:S(2)}) collective-permute-start(bf16[2,64,512]{2,1,0:T(8,128)(2,1)} %bitcast.61), channel_id=1, source_target_pairs={{0,1},{1,2},{2,3},{3,4},{4,5},{5,6},{6,7},{7,0},{8,9},{9,10},{10,1... | collective-permute-start | bytes 393224 | tf_op jit(solution)/shard_map/ppermute | solution.py:15
  33.9 7.9 %collective-permute-start = (f32[512,1,128]{2,0,1:T(8,128)S(1)}, f32[512,1,128]{2,0,1:T(8,128)S(1)}, u32[]{:S(2)}, u32[]{:S(2)}) collective-permute-start(f32[512,1,128]{2,0,1:T(8,128)S(1)} %bitcast.48), channel_id=1, source_target_pairs={{0,24},{8,0},{16,8},{24,16},{1,25},{9,1},{17,9},{25,17},{2,26},{10... | collective-permute-start | bytes 786440 | tf_op jit(solution)/shard_map/ppermute | solution.py:15
  35.1 13.2 %collective-permute-start.1 = (f32[512,1,128]{2,0,1:T(8,128)S(1)}, f32[512,1,128]{2,0,1:T(8,128)S(1)}, u32[]{:S(2)}, u32[]{:S(2)}) collective-permute-start(f32[512,1,128]{2,0,1:T(8,128)S(1)} %bitcast.49), channel_id=1, source_target_pairs={{0,16},{8,24},{16,0},{24,8},{1,17},{9,25},{17,1},{25,9},{2,18},{10... | collective-permute-start | bytes 786440 | tf_op jit(solution)/shard_map/ppermute | solution.py:15
  35.6 12.7 %collective-permute-start.2 = (f32[512,1,128]{2,0,1:T(8,128)S(1)}, f32[512,1,128]{2,0,1:T(8,128)S(1)}, u32[]{:S(2)}, u32[]{:S(2)}) collective-permute-start(f32[512,1,128]{2,0,1:T(8,128)S(1)} %bitcast.50), channel_id=1, source_target_pairs={{0,8},{8,16},{16,24},{24,0},{1,9},{9,17},{17,25},{25,1},{2,10},{10... | collective-permute-start | bytes 786440 | tf_op jit(solution)/shard_map/ppermute | solution.py:15
  55.6 1.2 %collective-permute-start.10 = (f32[2,1,512]{2,1,0:T(1,128)S(1)}, f32[2,1,512]{2,1,0:T(1,128)S(1)}, u32[]{:S(2)}, u32[]{:S(2)}) collective-permute-start(f32[2,1,512]{2,1,0:T(1,128)S(1)} %pad_maximum_fusion.2), channel_id=1, source_target_pairs={{0,8},{8,0},{16,24},{24,16},{1,9},{9,1},{17,25},{25,17},{2,10},{10... | collective-permute-start | bytes 12296 | tf_op jit(solution)/shard_map/ppermute | solution.py:23
  56.9 3.7 %collective-permute-start.11 = (f32[2,1,512]{2,1,0:T(1,128)S(1)}, f32[2,1,512]{2,1,0:T(1,128)S(1)}, u32[]{:S(2)}, u32[]{:S(2)}) collective-permute-start(f32[2,1,512]{2,1,0:T(1,128)S(1)} %fusion.18), channel_id=1, source_target_pairs={{0,16},{8,24},{16,0},{24,8},{1,17},{9,25},{17,1},{25,9},{2,18},{10... | collective-permute-start | bytes 12296 | tf_op jit(solution)/shard_map/ppermute | solution.py:23

commit v2 on v1

--- a/solution.py
+++ b/solution.py
@@ -16,6 +16,61 @@
     return pieces
 
 
+def chain(block, axis_name, size, stride, step, direction):
+    positions = size // stride
+    pairs = []
+    for z in range(positions):
+        target = z + direction
+        if 0 <= target < positions and 0 <= z - direction * (step - 1) < positions:
+            pairs += [(z * stride + y, target * stride + y) for y in range(stride)]
+    return lax.ppermute(block, axis_name, pairs)
+
+
+def line_gather(block, axis_name, size):
+    positions = size // 2
+    z = lax.axis_index(axis_name) // 2
+    left = [block]
+    right = [block]
+    for j in range(1, positions):
+        left.append(chain(left[-1], axis_name, size, 2, j, 1))
+        right.append(chain(right[-1], axis_name, size, 2, j, -1))
+    slots = left[:0:-1] + [block] + right[1:]
+    return slots, z
+
+
+def pair_swap(slots, axis_name, size):
+    positions = size // 2
+    centre = positions - 1
+    out = []
+    for i, piece in enumerate(slots):
+        d = i - centre
+        pairs = [(p * 2 + y, p * 2 + 1 - y) for p in range(positions) if 0 <= p + d < positions for y in range(2)]
+        out.append(lax.ppermute(piece, axis_name, pairs))
+    return out
+
+
+def gather_rows(block, axis_name, size):
+    positions = size // 2
+    slots, z = line_gather(block, axis_name, size)
+    other = pair_swap(slots, axis_name, size)
+    mine = lax.dynamic_slice_in_dim(jnp.stack(slots), positions - 1 - z, positions, 0)
+    theirs = lax.dynamic_slice_in_dim(jnp.stack(other), positions - 1 - z, positions, 0)
+    both = jnp.stack([mine, theirs], axis=1)
+    both = jnp.roll(both, lax.axis_index(axis_name) % 2, axis=1)
+    return both.reshape((size,) + block.shape)
+
+
+def gather_columns(block, axis_name, size):
+    outer = size // 2
+    same_core = [block]
+    for s in range(1, outer):
+        pairs = [(i, (i - 2 * s) % size) for i in range(size)]
+        same_core.append(lax.ppermute(block, axis_name, pairs))
+    swap = [(i, i ^ 1) for i in range(size)]
+    partner = [lax.ppermute(piece, axis_name, swap) for piece in same_core]
+    return jnp.stack([jnp.stack(same_core), jnp.stack(partner)], axis=1)
+
+
 def all_sum(value, axis_name, size):
     step = 1
     while step < size:
@@ -31,16 +86,15 @@
     k = lax.axis_index("tile")
     f = lax.axis_index("freq")
 
-    cap_pieces = gather_shifted(capture[0], "tile", tiles)
-    cap_perm = jnp.concatenate(cap_pieces, axis=1)
-    rows = cap_perm.shape[1]
-    own = capture.shape[2]
-    cap_real = cap_perm[0]
-    cap_imag = cap_perm[1]
+    cap_all = gather_rows(capture[0], "tile", tiles)
+    cap_all = jnp.moveaxis(cap_all, 0, 1)
+    cap_real = cap_all[0].reshape(-1, cap_all.shape[-1])
+    cap_imag = cap_all[1].reshape(-1, cap_all.shape[-1])
+    rows = cap_real.shape[0]
 
     regrouped = lax.all_to_all(travel_time, "tile", split_axis=1, concat_axis=0, tiled=True)
-    col_pieces = gather_shifted(regrouped, "freq", freqs)
-    view = jnp.stack(col_pieces, axis=2)
+    view = gather_columns(regrouped, "freq", freqs)
+    view = jnp.moveaxis(view.reshape((freqs,) + regrouped.shape), 0, 2)
     elements, row_count, _, width = view.shape
     voxels = row_count * freqs * width
 
@@ -61,16 +115,15 @@
     w_real = product[:rows]
     w_imag = product[rows:]
 
-    start = k * own
-    g_real = lax.dynamic_slice_in_dim(jnp.concatenate([field_real, field_real], axis=0), start, rows, 0)
-    g_imag = lax.dynamic_slice_in_dim(jnp.concatenate([field_imag, field_imag], axis=0), start, rows, 0)
-    g_real = g_real.astype(jnp.float32)
-    g_imag = g_imag.astype(jnp.float32)
+    g_real = field_real.astype(jnp.float32)
+    g_imag = field_imag.astype(jnp.float32)
     focus_real = jnp.sum(g_real * w_real - g_imag * w_imag, axis=0)
     focus_imag = jnp.sum(g_real * w_imag + g_imag * w_real, axis=0)
 
-    focus = jnp.stack([focus_real, focus_imag]).reshape(2, row_count, freqs, width)
-    focus = jnp.roll(focus, f, axis=2).reshape(2, row_count, freqs * width)
+    outer = freqs // 2
+    focus = jnp.stack([focus_real, focus_imag]).reshape(2, row_count, outer, 2, width)
+    focus = jnp.roll(focus, f % 2, axis=3)
+    focus = jnp.roll(focus, f // 2, axis=2).reshape(2, row_count, freqs * width)
     focus_real = focus[0]
     focus_imag = focus[1]
 

time: 62.1 us -> 64 us (1.031)
  the two profiles are of different devices: /device:TPU:16 before, /device:TPU:0 now
where the time goes in v2:
time: 64 us; the launch traced here: 63.5 us
  starting transfers between devices  32.9 us (51%)
  waiting for transfers between devices  17.9 us (28%)
  other arithmetic  6.57 us (10%)
  local copies, waits for them, and re-layouts  3.82 us (6%)
  matrix products  1.24 us (2%)
  between operations  1.11 us (2%)
    ppermute x7, starting transfers between devices, pair_swap(): out.append(lax.ppermute(piece, axis_name, pairs))  13.3 us
    ppermute x6, starting transfers between devices, chain(): return lax.ppermute(block, axis_name, pairs)  10.3 us
    ppermute x6, waiting for transfers between devices, chain(): return lax.ppermute(block, axis_name, pairs)  9.43 us
    all_to_all x1, starting transfers between devices, body(): lax.all_to_all(travel_time, 'tile', split_axis=1, concat_axis=0, tiled=True)  5.94 us
    another operation x1, other arithmetic  3.84 us
    ppermute x2, waiting for transfers between devices, all_sum(): value = value + lax.ppermute(value, axis_name, pairs)  3.16 us
    ppermute x7, waiting for transfers between devices, pair_swap(): out.append(lax.ppermute(piece, axis_name, pairs))  2.63 us
    unnamed x15, local copies, waits for them, and re-layouts  1.84 us
  transfers between devices with their start and end apart: 19, of which 8 were waited for; matrix products, arithmetic and copies ran while one was open for 7% of the time, Pallas kernels for 0%

profile of v2, /device:TPU:0, one launch (start us, length us, event | category | flops | bytes accessed | tf_op | source)
XLA Modules:
  0.0 63.5 jit_solution(8108796120977732849)
XLA Ops:
  0.0 5.1 %collective-permute-start.3 = (bf16[2,64,512]{2,1,0:T(8,128)(2,1)}, bf16[2,64,512]{2,1,0:T(8,128)(2,1)S(1)}, u32[]{:S(2)}, u32[]{:S(2)}) collective-permute-start(bf16[2,64,512]{2,1,0:T(8,128)(2,1)} %bitcast.102), channel_id=1, source_target_pairs={{0,2},{1,3},{2,4},{3,5},{4,6},{5,7},{8,10},{9,11},{10,12},{11,13},... | collective-permute-start | bytes 393224 | tf_op jit(solution)/shard_map/ppermute | solution.py:26
  5.1 1.6 %collective-permute-start.12 = (bf16[2,64,512]{2,1,0:T(8,128)(2,1)}, bf16[2,64,512]{2,1,0:T(8,128)(2,1)S(1)}, u32[]{:S(2)}, u32[]{:S(2)}) collective-permute-start(bf16[2,64,512]{2,1,0:T(8,128)(2,1)} %bitcast.103), channel_id=1, source_target_pairs={{0,1},{1,0},{2,3},{3,2},{4,5},{5,4},{6,7},{7,6},{8,9},{9,8},{10,11... | collective-permute-start | bytes 393224 | tf_op jit(solution)/shard_map/ppermute | solution.py:48
  6.7 1.3 %collective-permute-start.6 = (bf16[2,64,512]{2,1,0:T(8,128)(2,1)}, bf16[2,64,512]{2,1,0:T(8,128)(2,1)S(1)}, u32[]{:S(2)}, u32[]{:S(2)}) collective-permute-start(bf16[2,64,512]{2,1,0:T(8,128)(2,1)} %bitcast.104), channel_id=1, source_target_pairs={{2,0},{3,1},{4,2},{5,3},{6,4},{7,5},{10,8},{11,9},{12,10},{13,11},... | collective-permute-start | bytes 393224 | tf_op jit(solution)/shard_map/ppermute | solution.py:26
  7.9 1.7 %copy.14 = f32[64,8,128]{2,0,1:T(8,128)} copy(f32[64,8,128]{2,1,0:T(8,128)} %param.5) | data formatting | bytes 524288 | tf_op args[0]
  9.6 5.9 %all-to-all-start = ((f32[64,8,128]{2,0,1:T(8,128)}), f32[64,8,128]{2,0,1:T(8,128)S(1)}, u32[]{:S(2)}, u32[]{:S(2)}) async-start(f32[64,8,128]{2,0,1:T(8,128)} %copy.14), calls=%async_computation | async-start | bytes 524288 | tf_op jit(solution)/shard_map/all_to_all | solution.py:95
  15.6 0.0 collective-permute-done.3
  15.6 0.7 %collective-permute-start.4 = (bf16[2,64,512]{2,1,0:T(8,128)(2,1)S(1)}, bf16[2,64,512]{2,1,0:T(8,128)(2,1)S(1)}, u32[]{:S(2)}, u32[]{:S(2)}) collective-permute-start(bf16[2,64,512]{2,1,0:T(8,128)(2,1)S(1)} %collective-permute-done.3), channel_id=1, source_target_pairs={{2,4},{3,5},{4,6},{5,7},{10,12},{11,13},{12,14},{13,15},{18,20},{1... | collective-permute-start | bytes 393224 | tf_op jit(solution)/shard_map/ppermute | solution.py:26
  16.3 0.8 %slice_bitcast_fusion = (f32[64]{0:T(128)S(1)}, f32[64]{0:T(128)S(1)}) fusion(f32[1,2,64]{2,1,0:T(2,128)} %param.8), kind=kLoop, calls=%fused_computation.67 | loop fusion | bytes 1024 | tf_op jit(solution)/shard_map/jit(_where)/broadcast_in_dim | solution.py:133
  17.7 0.8 %select_reduce_fusion.1 = (f32[512]{0:T(512)S(1)}, f32[512]{0:T(512)S(1)}) fusion(f32[64]{0:T(128)S(1)} %get-tuple-element.20, s32[512]{0:T(512)} %bitcast.111, f32[64]{0:T(128)S(1)} %get-tuple-element.19), kind=kLoop, calls=%fused_computation.49 | loop fusion | flops 162816 | bytes 6656 | tf_op jit(solution)/shard_map/reduce_sum | solution.py:132
  18.5 0.0 collective-permute-done.6
  18.5 1.3 %collective-permute-start.7 = (bf16[2,64,512]{2,1,0:T(8,128)(2,1)S(1)}, bf16[2,64,512]{2,1,0:T(8,128)(2,1)S(1)}, u32[]{:S(2)}, u32[]{:S(2)}) collective-permute-start(bf16[2,64,512]{2,1,0:T(8,128)(2,1)S(1)} %collective-permute-done.6), channel_id=1, source_target_pairs={{2,0},{3,1},{4,2},{5,3},{10,8},{11,9},{12,10},{13,11},{18,16},{19,... | collective-permute-start | bytes 393224 | tf_op jit(solution)/shard_map/ppermute | solution.py:26
  19.8 0.0 collective-permute-done.4
  19.8 0.7 %collective-permute-start.5 = (bf16[2,64,512]{2,1,0:T(8,128)(2,1)S(1)}, bf16[2,64,512]{2,1,0:T(8,128)(2,1)S(1)}, u32[]{:S(2)}, u32[]{:S(2)}) collective-permute-start(bf16[2,64,512]{2,1,0:T(8,128)(2,1)S(1)} %collective-permute-done.4), channel_id=1, source_target_pairs={{4,6},{5,7},{12,14},{13,15},{20,22},{21,23},{28,30},{29,31}} | collective-permute-start | bytes 393224 | tf_op jit(solution)/shard_map/ppermute | solution.py:26
  20.5 0.7 %collective-permute-start.11 = (bf16[2,64,512]{2,1,0:T(8,128)(2,1)S(1)}, bf16[2,64,512]{2,1,0:T(8,128)(2,1)S(1)}, u32[]{:S(2)}, u32[]{:S(2)}) collective-permute-start(bf16[2,64,512]{2,1,0:T(8,128)(2,1)S(1)} %collective-permute-done.3), channel_id=1, source_target_pairs={{2,3},{3,2},{4,5},{5,4},{6,7},{7,6},{10,11},{11,10},{12,13},{13,12... | collective-permute-start | bytes 393224 | tf_op jit(solution)/shard_map/ppermute | solution.py:48
  21.2 3.9 %collective-permute-start.13 = (bf16[2,64,512]{2,1,0:T(8,128)(2,1)S(1)}, bf16[2,64,512]{2,1,0:T(8,128)(2,1)S(1)}, u32[]{:S(2)}, u32[]{:S(2)}) collective-permute-start(bf16[2,64,512]{2,1,0:T(8,128)(2,1)S(1)} %collective-permute-done.6), channel_id=1, source_target_pairs={{0,1},{1,0},{2,3},{3,2},{4,5},{5,4},{8,9},{9,8},{10,11},{11,10},{1... | collective-permute-start | bytes 393224 | tf_op jit(solution)/shard_map/ppermute | solution.py:48
  25.1 3.0 %collective-permute-done.7 = bf16[2,64,512]{2,1,0:T(8,128)(2,1)S(1)} collective-permute-done((bf16[2,64,512]{2,1,0:T(8,128)(2,1)S(1)}, bf16[2,64,512]{2,1,0:T(8,128)(2,1)S(1)}, u32[]{:S(2)}, u32[]{:S(2)}) %collective-permute-start.7) | collective-permute-done | bytes 131104 | tf_op jit(solution)/shard_map/ppermute | solution.py:26
  28.1 0.7 %collective-permute-start.10 = (bf16[2,64,512]{2,1,0:T(8,128)(2,1)S(1)}, bf16[2,64,512]{2,1,0:T(8,128)(2,1)S(1)}, u32[]{:S(2)}, u32[]{:S(2)}) collective-permute-start(bf16[2,64,512]{2,1,0:T(8,128)(2,1)S(1)} %collective-permute-done.4), channel_id=1, source_target_pairs={{4,5},{5,4},{6,7},{7,6},{12,13},{13,12},{14,15},{15,14},{20,21},{2... | collective-permute-start | bytes 393224 | tf_op jit(solution)/shard_map/ppermute | solution.py:48
  28.7 0.0 collective-permute-done.5
  28.7 1.3 %collective-permute-start.8 = (bf16[2,64,512]{2,1,0:T(8,128)(2,1)S(1)}, bf16[2,64,512]{2,1,0:T(8,128)(2,1)S(1)}, u32[]{:S(2)}, u32[]{:S(2)}) collective-permute-start(bf16[2,64,512]{2,1,0:T(8,128)(2,1)S(1)} %collective-permute-done.7), channel_id=1, source_target_pairs={{2,0},{3,1},{10,8},{11,9},{18,16},{19,17},{26,24},{27,25}} | collective-permute-start | bytes 393224 | tf_op jit(solution)/shard_map/ppermute | solution.py:26
  30.2 6.5 %collective-permute-done.8 = bf16[2,64,512]{2,1,0:T(8,128)(2,1)S(1)} collective-permute-done((bf16[2,64,512]{2,1,0:T(8,128)(2,1)S(1)}, bf16[2,64,512]{2,1,0:T(8,128)(2,1)S(1)}, u32[]{:S(2)}, u32[]{:S(2)}) %collective-permute-start.8) | collective-permute-done | bytes 131104 | tf_op jit(solution)/shard_map/ppermute | solution.py:26
  36.6 0.7 %collective-permute-start.9 = (bf16[2,64,512]{2,1,0:T(8,128)(2,1)S(1)}, bf16[2,64,512]{2,1,0:T(8,128)(2,1)S(1)}, u32[]{:S(2)}, u32[]{:S(2)}) collective-permute-start(bf16[2,64,512]{2,1,0:T(8,128)(2,1)S(1)} %collective-permute-done.5), channel_id=1, source_target_pairs={{6,7},{7,6},{14,15},{15,14},{22,23},{23,22},{30,31},{31,30}} | collective-permute-start | bytes 393224 | tf_op jit(solution)/shard_map/ppermute | solution.py:48
  37.4 0.0 collective-permute-done.9
  37.4 3.4 %collective-permute-start.14 = (bf16[2,64,512]{2,1,0:T(8,128)(2,1)S(1)}, bf16[2,64,512]{2,1,0:T(8,128)(2,1)S(1)}, u32[]{:S(2)}, u32[]{:S(2)}) collective-permute-start(bf16[2,64,512]{2,1,0:T(8,128)(2,1)S(1)} %collective-permute-done.7), channel_id=1, source_target_pairs={{0,1},{1,0},{2,3},{3,2},{8,9},{9,8},{10,11},{11,10},{16,17},{17,16... | collective-permute-start | bytes 393224 | tf_op jit(solution)/shard_map/ppermute | solution.py:48
  40.8 2.5 %collective-permute-start.15 = (bf16[2,64,512]{2,1,0:T(8,128)(2,1)S(1)}, bf16[2,64,512]{2,1,0:T(8,128)(2,1)S(1)}, u32[]{:S(2)}, u32[]{:S(2)}) collective-permute-start(bf16[2,64,512]{2,1,0:T(8,128)(2,1)S(1)} %collective-permute-done.8), channel_id=1, source_target_pairs={{0,1},{1,0},{8,9},{9,8},{16,17},{17,16},{24,25},{25,24}} | collective-permute-start | bytes 393224 | tf_op jit(solution)/shard_map/ppermute | solution.py:48
  43.3 0.0 all-to-all-done
  43.3 1.6 %collective-permute-start = (f32[512,1,128]{2,0,1:T(8,128)S(1)}, f32[512,1,128]{2,0,1:T(8,128)S(1)}, u32[]{:S(2)}, u32[]{:S(2)}) collective-permute-start(f32[512,1,128]{2,0,1:T(8,128)S(1)} %bitcast.95), channel_id=1, source_target_pairs={{0,16},{8,24},{16,0},{24,8},{1,17},{9,25},{17,1},{25,9},{2,18},{10... | collective-permute-start | bytes 786440 | tf_op jit(solution)/shard_map/ppermute | solution.py:68
  44.9 0.0 collective-permute-done.12
  44.9 0.1 collective-permute-start.1
  45.0 0.0 collective-permute-done.13
  45.0 0.5 collective-permute-done.14
  45.5 2.2 %collective-permute-done.15 = bf16[2,64,512]{2,1,0:T(8,128)(2,1)S(1)} collective-permute-done((bf16[2,64,512]{2,1,0:T(8,128)(2,1)S(1)}, bf16[2,64,512]{2,1,0:T(8,128)(2,1)S(1)}, u32[]{:S(2)}, u32[]{:S(2)}) %collective-permute-start.15) | collective-permute-done | bytes 131104 | tf_op jit(solution)/shard_map/ppermute | solution.py:48
  47.7 0.7 %fusion.14 = bf16[4,2,2,64,512]{4,3,2,1,0:T(8,128)(2,1)S(1)} fusion(s32[]{:T(128)S(6)} %select_n.83, bf16[4,1,2,64,512]{4,3,2,1,0:T(8,128)(2,1)S(1)} %dynamic-slice_bitcast_fusion.1, bf16[4,1,2,64,512]{4,3,2,1,0:T(8,128)(2,1)S(1)} %dynamic-slice_bitcast_fusion), kind=kLoop, calls=%fused_computation.22 | loop fusion | flops 1572864 | bytes 2097156 | tf_op jit(solution)/shard_map/jit(_roll_dynamic)/concatenate | solution.py:59
  48.4 0.1 fusion.24
  48.5 1.2 %collective-permute-done = f32[512,1,128]{2,0,1:T(8,128)S(1)} collective-permute-done((f32[512,1,128]{2,0,1:T(8,128)S(1)}, f32[512,1,128]{2,0,1:T(8,128)S(1)}, u32[]{:S(2)}, u32[]{:S(2)}) %collective-permute-start) | collective-permute-done | bytes 262176 | tf_op jit(solution)/shard_map/ppermute | solution.py:68
  49.7 0.0 collective-permute-start.2
  49.7 0.1 bitcast_negate_fusion
  49.9 1.4 %collective-permute-done.2 = f32[512,1,128]{2,0,1:T(8,128)S(1)} collective-permute-done((f32[512,1,128]{2,0,1:T(8,128)S(1)}, f32[512,1,128]{2,0,1:T(8,128)S(1)}, u32[]{:S(2)}, u32[]{:S(2)}) %collective-permute-start.2) | collective-permute-done | bytes 262176 | tf_op jit(solution)/shard_map/ppermute | solution.py:70
  51.3 3.8 %cosine_convert_fusion = (bf16[2,2,512,1,128]{4,2,0,3,1:T(8,128)(2,1)S(1)}, bf16[2,2,512,1,128]{4,2,0,3,1:T(8,128)(2,1)S(1)}) fusion(f32[2,1,512,1,128]{4,2,0,3,1:T(8,128)S(1)} %maximum_bitcast_fusion.1, f32[2,1,512,1,128]{4,2,0,3,1:T(8,128)S(1)} %maximum_bitcast_fusion, f32[]{:T(128)} %bitcast.4), kind=kLoop, calls=%fused_computation.28 | loop fusion | flops 1310720 | bytes 2097156 | tf_op jit(solution)/shard_map/convert.1
  55.2 0.4 copy.16
  55.7 0.4 copy.18
  56.1 0.2 copy_bitcast_fusion
  56.2 1.2 %fusion = f32[1024,512]{1,0:T(8,128)S(1)} fusion(bf16[512,512]{1,0:T(8,128)(2,1)S(1)} %bitcast.98, bf16[512,512]{1,0:T(8,128)(2,1)S(1)} %bitcast.94, bf16[512,512]{1,0:T(8,128)(2,1)S(1)} %bitcast_negate_fusion, bf16[512,512]{1,0:T(8,128)(2,1)S(1)} %get-tuple-element.21, bf16[512,512]{1,0:T(8,128)(2,1)S(1)} %get-tuple-element.22), kind=kOutput, calls=%fused_computation.4 | convolution fusion | flops 1084227584 | bytes 4718592 | tf_op jit(solution)/shard_map/dot_general | solution.py:114
  57.5 0.4 fusion.11
  58.0 0.2 collective-permute-start.16
  58.2 1.0 %collective-permute-done.16 = f32[2,1,512]{2,1,0:T(1,128)S(1)} collective-permute-done((f32[2,1,512]{2,1,0:T(1,128)S(1)}, f32[2,1,512]{2,1,0:T(1,128)S(1)}, u32[]{:S(2)}, u32[]{:S(2)}) %collective-permute-start.16) | collective-permute-done | bytes 4128 | tf_op jit(solution)/shard_map/ppermute | solution.py:78
  59.2 1.5 %collective-permute-start.17 = (f32[2,1,512]{2,1,0:T(1,128)S(1)}, f32[2,1,512]{2,1,0:T(1,128)S(1)}, u32[]{:S(2)}, u32[]{:S(2)}) collective-permute-start(f32[2,1,512]{2,1,0:T(1,128)S(1)} %fusion.23), channel_id=1, source_target_pairs={{0,16},{8,24},{16,0},{24,8},{1,17},{9,25},{17,1},{25,9},{2,18},{10... | collective-permute-start | bytes 12296 | tf_op jit(solution)/shard_map/ppermute | solution.py:78
  60.8 2.1 %collective-permute-done.17 = f32[2,1,512]{2,1,0:T(1,128)S(1)} collective-permute-done((f32[2,1,512]{2,1,0:T(1,128)S(1)}, f32[2,1,512]{2,1,0:T(1,128)S(1)}, u32[]{:S(2)}, u32[]{:S(2)}) %collective-permute-start.17) | collective-permute-done | bytes 4128 | tf_op jit(solution)/shard_map/ppermute | solution.py:78
  62.9 0.6 fusion.26
  (32 shorter events, 0.5 us)
Async XLA Ops:
  0.0 30.1 %copy-start = (bf16[1,2,64,512]{3,2,1,0:T(8,128)(2,1)S(1)}, bf16[1,2,64,512]{3,2,1,0:T(8,128)(2,1)}, u32[]{:S(2)}) copy-start(bf16[1,2,64,512]{3,2,1,0:T(8,128)(2,1)} %param.9) | copy-start | bytes 393220
  0.0 15.6 %collective-permute-start.3 = (bf16[2,64,512]{2,1,0:T(8,128)(2,1)}, bf16[2,64,512]{2,1,0:T(8,128)(2,1)S(1)}, u32[]{:S(2)}, u32[]{:S(2)}) collective-permute-start(bf16[2,64,512]{2,1,0:T(8,128)(2,1)} %bitcast.102), channel_id=1, source_target_pairs={{0,2},{1,3},{2,4},{3,5},{4,6},{5,7},{8,10},{9,11},{10,12},{11,13},... | collective-permute-start | bytes 393224 | tf_op jit(solution)/shard_map/ppermute | solution.py:26
  5.1 39.8 %collective-permute-start.12 = (bf16[2,64,512]{2,1,0:T(8,128)(2,1)}, bf16[2,64,512]{2,1,0:T(8,128)(2,1)S(1)}, u32[]{:S(2)}, u32[]{:S(2)}) collective-permute-start(bf16[2,64,512]{2,1,0:T(8,128)(2,1)} %bitcast.103), channel_id=1, source_target_pairs={{0,1},{1,0},{2,3},{3,2},{4,5},{5,4},{6,7},{7,6},{8,9},{9,8},{10,11... | collective-permute-start | bytes 393224 | tf_op jit(solution)/shard_map/ppermute | solution.py:48
  6.7 11.8 %collective-permute-start.6 = (bf16[2,64,512]{2,1,0:T(8,128)(2,1)}, bf16[2,64,512]{2,1,0:T(8,128)(2,1)S(1)}, u32[]{:S(2)}, u32[]{:S(2)}) collective-permute-start(bf16[2,64,512]{2,1,0:T(8,128)(2,1)} %bitcast.104), channel_id=1, source_target_pairs={{2,0},{3,1},{4,2},{5,3},{6,4},{7,5},{10,8},{11,9},{12,10},{13,11},... | collective-permute-start | bytes 393224 | tf_op jit(solution)/shard_map/ppermute | solution.py:26
  9.6 33.6 %all-to-all-start = ((f32[64,8,128]{2,0,1:T(8,128)}), f32[64,8,128]{2,0,1:T(8,128)S(1)}, u32[]{:S(2)}, u32[]{:S(2)}) async-start(f32[64,8,128]{2,0,1:T(8,128)} %copy.14), calls=%async_computation | async-start | bytes 524288 | tf_op jit(solution)/shard_map/all_to_all | solution.py:95
  15.6 4.2 %collective-permute-start.4 = (bf16[2,64,512]{2,1,0:T(8,128)(2,1)S(1)}, bf16[2,64,512]{2,1,0:T(8,128)(2,1)S(1)}, u32[]{:S(2)}, u32[]{:S(2)}) collective-permute-start(bf16[2,64,512]{2,1,0:T(8,128)(2,1)S(1)} %collective-permute-done.3), channel_id=1, source_target_pairs={{2,4},{3,5},{4,6},{5,7},{10,12},{11,13},{12,14},{13,15},{18,20},{1... | collective-permute-start | bytes 393224 | tf_op jit(solution)/shard_map/ppermute | solution.py:26
  18.5 9.6 %collective-permute-start.7 = (bf16[2,64,512]{2,1,0:T(8,128)(2,1)S(1)}, bf16[2,64,512]{2,1,0:T(8,128)(2,1)S(1)}, u32[]{:S(2)}, u32[]{:S(2)}) collective-permute-start(bf16[2,64,512]{2,1,0:T(8,128)(2,1)S(1)} %collective-permute-done.6), channel_id=1, source_target_pairs={{2,0},{3,1},{4,2},{5,3},{10,8},{11,9},{12,10},{13,11},{18,16},{19,... | collective-permute-start | bytes 393224 | tf_op jit(solution)/shard_map/ppermute | solution.py:26
  19.8 8.9 %collective-permute-start.5 = (bf16[2,64,512]{2,1,0:T(8,128)(2,1)S(1)}, bf16[2,64,512]{2,1,0:T(8,128)(2,1)S(1)}, u32[]{:S(2)}, u32[]{:S(2)}) collective-permute-start(bf16[2,64,512]{2,1,0:T(8,128)(2,1)S(1)} %collective-permute-done.4), channel_id=1, source_target_pairs={{4,6},{5,7},{12,14},{13,15},{20,22},{21,23},{28,30},{29,31}} | collective-permute-start | bytes 393224 | tf_op jit(solution)/shard_map/ppermute | solution.py:26
  20.5 22.8 %collective-permute-start.11 = (bf16[2,64,512]{2,1,0:T(8,128)(2,1)S(1)}, bf16[2,64,512]{2,1,0:T(8,128)(2,1)S(1)}, u32[]{:S(2)}, u32[]{:S(2)}) collective-permute-start(bf16[2,64,512]{2,1,0:T(8,128)(2,1)S(1)} %collective-permute-done.3), channel_id=1, source_target_pairs={{2,3},{3,2},{4,5},{5,4},{6,7},{7,6},{10,11},{11,10},{12,13},{13,12... | collective-permute-start | bytes 393224 | tf_op jit(solution)/shard_map/ppermute | solution.py:48
  21.2 23.8 %collective-permute-start.13 = (bf16[2,64,512]{2,1,0:T(8,128)(2,1)S(1)}, bf16[2,64,512]{2,1,0:T(8,128)(2,1)S(1)}, u32[]{:S(2)}, u32[]{:S(2)}) collective-permute-start(bf16[2,64,512]{2,1,0:T(8,128)(2,1)S(1)} %collective-permute-done.6), channel_id=1, source_target_pairs={{0,1},{1,0},{2,3},{3,2},{4,5},{5,4},{8,9},{9,8},{10,11},{11,10},{1... | collective-permute-start | bytes 393224 | tf_op jit(solution)/shard_map/ppermute | solution.py:48
  28.1 12.7 %collective-permute-start.10 = (bf16[2,64,512]{2,1,0:T(8,128)(2,1)S(1)}, bf16[2,64,512]{2,1,0:T(8,128)(2,1)S(1)}, u32[]{:S(2)}, u32[]{:S(2)}) collective-permute-start(bf16[2,64,512]{2,1,0:T(8,128)(2,1)S(1)} %collective-permute-done.4), channel_id=1, source_target_pairs={{4,5},{5,4},{6,7},{7,6},{12,13},{13,12},{14,15},{15,14},{20,21},{2... | collective-permute-start | bytes 393224 | tf_op jit(solution)/shard_map/ppermute | solution.py:48
  28.7 7.9 %collective-permute-start.8 = (bf16[2,64,512]{2,1,0:T(8,128)(2,1)S(1)}, bf16[2,64,512]{2,1,0:T(8,128)(2,1)S(1)}, u32[]{:S(2)}, u32[]{:S(2)}) collective-permute-start(bf16[2,64,512]{2,1,0:T(8,128)(2,1)S(1)} %collective-permute-done.7), channel_id=1, source_target_pairs={{2,0},{3,1},{10,8},{11,9},{18,16},{19,17},{26,24},{27,25}} | collective-permute-start | bytes 393224 | tf_op jit(solution)/shard_map/ppermute | solution.py:26
  36.6 0.7 %collective-permute-start.9 = (bf16[2,64,512]{2,1,0:T(8,128)(2,1)S(1)}, bf16[2,64,512]{2,1,0:T(8,128)(2,1)S(1)}, u32[]{:S(2)}, u32[]{:S(2)}) collective-permute-start(bf16[2,64,512]{2,1,0:T(8,128)(2,1)S(1)} %collective-permute-done.5), channel_id=1, source_target_pairs={{6,7},{7,6},{14,15},{15,14},{22,23},{23,22},{30,31},{31,30}} | collective-permute-start | bytes 393224 | tf_op jit(solution)/shard_map/ppermute | solution.py:48
  37.4 8.1 %collective-permute-start.14 = (bf16[2,64,512]{2,1,0:T(8,128)(2,1)S(1)}, bf16[2,64,512]{2,1,0:T(8,128)(2,1)S(1)}, u32[]{:S(2)}, u32[]{:S(2)}) collective-permute-start(bf16[2,64,512]{2,1,0:T(8,128)(2,1)S(1)} %collective-permute-done.7), channel_id=1, source_target_pairs={{0,1},{1,0},{2,3},{3,2},{8,9},{9,8},{10,11},{11,10},{16,17},{17,16... | collective-permute-start | bytes 393224 | tf_op jit(solution)/shard_map/ppermute | solution.py:48
  40.8 6.9 %collective-permute-start.15 = (bf16[2,64,512]{2,1,0:T(8,128)(2,1)S(1)}, bf16[2,64,512]{2,1,0:T(8,128)(2,1)S(1)}, u32[]{:S(2)}, u32[]{:S(2)}) collective-permute-start(bf16[2,64,512]{2,1,0:T(8,128)(2,1)S(1)} %collective-permute-done.8), channel_id=1, source_target_pairs={{0,1},{1,0},{8,9},{9,8},{16,17},{17,16},{24,25},{25,24}} | collective-permute-start | bytes 393224 | tf_op jit(solution)/shard_map/ppermute | solution.py:48
  43.3 6.4 %collective-permute-start = (f32[512,1,128]{2,0,1:T(8,128)S(1)}, f32[512,1,128]{2,0,1:T(8,128)S(1)}, u32[]{:S(2)}, u32[]{:S(2)}) collective-permute-start(f32[512,1,128]{2,0,1:T(8,128)S(1)} %bitcast.95), channel_id=1, source_target_pairs={{0,16},{8,24},{16,0},{24,8},{1,17},{9,25},{17,1},{25,9},{2,18},{10... | collective-permute-start | bytes 786440 | tf_op jit(solution)/shard_map/ppermute | solution.py:68
  44.9 5.0 %collective-permute-start.1 = (f32[512,1,128]{2,0,1:T(8,128)S(1)}, f32[512,1,128]{2,0,1:T(8,128)S(1)}, u32[]{:S(2)}, u32[]{:S(2)}) collective-permute-start(f32[512,1,128]{2,0,1:T(8,128)S(1)} %bitcast.96), channel_id=1, source_target_pairs={{0,8},{8,0},{16,24},{24,16},{1,9},{9,1},{17,25},{25,17},{2,10},{10... | collective-permute-start | bytes 786440 | tf_op jit(solution)/shard_map/ppermute | solution.py:70
  49.7 1.5 %collective-permute-start.2 = (f32[512,1,128]{2,0,1:T(8,128)S(1)}, f32[512,1,128]{2,0,1:T(8,128)S(1)}, u32[]{:S(2)}, u32[]{:S(2)}) collective-permute-start(f32[512,1,128]{2,0,1:T(8,128)S(1)} %collective-permute-done), channel_id=1, source_target_pairs={{0,8},{8,0},{16,24},{24,16},{1,9},{9,1},{17,25},{25,17},{2,10},{10... | collective-permute-start | bytes 786440 | tf_op jit(solution)/shard_map/ppermute | solution.py:70
  58.0 1.2 %collective-permute-start.16 = (f32[2,1,512]{2,1,0:T(1,128)S(1)}, f32[2,1,512]{2,1,0:T(1,128)S(1)}, u32[]{:S(2)}, u32[]{:S(2)}) collective-permute-start(f32[2,1,512]{2,1,0:T(1,128)S(1)} %pad_maximum_fusion), channel_id=1, source_target_pairs={{0,8},{8,0},{16,24},{24,16},{1,9},{9,1},{17,25},{25,17},{2,10},{10... | collective-permute-start | bytes 12296 | tf_op jit(solution)/shard_map/ppermute | solution.py:78
  59.2 3.7 %collective-permute-start.17 = (f32[2,1,512]{2,1,0:T(1,128)S(1)}, f32[2,1,512]{2,1,0:T(1,128)S(1)}, u32[]{:S(2)}, u32[]{:S(2)}) collective-permute-start(f32[2,1,512]{2,1,0:T(1,128)S(1)} %fusion.23), channel_id=1, source_target_pairs={{0,16},{8,24},{16,0},{24,8},{1,17},{9,25},{17,1},{25,9},{2,18},{10... | collective-permute-start | bytes 12296 | tf_op jit(solution)/shard_map/ppermute | solution.py:78

commit v3 on v2

--- a/solution.py
+++ b/solution.py
@@ -86,12 +86,6 @@
     k = lax.axis_index("tile")
     f = lax.axis_index("freq")
 
-    cap_all = gather_rows(capture[0], "tile", tiles)
-    cap_all = jnp.moveaxis(cap_all, 0, 1)
-    cap_real = cap_all[0].reshape(-1, cap_all.shape[-1])
-    cap_imag = cap_all[1].reshape(-1, cap_all.shape[-1])
-    rows = cap_real.shape[0]
-
     regrouped = lax.all_to_all(travel_time, "tile", split_axis=1, concat_axis=0, tiled=True)
     view = gather_columns(regrouped, "freq", freqs)
     view = jnp.moveaxis(view.reshape((freqs,) + regrouped.shape), 0, 2)
@@ -102,23 +96,28 @@
     angle = scaled * view.reshape(elements, voxels)
     field_real = jnp.cos(angle).astype(jnp.bfloat16)
     field_imag = (-jnp.sin(angle)).astype(jnp.bfloat16)
-    stacked = jnp.concatenate([field_real, field_imag], axis=0)
+    left = jnp.concatenate([field_real, field_imag], axis=1)
+    right = jnp.concatenate([-field_imag, field_real], axis=1)
 
-    block = jnp.concatenate(
-        [
-            jnp.concatenate([cap_real, -cap_imag], axis=1),
-            jnp.concatenate([cap_imag, cap_real], axis=1),
-        ],
-        axis=0,
-    )
-    product = jnp.dot(block, stacked, preferred_element_type=jnp.float32)
-    w_real = product[:rows]
-    w_imag = product[rows:]
-
-    g_real = field_real.astype(jnp.float32)
-    g_imag = field_imag.astype(jnp.float32)
-    focus_real = jnp.sum(g_real * w_real - g_imag * w_imag, axis=0)
-    focus_imag = jnp.sum(g_real * w_imag + g_imag * w_real, axis=0)
+    cap_pieces = gather_shifted(capture[0], "tile", tiles)
+    own = capture.shape[2]
+    focus_real = None
+    for s, piece in enumerate(cap_pieces):
+        product = jnp.dot(piece[0], left, preferred_element_type=jnp.float32) + jnp.dot(
+            piece[1], right, preferred_element_type=jnp.float32
+        )
+        w_real = product[:, :voxels]
+        w_imag = product[:, voxels:]
+        start = ((k + s) % tiles) * own
+        g_real = lax.dynamic_slice_in_dim(field_real, start, own, 0).astype(jnp.float32)
+        g_imag = lax.dynamic_slice_in_dim(field_imag, start, own, 0).astype(jnp.float32)
+        part_real = jnp.sum(g_real * w_real - g_imag * w_imag, axis=0)
+        part_imag = jnp.sum(g_real * w_imag + g_imag * w_real, axis=0)
+        if focus_real is None:
+            focus_real, focus_imag = part_real, part_imag
+        else:
+            focus_real = focus_real + part_real
+            focus_imag = focus_imag + part_imag
 
     outer = freqs // 2
     focus = jnp.stack([focus_real, focus_imag]).reshape(2, row_count, outer, 2, width)

time: 64 us -> 61.7 us (0.964)
  starting transfers between devices: 32.9 us -> 27.5 us
  matrix products: 1.24 us -> 4.75 us
  waiting for transfers between devices: 17.9 us -> 20 us
  other arithmetic: 6.57 us -> 5.39 us
  local copies, waits for them, and re-layouts: 3.82 us -> 2.88 us
    ppermute x13 -> x7, starting transfers between devices: 23.6 us -> 17 us  [gather_shifted(): pieces.append(lax.ppermute(block, axis_name, pairs))]
    ppermute x13 -> x7, waiting for transfers between devices: 12.1 us -> 7.44 us  [gather_shifted(): pieces.append(lax.ppermute(block, axis_name, pairs))]
    all_to_all x1, waiting for transfers between devices: 0.01 us -> 4.35 us  [body(): lax.all_to_all(travel_time, 'tile', split_axis=1, concat_axis=0, tiled=True)]
    dot_general x1 -> x16, matrix products: 1.24 us -> 4.75 us  [the longest x8 2.4 us: body(): jnp.dot(piece[0], left, preferred_element_type=jnp.float32)]
    ppermute x1, waiting for transfers between devices: 1.23 us -> 4.69 us  [gather_columns(): same_core.append(lax.ppermute(block, axis_name, pairs))]
    all_to_all x1, starting transfers between devices: 5.94 us -> 7.28 us  [body(): lax.all_to_all(travel_time, 'tile', split_axis=1, concat_axis=0, tiled=True)]
    ppermute x2, waiting for transfers between devices: 1.41 us -> 0.23 us  [gather_columns(): partner = [lax.ppermute(piece, axis_name, swap) for piece in same_core]]
    broadcast_in_dim x1, local copies, waits for them, and re-layouts: 0.76 us -> 0.01 us  [body(): jnp.where(match, transmission[0, 1][:, None, None], jnp.float32(0.0))]
  transfers between devices with their start and end apart: 19 -> 13, of which waited for: 8 -> 7; matrix products, arithmetic and copies ran while one was open for 7% -> 16% of each run, Pallas kernels for 0% -> 0%
where the time goes in v3:
time: 61.7 us; the launch traced here: 61.5 us
  starting transfers between devices  27.5 us (45%)
  waiting for transfers between devices  20 us (32%)
  other arithmetic  5.39 us (9%)
  matrix products  4.75 us (8%)
  local copies, waits for them, and re-layouts  2.88 us (5%)
  between operations  0.97 us (2%)
    ppermute x7, starting transfers between devices, gather_shifted(): pieces.append(lax.ppermute(block, axis_name, pairs))  17 us
    ppermute x7, waiting for transfers between devices, gather_shifted(): pieces.append(lax.ppermute(block, axis_name, pairs))  7.44 us
    all_to_all x1, starting transfers between devices, body(): lax.all_to_all(travel_time, 'tile', split_axis=1, concat_axis=0, tiled=True)  7.28 us
    ppermute x1, waiting for transfers between devices, gather_columns(): same_core.append(lax.ppermute(block, axis_name, pairs))  4.69 us
    all_to_all x1, waiting for transfers between devices, body(): lax.all_to_all(travel_time, 'tile', split_axis=1, concat_axis=0, tiled=True)  4.35 us
    another operation x1, other arithmetic  3.85 us
    ppermute x2, waiting for transfers between devices, all_sum(): value = value + lax.ppermute(value, axis_name, pairs)  3.27 us
    dot_general x8, matrix products, body(): jnp.dot(piece[0], left, preferred_element_type=jnp.float32)  2.4 us
  transfers between devices with their start and end apart: 13, of which 7 were waited for; matrix products, arithmetic and copies ran while one was open for 16% of the time, Pallas kernels for 0%

profile of v3, /device:TPU:0, one launch (start us, length us, event | category | flops | bytes accessed | tf_op | source)
XLA Modules:
  0.0 61.5 jit_solution(11220032559704106458)
XLA Ops:
  0.0 1.7 %copy.14 = f32[64,8,128]{2,0,1:T(8,128)} copy(f32[64,8,128]{2,1,0:T(8,128)} %param.5) | data formatting | bytes 524288 | tf_op args[0]
  1.7 7.3 %all-to-all-start = ((f32[64,8,128]{2,0,1:T(8,128)}), f32[64,8,128]{2,0,1:T(8,128)S(1)}, u32[]{:S(2)}, u32[]{:S(2)}) async-start(f32[64,8,128]{2,0,1:T(8,128)} %copy.14), calls=%async_computation | async-start | bytes 524288 | tf_op jit(solution)/shard_map/all_to_all | solution.py:89
  9.0 4.7 %collective-permute-start.3 = (bf16[2,64,512]{2,1,0:T(8,128)(2,1)S(1)}, bf16[2,64,512]{2,1,0:T(8,128)(2,1)S(1)}, u32[]{:S(2)}, u32[]{:S(2)}) collective-permute-start(bf16[2,64,512]{2,1,0:T(8,128)(2,1)S(1)} %bitcast.147), channel_id=1, source_target_pairs={{0,7},{1,0},{2,1},{3,2},{4,3},{5,4},{6,5},{7,6},{8,15},{9,8},{10,9... | collective-permute-start | bytes 393224 | tf_op jit(solution)/shard_map/ppermute | solution.py:15
  13.7 0.6 collective-permute-start.4
  14.3 0.0 collective-permute-start.5
  15.0 4.3 %all-to-all-done = f32[64,8,128]{2,0,1:T(8,128)S(1)} async-done(((f32[64,8,128]{2,0,1:T(8,128)}), f32[64,8,128]{2,0,1:T(8,128)S(1)}, u32[]{:S(2)}, u32[]{:S(2)}) %all-to-all-start) | async-done | bytes 262176 | tf_op jit(solution)/shard_map/all_to_all | solution.py:89
  19.3 1.5 %collective-permute-start = (f32[512,1,128]{2,0,1:T(8,128)S(1)}, f32[512,1,128]{2,0,1:T(8,128)S(1)}, u32[]{:S(2)}, u32[]{:S(2)}) collective-permute-start(f32[512,1,128]{2,0,1:T(8,128)S(1)} %bitcast.141), channel_id=1, source_target_pairs={{0,16},{8,24},{16,0},{24,8},{1,17},{9,25},{17,1},{25,9},{2,18},{10... | collective-permute-start | bytes 786440 | tf_op jit(solution)/shard_map/ppermute | solution.py:68
  20.8 0.1 select_reduce_fusion.1
  20.9 0.1 collective-permute-start.1
  21.0 4.7 %collective-permute-done = f32[512,1,128]{2,0,1:T(8,128)S(1)} collective-permute-done((f32[512,1,128]{2,0,1:T(8,128)S(1)}, f32[512,1,128]{2,0,1:T(8,128)S(1)}, u32[]{:S(2)}, u32[]{:S(2)}) %collective-permute-start) | collective-permute-done | bytes 262176 | tf_op jit(solution)/shard_map/ppermute | solution.py:68
  25.7 0.1 maximum_bitcast_fusion
  25.8 1.2 %collective-permute-start.9 = (bf16[2,64,512]{2,1,0:T(8,128)(2,1)S(1)}, bf16[2,64,512]{2,1,0:T(8,128)(2,1)S(1)}, u32[]{:S(2)}, u32[]{:S(2)}) collective-permute-start(bf16[2,64,512]{2,1,0:T(8,128)(2,1)S(1)} %bitcast.150), channel_id=1, source_target_pairs={{0,1},{1,2},{2,3},{3,4},{4,5},{5,6},{6,7},{7,0},{8,9},{9,10},{10,1... | collective-permute-start | bytes 393224 | tf_op jit(solution)/shard_map/ppermute | solution.py:15
  27.0 0.2 collective-permute-done.2
  27.2 6.5 %collective-permute-start.8 = (bf16[2,64,512]{2,1,0:T(8,128)(2,1)S(1)}, bf16[2,64,512]{2,1,0:T(8,128)(2,1)S(1)}, u32[]{:S(2)}, u32[]{:S(2)}) collective-permute-start(bf16[2,64,512]{2,1,0:T(8,128)(2,1)S(1)} %bitcast.151), channel_id=1, source_target_pairs={{0,2},{1,3},{2,4},{3,5},{4,6},{5,7},{6,0},{7,1},{8,10},{9,11},{10,... | collective-permute-start | bytes 393224 | tf_op jit(solution)/shard_map/ppermute | solution.py:15
  33.8 3.8 %negate_convert_fusion = (bf16[2,2,512,1,128]{4,2,0,3,1:T(8,128)(2,1)S(1)}, bf16[2,2,512,1,128]{4,2,0,3,1:T(8,128)(2,1)S(1)}) fusion(f32[2,1,512,1,128]{4,2,0,3,1:T(8,128)S(1)} %maximum_bitcast_fusion.1, f32[2,1,512,1,128]{4,2,0,3,1:T(8,128)S(1)} %maximum_bitcast_fusion, f32[]{:T(128)} %bitcast.4), kind=kLoop, calls=%fused_computation.18 | loop fusion | flops 1310720 | bytes 2097156 | tf_op jit(solution)/shard_map/convert
  37.7 0.4 copy.16
  38.1 0.1 constant_dynamic-update-slice_fusion.1
  38.2 0.4 copy.18
  38.7 0.2 constant_dynamic-update-slice_fusion
  38.9 0.1 copy.30
  39.0 3.2 %collective-permute-start.6 = (bf16[2,64,512]{2,1,0:T(8,128)(2,1)S(1)}, bf16[2,64,512]{2,1,0:T(8,128)(2,1)S(1)}, u32[]{:S(2)}, u32[]{:S(2)}) collective-permute-start(bf16[2,64,512]{2,1,0:T(8,128)(2,1)S(1)} %bitcast.152), channel_id=1, source_target_pairs={{0,4},{1,5},{2,6},{3,7},{4,0},{5,1},{6,2},{7,3},{8,12},{9,13},{10,... | collective-permute-start | bytes 393224 | tf_op jit(solution)/shard_map/ppermute | solution.py:15
  42.1 0.3 fusion.46
  42.4 0.8 %collective-permute-start.7 = (bf16[2,64,512]{2,1,0:T(8,128)(2,1)S(1)}, bf16[2,64,512]{2,1,0:T(8,128)(2,1)S(1)}, u32[]{:S(2)}, u32[]{:S(2)}) collective-permute-start(bf16[2,64,512]{2,1,0:T(8,128)(2,1)S(1)} %bitcast.153), channel_id=1, source_target_pairs={{0,3},{1,4},{2,5},{3,6},{4,7},{5,0},{6,1},{7,2},{8,11},{9,12},{10,... | collective-permute-start | bytes 393224 | tf_op jit(solution)/shard_map/ppermute | solution.py:15
  43.3 0.3 fusion.45
  43.6 0.3 fusion.6
  43.9 0.3 fusion.5
  44.2 0.3 fusion.44
  44.5 0.3 fusion.4
  44.8 0.1 copy.29
  44.9 0.3 fusion.40
  45.2 0.3 fusion
  45.5 0.3 fusion.48
  45.8 5.2 %collective-permute-done.6 = bf16[2,64,512]{2,1,0:T(8,128)(2,1)S(1)} collective-permute-done((bf16[2,64,512]{2,1,0:T(8,128)(2,1)S(1)}, bf16[2,64,512]{2,1,0:T(8,128)(2,1)S(1)}, u32[]{:S(2)}, u32[]{:S(2)}) %collective-permute-start.6) | collective-permute-done | bytes 131104 | tf_op jit(solution)/shard_map/ppermute | solution.py:15
  51.0 0.3 fusion.43
  51.3 0.3 fusion.3
  51.6 0.3 fusion.7
  51.9 2.2 %collective-permute-done.7 = bf16[2,64,512]{2,1,0:T(8,128)(2,1)S(1)} collective-permute-done((bf16[2,64,512]{2,1,0:T(8,128)(2,1)S(1)}, bf16[2,64,512]{2,1,0:T(8,128)(2,1)S(1)}, u32[]{:S(2)}, u32[]{:S(2)}) %collective-permute-start.7) | collective-permute-done | bytes 131104 | tf_op jit(solution)/shard_map/ppermute | solution.py:15
  54.1 0.3 fusion.42
  54.4 0.3 fusion.2
  54.7 0.2 fusion.11
  54.9 0.3 fusion.41
  55.2 0.3 fusion.1
  55.5 0.3 fusion.15
  55.9 0.1 collective-permute-start.10
  56.0 1.2 %collective-permute-done.10 = f32[2,1,512]{2,1,0:T(1,128)S(1)} collective-permute-done((f32[2,1,512]{2,1,0:T(1,128)S(1)}, f32[2,1,512]{2,1,0:T(1,128)S(1)}, u32[]{:S(2)}, u32[]{:S(2)}) %collective-permute-start.10) | collective-permute-done | bytes 4128 | tf_op jit(solution)/shard_map/ppermute | solution.py:78
  57.2 1.6 %collective-permute-start.11 = (f32[2,1,512]{2,1,0:T(1,128)S(1)}, f32[2,1,512]{2,1,0:T(1,128)S(1)}, u32[]{:S(2)}, u32[]{:S(2)}) collective-permute-start(f32[2,1,512]{2,1,0:T(1,128)S(1)} %fusion.56), channel_id=1, source_target_pairs={{0,16},{8,24},{16,0},{24,8},{1,17},{9,25},{17,1},{25,9},{2,18},{10... | collective-permute-start | bytes 12296 | tf_op jit(solution)/shard_map/ppermute | solution.py:78
  58.7 2.1 %collective-permute-done.11 = f32[2,1,512]{2,1,0:T(1,128)S(1)} collective-permute-done((f32[2,1,512]{2,1,0:T(1,128)S(1)}, f32[2,1,512]{2,1,0:T(1,128)S(1)}, u32[]{:S(2)}, u32[]{:S(2)}) %collective-permute-start.11) | collective-permute-done | bytes 4128 | tf_op jit(solution)/shard_map/ppermute | solution.py:78
  60.8 0.6 fusion.67
  (25 shorter events, 0.2 us)
Async XLA Ops:
  0.0 9.0 %copy-start = (bf16[1,2,64,512]{3,2,1,0:T(8,128)(2,1)S(1)}, bf16[1,2,64,512]{3,2,1,0:T(8,128)(2,1)}, u32[]{:S(2)}) copy-start(bf16[1,2,64,512]{3,2,1,0:T(8,128)(2,1)} %param.9) | copy-start | bytes 393220
  0.0 20.8 %copy-start.2 = (f32[1,2,64]{2,1,0:T(2,128)S(1)}, f32[1,2,64]{2,1,0:T(2,128)}, u32[]{:S(2)}) copy-start(f32[1,2,64]{2,1,0:T(2,128)} %param.8) | copy-start | bytes 1540
  0.0 20.8 %copy-start.1 = (s32[1,512]{1,0:T(1,128)S(1)}, s32[1,512]{1,0:T(1,128)}, u32[]{:S(2)}) copy-start(s32[1,512]{1,0:T(1,128)} %param.6) | copy-start | bytes 6148
  1.7 17.6 %all-to-all-start = ((f32[64,8,128]{2,0,1:T(8,128)}), f32[64,8,128]{2,0,1:T(8,128)S(1)}, u32[]{:S(2)}, u32[]{:S(2)}) async-start(f32[64,8,128]{2,0,1:T(8,128)} %copy.14), calls=%async_computation | async-start | bytes 524288 | tf_op jit(solution)/shard_map/all_to_all | solution.py:89
  9.0 29.9 %collective-permute-start.3 = (bf16[2,64,512]{2,1,0:T(8,128)(2,1)S(1)}, bf16[2,64,512]{2,1,0:T(8,128)(2,1)S(1)}, u32[]{:S(2)}, u32[]{:S(2)}) collective-permute-start(bf16[2,64,512]{2,1,0:T(8,128)(2,1)S(1)} %bitcast.147), channel_id=1, source_target_pairs={{0,7},{1,0},{2,1},{3,2},{4,3},{5,4},{6,5},{7,6},{8,15},{9,8},{10,9... | collective-permute-start | bytes 393224 | tf_op jit(solution)/shard_map/ppermute | solution.py:15
  13.7 28.7 %collective-permute-start.4 = (bf16[2,64,512]{2,1,0:T(8,128)(2,1)S(1)}, bf16[2,64,512]{2,1,0:T(8,128)(2,1)S(1)}, u32[]{:S(2)}, u32[]{:S(2)}) collective-permute-start(bf16[2,64,512]{2,1,0:T(8,128)(2,1)S(1)} %bitcast.148), channel_id=1, source_target_pairs={{0,6},{1,7},{2,0},{3,1},{4,2},{5,3},{6,4},{7,5},{8,14},{9,15},{10,... | collective-permute-start | bytes 393224 | tf_op jit(solution)/shard_map/ppermute | solution.py:15
  14.3 29.9 %collective-permute-start.5 = (bf16[2,64,512]{2,1,0:T(8,128)(2,1)S(1)}, bf16[2,64,512]{2,1,0:T(8,128)(2,1)S(1)}, u32[]{:S(2)}, u32[]{:S(2)}) collective-permute-start(bf16[2,64,512]{2,1,0:T(8,128)(2,1)S(1)} %bitcast.149), channel_id=1, source_target_pairs={{0,5},{1,6},{2,7},{3,0},{4,1},{5,2},{6,3},{7,4},{8,13},{9,14},{10,... | collective-permute-start | bytes 393224 | tf_op jit(solution)/shard_map/ppermute | solution.py:15
  19.3 6.4 %collective-permute-start = (f32[512,1,128]{2,0,1:T(8,128)S(1)}, f32[512,1,128]{2,0,1:T(8,128)S(1)}, u32[]{:S(2)}, u32[]{:S(2)}) collective-permute-start(f32[512,1,128]{2,0,1:T(8,128)S(1)} %bitcast.141), channel_id=1, source_target_pairs={{0,16},{8,24},{16,0},{24,8},{1,17},{9,25},{17,1},{25,9},{2,18},{10... | collective-permute-start | bytes 786440 | tf_op jit(solution)/shard_map/ppermute | solution.py:68
  20.9 4.8 %collective-permute-start.1 = (f32[512,1,128]{2,0,1:T(8,128)S(1)}, f32[512,1,128]{2,0,1:T(8,128)S(1)}, u32[]{:S(2)}, u32[]{:S(2)}) collective-permute-start(f32[512,1,128]{2,0,1:T(8,128)S(1)} %bitcast.142), channel_id=1, source_target_pairs={{0,8},{8,0},{16,24},{24,16},{1,9},{9,1},{17,25},{25,17},{2,10},{10... | collective-permute-start | bytes 786440 | tf_op jit(solution)/shard_map/ppermute | solution.py:70
  25.7 1.5 %collective-permute-start.2 = (f32[512,1,128]{2,0,1:T(8,128)S(1)}, f32[512,1,128]{2,0,1:T(8,128)S(1)}, u32[]{:S(2)}, u32[]{:S(2)}) collective-permute-start(f32[512,1,128]{2,0,1:T(8,128)S(1)} %collective-permute-done), channel_id=1, source_target_pairs={{0,8},{8,0},{16,24},{24,16},{1,9},{9,1},{17,25},{25,17},{2,10},{10... | collective-permute-start | bytes 786440 | tf_op jit(solution)/shard_map/ppermute | solution.py:70
  25.8 19.1 %collective-permute-start.9 = (bf16[2,64,512]{2,1,0:T(8,128)(2,1)S(1)}, bf16[2,64,512]{2,1,0:T(8,128)(2,1)S(1)}, u32[]{:S(2)}, u32[]{:S(2)}) collective-permute-start(bf16[2,64,512]{2,1,0:T(8,128)(2,1)S(1)} %bitcast.150), channel_id=1, source_target_pairs={{0,1},{1,2},{2,3},{3,4},{4,5},{5,6},{6,7},{7,0},{8,9},{9,10},{10,1... | collective-permute-start | bytes 393224 | tf_op jit(solution)/shard_map/ppermute | solution.py:15
  27.2 27.7 %collective-permute-start.8 = (bf16[2,64,512]{2,1,0:T(8,128)(2,1)S(1)}, bf16[2,64,512]{2,1,0:T(8,128)(2,1)S(1)}, u32[]{:S(2)}, u32[]{:S(2)}) collective-permute-start(bf16[2,64,512]{2,1,0:T(8,128)(2,1)S(1)} %bitcast.151), channel_id=1, source_target_pairs={{0,2},{1,3},{2,4},{3,5},{4,6},{5,7},{6,0},{7,1},{8,10},{9,11},{10,... | collective-permute-start | bytes 393224 | tf_op jit(solution)/shard_map/ppermute | solution.py:15
  39.0 12.0 %collective-permute-start.6 = (bf16[2,64,512]{2,1,0:T(8,128)(2,1)S(1)}, bf16[2,64,512]{2,1,0:T(8,128)(2,1)S(1)}, u32[]{:S(2)}, u32[]{:S(2)}) collective-permute-start(bf16[2,64,512]{2,1,0:T(8,128)(2,1)S(1)} %bitcast.152), channel_id=1, source_target_pairs={{0,4},{1,5},{2,6},{3,7},{4,0},{5,1},{6,2},{7,3},{8,12},{9,13},{10,... | collective-permute-start | bytes 393224 | tf_op jit(solution)/shard_map/ppermute | solution.py:15
  42.4 11.7 %collective-permute-start.7 = (bf16[2,64,512]{2,1,0:T(8,128)(2,1)S(1)}, bf16[2,64,512]{2,1,0:T(8,128)(2,1)S(1)}, u32[]{:S(2)}, u32[]{:S(2)}) collective-permute-start(bf16[2,64,512]{2,1,0:T(8,128)(2,1)S(1)} %bitcast.153), channel_id=1, source_target_pairs={{0,3},{1,4},{2,5},{3,6},{4,7},{5,0},{6,1},{7,2},{8,11},{9,12},{10,... | collective-permute-start | bytes 393224 | tf_op jit(solution)/shard_map/ppermute | solution.py:15
  55.9 1.2 %collective-permute-start.10 = (f32[2,1,512]{2,1,0:T(1,128)S(1)}, f32[2,1,512]{2,1,0:T(1,128)S(1)}, u32[]{:S(2)}, u32[]{:S(2)}) collective-permute-start(f32[2,1,512]{2,1,0:T(1,128)S(1)} %pad_maximum_fusion.1), channel_id=1, source_target_pairs={{0,8},{8,0},{16,24},{24,16},{1,9},{9,1},{17,25},{25,17},{2,10},{10... | collective-permute-start | bytes 12296 | tf_op jit(solution)/shard_map/ppermute | solution.py:78
  57.2 3.7 %collective-permute-start.11 = (f32[2,1,512]{2,1,0:T(1,128)S(1)}, f32[2,1,512]{2,1,0:T(1,128)S(1)}, u32[]{:S(2)}, u32[]{:S(2)}) collective-permute-start(f32[2,1,512]{2,1,0:T(1,128)S(1)} %fusion.56), channel_id=1, source_target_pairs={{0,16},{8,24},{16,0},{24,8},{1,17},{9,25},{17,1},{25,9},{2,18},{10... | collective-permute-start | bytes 12296 | tf_op jit(solution)/shard_map/ppermute | solution.py:78

commit v4 on v3

--- a/solution.py
+++ b/solution.py
@@ -71,6 +71,32 @@
     return jnp.stack([jnp.stack(same_core), jnp.stack(partner)], axis=1)
 
 
+def gather_row_blocks(block, axis_name, size):
+    positions = size // 2
+    i = lax.axis_index(axis_name)
+    z = i // 2
+    y = i % 2
+    row = [block]
+    for s in range(1, positions):
+        pairs = [(p * 2 + r, ((p - s) % positions) * 2 + r) for p in range(positions) for r in range(2)]
+        row.append(lax.ppermute(block, axis_name, pairs))
+    other = lax.ppermute(jnp.stack(row), axis_name, [(j, j ^ 1) for j in range(size)])
+    out = []
+    for s in range(positions):
+        out.append((((z + s) % positions) * 2 + y, row[s]))
+        out.append((((z + s) % positions) * 2 + 1 - y, other[s]))
+    return out
+
+
+def all_sum_once(value, axis_name, size):
+    pieces = gather_shifted(value, axis_name, size)
+    stacked = jnp.roll(jnp.stack(pieces), lax.axis_index(axis_name), axis=0)
+    total = stacked[0]
+    for j in range(1, size):
+        total = total + stacked[j]
+    return total
+
+
 def all_sum(value, axis_name, size):
     step = 1
     while step < size:
@@ -99,16 +125,16 @@
     left = jnp.concatenate([field_real, field_imag], axis=1)
     right = jnp.concatenate([-field_imag, field_real], axis=1)
 
-    cap_pieces = gather_shifted(capture[0], "tile", tiles)
+    cap_pieces = gather_row_blocks(capture[0], "tile", tiles)
     own = capture.shape[2]
     focus_real = None
-    for s, piece in enumerate(cap_pieces):
+    for index, piece in cap_pieces:
         product = jnp.dot(piece[0], left, preferred_element_type=jnp.float32) + jnp.dot(
             piece[1], right, preferred_element_type=jnp.float32
         )
         w_real = product[:, :voxels]
         w_imag = product[:, voxels:]
-        start = ((k + s) % tiles) * own
+        start = index * own
         g_real = lax.dynamic_slice_in_dim(field_real, start, own, 0).astype(jnp.float32)
         g_imag = lax.dynamic_slice_in_dim(field_imag, start, own, 0).astype(jnp.float32)
         part_real = jnp.sum(g_real * w_real - g_imag * w_imag, axis=0)
@@ -135,7 +161,7 @@
     part_real = square_real * focus_real - square_imag * focus_imag
     part_imag = square_real * focus_imag + square_imag * focus_real
     partial_image = jnp.stack([part_real, part_imag])
-    return all_sum(partial_image, "freq", freqs)
+    return all_sum_once(partial_image, "freq", freqs)
 
 
 def solution(mesh):

time: 61.7 us -> 52.6 us (0.85)
  the two profiles are of different devices: /device:TPU:0 before, /device:TPU:16 now
where the time goes in v4:
time: 52.6 us; the launch traced here: 52 us
  waiting for transfers between devices  24.3 us (46%)
  starting transfers between devices  13.4 us (25%)
  other arithmetic  5.45 us (10%)
  matrix products  4.76 us (9%)
  local copies, waits for them, and re-layouts  2.93 us (6%)
  between operations  1.14 us (2%)
    all_to_all x1, waiting for transfers between devices, body(): lax.all_to_all(travel_time, 'tile', split_axis=1, concat_axis=0, tiled=True)  8.71 us
    ppermute x1, waiting for transfers between devices, gather_row_blocks(): lax.ppermute(jnp.stack(row), axis_name, [(j, j ^ 1) for j in range(size)])  7.49 us
    all_to_all x1, starting transfers between devices, body(): lax.all_to_all(travel_time, 'tile', split_axis=1, concat_axis=0, tiled=True)  6.17 us
    ppermute x1, waiting for transfers between devices, gather_columns(): same_core.append(lax.ppermute(block, axis_name, pairs))  4.83 us
    another operation x1, other arithmetic  3.85 us
    ppermute x3, starting transfers between devices, gather_row_blocks(): row.append(lax.ppermute(block, axis_name, pairs))  3.83 us
    ppermute x3, waiting for transfers between devices, gather_shifted(): pieces.append(lax.ppermute(block, axis_name, pairs))  2.86 us
    dot_general x8, matrix products, body(): jnp.dot(piece[0], left, preferred_element_type=jnp.float32)  2.4 us
  transfers between devices with their start and end apart: 11, of which 7 were waited for; matrix products, arithmetic and copies ran while one was open for 12% of the time, Pallas kernels for 0%

profile of v4, /device:TPU:16, one launch (start us, length us, event | category | flops | bytes accessed | tf_op | source)
XLA Modules:
  0.0 52.0 jit_solution(12720232852777947215)
XLA Ops:
  0.0 1.7 %copy.14 = f32[64,8,128]{2,0,1:T(8,128)} copy(f32[64,8,128]{2,1,0:T(8,128)} %param.5) | data formatting | bytes 524288 | tf_op args[0]
  1.7 6.2 %all-to-all-start = ((f32[64,8,128]{2,0,1:T(8,128)}), f32[64,8,128]{2,0,1:T(8,128)S(1)}, u32[]{:S(2)}, u32[]{:S(2)}) async-start(f32[64,8,128]{2,0,1:T(8,128)} %copy.14), calls=%async_computation | async-start | bytes 524288 | tf_op jit(solution)/shard_map/all_to_all | solution.py:115
  7.9 0.6 %collective-permute-start.3 = (bf16[2,64,512]{2,1,0:T(8,128)(2,1)S(1)}, bf16[2,64,512]{2,1,0:T(8,128)(2,1)S(1)}, u32[]{:S(2)}, u32[]{:S(2)}) collective-permute-start(bf16[2,64,512]{2,1,0:T(8,128)(2,1)S(1)} %bitcast.156), channel_id=1, source_target_pairs={{0,6},{1,7},{2,0},{3,1},{4,2},{5,3},{6,4},{7,5},{8,14},{9,15},{10,... | collective-permute-start | bytes 393224 | tf_op jit(solution)/shard_map/ppermute | solution.py:82
  8.5 3.3 %collective-permute-start.4 = (bf16[2,64,512]{2,1,0:T(8,128)(2,1)S(1)}, bf16[2,64,512]{2,1,0:T(8,128)(2,1)S(1)}, u32[]{:S(2)}, u32[]{:S(2)}) collective-permute-start(bf16[2,64,512]{2,1,0:T(8,128)(2,1)S(1)} %bitcast.157), channel_id=1, source_target_pairs={{0,4},{1,5},{2,6},{3,7},{4,0},{5,1},{6,2},{7,3},{8,12},{9,13},{10,... | collective-permute-start | bytes 393224 | tf_op jit(solution)/shard_map/ppermute | solution.py:82
  11.7 0.0 collective-permute-start.5
  11.7 8.7 %all-to-all-done = f32[64,8,128]{2,0,1:T(8,128)S(1)} async-done(((f32[64,8,128]{2,0,1:T(8,128)}), f32[64,8,128]{2,0,1:T(8,128)S(1)}, u32[]{:S(2)}, u32[]{:S(2)}) %all-to-all-start) | async-done | bytes 262176 | tf_op jit(solution)/shard_map/all_to_all | solution.py:115
  20.4 1.5 %collective-permute-start = (f32[512,1,128]{2,0,1:T(8,128)S(1)}, f32[512,1,128]{2,0,1:T(8,128)S(1)}, u32[]{:S(2)}, u32[]{:S(2)}) collective-permute-start(f32[512,1,128]{2,0,1:T(8,128)S(1)} %bitcast.150), channel_id=1, source_target_pairs={{0,16},{8,24},{16,0},{24,8},{1,17},{9,25},{17,1},{25,9},{2,18},{10... | collective-permute-start | bytes 786440 | tf_op jit(solution)/shard_map/ppermute | solution.py:68
  21.9 0.1 select_reduce_fusion.1
  22.1 0.1 collective-permute-start.1
  22.1 4.8 %collective-permute-done = f32[512,1,128]{2,0,1:T(8,128)S(1)} collective-permute-done((f32[512,1,128]{2,0,1:T(8,128)S(1)}, f32[512,1,128]{2,0,1:T(8,128)S(1)}, u32[]{:S(2)}, u32[]{:S(2)}) %collective-permute-start) | collective-permute-done | bytes 262176 | tf_op jit(solution)/shard_map/ppermute | solution.py:68
  27.8 0.0 collective-permute-done.3
  27.8 0.0 collective-permute-done.5
  27.8 0.1 pad_maximum_fusion.1
  27.9 0.1 collective-permute-start.6
  28.1 0.4 collective-permute-done.2
  28.5 3.8 %negate_convert_fusion = (bf16[2,2,512,1,128]{4,2,0,3,1:T(8,128)(2,1)S(1)}, bf16[2,2,512,1,128]{4,2,0,3,1:T(8,128)(2,1)S(1)}) fusion(f32[2,1,512,1,128]{4,2,0,3,1:T(8,128)S(1)} %maximum_bitcast_fusion.1, f32[2,1,512,1,128]{4,2,0,3,1:T(8,128)S(1)} %maximum_bitcast_fusion, f32[]{:T(128)} %bitcast.4), kind=kLoop, calls=%fused_computation.14 | loop fusion | flops 1310720 | bytes 2097156 | tf_op jit(solution)/shard_map/convert
  32.4 0.4 copy.16
  32.8 0.1 constant_dynamic-update-slice_fusion.1
  32.9 0.1 copy.30
  33.1 0.4 copy.18
  33.5 0.2 constant_dynamic-update-slice_fusion
  33.7 0.3 fusion.39
  34.0 0.1 copy.29
  34.1 0.3 fusion.44
  34.4 0.3 fusion.3
  34.7 7.5 %collective-permute-done.6 = bf16[4,2,64,512]{3,2,1,0:T(8,128)(2,1)S(1)} collective-permute-done((bf16[4,2,64,512]{3,2,1,0:T(8,128)(2,1)S(1)}, bf16[4,2,64,512]{3,2,1,0:T(8,128)(2,1)S(1)}, u32[]{:S(2)}, u32[]{:S(2)}) %collective-permute-start.6) | collective-permute-done | bytes 524320 | tf_op jit(solution)/shard_map/ppermute | solution.py:83
  42.2 0.3 fusion.38
  42.5 0.3 convolution_add_fusion.5
  42.8 0.3 fusion.1
  43.1 0.2 fusion.7
  43.3 0.3 fusion.36
  43.6 0.3 fusion.40
  43.9 0.3 fusion.42
  44.2 0.3 fusion.37
  44.4 0.3 fusion.41
  44.7 0.3 convolution_add_fusion.4
  45.1 0.3 convolution_add_fusion.6
  45.4 0.3 convolution_add_fusion.7
  45.7 0.3 fusion
  46.0 0.3 fusion.2
  46.3 0.3 fusion.11
  46.7 0.7 %collective-permute-start.7 = (f32[2,1,512]{2,1,0:T(1,128)S(1)}, f32[2,1,512]{2,1,0:T(1,128)S(1)}, u32[]{:S(2)}, u32[]{:S(2)}) collective-permute-start(f32[2,1,512]{2,1,0:T(1,128)S(1)} %pad_maximum_fusion.2), channel_id=1, source_target_pairs={{0,24},{8,0},{16,8},{24,16},{1,25},{9,1},{17,9},{25,17},{2,26},{10... | collective-permute-start | bytes 12296 | tf_op jit(solution)/shard_map/ppermute | solution.py:15
  47.4 0.9 %collective-permute-start.8 = (f32[2,1,512]{2,1,0:T(1,128)S(1)}, f32[2,1,512]{2,1,0:T(1,128)S(1)}, u32[]{:S(2)}, u32[]{:S(2)}) collective-permute-start(f32[2,1,512]{2,1,0:T(1,128)S(1)} %pad_maximum_fusion.2), channel_id=1, source_target_pairs={{0,16},{8,24},{16,0},{24,8},{1,17},{9,25},{17,1},{25,9},{2,18},{10... | collective-permute-start | bytes 12296 | tf_op jit(solution)/shard_map/ppermute | solution.py:15
  48.3 0.2 collective-permute-start.9
  48.5 0.2 collective-permute-done.7
  48.7 2.3 %collective-permute-done.8 = f32[2,1,512]{2,1,0:T(1,128)S(1)} collective-permute-done((f32[2,1,512]{2,1,0:T(1,128)S(1)}, f32[2,1,512]{2,1,0:T(1,128)S(1)}, u32[]{:S(2)}, u32[]{:S(2)}) %collective-permute-start.8) | collective-permute-done | bytes 4128 | tf_op jit(solution)/shard_map/ppermute | solution.py:15
  51.0 0.3 collective-permute-done.9
  51.4 0.6 %fusion.49 = f32[2,1,512]{2,1,0:T(1,128)} fusion(f32[8,2,1,512]{3,2,1,0:T(1,128)S(1)} %constant_dynamic-update-slice_fusion.2, s32[]{:T(128)S(6)} %add.477, s32[]{:T(128)S(6)} %select_n.152, s32[]{:T(128)S(6)} %add.475, s32[]{:T(128)S(6)} %add.476), kind=kLoop, calls=%fused_computation.135 | loop fusion | flops 3072 | bytes 20496 | tf_op jit(solution)/shard_map/add | solution.py:96
  (29 shorter events, 0.3 us)
Async XLA Ops:
  0.0 7.9 %copy-start = (bf16[1,2,64,512]{3,2,1,0:T(8,128)(2,1)S(1)}, bf16[1,2,64,512]{3,2,1,0:T(8,128)(2,1)}, u32[]{:S(2)}) copy-start(bf16[1,2,64,512]{3,2,1,0:T(8,128)(2,1)} %param.9) | copy-start | bytes 393220
  0.0 21.9 %copy-start.2 = (f32[1,2,64]{2,1,0:T(2,128)S(1)}, f32[1,2,64]{2,1,0:T(2,128)}, u32[]{:S(2)}) copy-start(f32[1,2,64]{2,1,0:T(2,128)} %param.8) | copy-start | bytes 1540
  0.0 21.9 %copy-start.1 = (s32[1,512]{1,0:T(1,128)S(1)}, s32[1,512]{1,0:T(1,128)}, u32[]{:S(2)}) copy-start(s32[1,512]{1,0:T(1,128)} %param.6) | copy-start | bytes 6148
  1.7 18.7 %all-to-all-start = ((f32[64,8,128]{2,0,1:T(8,128)}), f32[64,8,128]{2,0,1:T(8,128)S(1)}, u32[]{:S(2)}, u32[]{:S(2)}) async-start(f32[64,8,128]{2,0,1:T(8,128)} %copy.14), calls=%async_computation | async-start | bytes 524288 | tf_op jit(solution)/shard_map/all_to_all | solution.py:115
  7.9 19.9 %collective-permute-start.3 = (bf16[2,64,512]{2,1,0:T(8,128)(2,1)S(1)}, bf16[2,64,512]{2,1,0:T(8,128)(2,1)S(1)}, u32[]{:S(2)}, u32[]{:S(2)}) collective-permute-start(bf16[2,64,512]{2,1,0:T(8,128)(2,1)S(1)} %bitcast.156), channel_id=1, source_target_pairs={{0,6},{1,7},{2,0},{3,1},{4,2},{5,3},{6,4},{7,5},{8,14},{9,15},{10,... | collective-permute-start | bytes 393224 | tf_op jit(solution)/shard_map/ppermute | solution.py:82
  8.5 19.4 %collective-permute-start.4 = (bf16[2,64,512]{2,1,0:T(8,128)(2,1)S(1)}, bf16[2,64,512]{2,1,0:T(8,128)(2,1)S(1)}, u32[]{:S(2)}, u32[]{:S(2)}) collective-permute-start(bf16[2,64,512]{2,1,0:T(8,128)(2,1)S(1)} %bitcast.157), channel_id=1, source_target_pairs={{0,4},{1,5},{2,6},{3,7},{4,0},{5,1},{6,2},{7,3},{8,12},{9,13},{10,... | collective-permute-start | bytes 393224 | tf_op jit(solution)/shard_map/ppermute | solution.py:82
  11.7 16.1 %collective-permute-start.5 = (bf16[2,64,512]{2,1,0:T(8,128)(2,1)S(1)}, bf16[2,64,512]{2,1,0:T(8,128)(2,1)S(1)}, u32[]{:S(2)}, u32[]{:S(2)}) collective-permute-start(bf16[2,64,512]{2,1,0:T(8,128)(2,1)S(1)} %bitcast.158), channel_id=1, source_target_pairs={{0,2},{1,3},{2,4},{3,5},{4,6},{5,7},{6,0},{7,1},{8,10},{9,11},{10,... | collective-permute-start | bytes 393224 | tf_op jit(solution)/shard_map/ppermute | solution.py:82
  20.4 6.5 %collective-permute-start = (f32[512,1,128]{2,0,1:T(8,128)S(1)}, f32[512,1,128]{2,0,1:T(8,128)S(1)}, u32[]{:S(2)}, u32[]{:S(2)}) collective-permute-start(f32[512,1,128]{2,0,1:T(8,128)S(1)} %bitcast.150), channel_id=1, source_target_pairs={{0,16},{8,24},{16,0},{24,8},{1,17},{9,25},{17,1},{25,9},{2,18},{10... | collective-permute-start | bytes 786440 | tf_op jit(solution)/shard_map/ppermute | solution.py:68
  22.1 6.0 %collective-permute-start.1 = (f32[512,1,128]{2,0,1:T(8,128)S(1)}, f32[512,1,128]{2,0,1:T(8,128)S(1)}, u32[]{:S(2)}, u32[]{:S(2)}) collective-permute-start(f32[512,1,128]{2,0,1:T(8,128)S(1)} %bitcast.151), channel_id=1, source_target_pairs={{0,8},{8,0},{16,24},{24,16},{1,9},{9,1},{17,25},{25,17},{2,10},{10... | collective-permute-start | bytes 786440 | tf_op jit(solution)/shard_map/ppermute | solution.py:70
  27.0 1.5 %collective-permute-start.2 = (f32[512,1,128]{2,0,1:T(8,128)S(1)}, f32[512,1,128]{2,0,1:T(8,128)S(1)}, u32[]{:S(2)}, u32[]{:S(2)}) collective-permute-start(f32[512,1,128]{2,0,1:T(8,128)S(1)} %collective-permute-done), channel_id=1, source_target_pairs={{0,8},{8,0},{16,24},{24,16},{1,9},{9,1},{17,25},{25,17},{2,10},{10... | collective-permute-start | bytes 786440 | tf_op jit(solution)/shard_map/ppermute | solution.py:70
  27.9 14.2 %collective-permute-start.6 = (bf16[4,2,64,512]{3,2,1,0:T(8,128)(2,1)S(1)}, bf16[4,2,64,512]{3,2,1,0:T(8,128)(2,1)S(1)}, u32[]{:S(2)}, u32[]{:S(2)}) collective-permute-start(bf16[4,2,64,512]{3,2,1,0:T(8,128)(2,1)S(1)} %pad_maximum_fusion.1), channel_id=1, source_target_pairs={{0,1},{1,0},{2,3},{3,2},{4,5},{5,4},{6,7},{7,6},{8,9},{9,8},{10,11... | collective-permute-start | bytes 1572872 | tf_op jit(solution)/shard_map/ppermute | solution.py:83
  46.7 2.0 %collective-permute-start.7 = (f32[2,1,512]{2,1,0:T(1,128)S(1)}, f32[2,1,512]{2,1,0:T(1,128)S(1)}, u32[]{:S(2)}, u32[]{:S(2)}) collective-permute-start(f32[2,1,512]{2,1,0:T(1,128)S(1)} %pad_maximum_fusion.2), channel_id=1, source_target_pairs={{0,24},{8,0},{16,8},{24,16},{1,25},{9,1},{17,9},{25,17},{2,26},{10... | collective-permute-start | bytes 12296 | tf_op jit(solution)/shard_map/ppermute | solution.py:15
  47.4 3.6 %collective-permute-start.8 = (f32[2,1,512]{2,1,0:T(1,128)S(1)}, f32[2,1,512]{2,1,0:T(1,128)S(1)}, u32[]{:S(2)}, u32[]{:S(2)}) collective-permute-start(f32[2,1,512]{2,1,0:T(1,128)S(1)} %pad_maximum_fusion.2), channel_id=1, source_target_pairs={{0,16},{8,24},{16,0},{24,8},{1,17},{9,25},{17,1},{25,9},{2,18},{10... | collective-permute-start | bytes 12296 | tf_op jit(solution)/shard_map/ppermute | solution.py:15
  48.3 3.0 %collective-permute-start.9 = (f32[2,1,512]{2,1,0:T(1,128)S(1)}, f32[2,1,512]{2,1,0:T(1,128)S(1)}, u32[]{:S(2)}, u32[]{:S(2)}) collective-permute-start(f32[2,1,512]{2,1,0:T(1,128)S(1)} %pad_maximum_fusion.2), channel_id=1, source_target_pairs={{0,8},{8,16},{16,24},{24,0},{1,9},{9,17},{17,25},{25,1},{2,10},{10... | collective-permute-start | bytes 12296 | tf_op jit(solution)/shard_map/ppermute | solution.py:15

commit v5 on v4

--- a/solution.py
+++ b/solution.py
@@ -125,25 +125,43 @@
     left = jnp.concatenate([field_real, field_imag], axis=1)
     right = jnp.concatenate([-field_imag, field_real], axis=1)
 
-    cap_pieces = gather_row_blocks(capture[0], "tile", tiles)
-    own = capture.shape[2]
-    focus_real = None
-    for index, piece in cap_pieces:
-        product = jnp.dot(piece[0], left, preferred_element_type=jnp.float32) + jnp.dot(
-            piece[1], right, preferred_element_type=jnp.float32
+    positions = tiles // 2
+    z = k // 2
+    y = k % 2
+    row = [capture[0]]
+    for s in range(1, positions):
+        pairs = [(p * 2 + r, ((p - s) % positions) * 2 + r) for p in range(positions) for r in range(2)]
+        row.append(lax.ppermute(capture[0], "tile", pairs))
+    row = jnp.stack(row)
+    other = lax.ppermute(row, "tile", [(j, j ^ 1) for j in range(tiles)])
+
+    def partial_focus(group, which_row):
+        own = group.shape[2]
+        cap_real = group[:, 0].reshape(-1, group.shape[-1])
+        cap_imag = group[:, 1].reshape(-1, group.shape[-1])
+        product = jnp.dot(cap_real, left, preferred_element_type=jnp.float32) + jnp.dot(
+            cap_imag, right, preferred_element_type=jnp.float32
         )
         w_real = product[:, :voxels]
         w_imag = product[:, voxels:]
-        start = index * own
-        g_real = lax.dynamic_slice_in_dim(field_real, start, own, 0).astype(jnp.float32)
-        g_imag = lax.dynamic_slice_in_dim(field_imag, start, own, 0).astype(jnp.float32)
+
+        def rows_of(field):
+            grid = field.reshape(positions, 2, own, voxels)
+            picked = lax.dynamic_index_in_dim(grid, which_row, 1, keepdims=False)
+            picked = jnp.roll(picked, -z, axis=0)
+            return picked.reshape(-1, voxels).astype(jnp.float32)
+
+        g_real = rows_of(field_real)
+        g_imag = rows_of(field_imag)
         part_real = jnp.sum(g_real * w_real - g_imag * w_imag, axis=0)
         part_imag = jnp.sum(g_real * w_imag + g_imag * w_real, axis=0)
-        if focus_real is None:
-            focus_real, focus_imag = part_real, part_imag
-        else:
-            focus_real = focus_real + part_real
-            focus_imag = focus_imag + part_imag
+        return part_real, part_imag
+
+    mine_real, mine_imag = partial_focus(row, y)
+    mine_real, mine_imag, other = lax.optimization_barrier((mine_real, mine_imag, other))
+    theirs_real, theirs_imag = partial_focus(other, 1 - y)
+    focus_real = mine_real + theirs_real
+    focus_imag = mine_imag + theirs_imag
 
     outer = freqs // 2
     focus = jnp.stack([focus_real, focus_imag]).reshape(2, row_count, outer, 2, width)

time: 52.6 us -> 50.2 us (0.954)
  the two profiles are of different devices: /device:TPU:16 before, /device:TPU:0 now
where the time goes in v5:
time: 50.2 us; the launch traced here: 49.9 us
  waiting for transfers between devices  17.6 us (35%)
  starting transfers between devices  17.5 us (35%)
  local copies, waits for them, and re-layouts  6.23 us (12%)
  other arithmetic  5.73 us (11%)
  matrix products  1.87 us (4%)
  between operations  0.95 us (2%)
    ppermute x3, waiting for transfers between devices, body(): row.append(lax.ppermute(capture[0], 'tile', pairs))  7.73 us
    all_to_all x1, starting transfers between devices, body(): lax.all_to_all(travel_time, 'tile', split_axis=1, concat_axis=0, tiled=True)  7.28 us
    all_to_all x1, waiting for transfers between devices, body(): lax.all_to_all(travel_time, 'tile', split_axis=1, concat_axis=0, tiled=True)  5.17 us
    ppermute x3, starting transfers between devices, body(): row.append(lax.ppermute(capture[0], 'tile', pairs))  4.94 us
    another operation x1, other arithmetic  3.84 us
    ppermute x3, waiting for transfers between devices, gather_shifted(): pieces.append(lax.ppermute(block, axis_name, pairs))  2.86 us
    unnamed x14, local copies, waits for them, and re-layouts  2.6 us
    slice x2, local copies, waits for them, and re-layouts, partial_focus(): cap_imag = group[:, 1].reshape(-1, group.shape[-1])  1.81 us
  transfers between devices with their start and end apart: 11, of which 7 were waited for; matrix products, arithmetic and copies ran while one was open for 16% of the time, Pallas kernels for 0%

profile of v5, /device:TPU:0, one launch (start us, length us, event | category | flops | bytes accessed | tf_op | source)
XLA Modules:
  0.0 49.9 jit_solution(14512227754037219837)
XLA Ops:
  0.0 1.7 %copy.15 = f32[64,8,128]{2,0,1:T(8,128)} copy(f32[64,8,128]{2,1,0:T(8,128)} %param.7) | data formatting | bytes 524288 | tf_op args[0]
  1.7 7.3 %all-to-all-start = ((f32[64,8,128]{2,0,1:T(8,128)}), f32[64,8,128]{2,0,1:T(8,128)S(1)}, u32[]{:S(2)}, u32[]{:S(2)}) async-start(f32[64,8,128]{2,0,1:T(8,128)} %copy.15), calls=%async_computation | async-start | bytes 524288 | tf_op jit(solution)/shard_map/all_to_all | solution.py:115
  9.0 0.0 copy-done.1
  9.0 3.8 %collective-permute-start.3 = (bf16[2,64,512]{2,1,0:T(8,128)(2,1)S(1)}, bf16[2,64,512]{2,1,0:T(8,128)(2,1)S(1)}, u32[]{:S(2)}, u32[]{:S(2)}) collective-permute-start(bf16[2,64,512]{2,1,0:T(8,128)(2,1)S(1)} %bitcast.109), channel_id=1, source_target_pairs={{0,6},{1,7},{2,0},{3,1},{4,2},{5,3},{6,4},{7,5},{8,14},{9,15},{10,... | collective-permute-start | bytes 393224 | tf_op jit(solution)/shard_map/ppermute | solution.py:134
  12.9 0.0 collective-permute-start.4
  12.9 1.1 %collective-permute-start.5 = (bf16[2,64,512]{2,1,0:T(8,128)(2,1)S(1)}, bf16[2,64,512]{2,1,0:T(8,128)(2,1)S(1)}, u32[]{:S(2)}, u32[]{:S(2)}) collective-permute-start(bf16[2,64,512]{2,1,0:T(8,128)(2,1)S(1)} %bitcast.111), channel_id=1, source_target_pairs={{0,2},{1,3},{2,4},{3,5},{4,6},{5,7},{6,0},{7,1},{8,10},{9,11},{10,... | collective-permute-start | bytes 393224 | tf_op jit(solution)/shard_map/ppermute | solution.py:134
  14.7 0.0 copy-done.3
  14.7 0.1 select_reduce_fusion.1
  14.8 5.2 %all-to-all-done = f32[64,8,128]{2,0,1:T(8,128)S(1)} async-done(((f32[64,8,128]{2,0,1:T(8,128)}), f32[64,8,128]{2,0,1:T(8,128)S(1)}, u32[]{:S(2)}, u32[]{:S(2)}) %all-to-all-start) | async-done | bytes 262176 | tf_op jit(solution)/shard_map/all_to_all | solution.py:115
  20.0 1.5 %collective-permute-start = (f32[512,1,128]{2,0,1:T(8,128)S(1)}, f32[512,1,128]{2,0,1:T(8,128)S(1)}, u32[]{:S(2)}, u32[]{:S(2)}) collective-permute-start(f32[512,1,128]{2,0,1:T(8,128)S(1)} %bitcast.99), channel_id=1, source_target_pairs={{0,16},{8,24},{16,0},{24,8},{1,17},{9,25},{17,1},{25,9},{2,18},{10... | collective-permute-start | bytes 786440 | tf_op jit(solution)/shard_map/ppermute | solution.py:68
  21.5 0.0 collective-permute-done.3
  21.5 7.7 %collective-permute-done.4 = bf16[2,64,512]{2,1,0:T(8,128)(2,1)S(1)} collective-permute-done((bf16[2,64,512]{2,1,0:T(8,128)(2,1)S(1)}, bf16[2,64,512]{2,1,0:T(8,128)(2,1)S(1)}, u32[]{:S(2)}, u32[]{:S(2)}) %collective-permute-start.4) | collective-permute-done | bytes 131104 | tf_op jit(solution)/shard_map/ppermute | solution.py:134
  29.2 0.0 collective-permute-done.5
  29.2 0.1 pad_maximum_fusion.6
  29.3 1.5 %collective-permute-start.6 = (bf16[4,2,64,512]{3,2,1,0:T(8,128)(2,1)S(1)}, bf16[4,2,64,512]{3,2,1,0:T(8,128)(2,1)}, u32[]{:S(2)}, u32[]{:S(2)}) collective-permute-start(bf16[4,2,64,512]{3,2,1,0:T(8,128)(2,1)S(1)} %pad_maximum_fusion.6), channel_id=1, source_target_pairs={{0,1},{1,0},{2,3},{3,2},{4,5},{5,4},{6,7},{7,6},{8,9},{9,8},{10,11... | collective-permute-start | bytes 1572872 | tf_op jit(solution)/shard_map/ppermute | solution.py:136
  30.8 0.0 collective-permute-start.1
  30.8 0.0 collective-permute-done
  30.8 0.5 %collective-permute-start.2 = (f32[512,1,128]{2,0,1:T(8,128)S(1)}, f32[512,1,128]{2,0,1:T(8,128)S(1)}, u32[]{:S(2)}, u32[]{:S(2)}) collective-permute-start(f32[512,1,128]{2,0,1:T(8,128)S(1)} %collective-permute-done), channel_id=1, source_target_pairs={{0,8},{8,0},{16,24},{24,16},{1,9},{9,1},{17,25},{25,17},{2,10},{10... | collective-permute-start | bytes 786440 | tf_op jit(solution)/shard_map/ppermute | solution.py:70
  31.3 0.7 %fusion.27 = (bf16[4,1,64,512]{3,2,1,0:T(8,128)(2,1)S(1)}, bf16[4,1,64,512]{3,2,1,0:T(8,128)(2,1)}) fusion(bf16[4,2,64,512]{3,2,1,0:T(8,128)(2,1)S(1)} %pad_maximum_fusion.6), kind=kLoop, calls=%fused_computation.86 | loop fusion | bytes 1048576 | tf_op jit(solution)/shard_map/slice | solution.py:141
  32.1 0.2 collective-permute-done.1
  32.3 0.4 collective-permute-done.2
  32.7 3.8 %cosine_convert_fusion = (bf16[2,2,512,1,128]{4,2,0,3,1:T(8,128)(2,1)S(1)}, bf16[2,2,512,1,128]{4,2,0,3,1:T(8,128)(2,1)S(1)}) fusion(f32[2,1,512,1,128]{4,2,0,3,1:T(8,128)S(1)} %maximum_bitcast_fusion.1, f32[2,1,512,1,128]{4,2,0,3,1:T(8,128)S(1)} %maximum_bitcast_fusion, f32[]{:T(128)} %bitcast.4), kind=kLoop, calls=%fused_computation.6 | loop fusion | flops 1310720 | bytes 2097156 | tf_op jit(solution)/shard_map/convert.7
  36.6 0.4 copy.17
  37.0 0.2 copy.18
  37.3 0.4 copy.21
  37.7 0.2 copy.20
  37.9 0.2 convert_element_type.50
  38.2 0.2 convert_element_type.55
  38.4 0.0 copy-start
  38.5 0.1 bitcast_negate_fusion
  38.5 0.8 %copy-done = bf16[4,1,64,512]{3,2,1,0:T(8,128)(2,1)S(1)} copy-done((bf16[4,1,64,512]{3,2,1,0:T(8,128)(2,1)S(1)}, bf16[4,1,64,512]{3,2,1,0:T(8,128)(2,1)}, u32[]{:S(2)}) %copy-start) | copy-done | bytes 262168
  39.4 0.5 fusion.1
  39.8 0.2 fusion.12
  40.0 0.5 convolution_add_fusion.1
  40.5 0.2 fusion.5
  40.8 1.2 %collective-permute-done.6 = bf16[4,2,64,512]{3,2,1,0:T(8,128)(2,1)} collective-permute-done((bf16[4,2,64,512]{3,2,1,0:T(8,128)(2,1)S(1)}, bf16[4,2,64,512]{3,2,1,0:T(8,128)(2,1)}, u32[]{:S(2)}, u32[]{:S(2)}) %collective-permute-start.6) | collective-permute-done | bytes 524320 | tf_op jit(solution)/shard_map/ppermute | solution.py:136
  42.0 1.1 %fusion.26 = (bf16[4,1,64,512]{3,2,1,0:T(8,128)(2,1)S(1)}, bf16[4,1,64,512]{3,2,1,0:T(8,128)(2,1)S(1)}) fusion(bf16[4,2,64,512]{3,2,1,0:T(8,128)(2,1)} %collective-permute-done.6), kind=kLoop, calls=%fused_computation.85 | loop fusion | bytes 1048576 | tf_op jit(solution)/shard_map/slice | solution.py:141
  43.1 0.5 fusion
  43.5 0.2 fusion.10
  43.7 0.5 convolution_add_fusion
  44.2 0.2 fusion.9
  44.6 0.1 collective-permute-start.7
  44.7 1.5 %collective-permute-start.8 = (f32[2,1,512]{2,1,0:T(1,128)S(1)}, f32[2,1,512]{2,1,0:T(1,128)S(1)}, u32[]{:S(2)}, u32[]{:S(2)}) collective-permute-start(f32[2,1,512]{2,1,0:T(1,128)S(1)} %pad_maximum_fusion.7), channel_id=1, source_target_pairs={{0,16},{8,24},{16,0},{24,8},{1,17},{9,25},{17,1},{25,9},{2,18},{10... | collective-permute-start | bytes 12296 | tf_op jit(solution)/shard_map/ppermute | solution.py:15
  46.2 0.2 collective-permute-start.9
  46.4 0.0 collective-permute-done.7
  46.4 1.9 %collective-permute-done.8 = f32[2,1,512]{2,1,0:T(1,128)S(1)} collective-permute-done((f32[2,1,512]{2,1,0:T(1,128)S(1)}, f32[2,1,512]{2,1,0:T(1,128)S(1)}, u32[]{:S(2)}, u32[]{:S(2)}) %collective-permute-start.8) | collective-permute-done | bytes 4128 | tf_op jit(solution)/shard_map/ppermute | solution.py:15
  48.3 0.9 %collective-permute-done.9 = f32[2,1,512]{2,1,0:T(1,128)S(1)} collective-permute-done((f32[2,1,512]{2,1,0:T(1,128)S(1)}, f32[2,1,512]{2,1,0:T(1,128)S(1)}, u32[]{:S(2)}, u32[]{:S(2)}) %collective-permute-start.9) | collective-permute-done | bytes 4128 | tf_op jit(solution)/shard_map/ppermute | solution.py:15
  49.3 0.6 %fusion.15 = f32[2,1,512]{2,1,0:T(1,128)} fusion(f32[8,2,1,512]{3,2,1,0:T(1,128)S(1)} %constant_dynamic-update-slice_fusion, s32[]{:T(128)S(6)} %add.159, s32[]{:T(128)S(6)} %add.158, s32[]{:T(128)S(6)} %add.157, s32[]{:T(128)S(6)} %select_n.102), kind=kLoop, calls=%fused_computation.66 | loop fusion | flops 3072 | bytes 20496 | tf_op jit(solution)/shard_map/add | solution.py:96
  (27 shorter events, 0.4 us)
Async XLA Ops:
  0.0 9.0 %copy-start.1 = (bf16[1,2,64,512]{3,2,1,0:T(8,128)(2,1)S(1)}, bf16[1,2,64,512]{3,2,1,0:T(8,128)(2,1)}, u32[]{:S(2)}) copy-start(bf16[1,2,64,512]{3,2,1,0:T(8,128)(2,1)} %param.11) | copy-start | bytes 393220
  0.0 14.7 %copy-start.3 = (f32[1,2,64]{2,1,0:T(2,128)S(1)}, f32[1,2,64]{2,1,0:T(2,128)}, u32[]{:S(2)}) copy-start(f32[1,2,64]{2,1,0:T(2,128)} %param.10) | copy-start | bytes 1540
  0.0 14.7 %copy-start.2 = (s32[1,512]{1,0:T(1,128)S(1)}, s32[1,512]{1,0:T(1,128)}, u32[]{:S(2)}) copy-start(s32[1,512]{1,0:T(1,128)} %param.8) | copy-start | bytes 6148
  1.7 18.2 %all-to-all-start = ((f32[64,8,128]{2,0,1:T(8,128)}), f32[64,8,128]{2,0,1:T(8,128)S(1)}, u32[]{:S(2)}, u32[]{:S(2)}) async-start(f32[64,8,128]{2,0,1:T(8,128)} %copy.15), calls=%async_computation | async-start | bytes 524288 | tf_op jit(solution)/shard_map/all_to_all | solution.py:115
  9.0 12.4 %collective-permute-start.3 = (bf16[2,64,512]{2,1,0:T(8,128)(2,1)S(1)}, bf16[2,64,512]{2,1,0:T(8,128)(2,1)S(1)}, u32[]{:S(2)}, u32[]{:S(2)}) collective-permute-start(bf16[2,64,512]{2,1,0:T(8,128)(2,1)S(1)} %bitcast.109), channel_id=1, source_target_pairs={{0,6},{1,7},{2,0},{3,1},{4,2},{5,3},{6,4},{7,5},{8,14},{9,15},{10,... | collective-permute-start | bytes 393224 | tf_op jit(solution)/shard_map/ppermute | solution.py:134
  12.9 16.3 %collective-permute-start.4 = (bf16[2,64,512]{2,1,0:T(8,128)(2,1)S(1)}, bf16[2,64,512]{2,1,0:T(8,128)(2,1)S(1)}, u32[]{:S(2)}, u32[]{:S(2)}) collective-permute-start(bf16[2,64,512]{2,1,0:T(8,128)(2,1)S(1)} %bitcast.110), channel_id=1, source_target_pairs={{0,4},{1,5},{2,6},{3,7},{4,0},{5,1},{6,2},{7,3},{8,12},{9,13},{10,... | collective-permute-start | bytes 393224 | tf_op jit(solution)/shard_map/ppermute | solution.py:134
  12.9 16.3 %collective-permute-start.5 = (bf16[2,64,512]{2,1,0:T(8,128)(2,1)S(1)}, bf16[2,64,512]{2,1,0:T(8,128)(2,1)S(1)}, u32[]{:S(2)}, u32[]{:S(2)}) collective-permute-start(bf16[2,64,512]{2,1,0:T(8,128)(2,1)S(1)} %bitcast.111), channel_id=1, source_target_pairs={{0,2},{1,3},{2,4},{3,5},{4,6},{5,7},{6,0},{7,1},{8,10},{9,11},{10,... | collective-permute-start | bytes 393224 | tf_op jit(solution)/shard_map/ppermute | solution.py:134
  20.0 10.8 %collective-permute-start = (f32[512,1,128]{2,0,1:T(8,128)S(1)}, f32[512,1,128]{2,0,1:T(8,128)S(1)}, u32[]{:S(2)}, u32[]{:S(2)}) collective-permute-start(f32[512,1,128]{2,0,1:T(8,128)S(1)} %bitcast.99), channel_id=1, source_target_pairs={{0,16},{8,24},{16,0},{24,8},{1,17},{9,25},{17,1},{25,9},{2,18},{10... | collective-permute-start | bytes 786440 | tf_op jit(solution)/shard_map/ppermute | solution.py:68
  29.3 12.7 %collective-permute-start.6 = (bf16[4,2,64,512]{3,2,1,0:T(8,128)(2,1)S(1)}, bf16[4,2,64,512]{3,2,1,0:T(8,128)(2,1)}, u32[]{:S(2)}, u32[]{:S(2)}) collective-permute-start(bf16[4,2,64,512]{3,2,1,0:T(8,128)(2,1)S(1)} %pad_maximum_fusion.6), channel_id=1, source_target_pairs={{0,1},{1,0},{2,3},{3,2},{4,5},{5,4},{6,7},{7,6},{8,9},{9,8},{10,11... | collective-permute-start | bytes 1572872 | tf_op jit(solution)/shard_map/ppermute | solution.py:136
  30.8 1.5 %collective-permute-start.1 = (f32[512,1,128]{2,0,1:T(8,128)S(1)}, f32[512,1,128]{2,0,1:T(8,128)S(1)}, u32[]{:S(2)}, u32[]{:S(2)}) collective-permute-start(f32[512,1,128]{2,0,1:T(8,128)S(1)} %bitcast.100), channel_id=1, source_target_pairs={{0,8},{8,0},{16,24},{24,16},{1,9},{9,1},{17,25},{25,17},{2,10},{10... | collective-permute-start | bytes 786440 | tf_op jit(solution)/shard_map/ppermute | solution.py:70
  30.8 1.9 %collective-permute-start.2 = (f32[512,1,128]{2,0,1:T(8,128)S(1)}, f32[512,1,128]{2,0,1:T(8,128)S(1)}, u32[]{:S(2)}, u32[]{:S(2)}) collective-permute-start(f32[512,1,128]{2,0,1:T(8,128)S(1)} %collective-permute-done), channel_id=1, source_target_pairs={{0,8},{8,0},{16,24},{24,16},{1,9},{9,1},{17,25},{25,17},{2,10},{10... | collective-permute-start | bytes 786440 | tf_op jit(solution)/shard_map/ppermute | solution.py:70
  38.4 1.0 %copy-start = (bf16[4,1,64,512]{3,2,1,0:T(8,128)(2,1)S(1)}, bf16[4,1,64,512]{3,2,1,0:T(8,128)(2,1)}, u32[]{:S(2)}) copy-start(bf16[4,1,64,512]{3,2,1,0:T(8,128)(2,1)} %get-tuple-element.27) | copy-start | bytes 786436
  44.6 1.8 %collective-permute-start.7 = (f32[2,1,512]{2,1,0:T(1,128)S(1)}, f32[2,1,512]{2,1,0:T(1,128)S(1)}, u32[]{:S(2)}, u32[]{:S(2)}) collective-permute-start(f32[2,1,512]{2,1,0:T(1,128)S(1)} %pad_maximum_fusion.7), channel_id=1, source_target_pairs={{0,24},{8,0},{16,8},{24,16},{1,25},{9,1},{17,9},{25,17},{2,26},{10... | collective-permute-start | bytes 12296 | tf_op jit(solution)/shard_map/ppermute | solution.py:15
  44.7 3.7 %collective-permute-start.8 = (f32[2,1,512]{2,1,0:T(1,128)S(1)}, f32[2,1,512]{2,1,0:T(1,128)S(1)}, u32[]{:S(2)}, u32[]{:S(2)}) collective-permute-start(f32[2,1,512]{2,1,0:T(1,128)S(1)} %pad_maximum_fusion.7), channel_id=1, source_target_pairs={{0,16},{8,24},{16,0},{24,8},{1,17},{9,25},{17,1},{25,9},{2,18},{10... | collective-permute-start | bytes 12296 | tf_op jit(solution)/shard_map/ppermute | solution.py:15
  46.2 3.0 %collective-permute-start.9 = (f32[2,1,512]{2,1,0:T(1,128)S(1)}, f32[2,1,512]{2,1,0:T(1,128)S(1)}, u32[]{:S(2)}, u32[]{:S(2)}) collective-permute-start(f32[2,1,512]{2,1,0:T(1,128)S(1)} %pad_maximum_fusion.7), channel_id=1, source_target_pairs={{0,8},{8,16},{16,24},{24,0},{1,9},{9,17},{17,25},{25,1},{2,10},{10... | collective-permute-start | bytes 12296 | tf_op jit(solution)/shard_map/ppermute | solution.py:15

commit v6 on v5

--- a/solution.py
+++ b/solution.py
@@ -132,8 +132,9 @@
     for s in range(1, positions):
         pairs = [(p * 2 + r, ((p - s) % positions) * 2 + r) for p in range(positions) for r in range(2)]
         row.append(lax.ppermute(capture[0], "tile", pairs))
+    swap = [(j, j ^ 1) for j in range(tiles)]
+    other = jnp.stack([lax.ppermute(piece, "tile", swap) for piece in row])
     row = jnp.stack(row)
-    other = lax.ppermute(row, "tile", [(j, j ^ 1) for j in range(tiles)])
 
     def partial_focus(group, which_row):
         own = group.shape[2]

time: 50.2 us -> 51.4 us (1.024)
  starting transfers between devices: 17.5 us -> 20.5 us
  local copies, waits for them, and re-layouts: 6.23 us -> 5.02 us
  waiting for transfers between devices: 17.6 us -> 16.9 us
    ppermute x1 -> x4, starting transfers between devices: 1.52 us -> 4.43 us  [body(): other = jnp.stack([lax.ppermute(piece, 'tile', swap) for piece in row])]
    ppermute x1 -> x4, waiting for transfers between devices: 1.22 us -> 3.56 us  [body(): other = jnp.stack([lax.ppermute(piece, 'tile', swap) for piece in row])]
    ppermute x3, waiting for transfers between devices: 7.73 us -> 6.1 us  [body(): row.append(lax.ppermute(capture[0], 'tile', pairs))]
    slice x2, local copies, waits for them, and re-layouts: 1.81 us -> 0.77 us  [partial_focus(): cap_imag = group[:, 1].reshape(-1, group.shape[-1])]
    all_to_all x1, waiting for transfers between devices: 5.17 us -> 4.4 us  [body(): lax.all_to_all(travel_time, 'tile', split_axis=1, concat_axis=0, tiled=True)]
    ppermute x2, waiting for transfers between devices: 0.62 us -> 0.01 us  [gather_columns(): partner = [lax.ppermute(piece, axis_name, swap) for piece in same_core]]
    another operation x1 -> x2, other arithmetic: 3.84 us -> 3.91 us
  transfers between devices with their start and end apart: 11 -> 14, of which waited for: 7 -> 6; matrix products, arithmetic and copies ran while one was open for 16% -> 2% of each run, Pallas kernels for 0% -> 0%
where the time goes in v6:
time: 51.4 us; the launch traced here: 51.1 us
  starting transfers between devices  20.5 us (40%)
  waiting for transfers between devices  16.9 us (33%)
  other arithmetic  5.81 us (11%)
  local copies, waits for them, and re-layouts  5.02 us (10%)
  matrix products  1.87 us (4%)
  between operations  1.01 us (2%)
    all_to_all x1, starting transfers between devices, body(): lax.all_to_all(travel_time, 'tile', split_axis=1, concat_axis=0, tiled=True)  7.28 us
    ppermute x3, waiting for transfers between devices, body(): row.append(lax.ppermute(capture[0], 'tile', pairs))  6.1 us
    ppermute x3, starting transfers between devices, body(): row.append(lax.ppermute(capture[0], 'tile', pairs))  4.94 us
    ppermute x4, starting transfers between devices, body(): other = jnp.stack([lax.ppermute(piece, 'tile', swap) for piece in row])  4.43 us
    all_to_all x1, waiting for transfers between devices, body(): lax.all_to_all(travel_time, 'tile', split_axis=1, concat_axis=0, tiled=True)  4.4 us
    another operation x1, other arithmetic  3.84 us
    ppermute x4, waiting for transfers between devices, body(): other = jnp.stack([lax.ppermute(piece, 'tile', swap) for piece in row])  3.56 us
    ppermute x3, waiting for transfers between devices, gather_shifted(): pieces.append(lax.ppermute(block, axis_name, pairs))  2.86 us
  transfers between devices with their start and end apart: 14, of which 6 were waited for; matrix products, arithmetic and copies ran while one was open for 2% of the time, Pallas kernels for 0%

profile of v6, /device:TPU:0, one launch (start us, length us, event | category | flops | bytes accessed | tf_op | source)
XLA Modules:
  0.0 51.1 jit_solution(1121789459494478593)
XLA Ops:
  0.0 1.7 %copy.15 = f32[64,8,128]{2,0,1:T(8,128)} copy(f32[64,8,128]{2,1,0:T(8,128)} %param.7) | data formatting | bytes 524288 | tf_op args[0]
  1.7 7.3 %all-to-all-start = ((f32[64,8,128]{2,0,1:T(8,128)}), f32[64,8,128]{2,0,1:T(8,128)S(1)}, u32[]{:S(2)}, u32[]{:S(2)}) async-start(f32[64,8,128]{2,0,1:T(8,128)} %copy.15), calls=%async_computation | async-start | bytes 524288 | tf_op jit(solution)/shard_map/all_to_all | solution.py:115
  9.0 3.8 %collective-permute-start.3 = (bf16[2,64,512]{2,1,0:T(8,128)(2,1)S(1)}, bf16[2,64,512]{2,1,0:T(8,128)(2,1)S(1)}, u32[]{:S(2)}, u32[]{:S(2)}) collective-permute-start(bf16[2,64,512]{2,1,0:T(8,128)(2,1)S(1)} %bitcast.113), channel_id=1, source_target_pairs={{0,6},{1,7},{2,0},{3,1},{4,2},{5,3},{6,4},{7,5},{8,14},{9,15},{10,... | collective-permute-start | bytes 393224 | tf_op jit(solution)/shard_map/ppermute | solution.py:134
  12.9 0.0 collective-permute-start.4
  12.9 1.1 %collective-permute-start.5 = (bf16[2,64,512]{2,1,0:T(8,128)(2,1)S(1)}, bf16[2,64,512]{2,1,0:T(8,128)(2,1)S(1)}, u32[]{:S(2)}, u32[]{:S(2)}) collective-permute-start(bf16[2,64,512]{2,1,0:T(8,128)(2,1)S(1)} %bitcast.115), channel_id=1, source_target_pairs={{0,2},{1,3},{2,4},{3,5},{4,6},{5,7},{6,0},{7,1},{8,10},{9,11},{10,... | collective-permute-start | bytes 393224 | tf_op jit(solution)/shard_map/ppermute | solution.py:134
  14.0 1.5 %collective-permute-start.6 = (bf16[2,64,512]{2,1,0:T(8,128)(2,1)S(1)}, bf16[2,64,512]{2,1,0:T(8,128)(2,1)S(1)}, u32[]{:S(2)}, u32[]{:S(2)}) collective-permute-start(bf16[2,64,512]{2,1,0:T(8,128)(2,1)S(1)} %bitcast.116), channel_id=1, source_target_pairs={{0,1},{1,0},{2,3},{3,2},{4,5},{5,4},{6,7},{7,6},{8,9},{9,8},{10,11... | collective-permute-start | bytes 393224 | tf_op jit(solution)/shard_map/ppermute | solution.py:136
  15.5 0.1 select_reduce_fusion.1
  15.6 4.4 %all-to-all-done = f32[64,8,128]{2,0,1:T(8,128)S(1)} async-done(((f32[64,8,128]{2,0,1:T(8,128)}), f32[64,8,128]{2,0,1:T(8,128)S(1)}, u32[]{:S(2)}, u32[]{:S(2)}) %all-to-all-start) | async-done | bytes 262176 | tf_op jit(solution)/shard_map/all_to_all | solution.py:115
  20.0 1.5 %collective-permute-start = (f32[512,1,128]{2,0,1:T(8,128)S(1)}, f32[512,1,128]{2,0,1:T(8,128)S(1)}, u32[]{:S(2)}, u32[]{:S(2)}) collective-permute-start(f32[512,1,128]{2,0,1:T(8,128)S(1)} %bitcast.103), channel_id=1, source_target_pairs={{0,16},{8,24},{16,0},{24,8},{1,17},{9,25},{17,1},{25,9},{2,18},{10... | collective-permute-start | bytes 786440 | tf_op jit(solution)/shard_map/ppermute | solution.py:68
  22.1 0.0 collective-permute-done.3
  22.1 0.9 %collective-permute-start.7 = (bf16[2,64,512]{2,1,0:T(8,128)(2,1)S(1)}, bf16[2,64,512]{2,1,0:T(8,128)(2,1)S(1)}, u32[]{:S(2)}, u32[]{:S(2)}) collective-permute-start(bf16[2,64,512]{2,1,0:T(8,128)(2,1)S(1)} %collective-permute-done.3), channel_id=1, source_target_pairs={{0,1},{1,0},{2,3},{3,2},{4,5},{5,4},{6,7},{7,6},{8,9},{9,8},{10,11... | collective-permute-start | bytes 393224 | tf_op jit(solution)/shard_map/ppermute | solution.py:136
  23.1 6.1 %collective-permute-done.4 = bf16[2,64,512]{2,1,0:T(8,128)(2,1)S(1)} collective-permute-done((bf16[2,64,512]{2,1,0:T(8,128)(2,1)S(1)}, bf16[2,64,512]{2,1,0:T(8,128)(2,1)S(1)}, u32[]{:S(2)}, u32[]{:S(2)}) %collective-permute-start.4) | collective-permute-done | bytes 131104 | tf_op jit(solution)/shard_map/ppermute | solution.py:134
  29.2 1.5 %collective-permute-start.8 = (bf16[2,64,512]{2,1,0:T(8,128)(2,1)S(1)}, bf16[2,64,512]{2,1,0:T(8,128)(2,1)S(1)}, u32[]{:S(2)}, u32[]{:S(2)}) collective-permute-start(bf16[2,64,512]{2,1,0:T(8,128)(2,1)S(1)} %collective-permute-done.4), channel_id=1, source_target_pairs={{0,1},{1,0},{2,3},{3,2},{4,5},{5,4},{6,7},{7,6},{8,9},{9,8},{10,11... | collective-permute-start | bytes 393224 | tf_op jit(solution)/shard_map/ppermute | solution.py:136
  30.6 0.0 collective-permute-done.5
  30.6 0.6 %collective-permute-start.9 = (bf16[2,64,512]{2,1,0:T(8,128)(2,1)S(1)}, bf16[2,64,512]{2,1,0:T(8,128)(2,1)S(1)}, u32[]{:S(2)}, u32[]{:S(2)}) collective-permute-start(bf16[2,64,512]{2,1,0:T(8,128)(2,1)S(1)} %collective-permute-done.5), channel_id=1, source_target_pairs={{0,1},{1,0},{2,3},{3,2},{4,5},{5,4},{6,7},{7,6},{8,9},{9,8},{10,11... | collective-permute-start | bytes 393224 | tf_op jit(solution)/shard_map/ppermute | solution.py:136
  31.2 0.1 pad_maximum_fusion.6
  31.3 0.0 collective-permute-done.6
  31.3 0.1 collective-permute-start.1
  31.4 0.0 collective-permute-done
  31.4 0.5 collective-permute-start.2
  31.9 0.7 %fusion.27 = (bf16[4,1,64,512]{3,2,1,0:T(8,128)(2,1)S(1)}, bf16[4,1,64,512]{3,2,1,0:T(8,128)(2,1)}) fusion(bf16[4,2,64,512]{3,2,1,0:T(8,128)(2,1)S(1)} %pad_maximum_fusion.6), kind=kLoop, calls=%fused_computation.87 | loop fusion | bytes 1048576 | tf_op jit(solution)/shard_map/slice | solution.py:142
  32.6 2.2 %collective-permute-done.8 = bf16[2,64,512]{2,1,0:T(8,128)(2,1)S(1)} collective-permute-done((bf16[2,64,512]{2,1,0:T(8,128)(2,1)S(1)}, bf16[2,64,512]{2,1,0:T(8,128)(2,1)S(1)}, u32[]{:S(2)}, u32[]{:S(2)}) %collective-permute-start.8) | collective-permute-done | bytes 131104 | tf_op jit(solution)/shard_map/ppermute | solution.py:136
  34.8 1.4 %collective-permute-done.9 = bf16[2,64,512]{2,1,0:T(8,128)(2,1)S(1)} collective-permute-done((bf16[2,64,512]{2,1,0:T(8,128)(2,1)S(1)}, bf16[2,64,512]{2,1,0:T(8,128)(2,1)S(1)}, u32[]{:S(2)}, u32[]{:S(2)}) %collective-permute-start.9) | collective-permute-done | bytes 131104 | tf_op jit(solution)/shard_map/ppermute | solution.py:136
  36.2 0.1 pad_maximum_fusion.7
  36.3 0.0 collective-permute-done.1
  36.3 3.8 %cosine_convert_fusion = (bf16[2,2,512,1,128]{4,2,0,3,1:T(8,128)(2,1)S(1)}, bf16[2,2,512,1,128]{4,2,0,3,1:T(8,128)(2,1)S(1)}) fusion(f32[2,1,512,1,128]{4,2,0,3,1:T(8,128)S(1)} %maximum_bitcast_fusion.1, f32[2,1,512,1,128]{4,2,0,3,1:T(8,128)S(1)} %maximum_bitcast_fusion, f32[]{:T(128)} %bitcast.4), kind=kLoop, calls=%fused_computation.6 | loop fusion | flops 1310720 | bytes 2097156 | tf_op jit(solution)/shard_map/convert.7
  40.2 0.4 copy.17
  40.7 0.2 copy.18
  40.9 0.4 copy.21
  41.3 0.2 copy.20
  41.6 0.2 convert_element_type.50
  41.8 0.2 convert_element_type.55
  42.1 0.1 bitcast_negate_fusion
  42.2 0.2 fusion.12
  42.4 0.6 %copy-done = bf16[4,1,64,512]{3,2,1,0:T(8,128)(2,1)S(1)} copy-done((bf16[4,1,64,512]{3,2,1,0:T(8,128)(2,1)S(1)}, bf16[4,1,64,512]{3,2,1,0:T(8,128)(2,1)}, u32[]{:S(2)}) %copy-start) | copy-done | bytes 262168
  43.0 0.5 fusion.1
  43.5 0.5 convolution_add_fusion.1
  44.0 0.2 fusion.5
  44.3 0.5 fusion
  44.7 0.2 fusion.10
  44.9 0.5 convolution_add_fusion
  45.4 0.2 fusion.9
  45.8 0.1 collective-permute-start.10
  45.9 1.6 %collective-permute-start.11 = (f32[2,1,512]{2,1,0:T(1,128)S(1)}, f32[2,1,512]{2,1,0:T(1,128)S(1)}, u32[]{:S(2)}, u32[]{:S(2)}) collective-permute-start(f32[2,1,512]{2,1,0:T(1,128)S(1)} %pad_maximum_fusion.8), channel_id=1, source_target_pairs={{0,16},{8,24},{16,0},{24,8},{1,17},{9,25},{17,1},{25,9},{2,18},{10... | collective-permute-start | bytes 12296 | tf_op jit(solution)/shard_map/ppermute | solution.py:15
  47.4 0.2 collective-permute-start.12
  47.6 1.9 %collective-permute-done.11 = f32[2,1,512]{2,1,0:T(1,128)S(1)} collective-permute-done((f32[2,1,512]{2,1,0:T(1,128)S(1)}, f32[2,1,512]{2,1,0:T(1,128)S(1)}, u32[]{:S(2)}, u32[]{:S(2)}) %collective-permute-start.11) | collective-permute-done | bytes 4128 | tf_op jit(solution)/shard_map/ppermute | solution.py:15
  49.5 0.9 %collective-permute-done.12 = f32[2,1,512]{2,1,0:T(1,128)S(1)} collective-permute-done((f32[2,1,512]{2,1,0:T(1,128)S(1)}, f32[2,1,512]{2,1,0:T(1,128)S(1)}, u32[]{:S(2)}, u32[]{:S(2)}) %collective-permute-start.12) | collective-permute-done | bytes 4128 | tf_op jit(solution)/shard_map/ppermute | solution.py:15
  50.5 0.6 %fusion.15 = f32[2,1,512]{2,1,0:T(1,128)} fusion(f32[8,2,1,512]{3,2,1,0:T(1,128)S(1)} %constant_dynamic-update-slice_fusion, s32[]{:T(128)S(6)} %add.159, s32[]{:T(128)S(6)} %add.158, s32[]{:T(128)S(6)} %add.157, s32[]{:T(128)S(6)} %select_n.102), kind=kLoop, calls=%fused_computation.67 | loop fusion | flops 3072 | bytes 20496 | tf_op jit(solution)/shard_map/add | solution.py:96
  (34 shorter events, 0.4 us)
Async XLA Ops:
  0.0 9.0 %copy-start.1 = (bf16[1,2,64,512]{3,2,1,0:T(8,128)(2,1)S(1)}, bf16[1,2,64,512]{3,2,1,0:T(8,128)(2,1)}, u32[]{:S(2)}) copy-start(bf16[1,2,64,512]{3,2,1,0:T(8,128)(2,1)} %param.11) | copy-start | bytes 393220
  0.0 15.4 %copy-start.3 = (f32[1,2,64]{2,1,0:T(2,128)S(1)}, f32[1,2,64]{2,1,0:T(2,128)}, u32[]{:S(2)}) copy-start(f32[1,2,64]{2,1,0:T(2,128)} %param.10) | copy-start | bytes 1540
  0.0 15.4 %copy-start.2 = (s32[1,512]{1,0:T(1,128)S(1)}, s32[1,512]{1,0:T(1,128)}, u32[]{:S(2)}) copy-start(s32[1,512]{1,0:T(1,128)} %param.8) | copy-start | bytes 6148
  1.7 18.2 %all-to-all-start = ((f32[64,8,128]{2,0,1:T(8,128)}), f32[64,8,128]{2,0,1:T(8,128)S(1)}, u32[]{:S(2)}, u32[]{:S(2)}) async-start(f32[64,8,128]{2,0,1:T(8,128)} %copy.15), calls=%async_computation | async-start | bytes 524288 | tf_op jit(solution)/shard_map/all_to_all | solution.py:115
  9.0 13.1 %collective-permute-start.3 = (bf16[2,64,512]{2,1,0:T(8,128)(2,1)S(1)}, bf16[2,64,512]{2,1,0:T(8,128)(2,1)S(1)}, u32[]{:S(2)}, u32[]{:S(2)}) collective-permute-start(bf16[2,64,512]{2,1,0:T(8,128)(2,1)S(1)} %bitcast.113), channel_id=1, source_target_pairs={{0,6},{1,7},{2,0},{3,1},{4,2},{5,3},{6,4},{7,5},{8,14},{9,15},{10,... | collective-permute-start | bytes 393224 | tf_op jit(solution)/shard_map/ppermute | solution.py:134
  12.9 16.3 %collective-permute-start.4 = (bf16[2,64,512]{2,1,0:T(8,128)(2,1)S(1)}, bf16[2,64,512]{2,1,0:T(8,128)(2,1)S(1)}, u32[]{:S(2)}, u32[]{:S(2)}) collective-permute-start(bf16[2,64,512]{2,1,0:T(8,128)(2,1)S(1)} %bitcast.114), channel_id=1, source_target_pairs={{0,4},{1,5},{2,6},{3,7},{4,0},{5,1},{6,2},{7,3},{8,12},{9,13},{10,... | collective-permute-start | bytes 393224 | tf_op jit(solution)/shard_map/ppermute | solution.py:134
  12.9 17.8 %collective-permute-start.5 = (bf16[2,64,512]{2,1,0:T(8,128)(2,1)S(1)}, bf16[2,64,512]{2,1,0:T(8,128)(2,1)S(1)}, u32[]{:S(2)}, u32[]{:S(2)}) collective-permute-start(bf16[2,64,512]{2,1,0:T(8,128)(2,1)S(1)} %bitcast.115), channel_id=1, source_target_pairs={{0,2},{1,3},{2,4},{3,5},{4,6},{5,7},{6,0},{7,1},{8,10},{9,11},{10,... | collective-permute-start | bytes 393224 | tf_op jit(solution)/shard_map/ppermute | solution.py:134
  14.0 17.3 %collective-permute-start.6 = (bf16[2,64,512]{2,1,0:T(8,128)(2,1)S(1)}, bf16[2,64,512]{2,1,0:T(8,128)(2,1)S(1)}, u32[]{:S(2)}, u32[]{:S(2)}) collective-permute-start(bf16[2,64,512]{2,1,0:T(8,128)(2,1)S(1)} %bitcast.116), channel_id=1, source_target_pairs={{0,1},{1,0},{2,3},{3,2},{4,5},{5,4},{6,7},{7,6},{8,9},{9,8},{10,11... | collective-permute-start | bytes 393224 | tf_op jit(solution)/shard_map/ppermute | solution.py:136
  20.0 11.4 %collective-permute-start = (f32[512,1,128]{2,0,1:T(8,128)S(1)}, f32[512,1,128]{2,0,1:T(8,128)S(1)}, u32[]{:S(2)}, u32[]{:S(2)}) collective-permute-start(f32[512,1,128]{2,0,1:T(8,128)S(1)} %bitcast.103), channel_id=1, source_target_pairs={{0,16},{8,24},{16,0},{24,8},{1,17},{9,25},{17,1},{25,9},{2,18},{10... | collective-permute-start | bytes 786440 | tf_op jit(solution)/shard_map/ppermute | solution.py:68
  22.1 10.5 %collective-permute-start.7 = (bf16[2,64,512]{2,1,0:T(8,128)(2,1)S(1)}, bf16[2,64,512]{2,1,0:T(8,128)(2,1)S(1)}, u32[]{:S(2)}, u32[]{:S(2)}) collective-permute-start(bf16[2,64,512]{2,1,0:T(8,128)(2,1)S(1)} %collective-permute-done.3), channel_id=1, source_target_pairs={{0,1},{1,0},{2,3},{3,2},{4,5},{5,4},{6,7},{7,6},{8,9},{9,8},{10,11... | collective-permute-start | bytes 393224 | tf_op jit(solution)/shard_map/ppermute | solution.py:136
  29.2 5.6 %collective-permute-start.8 = (bf16[2,64,512]{2,1,0:T(8,128)(2,1)S(1)}, bf16[2,64,512]{2,1,0:T(8,128)(2,1)S(1)}, u32[]{:S(2)}, u32[]{:S(2)}) collective-permute-start(bf16[2,64,512]{2,1,0:T(8,128)(2,1)S(1)} %collective-permute-done.4), channel_id=1, source_target_pairs={{0,1},{1,0},{2,3},{3,2},{4,5},{5,4},{6,7},{7,6},{8,9},{9,8},{10,11... | collective-permute-start | bytes 393224 | tf_op jit(solution)/shard_map/ppermute | solution.py:136
  30.6 5.5 %collective-permute-start.9 = (bf16[2,64,512]{2,1,0:T(8,128)(2,1)S(1)}, bf16[2,64,512]{2,1,0:T(8,128)(2,1)S(1)}, u32[]{:S(2)}, u32[]{:S(2)}) collective-permute-start(bf16[2,64,512]{2,1,0:T(8,128)(2,1)S(1)} %collective-permute-done.5), channel_id=1, source_target_pairs={{0,1},{1,0},{2,3},{3,2},{4,5},{5,4},{6,7},{7,6},{8,9},{9,8},{10,11... | collective-permute-start | bytes 393224 | tf_op jit(solution)/shard_map/ppermute | solution.py:136
  31.3 5.0 %collective-permute-start.1 = (f32[512,1,128]{2,0,1:T(8,128)S(1)}, f32[512,1,128]{2,0,1:T(8,128)S(1)}, u32[]{:S(2)}, u32[]{:S(2)}) collective-permute-start(f32[512,1,128]{2,0,1:T(8,128)S(1)} %bitcast.104), channel_id=1, source_target_pairs={{0,8},{8,0},{16,24},{24,16},{1,9},{9,1},{17,25},{25,17},{2,10},{10... | collective-permute-start | bytes 786440 | tf_op jit(solution)/shard_map/ppermute | solution.py:70
  31.4 4.9 %collective-permute-start.2 = (f32[512,1,128]{2,0,1:T(8,128)S(1)}, f32[512,1,128]{2,0,1:T(8,128)S(1)}, u32[]{:S(2)}, u32[]{:S(2)}) collective-permute-start(f32[512,1,128]{2,0,1:T(8,128)S(1)} %collective-permute-done), channel_id=1, source_target_pairs={{0,8},{8,0},{16,24},{24,16},{1,9},{9,1},{17,25},{25,17},{2,10},{10... | collective-permute-start | bytes 786440 | tf_op jit(solution)/shard_map/ppermute | solution.py:70
  42.1 1.0 %copy-start = (bf16[4,1,64,512]{3,2,1,0:T(8,128)(2,1)S(1)}, bf16[4,1,64,512]{3,2,1,0:T(8,128)(2,1)}, u32[]{:S(2)}) copy-start(bf16[4,1,64,512]{3,2,1,0:T(8,128)(2,1)} %get-tuple-element.27) | copy-start | bytes 786436
  45.8 1.8 %collective-permute-start.10 = (f32[2,1,512]{2,1,0:T(1,128)S(1)}, f32[2,1,512]{2,1,0:T(1,128)S(1)}, u32[]{:S(2)}, u32[]{:S(2)}) collective-permute-start(f32[2,1,512]{2,1,0:T(1,128)S(1)} %pad_maximum_fusion.8), channel_id=1, source_target_pairs={{0,24},{8,0},{16,8},{24,16},{1,25},{9,1},{17,9},{25,17},{2,26},{10... | collective-permute-start | bytes 12296 | tf_op jit(solution)/shard_map/ppermute | solution.py:15
  45.9 3.7 %collective-permute-start.11 = (f32[2,1,512]{2,1,0:T(1,128)S(1)}, f32[2,1,512]{2,1,0:T(1,128)S(1)}, u32[]{:S(2)}, u32[]{:S(2)}) collective-permute-start(f32[2,1,512]{2,1,0:T(1,128)S(1)} %pad_maximum_fusion.8), channel_id=1, source_target_pairs={{0,16},{8,24},{16,0},{24,8},{1,17},{9,25},{17,1},{25,9},{2,18},{10... | collective-permute-start | bytes 12296 | tf_op jit(solution)/shard_map/ppermute | solution.py:15
  47.4 3.0 %collective-permute-start.12 = (f32[2,1,512]{2,1,0:T(1,128)S(1)}, f32[2,1,512]{2,1,0:T(1,128)S(1)}, u32[]{:S(2)}, u32[]{:S(2)}) collective-permute-start(f32[2,1,512]{2,1,0:T(1,128)S(1)} %pad_maximum_fusion.8), channel_id=1, source_target_pairs={{0,8},{8,16},{16,24},{24,0},{1,9},{9,17},{17,25},{25,1},{2,10},{10... | collective-permute-start | bytes 12296 | tf_op jit(solution)/shard_map/ppermute | solution.py:15

commit v7 on v5

--- a/solution.py
+++ b/solution.py
@@ -128,15 +128,25 @@
     positions = tiles // 2
     z = k // 2
     y = k % 2
-    row = [capture[0]]
+    own = capture.shape[2]
+    swap = [(j, j ^ 1) for j in range(tiles)]
+    own_swapped = lax.ppermute(capture[0], "tile", swap)
+    shifted = []
     for s in range(1, positions):
         pairs = [(p * 2 + r, ((p - s) % positions) * 2 + r) for p in range(positions) for r in range(2)]
-        row.append(lax.ppermute(capture[0], "tile", pairs))
-    row = jnp.stack(row)
-    other = lax.ppermute(row, "tile", [(j, j ^ 1) for j in range(tiles)])
+        shifted.append(lax.ppermute(capture[0], "tile", pairs))
 
-    def partial_focus(group, which_row):
-        own = group.shape[2]
+    def rows_of(field, which_row):
+        grid = field.reshape(positions, 2, own, voxels)
+        picked = lax.dynamic_index_in_dim(grid, which_row, 1, keepdims=False)
+        return jnp.roll(picked, -z, axis=0).reshape(-1, voxels)
+
+    rows = (rows_of(field_real, y), rows_of(field_imag, y), rows_of(field_real, 1 - y), rows_of(field_imag, 1 - y))
+    (left, right, rows), shifted = lax.optimization_barrier(((left, right, rows), shifted))
+    other = jnp.stack([own_swapped] + [lax.ppermute(piece, "tile", swap) for piece in shifted])
+    row = jnp.stack([capture[0]] + shifted)
+
+    def partial_focus(group, g_real, g_imag):
         cap_real = group[:, 0].reshape(-1, group.shape[-1])
         cap_imag = group[:, 1].reshape(-1, group.shape[-1])
         product = jnp.dot(cap_real, left, preferred_element_type=jnp.float32) + jnp.dot(
@@ -144,22 +154,15 @@
         )
         w_real = product[:, :voxels]
         w_imag = product[:, voxels:]
-
-        def rows_of(field):
-            grid = field.reshape(positions, 2, own, voxels)
-            picked = lax.dynamic_index_in_dim(grid, which_row, 1, keepdims=False)
-            picked = jnp.roll(picked, -z, axis=0)
-            return picked.reshape(-1, voxels).astype(jnp.float32)
-
-        g_real = rows_of(field_real)
-        g_imag = rows_of(field_imag)
+        g_real = g_real.astype(jnp.float32)
+        g_imag = g_imag.astype(jnp.float32)
         part_real = jnp.sum(g_real * w_real - g_imag * w_imag, axis=0)
         part_imag = jnp.sum(g_real * w_imag + g_imag * w_real, axis=0)
         return part_real, part_imag
 
-    mine_real, mine_imag = partial_focus(row, y)
+    mine_real, mine_imag = partial_focus(row, rows[0], rows[1])
     mine_real, mine_imag, other = lax.optimization_barrier((mine_real, mine_imag, other))
-    theirs_real, theirs_imag = partial_focus(other, 1 - y)
+    theirs_real, theirs_imag = partial_focus(other, rows[2], rows[3])
     focus_real = mine_real + theirs_real
     focus_imag = mine_imag + theirs_imag
 

time: 50.2 us -> 54.9 us (1.094)
  the two profiles are of different devices: /device:TPU:0 before, /device:TPU:16 now
where the time goes in v7:
time: 54.9 us; the launch traced here: 54.1 us
  waiting for transfers between devices  23.6 us (43%)
  starting transfers between devices  16.2 us (30%)
  other arithmetic  7.74 us (14%)
  local copies, waits for them, and re-layouts  3.69 us (7%)
  matrix products  1.86 us (3%)
  between operations  0.99 us (2%)
    all_to_all x1, waiting for transfers between devices, body(): lax.all_to_all(travel_time, 'tile', split_axis=1, concat_axis=0, tiled=True)  8.03 us
    ppermute x3, waiting for transfers between devices, body(): lax.ppermute(piece, 'tile', swap)  6.52 us
    all_to_all x1, starting transfers between devices, body(): lax.all_to_all(travel_time, 'tile', split_axis=1, concat_axis=0, tiled=True)  6.17 us
    ppermute x1, waiting for transfers between devices, gather_columns(): same_core.append(lax.ppermute(block, axis_name, pairs))  4.83 us
    another operation x1, other arithmetic  3.84 us
    ppermute x3, starting transfers between devices, body(): shifted.append(lax.ppermute(capture[0], 'tile', pairs))  3.83 us
    ppermute x3, waiting for transfers between devices, gather_shifted(): pieces.append(lax.ppermute(block, axis_name, pairs))  2.86 us
    ppermute x3, starting transfers between devices, body(): lax.ppermute(piece, 'tile', swap)  2.73 us
  transfers between devices with their start and end apart: 14, of which 8 were waited for; matrix products, arithmetic and copies ran while one was open for 16% of the time, Pallas kernels for 0%

profile of v7, /device:TPU:16, one launch (start us, length us, event | category | flops | bytes accessed | tf_op | source)
XLA Modules:
  0.0 54.1 jit_solution(1748218353728892372)
XLA Ops:
  0.0 1.7 %copy.15 = f32[64,8,128]{2,0,1:T(8,128)} copy(f32[64,8,128]{2,1,0:T(8,128)} %param.7) | data formatting | bytes 524288 | tf_op args[0]
  1.7 6.2 %all-to-all-start = ((f32[64,8,128]{2,0,1:T(8,128)}), f32[64,8,128]{2,0,1:T(8,128)S(1)}, u32[]{:S(2)}, u32[]{:S(2)}) async-start(f32[64,8,128]{2,0,1:T(8,128)} %copy.15), calls=%async_computation | async-start | bytes 524288 | tf_op jit(solution)/shard_map/all_to_all | solution.py:115
  7.9 0.6 %collective-permute-start.3 = (bf16[2,64,512]{2,1,0:T(8,128)(2,1)S(1)}, bf16[2,64,512]{2,1,0:T(8,128)(2,1)S(1)}, u32[]{:S(2)}, u32[]{:S(2)}) collective-permute-start(bf16[2,64,512]{2,1,0:T(8,128)(2,1)S(1)} %bitcast.105), channel_id=1, source_target_pairs={{0,6},{1,7},{2,0},{3,1},{4,2},{5,3},{6,4},{7,5},{8,14},{9,15},{10,... | collective-permute-start | bytes 393224 | tf_op jit(solution)/shard_map/ppermute | solution.py:137
  8.5 3.3 %collective-permute-start.4 = (bf16[2,64,512]{2,1,0:T(8,128)(2,1)S(1)}, bf16[2,64,512]{2,1,0:T(8,128)(2,1)S(1)}, u32[]{:S(2)}, u32[]{:S(2)}) collective-permute-start(bf16[2,64,512]{2,1,0:T(8,128)(2,1)S(1)} %bitcast.106), channel_id=1, source_target_pairs={{0,4},{1,5},{2,6},{3,7},{4,0},{5,1},{6,2},{7,3},{8,12},{9,13},{10,... | collective-permute-start | bytes 393224 | tf_op jit(solution)/shard_map/ppermute | solution.py:137
  12.4 8.0 %all-to-all-done = f32[64,8,128]{2,0,1:T(8,128)S(1)} async-done(((f32[64,8,128]{2,0,1:T(8,128)}), f32[64,8,128]{2,0,1:T(8,128)S(1)}, u32[]{:S(2)}, u32[]{:S(2)}) %all-to-all-start) | async-done | bytes 262176 | tf_op jit(solution)/shard_map/all_to_all | solution.py:115
  20.5 1.5 %collective-permute-start = (f32[512,1,128]{2,0,1:T(8,128)S(1)}, f32[512,1,128]{2,0,1:T(8,128)S(1)}, u32[]{:S(2)}, u32[]{:S(2)}) collective-permute-start(f32[512,1,128]{2,0,1:T(8,128)S(1)} %bitcast.93), channel_id=1, source_target_pairs={{0,16},{8,24},{16,0},{24,8},{1,17},{9,25},{17,1},{25,9},{2,18},{10... | collective-permute-start | bytes 786440 | tf_op jit(solution)/shard_map/ppermute | solution.py:68
  22.0 0.1 select_reduce_fusion.1
  22.1 0.1 collective-permute-start.1
  22.1 4.8 %collective-permute-done = f32[512,1,128]{2,0,1:T(8,128)S(1)} collective-permute-done((f32[512,1,128]{2,0,1:T(8,128)S(1)}, f32[512,1,128]{2,0,1:T(8,128)S(1)}, u32[]{:S(2)}, u32[]{:S(2)}) %collective-permute-start) | collective-permute-done | bytes 262176 | tf_op jit(solution)/shard_map/ppermute | solution.py:68
  27.0 0.0 collective-permute-start.2
  27.0 0.1 maximum_bitcast_fusion
  27.0 0.0 collective-permute-done.1
  27.1 0.1 collective-permute-start.6
  27.1 1.4 %collective-permute-done.2 = f32[512,1,128]{2,0,1:T(8,128)S(1)} collective-permute-done((f32[512,1,128]{2,0,1:T(8,128)S(1)}, f32[512,1,128]{2,0,1:T(8,128)S(1)}, u32[]{:S(2)}, u32[]{:S(2)}) %collective-permute-start.2) | collective-permute-done | bytes 262176 | tf_op jit(solution)/shard_map/ppermute | solution.py:70
  28.5 3.8 %cosine_convert_fusion = (bf16[2,2,512,1,128]{4,2,0,3,1:T(8,128)(2,1)S(1)}, bf16[2,2,512,1,128]{4,2,0,3,1:T(8,128)(2,1)S(1)}) fusion(f32[2,1,512,1,128]{4,2,0,3,1:T(8,128)S(1)} %maximum_bitcast_fusion.1, f32[2,1,512,1,128]{4,2,0,3,1:T(8,128)S(1)} %maximum_bitcast_fusion, f32[]{:T(128)} %bitcast.4), kind=kLoop, calls=%fused_computation.6 | loop fusion | flops 1310720 | bytes 2097156 | tf_op jit(solution)/shard_map/convert.3
  32.4 0.2 copy.19
  32.7 0.4 copy.21
  33.1 0.2 copy.17
  33.3 0.4 copy.20
  33.8 0.1 bitcast_negate_fusion
  33.8 0.2 convert_element_type.41
  34.0 0.2 convert_element_type.40
  34.2 0.1 dynamic-slice_bitcast_fusion
  34.3 0.1 dynamic-slice_bitcast_fusion.1
  34.4 0.2 pad_maximum_fusion.1
  34.5 0.2 fusion.10
  34.8 0.2 fusion.8
  35.0 0.0 collective-permute-done.5
  35.0 0.7 %collective-permute-start.9 = (bf16[2,64,512]{2,1,0:T(8,128)(2,1)}, bf16[2,64,512]{2,1,0:T(8,128)(2,1)S(1)}, u32[]{:S(2)}, u32[]{:S(2)}) collective-permute-start(bf16[2,64,512]{2,1,0:T(8,128)(2,1)} %collective-permute-done.5), channel_id=1, source_target_pairs={{0,1},{1,0},{2,3},{3,2},{4,5},{5,4},{6,7},{7,6},{8,9},{9,8},{10,11... | collective-permute-start | bytes 393224 | tf_op jit(solution)/shard_map/ppermute | solution.py:146
  35.7 1.4 %collective-permute-start.8 = (bf16[2,64,512]{2,1,0:T(8,128)(2,1)S(1)}, bf16[2,64,512]{2,1,0:T(8,128)(2,1)S(1)}, u32[]{:S(2)}, u32[]{:S(2)}) collective-permute-start(bf16[2,64,512]{2,1,0:T(8,128)(2,1)S(1)} %collective-permute-done.4), channel_id=1, source_target_pairs={{0,1},{1,0},{2,3},{3,2},{4,5},{5,4},{6,7},{7,6},{8,9},{9,8},{10,11... | collective-permute-start | bytes 393224 | tf_op jit(solution)/shard_map/ppermute | solution.py:146
  37.1 0.6 %collective-permute-start.7 = (bf16[2,64,512]{2,1,0:T(8,128)(2,1)S(1)}, bf16[2,64,512]{2,1,0:T(8,128)(2,1)S(1)}, u32[]{:S(2)}, u32[]{:S(2)}) collective-permute-start(bf16[2,64,512]{2,1,0:T(8,128)(2,1)S(1)} %collective-permute-done.3), channel_id=1, source_target_pairs={{0,1},{1,0},{2,3},{3,2},{4,5},{5,4},{6,7},{7,6},{8,9},{9,8},{10,11... | collective-permute-start | bytes 393224 | tf_op jit(solution)/shard_map/ppermute | solution.py:146
  37.7 1.0 %pad_maximum_fusion.2 = bf16[4,2,64,512]{3,2,1,0:T(8,128)(2,1)S(1)} fusion(bf16[1,2,64,512]{3,2,1,0:T(8,128)(2,1)} %bitcast.35, bf16[1,2,64,512]{3,2,1,0:T(8,128)(2,1)S(1)} %bitcast.110, bf16[1,2,64,512]{3,2,1,0:T(8,128)(2,1)S(1)} %bitcast.109, bf16[1,2,64,512]{3,2,1,0:T(8,128)(2,1)S(1)} %copy-done), kind=kLoop, calls=%fused_computation.33 | loop fusion | flops 786432 | bytes 1048576 | tf_op jit(solution)/shard_map/stack | solution.py:147
  38.8 0.5 fusion.23
  39.2 0.5 convolution_add_fusion.1
  39.7 0.2 fusion.3
  39.9 1.7 %collective-permute-done.9 = bf16[2,64,512]{2,1,0:T(8,128)(2,1)S(1)} collective-permute-done((bf16[2,64,512]{2,1,0:T(8,128)(2,1)}, bf16[2,64,512]{2,1,0:T(8,128)(2,1)S(1)}, u32[]{:S(2)}, u32[]{:S(2)}) %collective-permute-start.9) | collective-permute-done | bytes 131104 | tf_op jit(solution)/shard_map/ppermute | solution.py:146
  41.6 2.8 %collective-permute-done.8 = bf16[2,64,512]{2,1,0:T(8,128)(2,1)S(1)} collective-permute-done((bf16[2,64,512]{2,1,0:T(8,128)(2,1)S(1)}, bf16[2,64,512]{2,1,0:T(8,128)(2,1)S(1)}, u32[]{:S(2)}, u32[]{:S(2)}) %collective-permute-start.8) | collective-permute-done | bytes 131104 | tf_op jit(solution)/shard_map/ppermute | solution.py:146
  44.4 2.0 %collective-permute-done.7 = bf16[2,64,512]{2,1,0:T(8,128)(2,1)S(1)} collective-permute-done((bf16[2,64,512]{2,1,0:T(8,128)(2,1)S(1)}, bf16[2,64,512]{2,1,0:T(8,128)(2,1)S(1)}, u32[]{:S(2)}, u32[]{:S(2)}) %collective-permute-start.7) | collective-permute-done | bytes 131104 | tf_op jit(solution)/shard_map/ppermute | solution.py:146
  46.4 1.0 %pad_maximum_fusion.3 = bf16[4,2,64,512]{3,2,1,0:T(8,128)(2,1)S(1)} fusion(bf16[1,2,64,512]{3,2,1,0:T(8,128)(2,1)S(1)} %bitcast.111, bf16[1,2,64,512]{3,2,1,0:T(8,128)(2,1)S(1)} %bitcast.112, bf16[1,2,64,512]{3,2,1,0:T(8,128)(2,1)S(1)} %bitcast.113, bf16[1,2,64,512]{3,2,1,0:T(8,128)(2,1)} %bitcast.38), kind=kLoop, calls=%fused_computation.34 | loop fusion | flops 786432 | bytes 1048576 | tf_op jit(solution)/shard_map/stack | solution.py:146
  47.5 0.5 fusion.24
  47.9 0.5 convolution_add_fusion
  48.4 0.2 fusion.7
  48.7 0.5 collective-permute-start.10
  49.2 1.2 %collective-permute-start.11 = (f32[2,1,512]{2,1,0:T(1,128)S(1)}, f32[2,1,512]{2,1,0:T(1,128)S(1)}, u32[]{:S(2)}, u32[]{:S(2)}) collective-permute-start(f32[2,1,512]{2,1,0:T(1,128)S(1)} %pad_maximum_fusion.4), channel_id=1, source_target_pairs={{0,16},{8,24},{16,0},{24,8},{1,17},{9,25},{17,1},{25,9},{2,18},{10... | collective-permute-start | bytes 12296 | tf_op jit(solution)/shard_map/ppermute | solution.py:15
  50.4 0.2 collective-permute-start.12
  50.5 2.3 %collective-permute-done.11 = f32[2,1,512]{2,1,0:T(1,128)S(1)} collective-permute-done((f32[2,1,512]{2,1,0:T(1,128)S(1)}, f32[2,1,512]{2,1,0:T(1,128)S(1)}, u32[]{:S(2)}, u32[]{:S(2)}) %collective-permute-start.11) | collective-permute-done | bytes 4128 | tf_op jit(solution)/shard_map/ppermute | solution.py:15
  52.8 0.6 %collective-permute-done.12 = f32[2,1,512]{2,1,0:T(1,128)S(1)} collective-permute-done((f32[2,1,512]{2,1,0:T(1,128)S(1)}, f32[2,1,512]{2,1,0:T(1,128)S(1)}, u32[]{:S(2)}, u32[]{:S(2)}) %collective-permute-start.12) | collective-permute-done | bytes 4128 | tf_op jit(solution)/shard_map/ppermute | solution.py:15
  53.4 0.6 %fusion.13 = f32[2,1,512]{2,1,0:T(1,128)} fusion(f32[8,2,1,512]{3,2,1,0:T(1,128)S(1)} %constant_dynamic-update-slice_fusion, s32[]{:T(128)S(6)} %add.159, s32[]{:T(128)S(6)} %add.158, s32[]{:T(128)S(6)} %add.157, s32[]{:T(128)S(6)} %select_n.102), kind=kLoop, calls=%fused_computation.65 | loop fusion | flops 3072 | bytes 20496 | tf_op jit(solution)/shard_map/add | solution.py:96
  (33 shorter events, 0.3 us)
Async XLA Ops:
  0.0 7.9 %copy-start = (bf16[1,2,64,512]{3,2,1,0:T(8,128)(2,1)S(1)}, bf16[1,2,64,512]{3,2,1,0:T(8,128)(2,1)}, u32[]{:S(2)}) copy-start(bf16[1,2,64,512]{3,2,1,0:T(8,128)(2,1)} %param.11) | copy-start | bytes 393220
  0.0 21.9 %copy-start.2 = (f32[1,2,64]{2,1,0:T(2,128)S(1)}, f32[1,2,64]{2,1,0:T(2,128)}, u32[]{:S(2)}) copy-start(f32[1,2,64]{2,1,0:T(2,128)} %param.10) | copy-start | bytes 1540
  0.0 21.9 %copy-start.1 = (s32[1,512]{1,0:T(1,128)S(1)}, s32[1,512]{1,0:T(1,128)}, u32[]{:S(2)}) copy-start(s32[1,512]{1,0:T(1,128)} %param.8) | copy-start | bytes 6148
  1.7 18.7 %all-to-all-start = ((f32[64,8,128]{2,0,1:T(8,128)}), f32[64,8,128]{2,0,1:T(8,128)S(1)}, u32[]{:S(2)}, u32[]{:S(2)}) async-start(f32[64,8,128]{2,0,1:T(8,128)} %copy.15), calls=%async_computation | async-start | bytes 524288 | tf_op jit(solution)/shard_map/all_to_all | solution.py:115
  7.9 27.1 %collective-permute-start.3 = (bf16[2,64,512]{2,1,0:T(8,128)(2,1)S(1)}, bf16[2,64,512]{2,1,0:T(8,128)(2,1)S(1)}, u32[]{:S(2)}, u32[]{:S(2)}) collective-permute-start(bf16[2,64,512]{2,1,0:T(8,128)(2,1)S(1)} %bitcast.105), channel_id=1, source_target_pairs={{0,6},{1,7},{2,0},{3,1},{4,2},{5,3},{6,4},{7,5},{8,14},{9,15},{10,... | collective-permute-start | bytes 393224 | tf_op jit(solution)/shard_map/ppermute | solution.py:137
  8.5 26.5 %collective-permute-start.4 = (bf16[2,64,512]{2,1,0:T(8,128)(2,1)S(1)}, bf16[2,64,512]{2,1,0:T(8,128)(2,1)S(1)}, u32[]{:S(2)}, u32[]{:S(2)}) collective-permute-start(bf16[2,64,512]{2,1,0:T(8,128)(2,1)S(1)} %bitcast.106), channel_id=1, source_target_pairs={{0,4},{1,5},{2,6},{3,7},{4,0},{5,1},{6,2},{7,3},{8,12},{9,13},{10,... | collective-permute-start | bytes 393224 | tf_op jit(solution)/shard_map/ppermute | solution.py:137
  11.7 23.3 %collective-permute-start.5 = (bf16[2,64,512]{2,1,0:T(8,128)(2,1)S(1)}, bf16[2,64,512]{2,1,0:T(8,128)(2,1)}, u32[]{:S(2)}, u32[]{:S(2)}) collective-permute-start(bf16[2,64,512]{2,1,0:T(8,128)(2,1)S(1)} %bitcast.107), channel_id=1, source_target_pairs={{0,2},{1,3},{2,4},{3,5},{4,6},{5,7},{6,0},{7,1},{8,10},{9,11},{10,... | collective-permute-start | bytes 393224 | tf_op jit(solution)/shard_map/ppermute | solution.py:137
  20.5 6.5 %collective-permute-start = (f32[512,1,128]{2,0,1:T(8,128)S(1)}, f32[512,1,128]{2,0,1:T(8,128)S(1)}, u32[]{:S(2)}, u32[]{:S(2)}) collective-permute-start(f32[512,1,128]{2,0,1:T(8,128)S(1)} %bitcast.93), channel_id=1, source_target_pairs={{0,16},{8,24},{16,0},{24,8},{1,17},{9,25},{17,1},{25,9},{2,18},{10... | collective-permute-start | bytes 786440 | tf_op jit(solution)/shard_map/ppermute | solution.py:68
  22.1 5.0 %collective-permute-start.1 = (f32[512,1,128]{2,0,1:T(8,128)S(1)}, f32[512,1,128]{2,0,1:T(8,128)S(1)}, u32[]{:S(2)}, u32[]{:S(2)}) collective-permute-start(f32[512,1,128]{2,0,1:T(8,128)S(1)} %bitcast.94), channel_id=1, source_target_pairs={{0,8},{8,0},{16,24},{24,16},{1,9},{9,1},{17,25},{25,17},{2,10},{10... | collective-permute-start | bytes 786440 | tf_op jit(solution)/shard_map/ppermute | solution.py:70
  27.0 1.5 %collective-permute-start.2 = (f32[512,1,128]{2,0,1:T(8,128)S(1)}, f32[512,1,128]{2,0,1:T(8,128)S(1)}, u32[]{:S(2)}, u32[]{:S(2)}) collective-permute-start(f32[512,1,128]{2,0,1:T(8,128)S(1)} %collective-permute-done), channel_id=1, source_target_pairs={{0,8},{8,0},{16,24},{24,16},{1,9},{9,1},{17,25},{25,17},{2,10},{10... | collective-permute-start | bytes 786440 | tf_op jit(solution)/shard_map/ppermute | solution.py:70
  27.1 12.9 %collective-permute-start.6 = (bf16[2,64,512]{2,1,0:T(8,128)(2,1)S(1)}, bf16[2,64,512]{2,1,0:T(8,128)(2,1)}, u32[]{:S(2)}, u32[]{:S(2)}) collective-permute-start(bf16[2,64,512]{2,1,0:T(8,128)(2,1)S(1)} %bitcast.108), channel_id=1, source_target_pairs={{0,1},{1,0},{2,3},{3,2},{4,5},{5,4},{6,7},{7,6},{8,9},{9,8},{10,11... | collective-permute-start | bytes 393224 | tf_op jit(solution)/shard_map/ppermute | solution.py:133
  35.0 6.6 %collective-permute-start.9 = (bf16[2,64,512]{2,1,0:T(8,128)(2,1)}, bf16[2,64,512]{2,1,0:T(8,128)(2,1)S(1)}, u32[]{:S(2)}, u32[]{:S(2)}) collective-permute-start(bf16[2,64,512]{2,1,0:T(8,128)(2,1)} %collective-permute-done.5), channel_id=1, source_target_pairs={{0,1},{1,0},{2,3},{3,2},{4,5},{5,4},{6,7},{7,6},{8,9},{9,8},{10,11... | collective-permute-start | bytes 393224 | tf_op jit(solution)/shard_map/ppermute | solution.py:146
  35.7 8.7 %collective-permute-start.8 = (bf16[2,64,512]{2,1,0:T(8,128)(2,1)S(1)}, bf16[2,64,512]{2,1,0:T(8,128)(2,1)S(1)}, u32[]{:S(2)}, u32[]{:S(2)}) collective-permute-start(bf16[2,64,512]{2,1,0:T(8,128)(2,1)S(1)} %collective-permute-done.4), channel_id=1, source_target_pairs={{0,1},{1,0},{2,3},{3,2},{4,5},{5,4},{6,7},{7,6},{8,9},{9,8},{10,11... | collective-permute-start | bytes 393224 | tf_op jit(solution)/shard_map/ppermute | solution.py:146
  37.1 9.3 %collective-permute-start.7 = (bf16[2,64,512]{2,1,0:T(8,128)(2,1)S(1)}, bf16[2,64,512]{2,1,0:T(8,128)(2,1)S(1)}, u32[]{:S(2)}, u32[]{:S(2)}) collective-permute-start(bf16[2,64,512]{2,1,0:T(8,128)(2,1)S(1)} %collective-permute-done.3), channel_id=1, source_target_pairs={{0,1},{1,0},{2,3},{3,2},{4,5},{5,4},{6,7},{7,6},{8,9},{9,8},{10,11... | collective-permute-start | bytes 393224 | tf_op jit(solution)/shard_map/ppermute | solution.py:146
  48.7 1.8 %collective-permute-start.10 = (f32[2,1,512]{2,1,0:T(1,128)S(1)}, f32[2,1,512]{2,1,0:T(1,128)S(1)}, u32[]{:S(2)}, u32[]{:S(2)}) collective-permute-start(f32[2,1,512]{2,1,0:T(1,128)S(1)} %pad_maximum_fusion.4), channel_id=1, source_target_pairs={{0,24},{8,0},{16,8},{24,16},{1,25},{9,1},{17,9},{25,17},{2,26},{10... | collective-permute-start | bytes 12296 | tf_op jit(solution)/shard_map/ppermute | solution.py:15
  49.2 3.6 %collective-permute-start.11 = (f32[2,1,512]{2,1,0:T(1,128)S(1)}, f32[2,1,512]{2,1,0:T(1,128)S(1)}, u32[]{:S(2)}, u32[]{:S(2)}) collective-permute-start(f32[2,1,512]{2,1,0:T(1,128)S(1)} %pad_maximum_fusion.4), channel_id=1, source_target_pairs={{0,16},{8,24},{16,0},{24,8},{1,17},{9,25},{17,1},{25,9},{2,18},{10... | collective-permute-start | bytes 12296 | tf_op jit(solution)/shard_map/ppermute | solution.py:15
  50.4 3.0 %collective-permute-start.12 = (f32[2,1,512]{2,1,0:T(1,128)S(1)}, f32[2,1,512]{2,1,0:T(1,128)S(1)}, u32[]{:S(2)}, u32[]{:S(2)}) collective-permute-start(f32[2,1,512]{2,1,0:T(1,128)S(1)} %pad_maximum_fusion.4), channel_id=1, source_target_pairs={{0,8},{8,16},{16,24},{24,0},{1,9},{9,17},{17,25},{25,1},{2,10},{10... | collective-permute-start | bytes 12296 | tf_op jit(solution)/shard_map/ppermute | solution.py:15

commit v8 on v5

--- a/solution.py
+++ b/solution.py
@@ -112,6 +112,17 @@
     k = lax.axis_index("tile")
     f = lax.axis_index("freq")
 
+    positions = tiles // 2
+    z = k // 2
+    y = k % 2
+    swap = [(j, j ^ 1) for j in range(tiles)]
+    row = [capture[0]]
+    for s in range(1, positions):
+        pairs = [(p * 2 + r, ((p - s) % positions) * 2 + r) for p in range(positions) for r in range(2)]
+        row.append(lax.ppermute(capture[0], "tile", pairs))
+    own_swapped = lax.ppermute(capture[0], "tile", swap)
+    travel_time, own_swapped = lax.optimization_barrier((travel_time, own_swapped))
+
     regrouped = lax.all_to_all(travel_time, "tile", split_axis=1, concat_axis=0, tiled=True)
     view = gather_columns(regrouped, "freq", freqs)
     view = jnp.moveaxis(view.reshape((freqs,) + regrouped.shape), 0, 2)
@@ -125,15 +136,8 @@
     left = jnp.concatenate([field_real, field_imag], axis=1)
     right = jnp.concatenate([-field_imag, field_real], axis=1)
 
-    positions = tiles // 2
-    z = k // 2
-    y = k % 2
-    row = [capture[0]]
-    for s in range(1, positions):
-        pairs = [(p * 2 + r, ((p - s) % positions) * 2 + r) for p in range(positions) for r in range(2)]
-        row.append(lax.ppermute(capture[0], "tile", pairs))
+    other = jnp.stack([own_swapped] + [lax.ppermute(piece, "tile", swap) for piece in row[1:]])
     row = jnp.stack(row)
-    other = lax.ppermute(row, "tile", [(j, j ^ 1) for j in range(tiles)])
 
     def partial_focus(group, which_row):
         own = group.shape[2]

time: 50.2 us -> 55.4 us (1.10)
  starting transfers between devices: 17.5 us -> 21.3 us
  waiting for transfers between devices: 17.6 us -> 20.1 us
  local copies, waits for them, and re-layouts: 6.23 us -> 4.99 us
    ppermute x1 -> x4, waiting for transfers between devices: 1.22 us -> 6.68 us  [the longest x1 3.71 us: body(): own_swapped = lax.ppermute(capture[0], 'tile', swap)]
    ppermute x1 -> x4, starting transfers between devices: 1.52 us -> 6.48 us  [the longest x3 3.44 us: body(): lax.ppermute(piece, 'tile', swap)]
    ppermute x3, waiting for transfers between devices: 7.73 us -> 4.98 us  [body(): row.append(lax.ppermute(capture[0], 'tile', pairs))]
    unnamed x14 -> x13, local copies, waits for them, and re-layouts: 2.6 us -> 0.7 us
    optimization_barrier x0 -> x1, local copies, waits for them, and re-layouts: none -> 1.7 us  [body(): lax.optimization_barrier((travel_time, own_swapped))]
    all_to_all x1, starting transfers between devices: 7.28 us -> 6.05 us  [body(): lax.all_to_all(travel_time, 'tile', split_axis=1, concat_axis=0, tiled=True)]
    slice x2, local copies, waits for them, and re-layouts: 1.81 us -> 0.77 us  [partial_focus(): cap_imag = group[:, 1].reshape(-1, group.shape[-1])]
    ppermute x2, waiting for transfers between devices: 0.62 us -> 0.01 us  [gather_columns(): partner = [lax.ppermute(piece, axis_name, swap) for piece in same_core]]
  transfers between devices with their start and end apart: 11 -> 14, of which waited for: 7 -> 7; matrix products, arithmetic and copies ran while one was open for 16% -> 2% of each run, Pallas kernels for 0% -> 0%
where the time goes in v8:
time: 55.4 us; the launch traced here: 55.1 us
  starting transfers between devices  21.3 us (38%)
  waiting for transfers between devices  20.1 us (36%)
  other arithmetic  5.81 us (10%)
  local copies, waits for them, and re-layouts  4.99 us (9%)
  matrix products  1.86 us (3%)
  between operations  1.01 us (2%)
    all_to_all x1, starting transfers between devices, body(): lax.all_to_all(travel_time, 'tile', split_axis=1, concat_axis=0, tiled=True)  6.05 us
    all_to_all x1, waiting for transfers between devices, body(): lax.all_to_all(travel_time, 'tile', split_axis=1, concat_axis=0, tiled=True)  5.63 us
    ppermute x3, waiting for transfers between devices, body(): row.append(lax.ppermute(capture[0], 'tile', pairs))  4.98 us
    ppermute x3, starting transfers between devices, body(): row.append(lax.ppermute(capture[0], 'tile', pairs))  4.94 us
    another operation x1, other arithmetic  3.84 us
    ppermute x1, waiting for transfers between devices, body(): own_swapped = lax.ppermute(capture[0], 'tile', swap)  3.71 us
    ppermute x3, starting transfers between devices, body(): lax.ppermute(piece, 'tile', swap)  3.44 us
    ppermute x1, starting transfers between devices, body(): own_swapped = lax.ppermute(capture[0], 'tile', swap)  3.03 us
  transfers between devices with their start and end apart: 14, of which 7 were waited for; matrix products, arithmetic and copies ran while one was open for 2% of the time, Pallas kernels for 0%

profile of v8, /device:TPU:0, one launch (start us, length us, event | category | flops | bytes accessed | tf_op | source)
XLA Modules:
  0.0 55.1 jit_solution(17354113987044556206)
XLA Ops:
  0.0 3.0 %collective-permute-start = (bf16[2,64,512]{2,1,0:T(8,128)(2,1)}, bf16[2,64,512]{2,1,0:T(8,128)(2,1)S(1)}, u32[]{:S(2)}, u32[]{:S(2)}) collective-permute-start(bf16[2,64,512]{2,1,0:T(8,128)(2,1)} %bitcast.113), channel_id=1, source_target_pairs={{0,1},{1,0},{2,3},{3,2},{4,5},{5,4},{6,7},{7,6},{8,9},{9,8},{10,11... | collective-permute-start | bytes 393224 | tf_op jit(solution)/shard_map/ppermute | solution.py:123
  3.0 3.7 %collective-permute-done = bf16[2,64,512]{2,1,0:T(8,128)(2,1)S(1)} collective-permute-done((bf16[2,64,512]{2,1,0:T(8,128)(2,1)}, bf16[2,64,512]{2,1,0:T(8,128)(2,1)S(1)}, u32[]{:S(2)}, u32[]{:S(2)}) %collective-permute-start) | collective-permute-done | bytes 131104 | tf_op jit(solution)/shard_map/ppermute | solution.py:123
  6.7 1.7 %copy.15 = f32[64,8,128]{2,0,1:T(8,128)} copy(f32[64,8,128]{2,1,0:T(8,128)} %param.7) | data formatting | bytes 524288 | tf_op jit(solution)/shard_map/optimization_barrier | solution.py:124
  8.4 6.1 %all-to-all-start = ((f32[64,8,128]{2,0,1:T(8,128)}), f32[64,8,128]{2,0,1:T(8,128)S(1)}, u32[]{:S(2)}, u32[]{:S(2)}) async-start(f32[64,8,128]{2,0,1:T(8,128)} %copy.15), calls=%async_computation | async-start | bytes 524288 | tf_op jit(solution)/shard_map/all_to_all | solution.py:126
  14.5 3.8 %collective-permute-start.4 = (bf16[2,64,512]{2,1,0:T(8,128)(2,1)S(1)}, bf16[2,64,512]{2,1,0:T(8,128)(2,1)S(1)}, u32[]{:S(2)}, u32[]{:S(2)}) collective-permute-start(bf16[2,64,512]{2,1,0:T(8,128)(2,1)S(1)} %bitcast.114), channel_id=1, source_target_pairs={{0,6},{1,7},{2,0},{3,1},{4,2},{5,3},{6,4},{7,5},{8,14},{9,15},{10,... | collective-permute-start | bytes 393224 | tf_op jit(solution)/shard_map/ppermute | solution.py:122
  18.3 0.0 collective-permute-start.5
  18.3 1.1 %collective-permute-start.6 = (bf16[2,64,512]{2,1,0:T(8,128)(2,1)S(1)}, bf16[2,64,512]{2,1,0:T(8,128)(2,1)S(1)}, u32[]{:S(2)}, u32[]{:S(2)}) collective-permute-start(bf16[2,64,512]{2,1,0:T(8,128)(2,1)S(1)} %bitcast.116), channel_id=1, source_target_pairs={{0,2},{1,3},{2,4},{3,5},{4,6},{5,7},{6,0},{7,1},{8,10},{9,11},{10,... | collective-permute-start | bytes 393224 | tf_op jit(solution)/shard_map/ppermute | solution.py:122
  20.2 0.1 select_reduce_fusion.1
  20.3 5.6 %all-to-all-done = f32[64,8,128]{2,0,1:T(8,128)S(1)} async-done(((f32[64,8,128]{2,0,1:T(8,128)}), f32[64,8,128]{2,0,1:T(8,128)S(1)}, u32[]{:S(2)}, u32[]{:S(2)}) %all-to-all-start) | async-done | bytes 262176 | tf_op jit(solution)/shard_map/all_to_all | solution.py:126
  25.9 1.5 %collective-permute-start.1 = (f32[512,1,128]{2,0,1:T(8,128)S(1)}, f32[512,1,128]{2,0,1:T(8,128)S(1)}, u32[]{:S(2)}, u32[]{:S(2)}) collective-permute-start(f32[512,1,128]{2,0,1:T(8,128)S(1)} %bitcast.103), channel_id=1, source_target_pairs={{0,16},{8,24},{16,0},{24,8},{1,17},{9,25},{17,1},{25,9},{2,18},{10... | collective-permute-start | bytes 786440 | tf_op jit(solution)/shard_map/ppermute | solution.py:68
  27.4 0.0 collective-permute-done.4
  27.4 1.4 %collective-permute-start.7 = (bf16[2,64,512]{2,1,0:T(8,128)(2,1)S(1)}, bf16[2,64,512]{2,1,0:T(8,128)(2,1)S(1)}, u32[]{:S(2)}, u32[]{:S(2)}) collective-permute-start(bf16[2,64,512]{2,1,0:T(8,128)(2,1)S(1)} %collective-permute-done.4), channel_id=1, source_target_pairs={{0,1},{1,0},{2,3},{3,2},{4,5},{5,4},{6,7},{7,6},{8,9},{9,8},{10,11... | collective-permute-start | bytes 393224 | tf_op jit(solution)/shard_map/ppermute | solution.py:139
  28.8 5.0 %collective-permute-done.5 = bf16[2,64,512]{2,1,0:T(8,128)(2,1)S(1)} collective-permute-done((bf16[2,64,512]{2,1,0:T(8,128)(2,1)S(1)}, bf16[2,64,512]{2,1,0:T(8,128)(2,1)S(1)}, u32[]{:S(2)}, u32[]{:S(2)}) %collective-permute-start.5) | collective-permute-done | bytes 131104 | tf_op jit(solution)/shard_map/ppermute | solution.py:122
  33.8 1.4 %collective-permute-start.8 = (bf16[2,64,512]{2,1,0:T(8,128)(2,1)S(1)}, bf16[2,64,512]{2,1,0:T(8,128)(2,1)S(1)}, u32[]{:S(2)}, u32[]{:S(2)}) collective-permute-start(bf16[2,64,512]{2,1,0:T(8,128)(2,1)S(1)} %collective-permute-done.5), channel_id=1, source_target_pairs={{0,1},{1,0},{2,3},{3,2},{4,5},{5,4},{6,7},{7,6},{8,9},{9,8},{10,11... | collective-permute-start | bytes 393224 | tf_op jit(solution)/shard_map/ppermute | solution.py:139
  35.2 0.0 collective-permute-done.6
  35.2 0.6 %collective-permute-start.9 = (bf16[2,64,512]{2,1,0:T(8,128)(2,1)S(1)}, bf16[2,64,512]{2,1,0:T(8,128)(2,1)S(1)}, u32[]{:S(2)}, u32[]{:S(2)}) collective-permute-start(bf16[2,64,512]{2,1,0:T(8,128)(2,1)S(1)} %collective-permute-done.6), channel_id=1, source_target_pairs={{0,1},{1,0},{2,3},{3,2},{4,5},{5,4},{6,7},{7,6},{8,9},{9,8},{10,11... | collective-permute-start | bytes 393224 | tf_op jit(solution)/shard_map/ppermute | solution.py:139
  35.8 0.1 pad_maximum_fusion.6
  35.9 0.1 collective-permute-start.2
  36.0 0.5 collective-permute-start.3
  36.5 0.7 %fusion.27 = (bf16[4,1,64,512]{3,2,1,0:T(8,128)(2,1)S(1)}, bf16[4,1,64,512]{3,2,1,0:T(8,128)(2,1)}) fusion(bf16[4,2,64,512]{3,2,1,0:T(8,128)(2,1)S(1)} %pad_maximum_fusion.6), kind=kLoop, calls=%fused_computation.87 | loop fusion | bytes 1048576 | tf_op jit(solution)/shard_map/slice | solution.py:145
  37.2 0.0 collective-permute-done.7
  37.2 1.6 %collective-permute-done.8 = bf16[2,64,512]{2,1,0:T(8,128)(2,1)S(1)} collective-permute-done((bf16[2,64,512]{2,1,0:T(8,128)(2,1)S(1)}, bf16[2,64,512]{2,1,0:T(8,128)(2,1)S(1)}, u32[]{:S(2)}, u32[]{:S(2)}) %collective-permute-start.8) | collective-permute-done | bytes 131104 | tf_op jit(solution)/shard_map/ppermute | solution.py:139
  38.8 1.4 %collective-permute-done.9 = bf16[2,64,512]{2,1,0:T(8,128)(2,1)S(1)} collective-permute-done((bf16[2,64,512]{2,1,0:T(8,128)(2,1)S(1)}, bf16[2,64,512]{2,1,0:T(8,128)(2,1)S(1)}, u32[]{:S(2)}, u32[]{:S(2)}) %collective-permute-start.9) | collective-permute-done | bytes 131104 | tf_op jit(solution)/shard_map/ppermute | solution.py:139
  40.2 0.1 pad_maximum_fusion.7
  40.3 0.0 collective-permute-done.3
  40.4 3.8 %cosine_convert_fusion = (bf16[2,2,512,1,128]{4,2,0,3,1:T(8,128)(2,1)S(1)}, bf16[2,2,512,1,128]{4,2,0,3,1:T(8,128)(2,1)S(1)}) fusion(f32[2,1,512,1,128]{4,2,0,3,1:T(8,128)S(1)} %maximum_bitcast_fusion.1, f32[2,1,512,1,128]{4,2,0,3,1:T(8,128)S(1)} %maximum_bitcast_fusion, f32[]{:T(128)} %bitcast.4), kind=kLoop, calls=%fused_computation.6 | loop fusion | flops 1310720 | bytes 2097156 | tf_op jit(solution)/shard_map/convert.7
  44.3 0.4 copy.17
  44.7 0.2 copy.18
  44.9 0.4 copy.21
  45.3 0.2 copy.20
  45.6 0.2 convert_element_type.50
  45.8 0.2 convert_element_type.55
  46.1 0.1 bitcast_negate_fusion
  46.2 0.2 fusion.12
  46.4 0.6 %copy-done = bf16[4,1,64,512]{3,2,1,0:T(8,128)(2,1)S(1)} copy-done((bf16[4,1,64,512]{3,2,1,0:T(8,128)(2,1)S(1)}, bf16[4,1,64,512]{3,2,1,0:T(8,128)(2,1)}, u32[]{:S(2)}) %copy-start) | copy-done | bytes 262168
  47.0 0.5 fusion.1
  47.5 0.5 convolution_add_fusion.1
  48.0 0.2 fusion.5
  48.3 0.5 fusion
  48.7 0.2 fusion.10
  48.9 0.5 convolution_add_fusion
  49.4 0.2 fusion.9
  49.8 0.1 collective-permute-start.10
  49.9 1.6 %collective-permute-start.11 = (f32[2,1,512]{2,1,0:T(1,128)S(1)}, f32[2,1,512]{2,1,0:T(1,128)S(1)}, u32[]{:S(2)}, u32[]{:S(2)}) collective-permute-start(f32[2,1,512]{2,1,0:T(1,128)S(1)} %pad_maximum_fusion.8), channel_id=1, source_target_pairs={{0,16},{8,24},{16,0},{24,8},{1,17},{9,25},{17,1},{25,9},{2,18},{10... | collective-permute-start | bytes 12296 | tf_op jit(solution)/shard_map/ppermute | solution.py:15
  51.4 0.2 collective-permute-start.12
  51.6 1.9 %collective-permute-done.11 = f32[2,1,512]{2,1,0:T(1,128)S(1)} collective-permute-done((f32[2,1,512]{2,1,0:T(1,128)S(1)}, f32[2,1,512]{2,1,0:T(1,128)S(1)}, u32[]{:S(2)}, u32[]{:S(2)}) %collective-permute-start.11) | collective-permute-done | bytes 4128 | tf_op jit(solution)/shard_map/ppermute | solution.py:15
  53.5 0.9 %collective-permute-done.12 = f32[2,1,512]{2,1,0:T(1,128)S(1)} collective-permute-done((f32[2,1,512]{2,1,0:T(1,128)S(1)}, f32[2,1,512]{2,1,0:T(1,128)S(1)}, u32[]{:S(2)}, u32[]{:S(2)}) %collective-permute-start.12) | collective-permute-done | bytes 4128 | tf_op jit(solution)/shard_map/ppermute | solution.py:15
  54.5 0.6 %fusion.15 = f32[2,1,512]{2,1,0:T(1,128)} fusion(f32[8,2,1,512]{3,2,1,0:T(1,128)S(1)} %constant_dynamic-update-slice_fusion, s32[]{:T(128)S(6)} %add.159, s32[]{:T(128)S(6)} %add.158, s32[]{:T(128)S(6)} %add.157, s32[]{:T(128)S(6)} %select_n.102), kind=kLoop, calls=%fused_computation.67 | loop fusion | flops 3072 | bytes 20496 | tf_op jit(solution)/shard_map/add | solution.py:96
  (34 shorter events, 0.4 us)
Async XLA Ops:
  0.0 14.5 %copy-start.1 = (bf16[1,2,64,512]{3,2,1,0:T(8,128)(2,1)S(1)}, bf16[1,2,64,512]{3,2,1,0:T(8,128)(2,1)}, u32[]{:S(2)}) copy-start(bf16[1,2,64,512]{3,2,1,0:T(8,128)(2,1)} %param.11) | copy-start | bytes 393220
  0.0 20.1 %copy-start.3 = (f32[1,2,64]{2,1,0:T(2,128)S(1)}, f32[1,2,64]{2,1,0:T(2,128)}, u32[]{:S(2)}) copy-start(f32[1,2,64]{2,1,0:T(2,128)} %param.10) | copy-start | bytes 1540
  0.0 20.2 %copy-start.2 = (s32[1,512]{1,0:T(1,128)S(1)}, s32[1,512]{1,0:T(1,128)}, u32[]{:S(2)}) copy-start(s32[1,512]{1,0:T(1,128)} %param.8) | copy-start | bytes 6148
  0.0 6.7 %collective-permute-start = (bf16[2,64,512]{2,1,0:T(8,128)(2,1)}, bf16[2,64,512]{2,1,0:T(8,128)(2,1)S(1)}, u32[]{:S(2)}, u32[]{:S(2)}) collective-permute-start(bf16[2,64,512]{2,1,0:T(8,128)(2,1)} %bitcast.113), channel_id=1, source_target_pairs={{0,1},{1,0},{2,3},{3,2},{4,5},{5,4},{6,7},{7,6},{8,9},{9,8},{10,11... | collective-permute-start | bytes 393224 | tf_op jit(solution)/shard_map/ppermute | solution.py:123
  8.4 17.4 %all-to-all-start = ((f32[64,8,128]{2,0,1:T(8,128)}), f32[64,8,128]{2,0,1:T(8,128)S(1)}, u32[]{:S(2)}, u32[]{:S(2)}) async-start(f32[64,8,128]{2,0,1:T(8,128)} %copy.15), calls=%async_computation | async-start | bytes 524288 | tf_op jit(solution)/shard_map/all_to_all | solution.py:126
  14.5 12.9 %collective-permute-start.4 = (bf16[2,64,512]{2,1,0:T(8,128)(2,1)S(1)}, bf16[2,64,512]{2,1,0:T(8,128)(2,1)S(1)}, u32[]{:S(2)}, u32[]{:S(2)}) collective-permute-start(bf16[2,64,512]{2,1,0:T(8,128)(2,1)S(1)} %bitcast.114), channel_id=1, source_target_pairs={{0,6},{1,7},{2,0},{3,1},{4,2},{5,3},{6,4},{7,5},{8,14},{9,15},{10,... | collective-permute-start | bytes 393224 | tf_op jit(solution)/shard_map/ppermute | solution.py:122
  18.3 15.5 %collective-permute-start.5 = (bf16[2,64,512]{2,1,0:T(8,128)(2,1)S(1)}, bf16[2,64,512]{2,1,0:T(8,128)(2,1)S(1)}, u32[]{:S(2)}, u32[]{:S(2)}) collective-permute-start(bf16[2,64,512]{2,1,0:T(8,128)(2,1)S(1)} %bitcast.115), channel_id=1, source_target_pairs={{0,4},{1,5},{2,6},{3,7},{4,0},{5,1},{6,2},{7,3},{8,12},{9,13},{10,... | collective-permute-start | bytes 393224 | tf_op jit(solution)/shard_map/ppermute | solution.py:122
  18.3 16.9 %collective-permute-start.6 = (bf16[2,64,512]{2,1,0:T(8,128)(2,1)S(1)}, bf16[2,64,512]{2,1,0:T(8,128)(2,1)S(1)}, u32[]{:S(2)}, u32[]{:S(2)}) collective-permute-start(bf16[2,64,512]{2,1,0:T(8,128)(2,1)S(1)} %bitcast.116), channel_id=1, source_target_pairs={{0,2},{1,3},{2,4},{3,5},{4,6},{5,7},{6,0},{7,1},{8,10},{9,11},{10,... | collective-permute-start | bytes 393224 | tf_op jit(solution)/shard_map/ppermute | solution.py:122
  25.9 10.1 %collective-permute-start.1 = (f32[512,1,128]{2,0,1:T(8,128)S(1)}, f32[512,1,128]{2,0,1:T(8,128)S(1)}, u32[]{:S(2)}, u32[]{:S(2)}) collective-permute-start(f32[512,1,128]{2,0,1:T(8,128)S(1)} %bitcast.103), channel_id=1, source_target_pairs={{0,16},{8,24},{16,0},{24,8},{1,17},{9,25},{17,1},{25,9},{2,18},{10... | collective-permute-start | bytes 786440 | tf_op jit(solution)/shard_map/ppermute | solution.py:68
  27.4 9.8 %collective-permute-start.7 = (bf16[2,64,512]{2,1,0:T(8,128)(2,1)S(1)}, bf16[2,64,512]{2,1,0:T(8,128)(2,1)S(1)}, u32[]{:S(2)}, u32[]{:S(2)}) collective-permute-start(bf16[2,64,512]{2,1,0:T(8,128)(2,1)S(1)} %collective-permute-done.4), channel_id=1, source_target_pairs={{0,1},{1,0},{2,3},{3,2},{4,5},{5,4},{6,7},{7,6},{8,9},{9,8},{10,11... | collective-permute-start | bytes 393224 | tf_op jit(solution)/shard_map/ppermute | solution.py:139
  33.8 5.0 %collective-permute-start.8 = (bf16[2,64,512]{2,1,0:T(8,128)(2,1)S(1)}, bf16[2,64,512]{2,1,0:T(8,128)(2,1)S(1)}, u32[]{:S(2)}, u32[]{:S(2)}) collective-permute-start(bf16[2,64,512]{2,1,0:T(8,128)(2,1)S(1)} %collective-permute-done.5), channel_id=1, source_target_pairs={{0,1},{1,0},{2,3},{3,2},{4,5},{5,4},{6,7},{7,6},{8,9},{9,8},{10,11... | collective-permute-start | bytes 393224 | tf_op jit(solution)/shard_map/ppermute | solution.py:139
  35.2 5.0 %collective-permute-start.9 = (bf16[2,64,512]{2,1,0:T(8,128)(2,1)S(1)}, bf16[2,64,512]{2,1,0:T(8,128)(2,1)S(1)}, u32[]{:S(2)}, u32[]{:S(2)}) collective-permute-start(bf16[2,64,512]{2,1,0:T(8,128)(2,1)S(1)} %collective-permute-done.6), channel_id=1, source_target_pairs={{0,1},{1,0},{2,3},{3,2},{4,5},{5,4},{6,7},{7,6},{8,9},{9,8},{10,11... | collective-permute-start | bytes 393224 | tf_op jit(solution)/shard_map/ppermute | solution.py:139
  35.9 4.4 %collective-permute-start.2 = (f32[512,1,128]{2,0,1:T(8,128)S(1)}, f32[512,1,128]{2,0,1:T(8,128)S(1)}, u32[]{:S(2)}, u32[]{:S(2)}) collective-permute-start(f32[512,1,128]{2,0,1:T(8,128)S(1)} %bitcast.104), channel_id=1, source_target_pairs={{0,8},{8,0},{16,24},{24,16},{1,9},{9,1},{17,25},{25,17},{2,10},{10... | collective-permute-start | bytes 786440 | tf_op jit(solution)/shard_map/ppermute | solution.py:70
  36.0 4.3 %collective-permute-start.3 = (f32[512,1,128]{2,0,1:T(8,128)S(1)}, f32[512,1,128]{2,0,1:T(8,128)S(1)}, u32[]{:S(2)}, u32[]{:S(2)}) collective-permute-start(f32[512,1,128]{2,0,1:T(8,128)S(1)} %collective-permute-done.1), channel_id=1, source_target_pairs={{0,8},{8,0},{16,24},{24,16},{1,9},{9,1},{17,25},{25,17},{2,10},{10... | collective-permute-start | bytes 786440 | tf_op jit(solution)/shard_map/ppermute | solution.py:70
  46.1 1.0 %copy-start = (bf16[4,1,64,512]{3,2,1,0:T(8,128)(2,1)S(1)}, bf16[4,1,64,512]{3,2,1,0:T(8,128)(2,1)}, u32[]{:S(2)}) copy-start(bf16[4,1,64,512]{3,2,1,0:T(8,128)(2,1)} %get-tuple-element.31) | copy-start | bytes 786436
  49.8 1.8 %collective-permute-start.10 = (f32[2,1,512]{2,1,0:T(1,128)S(1)}, f32[2,1,512]{2,1,0:T(1,128)S(1)}, u32[]{:S(2)}, u32[]{:S(2)}) collective-permute-start(f32[2,1,512]{2,1,0:T(1,128)S(1)} %pad_maximum_fusion.8), channel_id=1, source_target_pairs={{0,24},{8,0},{16,8},{24,16},{1,25},{9,1},{17,9},{25,17},{2,26},{10... | collective-permute-start | bytes 12296 | tf_op jit(solution)/shard_map/ppermute | solution.py:15
  49.9 3.7 %collective-permute-start.11 = (f32[2,1,512]{2,1,0:T(1,128)S(1)}, f32[2,1,512]{2,1,0:T(1,128)S(1)}, u32[]{:S(2)}, u32[]{:S(2)}) collective-permute-start(f32[2,1,512]{2,1,0:T(1,128)S(1)} %pad_maximum_fusion.8), channel_id=1, source_target_pairs={{0,16},{8,24},{16,0},{24,8},{1,17},{9,25},{17,1},{25,9},{2,18},{10... | collective-permute-start | bytes 12296 | tf_op jit(solution)/shard_map/ppermute | solution.py:15
  51.4 3.0 %collective-permute-start.12 = (f32[2,1,512]{2,1,0:T(1,128)S(1)}, f32[2,1,512]{2,1,0:T(1,128)S(1)}, u32[]{:S(2)}, u32[]{:S(2)}) collective-permute-start(f32[2,1,512]{2,1,0:T(1,128)S(1)} %pad_maximum_fusion.8), channel_id=1, source_target_pairs={{0,8},{8,16},{16,24},{24,0},{1,9},{9,17},{17,25},{25,1},{2,10},{10... | collective-permute-start | bytes 12296 | tf_op jit(solution)/shard_map/ppermute | solution.py:15

commit v9 on v5

--- a/solution.py
+++ b/solution.py
@@ -112,7 +112,24 @@
     k = lax.axis_index("tile")
     f = lax.axis_index("freq")
 
-    regrouped = lax.all_to_all(travel_time, "tile", split_axis=1, concat_axis=0, tiled=True)
+    positions = tiles // 2
+    z = k // 2
+    y = k % 2
+    per_tile = travel_time.shape[1] // tiles
+    pieces = [lax.dynamic_slice_in_dim(travel_time, 2 * z * per_tile, 2 * per_tile, 1)]
+    for s in range(1, positions):
+        target = (z - s) % positions
+        sent = lax.dynamic_slice_in_dim(travel_time, 2 * target * per_tile, 2 * per_tile, 1)
+        pairs = [(p * 2 + r, ((p - s) % positions) * 2 + r) for p in range(positions) for r in range(2)]
+        pieces.append(lax.ppermute(sent, "tile", pairs))
+    pieces = jnp.stack(pieces)
+    mine_tt = lax.dynamic_slice_in_dim(pieces, y * per_tile, per_tile, 2)
+    theirs_tt = lax.ppermute(
+        lax.dynamic_slice_in_dim(pieces, (1 - y) * per_tile, per_tile, 2), "tile", [(j, j ^ 1) for j in range(tiles)]
+    )
+    both_tt = jnp.stack([mine_tt, theirs_tt], axis=1)
+    both_tt = jnp.roll(jnp.roll(both_tt, z, axis=0), y, axis=1)
+    regrouped = both_tt.reshape((-1,) + both_tt.shape[3:])
     view = gather_columns(regrouped, "freq", freqs)
     view = jnp.moveaxis(view.reshape((freqs,) + regrouped.shape), 0, 2)
     elements, row_count, _, width = view.shape
@@ -125,9 +142,6 @@
     left = jnp.concatenate([field_real, field_imag], axis=1)
     right = jnp.concatenate([-field_imag, field_real], axis=1)
 
-    positions = tiles // 2
-    z = k // 2
-    y = k % 2
     row = [capture[0]]
     for s in range(1, positions):
         pairs = [(p * 2 + r, ((p - s) % positions) * 2 + r) for p in range(positions) for r in range(2)]

time: 50.2 us -> 46.6 us (0.928)
  the two profiles are of different devices: /device:TPU:0 before, /device:TPU:16 now
where the time goes in v9:
time: 46.6 us; the launch traced here: 46.4 us
  waiting for transfers between devices  16.8 us (36%)
  starting transfers between devices  14.9 us (32%)
  other arithmetic  5.91 us (13%)
  local copies, waits for them, and re-layouts  5.87 us (13%)
  matrix products  1.87 us (4%)
  between operations  1.03 us (2%)
    ppermute x3, waiting for transfers between devices, body(): pieces.append(lax.ppermute(sent, 'tile', pairs))  7.15 us
    ppermute x3, starting transfers between devices, body(): row.append(lax.ppermute(capture[0], 'tile', pairs))  4.38 us
    ppermute x3, starting transfers between devices, body(): pieces.append(lax.ppermute(sent, 'tile', pairs))  3.99 us
    another operation x1, other arithmetic  3.84 us
    ppermute x1, waiting for transfers between devices, gather_columns(): same_core.append(lax.ppermute(block, axis_name, pairs))  3.19 us
    ppermute x3, waiting for transfers between devices, gather_shifted(): pieces.append(lax.ppermute(block, axis_name, pairs))  3.07 us
    ppermute x1, waiting for transfers between devices, body(): lax.ppermute(lax.dynamic_slice_in_dim(pieces, (1 - y) * per_tile, per_til...  2.65 us
    slice x2, local copies, waits for them, and re-layouts, partial_focus(): cap_imag = group[:, 1].reshape(-1, group.shape[-1])  1.83 us
  transfers between devices with their start and end apart: 14, of which 6 were waited for; matrix products, arithmetic and copies ran while one was open for 18% of the time, Pallas kernels for 0%

profile of v9, /device:TPU:16, one launch (start us, length us, event | category | flops | bytes accessed | tf_op | source)
XLA Modules:
  0.0 46.4 jit_solution(3501139376282591912)
XLA Ops:
  0.0 1.5 %constant_dynamic-slice_fusion.14 = (f32[64,2,128]{2,1,0:T(2,128)S(1)}, f32[64,2,128]{2,1,0:T(2,128)S(1)}, f32[64,2,128]{2,1,0:T(2,128)S(1)}, f32[64,2,128]{2,1,0:T(2,128)S(1)}) fusion(f32[64,8,128]{2,1,0:T(8,128)} %param.7, s32[]{:T(128)S(6)} %select_n.138, s32[]{:T(128)S(6)} %select_n.142, s32[]{:T(128)S(6)} %select_n.140, s32[]{:T(128)S(6)} %select_n.144), kind=kLoop, calls=%fused_computation.82 | loop fusion | bytes 524304 | tf_op jit(solution)/shard_map/dynamic_slice | solution.py:119
  1.5 0.0 copy-start.2
  1.5 0.5 %collective-permute-start = (f32[64,2,128]{2,0,1:T(8,128)S(1)}, f32[64,2,128]{2,0,1:T(8,128)S(1)}, u32[]{:S(2)}, u32[]{:S(2)}) collective-permute-start(f32[64,2,128]{2,0,1:T(8,128)S(1)} %copy.28), channel_id=1, source_target_pairs={{0,6},{1,7},{2,0},{3,1},{4,2},{5,3},{6,4},{7,5},{8,14},{9,15},{10,... | collective-permute-start | bytes 196616 | tf_op jit(solution)/shard_map/ppermute | solution.py:124
  2.0 3.5 %collective-permute-start.1 = (f32[64,2,128]{2,0,1:T(8,128)S(1)}, f32[64,2,128]{2,0,1:T(8,128)S(1)}, u32[]{:S(2)}, u32[]{:S(2)}) collective-permute-start(f32[64,2,128]{2,0,1:T(8,128)S(1)} %copy.29), channel_id=1, source_target_pairs={{0,4},{1,5},{2,6},{3,7},{4,0},{5,1},{6,2},{7,3},{8,12},{9,13},{10,... | collective-permute-start | bytes 196616 | tf_op jit(solution)/shard_map/ppermute | solution.py:124
  5.5 2.0 %collective-permute-start.7 = (bf16[2,64,512]{2,1,0:T(8,128)(2,1)S(1)}, bf16[2,64,512]{2,1,0:T(8,128)(2,1)S(1)}, u32[]{:S(2)}, u32[]{:S(2)}) collective-permute-start(bf16[2,64,512]{2,1,0:T(8,128)(2,1)S(1)} %bitcast.115), channel_id=1, source_target_pairs={{0,6},{1,7},{2,0},{3,1},{4,2},{5,3},{6,4},{7,5},{8,14},{9,15},{10,... | collective-permute-start | bytes 393224 | tf_op jit(solution)/shard_map/ppermute | solution.py:148
  7.6 1.9 %collective-permute-start.8 = (bf16[2,64,512]{2,1,0:T(8,128)(2,1)S(1)}, bf16[2,64,512]{2,1,0:T(8,128)(2,1)S(1)}, u32[]{:S(2)}, u32[]{:S(2)}) collective-permute-start(bf16[2,64,512]{2,1,0:T(8,128)(2,1)S(1)} %bitcast.116), channel_id=1, source_target_pairs={{0,4},{1,5},{2,6},{3,7},{4,0},{5,1},{6,2},{7,3},{8,12},{9,13},{10,... | collective-permute-start | bytes 393224 | tf_op jit(solution)/shard_map/ppermute | solution.py:148
  9.4 0.5 %collective-permute-start.9 = (bf16[2,64,512]{2,1,0:T(8,128)(2,1)S(1)}, bf16[2,64,512]{2,1,0:T(8,128)(2,1)S(1)}, u32[]{:S(2)}, u32[]{:S(2)}) collective-permute-start(bf16[2,64,512]{2,1,0:T(8,128)(2,1)S(1)} %bitcast.117), channel_id=1, source_target_pairs={{0,2},{1,3},{2,4},{3,5},{4,6},{5,7},{6,0},{7,1},{8,10},{9,11},{10,... | collective-permute-start | bytes 393224 | tf_op jit(solution)/shard_map/ppermute | solution.py:148
  9.9 0.0 collective-permute-done.1
  9.9 7.1 %collective-permute-done.2 = f32[64,2,128]{2,0,1:T(8,128)S(1)} collective-permute-done((f32[64,2,128]{2,0,1:T(8,128)S(1)}, f32[64,2,128]{2,0,1:T(8,128)S(1)}, u32[]{:S(2)}, u32[]{:S(2)}) %collective-permute-start.2) | collective-permute-done | bytes 65568 | tf_op jit(solution)/shard_map/ppermute | solution.py:124
  17.1 1.6 %collective-permute-start.3 = (f32[4,64,1,128]{3,1,0,2:T(8,128)S(1)}, f32[4,64,1,128]{3,1,0,2:T(8,128)S(1)}, u32[]{:S(2)}, u32[]{:S(2)}) collective-permute-start(f32[4,64,1,128]{3,1,0,2:T(8,128)S(1)} %get-tuple-element.28), channel_id=1, source_target_pairs={{0,1},{1,0},{2,3},{3,2},{4,5},{5,4},{6,7},{7,6},{8,9},{9,8},{10,11... | collective-permute-start | bytes 393224 | tf_op jit(solution)/shard_map/ppermute | solution.py:127
  19.4 0.1 select_reduce_fusion.1
  19.5 2.7 %collective-permute-done.3 = f32[4,64,1,128]{3,1,0,2:T(8,128)S(1)} collective-permute-done((f32[4,64,1,128]{3,1,0,2:T(8,128)S(1)}, f32[4,64,1,128]{3,1,0,2:T(8,128)S(1)}, u32[]{:S(2)}, u32[]{:S(2)}) %collective-permute-start.3) | collective-permute-done | bytes 131104 | tf_op jit(solution)/shard_map/ppermute | solution.py:127
  22.2 0.1 fusion.16
  22.2 0.1 fusion.14
  22.3 1.6 %collective-permute-start.4 = (f32[512,1,128]{2,0,1:T(8,128)S(1)}, f32[512,1,128]{2,0,1:T(8,128)S(1)}, u32[]{:S(2)}, u32[]{:S(2)}) collective-permute-start(f32[512,1,128]{2,0,1:T(8,128)S(1)} %bitcast.103), channel_id=1, source_target_pairs={{0,16},{8,24},{16,0},{24,8},{1,17},{9,25},{17,1},{25,9},{2,18},{10... | collective-permute-start | bytes 786440 | tf_op jit(solution)/shard_map/ppermute | solution.py:68
  23.9 0.0 collective-permute-done.7
  23.9 0.0 collective-permute-done.8
  23.9 0.1 pad_maximum_fusion.6
  24.0 1.6 %collective-permute-start.10 = (bf16[4,2,64,512]{3,2,1,0:T(8,128)(2,1)S(1)}, bf16[4,2,64,512]{3,2,1,0:T(8,128)(2,1)}, u32[]{:S(2)}, u32[]{:S(2)}) collective-permute-start(bf16[4,2,64,512]{3,2,1,0:T(8,128)(2,1)S(1)} %pad_maximum_fusion.6), channel_id=1, source_target_pairs={{0,1},{1,0},{2,3},{3,2},{4,5},{5,4},{6,7},{7,6},{8,9},{9,8},{10,11... | collective-permute-start | bytes 1572872 | tf_op jit(solution)/shard_map/ppermute | solution.py:150
  25.5 3.2 %collective-permute-done.4 = f32[512,1,128]{2,0,1:T(8,128)S(1)} collective-permute-done((f32[512,1,128]{2,0,1:T(8,128)S(1)}, f32[512,1,128]{2,0,1:T(8,128)S(1)}, u32[]{:S(2)}, u32[]{:S(2)}) %collective-permute-start.4) | collective-permute-done | bytes 262176 | tf_op jit(solution)/shard_map/ppermute | solution.py:68
  28.7 0.7 %fusion.31 = (bf16[4,1,64,512]{3,2,1,0:T(8,128)(2,1)S(1)}, bf16[4,1,64,512]{3,2,1,0:T(8,128)(2,1)}) fusion(bf16[4,2,64,512]{3,2,1,0:T(8,128)(2,1)S(1)} %pad_maximum_fusion.6), kind=kLoop, calls=%fused_computation.104 | loop fusion | bytes 1048576 | tf_op jit(solution)/shard_map/slice | solution.py:155
  29.5 0.7 %collective-permute-done.6 = f32[512,1,128]{2,0,1:T(8,128)S(1)} collective-permute-done((f32[512,1,128]{2,0,1:T(8,128)S(1)}, f32[512,1,128]{2,0,1:T(8,128)S(1)}, u32[]{:S(2)}, u32[]{:S(2)}) %collective-permute-start.6) | collective-permute-done | bytes 262176 | tf_op jit(solution)/shard_map/ppermute | solution.py:70
  30.3 3.8 %cosine_convert_fusion = (bf16[2,2,512,1,128]{4,2,0,3,1:T(8,128)(2,1)S(1)}, bf16[2,2,512,1,128]{4,2,0,3,1:T(8,128)(2,1)S(1)}) fusion(f32[2,1,512,1,128]{4,2,0,3,1:T(8,128)S(1)} %maximum_bitcast_fusion.1, f32[2,1,512,1,128]{4,2,0,3,1:T(8,128)S(1)} %maximum_bitcast_fusion, f32[]{:T(128)} %bitcast.4), kind=kLoop, calls=%fused_computation.6 | loop fusion | flops 1310720 | bytes 2097156 | tf_op jit(solution)/shard_map/convert.7
  34.2 0.4 copy.23
  34.6 0.2 copy.24
  34.9 0.4 copy.27
  35.3 0.2 copy.26
  35.5 0.2 convert_element_type.50
  35.7 0.2 convert_element_type.55
  35.9 0.1 dynamic-slice_bitcast_fusion
  36.0 0.1 fusion.11
  36.2 0.1 fusion.10
  36.3 0.1 fusion.13
  36.4 0.1 bitcast_negate_fusion
  36.5 0.6 %copy-done = bf16[4,1,64,512]{3,2,1,0:T(8,128)(2,1)S(1)} copy-done((bf16[4,1,64,512]{3,2,1,0:T(8,128)(2,1)S(1)}, bf16[4,1,64,512]{3,2,1,0:T(8,128)(2,1)}, u32[]{:S(2)}) %copy-start) | copy-done | bytes 262168
  37.1 0.5 fusion.1
  37.6 0.1 fusion.12
  37.7 0.5 %convolution_add_fusion.1 = f32[256,1024]{1,0:T(8,128)S(1)} fusion(f32[256,1024]{1,0:T(8,128)S(1)} %fusion.1, bf16[256,512]{1,0:T(8,128)(2,1)S(1)} %bitcast.106, bf16[512,512]{0,1:T(8,128)(2,1)S(1)} %bitcast.98, bf16[512,512]{0,1:T(8,128)(2,1)S(1)} %bitcast_negate_fusion), kind=kOutput, calls=%fused_computation.1 | convolution fusion | flops 270794752 | bytes 3407872 | tf_op jit(solution)/shard_map/dot_general | solution.py:156
  38.2 0.2 fusion.5
  38.4 1.1 %fusion.30 = (bf16[4,1,64,512]{3,2,1,0:T(8,128)(2,1)S(1)}, bf16[4,1,64,512]{3,2,1,0:T(8,128)(2,1)S(1)}) fusion(bf16[4,2,64,512]{3,2,1,0:T(8,128)(2,1)} %collective-permute-done.10), kind=kLoop, calls=%fused_computation.103 | loop fusion | bytes 1048576 | tf_op jit(solution)/shard_map/slice | solution.py:155
  39.5 0.5 %fusion = f32[256,1024]{1,0:T(8,128)S(1)} fusion(bf16[256,512]{1,0:T(8,128)(2,1)S(1)} %bitcast.112, bf16[512,512]{0,1:T(8,128)(2,1)S(1)} %bitcast.102, bf16[512,512]{0,1:T(8,128)(2,1)S(1)} %bitcast.99), kind=kOutput, calls=%fused_computation.7 | convolution fusion | flops 270532608 | bytes 2359296 | tf_op jit(solution)/shard_map/dot_general | solution.py:156
  40.0 0.5 %convolution_add_fusion = f32[256,1024]{1,0:T(8,128)S(1)} fusion(f32[256,1024]{1,0:T(8,128)S(1)} %fusion, bf16[256,512]{1,0:T(8,128)(2,1)S(1)} %bitcast.107, bf16[512,512]{0,1:T(8,128)(2,1)S(1)} %bitcast.100, bf16[512,512]{0,1:T(8,128)(2,1)S(1)} %bitcast_negate_fusion), kind=kOutput, calls=%fused_computation | convolution fusion | flops 270794752 | bytes 3407872 | tf_op jit(solution)/shard_map/dot_general | solution.py:156
  40.5 0.2 fusion.9
  40.8 1.3 %collective-permute-start.11 = (f32[2,1,512]{2,1,0:T(1,128)S(1)}, f32[2,1,512]{2,1,0:T(1,128)S(1)}, u32[]{:S(2)}, u32[]{:S(2)}) collective-permute-start(f32[2,1,512]{2,1,0:T(1,128)S(1)} %pad_maximum_fusion.8), channel_id=1, source_target_pairs={{0,24},{8,0},{16,8},{24,16},{1,25},{9,1},{17,9},{25,17},{2,26},{10... | collective-permute-start | bytes 12296 | tf_op jit(solution)/shard_map/ppermute | solution.py:15
  42.1 0.5 %collective-permute-start.12 = (f32[2,1,512]{2,1,0:T(1,128)S(1)}, f32[2,1,512]{2,1,0:T(1,128)S(1)}, u32[]{:S(2)}, u32[]{:S(2)}) collective-permute-start(f32[2,1,512]{2,1,0:T(1,128)S(1)} %pad_maximum_fusion.8), channel_id=1, source_target_pairs={{0,16},{8,24},{16,0},{24,8},{1,17},{9,25},{17,1},{25,9},{2,18},{10... | collective-permute-start | bytes 12296 | tf_op jit(solution)/shard_map/ppermute | solution.py:15
  42.6 0.8 %collective-permute-done.11 = f32[2,1,512]{2,1,0:T(1,128)S(1)} collective-permute-done((f32[2,1,512]{2,1,0:T(1,128)S(1)}, f32[2,1,512]{2,1,0:T(1,128)S(1)}, u32[]{:S(2)}, u32[]{:S(2)}) %collective-permute-start.11) | collective-permute-done | bytes 4128 | tf_op jit(solution)/shard_map/ppermute | solution.py:15
  43.4 2.3 %collective-permute-done.12 = f32[2,1,512]{2,1,0:T(1,128)S(1)} collective-permute-done((f32[2,1,512]{2,1,0:T(1,128)S(1)}, f32[2,1,512]{2,1,0:T(1,128)S(1)}, u32[]{:S(2)}, u32[]{:S(2)}) %collective-permute-start.12) | collective-permute-done | bytes 4128 | tf_op jit(solution)/shard_map/ppermute | solution.py:15
  45.8 0.6 %fusion.22 = f32[2,1,512]{2,1,0:T(1,128)} fusion(f32[8,2,1,512]{3,2,1,0:T(1,128)S(1)} %constant_dynamic-update-slice_fusion, s32[]{:T(128)S(6)} %add.214, s32[]{:T(128)S(6)} %add.213, s32[]{:T(128)S(6)} %add.212, s32[]{:T(128)S(6)} %select_n.159), kind=kLoop, calls=%fused_computation.87 | loop fusion | flops 3072 | bytes 20496 | tf_op jit(solution)/shard_map/add | solution.py:96
  (42 shorter events, 0.4 us)
Async XLA Ops:
  0.0 5.5 %copy-start.1 = (bf16[1,2,64,512]{3,2,1,0:T(8,128)(2,1)S(1)}, bf16[1,2,64,512]{3,2,1,0:T(8,128)(2,1)}, u32[]{:S(2)}) copy-start(bf16[1,2,64,512]{3,2,1,0:T(8,128)(2,1)} %param.11) | copy-start | bytes 393220
  0.0 18.7 %copy-start.3 = (f32[1,2,64]{2,1,0:T(2,128)S(1)}, f32[1,2,64]{2,1,0:T(2,128)}, u32[]{:S(2)}) copy-start(f32[1,2,64]{2,1,0:T(2,128)} %param.10) | copy-start | bytes 1540
  1.5 17.9 %copy-start.2 = (s32[1,512]{1,0:T(1,128)S(1)}, s32[1,512]{1,0:T(1,128)}, u32[]{:S(2)}) copy-start(s32[1,512]{1,0:T(1,128)} %param.8) | copy-start | bytes 6148
  1.5 7.9 %collective-permute-start = (f32[64,2,128]{2,0,1:T(8,128)S(1)}, f32[64,2,128]{2,0,1:T(8,128)S(1)}, u32[]{:S(2)}, u32[]{:S(2)}) collective-permute-start(f32[64,2,128]{2,0,1:T(8,128)S(1)} %copy.28), channel_id=1, source_target_pairs={{0,6},{1,7},{2,0},{3,1},{4,2},{5,3},{6,4},{7,5},{8,14},{9,15},{10,... | collective-permute-start | bytes 196616 | tf_op jit(solution)/shard_map/ppermute | solution.py:124
  2.0 7.9 %collective-permute-start.1 = (f32[64,2,128]{2,0,1:T(8,128)S(1)}, f32[64,2,128]{2,0,1:T(8,128)S(1)}, u32[]{:S(2)}, u32[]{:S(2)}) collective-permute-start(f32[64,2,128]{2,0,1:T(8,128)S(1)} %copy.29), channel_id=1, source_target_pairs={{0,4},{1,5},{2,6},{3,7},{4,0},{5,1},{6,2},{7,3},{8,12},{9,13},{10,... | collective-permute-start | bytes 196616 | tf_op jit(solution)/shard_map/ppermute | solution.py:124
  5.5 11.5 %collective-permute-start.2 = (f32[64,2,128]{2,0,1:T(8,128)S(1)}, f32[64,2,128]{2,0,1:T(8,128)S(1)}, u32[]{:S(2)}, u32[]{:S(2)}) collective-permute-start(f32[64,2,128]{2,0,1:T(8,128)S(1)} %copy.30), channel_id=1, source_target_pairs={{0,2},{1,3},{2,4},{3,5},{4,6},{5,7},{6,0},{7,1},{8,10},{9,11},{10,... | collective-permute-start | bytes 196616 | tf_op jit(solution)/shard_map/ppermute | solution.py:124
  5.5 18.3 %collective-permute-start.7 = (bf16[2,64,512]{2,1,0:T(8,128)(2,1)S(1)}, bf16[2,64,512]{2,1,0:T(8,128)(2,1)S(1)}, u32[]{:S(2)}, u32[]{:S(2)}) collective-permute-start(bf16[2,64,512]{2,1,0:T(8,128)(2,1)S(1)} %bitcast.115), channel_id=1, source_target_pairs={{0,6},{1,7},{2,0},{3,1},{4,2},{5,3},{6,4},{7,5},{8,14},{9,15},{10,... | collective-permute-start | bytes 393224 | tf_op jit(solution)/shard_map/ppermute | solution.py:148
  7.6 16.3 %collective-permute-start.8 = (bf16[2,64,512]{2,1,0:T(8,128)(2,1)S(1)}, bf16[2,64,512]{2,1,0:T(8,128)(2,1)S(1)}, u32[]{:S(2)}, u32[]{:S(2)}) collective-permute-start(bf16[2,64,512]{2,1,0:T(8,128)(2,1)S(1)} %bitcast.116), channel_id=1, source_target_pairs={{0,4},{1,5},{2,6},{3,7},{4,0},{5,1},{6,2},{7,3},{8,12},{9,13},{10,... | collective-permute-start | bytes 393224 | tf_op jit(solution)/shard_map/ppermute | solution.py:148
  9.4 14.4 %collective-permute-start.9 = (bf16[2,64,512]{2,1,0:T(8,128)(2,1)S(1)}, bf16[2,64,512]{2,1,0:T(8,128)(2,1)S(1)}, u32[]{:S(2)}, u32[]{:S(2)}) collective-permute-start(bf16[2,64,512]{2,1,0:T(8,128)(2,1)S(1)} %bitcast.117), channel_id=1, source_target_pairs={{0,2},{1,3},{2,4},{3,5},{4,6},{5,7},{6,0},{7,1},{8,10},{9,11},{10,... | collective-permute-start | bytes 393224 | tf_op jit(solution)/shard_map/ppermute | solution.py:148
  17.1 5.0 %collective-permute-start.3 = (f32[4,64,1,128]{3,1,0,2:T(8,128)S(1)}, f32[4,64,1,128]{3,1,0,2:T(8,128)S(1)}, u32[]{:S(2)}, u32[]{:S(2)}) collective-permute-start(f32[4,64,1,128]{3,1,0,2:T(8,128)S(1)} %get-tuple-element.28), channel_id=1, source_target_pairs={{0,1},{1,0},{2,3},{3,2},{4,5},{5,4},{6,7},{7,6},{8,9},{9,8},{10,11... | collective-permute-start | bytes 393224 | tf_op jit(solution)/shard_map/ppermute | solution.py:127
  22.3 6.4 %collective-permute-start.4 = (f32[512,1,128]{2,0,1:T(8,128)S(1)}, f32[512,1,128]{2,0,1:T(8,128)S(1)}, u32[]{:S(2)}, u32[]{:S(2)}) collective-permute-start(f32[512,1,128]{2,0,1:T(8,128)S(1)} %bitcast.103), channel_id=1, source_target_pairs={{0,16},{8,24},{16,0},{24,8},{1,17},{9,25},{17,1},{25,9},{2,18},{10... | collective-permute-start | bytes 786440 | tf_op jit(solution)/shard_map/ppermute | solution.py:68
  24.0 14.5 %collective-permute-start.10 = (bf16[4,2,64,512]{3,2,1,0:T(8,128)(2,1)S(1)}, bf16[4,2,64,512]{3,2,1,0:T(8,128)(2,1)}, u32[]{:S(2)}, u32[]{:S(2)}) collective-permute-start(bf16[4,2,64,512]{3,2,1,0:T(8,128)(2,1)S(1)} %pad_maximum_fusion.6), channel_id=1, source_target_pairs={{0,1},{1,0},{2,3},{3,2},{4,5},{5,4},{6,7},{7,6},{8,9},{9,8},{10,11... | collective-permute-start | bytes 1572872 | tf_op jit(solution)/shard_map/ppermute | solution.py:150
  25.5 4.0 %collective-permute-start.5 = (f32[512,1,128]{2,0,1:T(8,128)S(1)}, f32[512,1,128]{2,0,1:T(8,128)S(1)}, u32[]{:S(2)}, u32[]{:S(2)}) collective-permute-start(f32[512,1,128]{2,0,1:T(8,128)S(1)} %bitcast.104), channel_id=1, source_target_pairs={{0,8},{8,0},{16,24},{24,16},{1,9},{9,1},{17,25},{25,17},{2,10},{10... | collective-permute-start | bytes 786440 | tf_op jit(solution)/shard_map/ppermute | solution.py:70
  28.7 1.5 %collective-permute-start.6 = (f32[512,1,128]{2,0,1:T(8,128)S(1)}, f32[512,1,128]{2,0,1:T(8,128)S(1)}, u32[]{:S(2)}, u32[]{:S(2)}) collective-permute-start(f32[512,1,128]{2,0,1:T(8,128)S(1)} %collective-permute-done.4), channel_id=1, source_target_pairs={{0,8},{8,0},{16,24},{24,16},{1,9},{9,1},{17,25},{25,17},{2,10},{10... | collective-permute-start | bytes 786440 | tf_op jit(solution)/shard_map/ppermute | solution.py:70
  36.2 1.0 %copy-start = (bf16[4,1,64,512]{3,2,1,0:T(8,128)(2,1)S(1)}, bf16[4,1,64,512]{3,2,1,0:T(8,128)(2,1)}, u32[]{:S(2)}) copy-start(bf16[4,1,64,512]{3,2,1,0:T(8,128)(2,1)} %get-tuple-element.27) | copy-start | bytes 786436
  40.8 2.6 %collective-permute-start.11 = (f32[2,1,512]{2,1,0:T(1,128)S(1)}, f32[2,1,512]{2,1,0:T(1,128)S(1)}, u32[]{:S(2)}, u32[]{:S(2)}) collective-permute-start(f32[2,1,512]{2,1,0:T(1,128)S(1)} %pad_maximum_fusion.8), channel_id=1, source_target_pairs={{0,24},{8,0},{16,8},{24,16},{1,25},{9,1},{17,9},{25,17},{2,26},{10... | collective-permute-start | bytes 12296 | tf_op jit(solution)/shard_map/ppermute | solution.py:15
  42.1 3.6 %collective-permute-start.12 = (f32[2,1,512]{2,1,0:T(1,128)S(1)}, f32[2,1,512]{2,1,0:T(1,128)S(1)}, u32[]{:S(2)}, u32[]{:S(2)}) collective-permute-start(f32[2,1,512]{2,1,0:T(1,128)S(1)} %pad_maximum_fusion.8), channel_id=1, source_target_pairs={{0,16},{8,24},{16,0},{24,8},{1,17},{9,25},{17,1},{25,9},{2,18},{10... | collective-permute-start | bytes 12296 | tf_op jit(solution)/shard_map/ppermute | solution.py:15
  42.6 3.1 %collective-permute-start.13 = (f32[2,1,512]{2,1,0:T(1,128)S(1)}, f32[2,1,512]{2,1,0:T(1,128)S(1)}, u32[]{:S(2)}, u32[]{:S(2)}) collective-permute-start(f32[2,1,512]{2,1,0:T(1,128)S(1)} %pad_maximum_fusion.8), channel_id=1, source_target_pairs={{0,8},{8,16},{16,24},{24,0},{1,9},{9,17},{17,25},{25,1},{2,10},{10... | collective-permute-start | bytes 12296 | tf_op jit(solution)/shard_map/ppermute | solution.py:15

commit v10 on v9

--- a/solution.py
+++ b/solution.py
@@ -115,6 +115,14 @@
     positions = tiles // 2
     z = k // 2
     y = k % 2
+    swap = [(j, j ^ 1) for j in range(tiles)]
+
+    cap_row = [capture[0]]
+    for s in range(1, positions):
+        pairs = [(p * 2 + r, ((p - s) % positions) * 2 + r) for p in range(positions) for r in range(2)]
+        cap_row.append(lax.ppermute(capture[0], "tile", pairs))
+    own_swapped = lax.ppermute(capture[0], "tile", swap)
+
     per_tile = travel_time.shape[1] // tiles
     pieces = [lax.dynamic_slice_in_dim(travel_time, 2 * z * per_tile, 2 * per_tile, 1)]
     for s in range(1, positions):
@@ -142,15 +150,17 @@
     left = jnp.concatenate([field_real, field_imag], axis=1)
     right = jnp.concatenate([-field_imag, field_real], axis=1)
 
-    row = [capture[0]]
-    for s in range(1, positions):
-        pairs = [(p * 2 + r, ((p - s) % positions) * 2 + r) for p in range(positions) for r in range(2)]
-        row.append(lax.ppermute(capture[0], "tile", pairs))
+    row = cap_row
+    other = (own_swapped, lax.ppermute(jnp.stack(row[1:]), "tile", swap))
     row = jnp.stack(row)
-    other = lax.ppermute(row, "tile", [(j, j ^ 1) for j in range(tiles)])
-
-    def partial_focus(group, which_row):
-        own = group.shape[2]
+    own = capture.shape[2]
+
+    def rows_of(field, which_row):
+        grid = field.reshape(positions, 2, own, voxels)
+        picked = lax.dynamic_index_in_dim(grid, which_row, 1, keepdims=False)
+        return jnp.roll(picked, -z, axis=0).reshape(-1, voxels)
+
+    def partial_focus(group, g_real, g_imag):
         cap_real = group[:, 0].reshape(-1, group.shape[-1])
         cap_imag = group[:, 1].reshape(-1, group.shape[-1])
         product = jnp.dot(cap_real, left, preferred_element_type=jnp.float32) + jnp.dot(
@@ -158,22 +168,16 @@
         )
         w_real = product[:, :voxels]
         w_imag = product[:, voxels:]
-
-        def rows_of(field):
-            grid = field.reshape(positions, 2, own, voxels)
-            picked = lax.dynamic_index_in_dim(grid, which_row, 1, keepdims=False)
-            picked = jnp.roll(picked, -z, axis=0)
-            return picked.reshape(-1, voxels).astype(jnp.float32)
-
-        g_real = rows_of(field_real)
-        g_imag = rows_of(field_imag)
+        g_real = g_real.astype(jnp.float32)
+        g_imag = g_imag.astype(jnp.float32)
         part_real = jnp.sum(g_real * w_real - g_imag * w_imag, axis=0)
         part_imag = jnp.sum(g_real * w_imag + g_imag * w_real, axis=0)
         return part_real, part_imag
 
-    mine_real, mine_imag = partial_focus(row, y)
-    mine_real, mine_imag, other = lax.optimization_barrier((mine_real, mine_imag, other))
-    theirs_real, theirs_imag = partial_focus(other, 1 - y)
+    mine_real, mine_imag = partial_focus(row, rows_of(field_real, y), rows_of(field_imag, y))
+    theirs_rows = (rows_of(field_real, 1 - y), rows_of(field_imag, 1 - y))
+    mine_real, mine_imag, theirs_rows, other = lax.optimization_barrier((mine_real, mine_imag, theirs_rows, other))
+    theirs_real, theirs_imag = partial_focus(jnp.concatenate([other[0][None], other[1]]), *theirs_rows)
     focus_real = mine_real + theirs_real
     focus_imag = mine_imag + theirs_imag
 

time: 46.6 us -> 45.9 us (0.985)
  local copies, waits for them, and re-layouts: 5.87 us -> 3.42 us
  other arithmetic: 5.91 us -> 7.94 us
  waiting for transfers between devices: 16.8 us -> 15 us
  starting transfers between devices: 14.9 us -> 16.5 us
    slice x2 -> x1, local copies, waits for them, and re-layouts: 1.83 us -> 0.03 us  [partial_focus(): cap_imag = group[:, 1].reshape(-1, group.shape[-1])]
    ppermute x1, waiting for transfers between devices: 3.19 us -> 1.48 us  [gather_columns(): same_core.append(lax.ppermute(block, axis_name, pairs))]
    ppermute x4 -> x5, starting transfers between devices: 5.96 us -> 7.49 us  [the longest x3 4.39 us: body(): cap_row.append(lax.ppermute(capture[0], 'tile', pairs))]
    ppermute x3, waiting for transfers between devices: 7.15 us -> 5.63 us  [body(): pieces.append(lax.ppermute(sent, 'tile', pairs))]
    concatenate x4 -> x5, other arithmetic: 0.45 us -> 1.57 us  [the longest x1 1.11 us: body(): jnp.concatenate([other[0][None], other[1]])]
    another operation x1, other arithmetic: 0.07 us -> 0.97 us  [body(): row = jnp.stack(row)]
    ppermute x2, waiting for transfers between devices: 0.74 us -> 1.44 us  [gather_columns(): partner = [lax.ppermute(piece, axis_name, swap) for piece in same_core]]
    ppermute x1, waiting for transfers between devices: 2.65 us -> 3.33 us  [body(): lax.ppermute(lax.dynamic_slice_in_dim(pieces, (1 - y) * per_tile, per_til...]
  transfers between devices with their start and end apart: 14 -> 15, of which waited for: 6 -> 6; matrix products, arithmetic and copies ran while one was open for 18% -> 19% of each run, Pallas kernels for 0% -> 0%
where the time goes in v10:
time: 45.9 us; the launch traced here: 45.7 us
  starting transfers between devices  16.5 us (36%)
  waiting for transfers between devices  15 us (33%)
  other arithmetic  7.94 us (17%)
  local copies, waits for them, and re-layouts  3.42 us (7%)
  matrix products  1.87 us (4%)
  between operations  1.03 us (2%)
    ppermute x3, waiting for transfers between devices, body(): pieces.append(lax.ppermute(sent, 'tile', pairs))  5.63 us
    ppermute x3, starting transfers between devices, body(): cap_row.append(lax.ppermute(capture[0], 'tile', pairs))  4.39 us
    ppermute x3, starting transfers between devices, body(): pieces.append(lax.ppermute(sent, 'tile', pairs))  3.99 us
    another operation x1, other arithmetic  3.84 us
    ppermute x1, waiting for transfers between devices, body(): lax.ppermute(lax.dynamic_slice_in_dim(pieces, (1 - y) * per_tile, per_til...  3.33 us
    ppermute x3, waiting for transfers between devices, gather_shifted(): pieces.append(lax.ppermute(block, axis_name, pairs))  3.07 us
    ppermute x3, starting transfers between devices, gather_shifted(): pieces.append(lax.ppermute(block, axis_name, pairs))  1.82 us
    ppermute x1, starting transfers between devices, body(): lax.ppermute(lax.dynamic_slice_in_dim(pieces, (1 - y) * per_tile, per_til...  1.58 us
  transfers between devices with their start and end apart: 15, of which 6 were waited for; matrix products, arithmetic and copies ran while one was open for 19% of the time, Pallas kernels for 0%

profile of v10, /device:TPU:16, one launch (start us, length us, event | category | flops | bytes accessed | tf_op | source)
XLA Modules:
  0.0 45.7 jit_solution(3091139999054044858)
XLA Ops:
  0.0 1.5 %constant_dynamic-slice_fusion.14 = (f32[64,2,128]{2,1,0:T(2,128)S(1)}, f32[64,2,128]{2,1,0:T(2,128)S(1)}, f32[64,2,128]{2,1,0:T(2,128)S(1)}, f32[64,2,128]{2,1,0:T(2,128)S(1)}) fusion(f32[64,8,128]{2,1,0:T(8,128)} %param.7, s32[]{:T(128)S(6)} %select_n.138, s32[]{:T(128)S(6)} %select_n.142, s32[]{:T(128)S(6)} %select_n.140, s32[]{:T(128)S(6)} %select_n.144), kind=kLoop, calls=%fused_computation.87 | loop fusion | bytes 524304 | tf_op jit(solution)/shard_map/dynamic_slice | solution.py:127
  1.5 0.5 %collective-permute-start = (f32[64,2,128]{2,0,1:T(8,128)S(1)}, f32[64,2,128]{2,0,1:T(8,128)S(1)}, u32[]{:S(2)}, u32[]{:S(2)}) collective-permute-start(f32[64,2,128]{2,0,1:T(8,128)S(1)} %copy.28), channel_id=1, source_target_pairs={{0,6},{1,7},{2,0},{3,1},{4,2},{5,3},{6,4},{7,5},{8,14},{9,15},{10,... | collective-permute-start | bytes 196616 | tf_op jit(solution)/shard_map/ppermute | solution.py:132
  2.0 3.5 %collective-permute-start.1 = (f32[64,2,128]{2,0,1:T(8,128)S(1)}, f32[64,2,128]{2,0,1:T(8,128)S(1)}, u32[]{:S(2)}, u32[]{:S(2)}) collective-permute-start(f32[64,2,128]{2,0,1:T(8,128)S(1)} %copy.29), channel_id=1, source_target_pairs={{0,4},{1,5},{2,6},{3,7},{4,0},{5,1},{6,2},{7,3},{8,12},{9,13},{10,... | collective-permute-start | bytes 196616 | tf_op jit(solution)/shard_map/ppermute | solution.py:132
  5.5 2.0 %collective-permute-start.7 = (bf16[2,64,512]{2,1,0:T(8,128)(2,1)}, bf16[2,64,512]{2,1,0:T(8,128)(2,1)S(1)}, u32[]{:S(2)}, u32[]{:S(2)}) collective-permute-start(bf16[2,64,512]{2,1,0:T(8,128)(2,1)} %bitcast.22), channel_id=1, source_target_pairs={{0,6},{1,7},{2,0},{3,1},{4,2},{5,3},{6,4},{7,5},{8,14},{9,15},{10,... | collective-permute-start | bytes 393224 | tf_op jit(solution)/shard_map/ppermute | solution.py:123
  7.5 1.9 %collective-permute-start.8 = (bf16[2,64,512]{2,1,0:T(8,128)(2,1)}, bf16[2,64,512]{2,1,0:T(8,128)(2,1)S(1)}, u32[]{:S(2)}, u32[]{:S(2)}) collective-permute-start(bf16[2,64,512]{2,1,0:T(8,128)(2,1)} %bitcast.22), channel_id=1, source_target_pairs={{0,4},{1,5},{2,6},{3,7},{4,0},{5,1},{6,2},{7,3},{8,12},{9,13},{10,... | collective-permute-start | bytes 393224 | tf_op jit(solution)/shard_map/ppermute | solution.py:123
  9.4 0.0 collective-permute-done
  9.4 0.5 %collective-permute-start.9 = (bf16[2,64,512]{2,1,0:T(8,128)(2,1)}, bf16[2,64,512]{2,1,0:T(8,128)(2,1)S(1)}, u32[]{:S(2)}, u32[]{:S(2)}) collective-permute-start(bf16[2,64,512]{2,1,0:T(8,128)(2,1)} %bitcast.22), channel_id=1, source_target_pairs={{0,2},{1,3},{2,4},{3,5},{4,6},{5,7},{6,0},{7,1},{8,10},{9,11},{10,... | collective-permute-start | bytes 393224 | tf_op jit(solution)/shard_map/ppermute | solution.py:123
  9.9 0.0 collective-permute-done.1
  9.9 1.5 %collective-permute-start.10 = (bf16[2,64,512]{2,1,0:T(8,128)(2,1)}, bf16[2,64,512]{2,1,0:T(8,128)(2,1)}, u32[]{:S(2)}, u32[]{:S(2)}) collective-permute-start(bf16[2,64,512]{2,1,0:T(8,128)(2,1)} %bitcast.22), channel_id=1, source_target_pairs={{0,1},{1,0},{2,3},{3,2},{4,5},{5,4},{6,7},{7,6},{8,9},{9,8},{10,11... | collective-permute-start | bytes 393224 | tf_op jit(solution)/shard_map/ppermute | solution.py:124
  11.4 5.6 %collective-permute-done.2 = f32[64,2,128]{2,0,1:T(8,128)S(1)} collective-permute-done((f32[64,2,128]{2,0,1:T(8,128)S(1)}, f32[64,2,128]{2,0,1:T(8,128)S(1)}, u32[]{:S(2)}, u32[]{:S(2)}) %collective-permute-start.2) | collective-permute-done | bytes 65568 | tf_op jit(solution)/shard_map/ppermute | solution.py:132
  17.1 1.6 %collective-permute-start.3 = (f32[4,64,1,128]{3,1,0,2:T(8,128)S(1)}, f32[4,64,1,128]{3,1,0,2:T(8,128)S(1)}, u32[]{:S(2)}, u32[]{:S(2)}) collective-permute-start(f32[4,64,1,128]{3,1,0,2:T(8,128)S(1)} %get-tuple-element.34), channel_id=1, source_target_pairs={{0,1},{1,0},{2,3},{3,2},{4,5},{5,4},{6,7},{7,6},{8,9},{9,8},{10,11... | collective-permute-start | bytes 393224 | tf_op jit(solution)/shard_map/ppermute | solution.py:135
  18.7 0.1 select_reduce_fusion.1
  18.8 3.3 %collective-permute-done.3 = f32[4,64,1,128]{3,1,0,2:T(8,128)S(1)} collective-permute-done((f32[4,64,1,128]{3,1,0,2:T(8,128)S(1)}, f32[4,64,1,128]{3,1,0,2:T(8,128)S(1)}, u32[]{:S(2)}, u32[]{:S(2)}) %collective-permute-start.3) | collective-permute-done | bytes 131104 | tf_op jit(solution)/shard_map/ppermute | solution.py:135
  22.1 0.1 fusion.17
  22.2 0.1 fusion.15
  22.3 1.6 %collective-permute-start.4 = (f32[512,1,128]{2,0,1:T(8,128)S(1)}, f32[512,1,128]{2,0,1:T(8,128)S(1)}, u32[]{:S(2)}, u32[]{:S(2)}) collective-permute-start(f32[512,1,128]{2,0,1:T(8,128)S(1)} %bitcast.98), channel_id=1, source_target_pairs={{0,16},{8,24},{16,0},{24,8},{1,17},{9,25},{17,1},{25,9},{2,18},{10... | collective-permute-start | bytes 786440 | tf_op jit(solution)/shard_map/ppermute | solution.py:68
  24.5 0.0 collective-permute-done.7
  24.5 0.0 collective-permute-done.8
  24.6 1.6 %collective-permute-start.11 = (bf16[3,2,64,512]{3,2,1,0:T(8,128)(2,1)S(1)}, bf16[3,2,64,512]{3,2,1,0:T(8,128)(2,1)}, u32[]{:S(2)}, u32[]{:S(2)}) collective-permute-start(bf16[3,2,64,512]{3,2,1,0:T(8,128)(2,1)S(1)} %pad_maximum_fusion.7), channel_id=1, source_target_pairs={{0,1},{1,0},{2,3},{3,2},{4,5},{5,4},{6,7},{7,6},{8,9},{9,8},{10,11... | collective-permute-start | bytes 1179656 | tf_op jit(solution)/shard_map/ppermute | solution.py:154
  26.2 1.0 %pad_maximum_fusion.6 = bf16[4,2,64,512]{3,2,1,0:T(8,128)(2,1)S(1)} fusion(bf16[1,2,64,512]{3,2,1,0:T(8,128)(2,1)S(1)} %bitcast.110, bf16[1,2,64,512]{3,2,1,0:T(8,128)(2,1)S(1)} %bitcast.108, bf16[1,2,64,512]{3,2,1,0:T(8,128)(2,1)S(1)} %bitcast.106, bf16[1,2,64,512]{3,2,1,0:T(8,128)(2,1)} %param.11), kind=kLoop, calls=%fused_computation.35 | loop fusion | flops 786432 | bytes 1048576 | tf_op jit(solution)/shard_map/stack | solution.py:155
  27.1 0.1 collective-permute-start.5
  27.2 1.5 %collective-permute-done.4 = f32[512,1,128]{2,0,1:T(8,128)S(1)} collective-permute-done((f32[512,1,128]{2,0,1:T(8,128)S(1)}, f32[512,1,128]{2,0,1:T(8,128)S(1)}, u32[]{:S(2)}, u32[]{:S(2)}) %collective-permute-start.4) | collective-permute-done | bytes 262176 | tf_op jit(solution)/shard_map/ppermute | solution.py:68
  28.8 1.4 %collective-permute-done.6 = f32[512,1,128]{2,0,1:T(8,128)S(1)} collective-permute-done((f32[512,1,128]{2,0,1:T(8,128)S(1)}, f32[512,1,128]{2,0,1:T(8,128)S(1)}, u32[]{:S(2)}, u32[]{:S(2)}) %collective-permute-start.6) | collective-permute-done | bytes 262176 | tf_op jit(solution)/shard_map/ppermute | solution.py:70
  30.3 3.8 %cosine_convert_fusion = (bf16[2,2,512,1,128]{4,2,0,3,1:T(8,128)(2,1)S(1)}, bf16[2,2,512,1,128]{4,2,0,3,1:T(8,128)(2,1)S(1)}) fusion(f32[2,1,512,1,128]{4,2,0,3,1:T(8,128)S(1)} %maximum_bitcast_fusion.1, f32[2,1,512,1,128]{4,2,0,3,1:T(8,128)S(1)} %maximum_bitcast_fusion, f32[]{:T(128)} %bitcast.4), kind=kLoop, calls=%fused_computation.6 | loop fusion | flops 1310720 | bytes 2097156 | tf_op jit(solution)/shard_map/convert.5
  34.2 0.4 copy.23
  34.6 0.2 copy.24
  34.8 0.4 copy.27
  35.3 0.2 copy.26
  35.5 0.2 convert_element_type.44
  35.7 0.2 convert_element_type.49
  35.9 0.1 dynamic-slice_bitcast_fusion
  36.0 0.1 fusion.14
  36.1 0.1 fusion.13
  36.2 0.1 bitcast_negate_fusion
  36.3 0.5 %fusion.1 = f32[256,1024]{1,0:T(8,128)S(1)} fusion(bf16[256,512]{1,0:T(8,128)(2,1)S(1)} %bitcast.112, bf16[512,512]{0,1:T(8,128)(2,1)S(1)} %bitcast.96, bf16[512,512]{0,1:T(8,128)(2,1)S(1)} %bitcast.92), kind=kOutput, calls=%fused_computation.8 | convolution fusion | flops 270532608 | bytes 2359296 | tf_op jit(solution)/shard_map/dot_general | solution.py:166
  36.8 0.5 %convolution_add_fusion.1 = f32[256,1024]{1,0:T(8,128)S(1)} fusion(f32[256,1024]{1,0:T(8,128)S(1)} %fusion.1, bf16[256,512]{1,0:T(8,128)(2,1)S(1)} %bitcast.103, bf16[512,512]{0,1:T(8,128)(2,1)S(1)} %bitcast.93, bf16[512,512]{0,1:T(8,128)(2,1)S(1)} %bitcast_negate_fusion), kind=kOutput, calls=%fused_computation.1 | convolution fusion | flops 270794752 | bytes 3407872 | tf_op jit(solution)/shard_map/dot_general | solution.py:166
  37.3 0.2 fusion.9
  37.5 0.1 fusion.11
  37.6 0.1 fusion.12
  37.8 1.1 %pad_maximum_fusion.8 = (bf16[4,1,64,512]{3,2,1,0:T(8,128)(2,1)S(1)}, bf16[4,1,64,512]{3,2,1,0:T(8,128)(2,1)S(1)}) fusion(bf16[3,2,64,512]{3,2,1,0:T(8,128)(2,1)} %collective-permute-done.11, bf16[1,2,64,512]{3,2,1,0:T(8,128)(2,1)} %bitcast.42), kind=kLoop, calls=%fused_computation.54 | loop fusion | flops 262144 | bytes 1048576 | tf_op jit(solution)/shard_map/concatenate | solution.py:180
  38.9 0.5 %fusion = f32[256,1024]{1,0:T(8,128)S(1)} fusion(bf16[256,512]{1,0:T(8,128)(2,1)S(1)} %bitcast.115, bf16[512,512]{0,1:T(8,128)(2,1)S(1)} %bitcast.97, bf16[512,512]{0,1:T(8,128)(2,1)S(1)} %bitcast.94), kind=kOutput, calls=%fused_computation.7 | convolution fusion | flops 270532608 | bytes 2359296 | tf_op jit(solution)/shard_map/dot_general | solution.py:166
  39.4 0.5 %convolution_add_fusion = f32[256,1024]{1,0:T(8,128)S(1)} fusion(f32[256,1024]{1,0:T(8,128)S(1)} %fusion, bf16[256,512]{1,0:T(8,128)(2,1)S(1)} %bitcast.104, bf16[512,512]{0,1:T(8,128)(2,1)S(1)} %bitcast.95, bf16[512,512]{0,1:T(8,128)(2,1)S(1)} %bitcast_negate_fusion), kind=kOutput, calls=%fused_computation | convolution fusion | flops 270794752 | bytes 3407872 | tf_op jit(solution)/shard_map/dot_general | solution.py:166
  39.8 0.2 fusion.5
  40.2 1.3 %collective-permute-start.12 = (f32[2,1,512]{2,1,0:T(1,128)S(1)}, f32[2,1,512]{2,1,0:T(1,128)S(1)}, u32[]{:S(2)}, u32[]{:S(2)}) collective-permute-start(f32[2,1,512]{2,1,0:T(1,128)S(1)} %pad_maximum_fusion.10), channel_id=1, source_target_pairs={{0,24},{8,0},{16,8},{24,16},{1,25},{9,1},{17,9},{25,17},{2,26},{10... | collective-permute-start | bytes 12296 | tf_op jit(solution)/shard_map/ppermute | solution.py:15
  41.4 0.5 %collective-permute-start.13 = (f32[2,1,512]{2,1,0:T(1,128)S(1)}, f32[2,1,512]{2,1,0:T(1,128)S(1)}, u32[]{:S(2)}, u32[]{:S(2)}) collective-permute-start(f32[2,1,512]{2,1,0:T(1,128)S(1)} %pad_maximum_fusion.10), channel_id=1, source_target_pairs={{0,16},{8,24},{16,0},{24,8},{1,17},{9,25},{17,1},{25,9},{2,18},{10... | collective-permute-start | bytes 12296 | tf_op jit(solution)/shard_map/ppermute | solution.py:15
  42.0 0.8 %collective-permute-done.12 = f32[2,1,512]{2,1,0:T(1,128)S(1)} collective-permute-done((f32[2,1,512]{2,1,0:T(1,128)S(1)}, f32[2,1,512]{2,1,0:T(1,128)S(1)}, u32[]{:S(2)}, u32[]{:S(2)}) %collective-permute-start.12) | collective-permute-done | bytes 4128 | tf_op jit(solution)/shard_map/ppermute | solution.py:15
  42.8 2.3 %collective-permute-done.13 = f32[2,1,512]{2,1,0:T(1,128)S(1)} collective-permute-done((f32[2,1,512]{2,1,0:T(1,128)S(1)}, f32[2,1,512]{2,1,0:T(1,128)S(1)}, u32[]{:S(2)}, u32[]{:S(2)}) %collective-permute-start.13) | collective-permute-done | bytes 4128 | tf_op jit(solution)/shard_map/ppermute | solution.py:15
  45.1 0.6 %fusion.23 = f32[2,1,512]{2,1,0:T(1,128)} fusion(f32[8,2,1,512]{3,2,1,0:T(1,128)S(1)} %constant_dynamic-update-slice_fusion, s32[]{:T(128)S(6)} %add.214, s32[]{:T(128)S(6)} %add.213, s32[]{:T(128)S(6)} %add.212, s32[]{:T(128)S(6)} %select_n.159), kind=kLoop, calls=%fused_computation.92 | loop fusion | flops 3072 | bytes 20496 | tf_op jit(solution)/shard_map/add | solution.py:96
  (41 shorter events, 0.5 us)
Async XLA Ops:
  0.0 18.7 %copy-start.1 = (f32[1,2,64]{2,1,0:T(2,128)S(1)}, f32[1,2,64]{2,1,0:T(2,128)}, u32[]{:S(2)}) copy-start(f32[1,2,64]{2,1,0:T(2,128)} %param.10) | copy-start | bytes 1540
  0.0 18.7 %copy-start = (s32[1,512]{1,0:T(1,128)S(1)}, s32[1,512]{1,0:T(1,128)}, u32[]{:S(2)}) copy-start(s32[1,512]{1,0:T(1,128)} %param.8) | copy-start | bytes 6148
  1.5 7.9 %collective-permute-start = (f32[64,2,128]{2,0,1:T(8,128)S(1)}, f32[64,2,128]{2,0,1:T(8,128)S(1)}, u32[]{:S(2)}, u32[]{:S(2)}) collective-permute-start(f32[64,2,128]{2,0,1:T(8,128)S(1)} %copy.28), channel_id=1, source_target_pairs={{0,6},{1,7},{2,0},{3,1},{4,2},{5,3},{6,4},{7,5},{8,14},{9,15},{10,... | collective-permute-start | bytes 196616 | tf_op jit(solution)/shard_map/ppermute | solution.py:132
  2.0 7.9 %collective-permute-start.1 = (f32[64,2,128]{2,0,1:T(8,128)S(1)}, f32[64,2,128]{2,0,1:T(8,128)S(1)}, u32[]{:S(2)}, u32[]{:S(2)}) collective-permute-start(f32[64,2,128]{2,0,1:T(8,128)S(1)} %copy.29), channel_id=1, source_target_pairs={{0,4},{1,5},{2,6},{3,7},{4,0},{5,1},{6,2},{7,3},{8,12},{9,13},{10,... | collective-permute-start | bytes 196616 | tf_op jit(solution)/shard_map/ppermute | solution.py:132
  5.5 11.5 %collective-permute-start.2 = (f32[64,2,128]{2,0,1:T(8,128)S(1)}, f32[64,2,128]{2,0,1:T(8,128)S(1)}, u32[]{:S(2)}, u32[]{:S(2)}) collective-permute-start(f32[64,2,128]{2,0,1:T(8,128)S(1)} %copy.30), channel_id=1, source_target_pairs={{0,2},{1,3},{2,4},{3,5},{4,6},{5,7},{6,0},{7,1},{8,10},{9,11},{10,... | collective-permute-start | bytes 196616 | tf_op jit(solution)/shard_map/ppermute | solution.py:132
  5.5 19.0 %collective-permute-start.7 = (bf16[2,64,512]{2,1,0:T(8,128)(2,1)}, bf16[2,64,512]{2,1,0:T(8,128)(2,1)S(1)}, u32[]{:S(2)}, u32[]{:S(2)}) collective-permute-start(bf16[2,64,512]{2,1,0:T(8,128)(2,1)} %bitcast.22), channel_id=1, source_target_pairs={{0,6},{1,7},{2,0},{3,1},{4,2},{5,3},{6,4},{7,5},{8,14},{9,15},{10,... | collective-permute-start | bytes 393224 | tf_op jit(solution)/shard_map/ppermute | solution.py:123
  7.5 17.0 %collective-permute-start.8 = (bf16[2,64,512]{2,1,0:T(8,128)(2,1)}, bf16[2,64,512]{2,1,0:T(8,128)(2,1)S(1)}, u32[]{:S(2)}, u32[]{:S(2)}) collective-permute-start(bf16[2,64,512]{2,1,0:T(8,128)(2,1)} %bitcast.22), channel_id=1, source_target_pairs={{0,4},{1,5},{2,6},{3,7},{4,0},{5,1},{6,2},{7,3},{8,12},{9,13},{10,... | collective-permute-start | bytes 393224 | tf_op jit(solution)/shard_map/ppermute | solution.py:123
  9.4 15.1 %collective-permute-start.9 = (bf16[2,64,512]{2,1,0:T(8,128)(2,1)}, bf16[2,64,512]{2,1,0:T(8,128)(2,1)S(1)}, u32[]{:S(2)}, u32[]{:S(2)}) collective-permute-start(bf16[2,64,512]{2,1,0:T(8,128)(2,1)} %bitcast.22), channel_id=1, source_target_pairs={{0,2},{1,3},{2,4},{3,5},{4,6},{5,7},{6,0},{7,1},{8,10},{9,11},{10,... | collective-permute-start | bytes 393224 | tf_op jit(solution)/shard_map/ppermute | solution.py:123
  9.9 27.8 %collective-permute-start.10 = (bf16[2,64,512]{2,1,0:T(8,128)(2,1)}, bf16[2,64,512]{2,1,0:T(8,128)(2,1)}, u32[]{:S(2)}, u32[]{:S(2)}) collective-permute-start(bf16[2,64,512]{2,1,0:T(8,128)(2,1)} %bitcast.22), channel_id=1, source_target_pairs={{0,1},{1,0},{2,3},{3,2},{4,5},{5,4},{6,7},{7,6},{8,9},{9,8},{10,11... | collective-permute-start | bytes 393224 | tf_op jit(solution)/shard_map/ppermute | solution.py:124
  17.1 5.0 %collective-permute-start.3 = (f32[4,64,1,128]{3,1,0,2:T(8,128)S(1)}, f32[4,64,1,128]{3,1,0,2:T(8,128)S(1)}, u32[]{:S(2)}, u32[]{:S(2)}) collective-permute-start(f32[4,64,1,128]{3,1,0,2:T(8,128)S(1)} %get-tuple-element.34), channel_id=1, source_target_pairs={{0,1},{1,0},{2,3},{3,2},{4,5},{5,4},{6,7},{7,6},{8,9},{9,8},{10,11... | collective-permute-start | bytes 393224 | tf_op jit(solution)/shard_map/ppermute | solution.py:135
  22.3 6.4 %collective-permute-start.4 = (f32[512,1,128]{2,0,1:T(8,128)S(1)}, f32[512,1,128]{2,0,1:T(8,128)S(1)}, u32[]{:S(2)}, u32[]{:S(2)}) collective-permute-start(f32[512,1,128]{2,0,1:T(8,128)S(1)} %bitcast.98), channel_id=1, source_target_pairs={{0,16},{8,24},{16,0},{24,8},{1,17},{9,25},{17,1},{25,9},{2,18},{10... | collective-permute-start | bytes 786440 | tf_op jit(solution)/shard_map/ppermute | solution.py:68
  24.6 13.2 %collective-permute-start.11 = (bf16[3,2,64,512]{3,2,1,0:T(8,128)(2,1)S(1)}, bf16[3,2,64,512]{3,2,1,0:T(8,128)(2,1)}, u32[]{:S(2)}, u32[]{:S(2)}) collective-permute-start(bf16[3,2,64,512]{3,2,1,0:T(8,128)(2,1)S(1)} %pad_maximum_fusion.7), channel_id=1, source_target_pairs={{0,1},{1,0},{2,3},{3,2},{4,5},{5,4},{6,7},{7,6},{8,9},{9,8},{10,11... | collective-permute-start | bytes 1179656 | tf_op jit(solution)/shard_map/ppermute | solution.py:154
  27.1 1.7 %collective-permute-start.5 = (f32[512,1,128]{2,0,1:T(8,128)S(1)}, f32[512,1,128]{2,0,1:T(8,128)S(1)}, u32[]{:S(2)}, u32[]{:S(2)}) collective-permute-start(f32[512,1,128]{2,0,1:T(8,128)S(1)} %bitcast.99), channel_id=1, source_target_pairs={{0,8},{8,0},{16,24},{24,16},{1,9},{9,1},{17,25},{25,17},{2,10},{10... | collective-permute-start | bytes 786440 | tf_op jit(solution)/shard_map/ppermute | solution.py:70
  28.7 1.5 %collective-permute-start.6 = (f32[512,1,128]{2,0,1:T(8,128)S(1)}, f32[512,1,128]{2,0,1:T(8,128)S(1)}, u32[]{:S(2)}, u32[]{:S(2)}) collective-permute-start(f32[512,1,128]{2,0,1:T(8,128)S(1)} %collective-permute-done.4), channel_id=1, source_target_pairs={{0,8},{8,0},{16,24},{24,16},{1,9},{9,1},{17,25},{25,17},{2,10},{10... | collective-permute-start | bytes 786440 | tf_op jit(solution)/shard_map/ppermute | solution.py:70
  40.2 2.6 %collective-permute-start.12 = (f32[2,1,512]{2,1,0:T(1,128)S(1)}, f32[2,1,512]{2,1,0:T(1,128)S(1)}, u32[]{:S(2)}, u32[]{:S(2)}) collective-permute-start(f32[2,1,512]{2,1,0:T(1,128)S(1)} %pad_maximum_fusion.10), channel_id=1, source_target_pairs={{0,24},{8,0},{16,8},{24,16},{1,25},{9,1},{17,9},{25,17},{2,26},{10... | collective-permute-start | bytes 12296 | tf_op jit(solution)/shard_map/ppermute | solution.py:15
  41.4 3.6 %collective-permute-start.13 = (f32[2,1,512]{2,1,0:T(1,128)S(1)}, f32[2,1,512]{2,1,0:T(1,128)S(1)}, u32[]{:S(2)}, u32[]{:S(2)}) collective-permute-start(f32[2,1,512]{2,1,0:T(1,128)S(1)} %pad_maximum_fusion.10), channel_id=1, source_target_pairs={{0,16},{8,24},{16,0},{24,8},{1,17},{9,25},{17,1},{25,9},{2,18},{10... | collective-permute-start | bytes 12296 | tf_op jit(solution)/shard_map/ppermute | solution.py:15
  42.0 3.1 %collective-permute-start.14 = (f32[2,1,512]{2,1,0:T(1,128)S(1)}, f32[2,1,512]{2,1,0:T(1,128)S(1)}, u32[]{:S(2)}, u32[]{:S(2)}) collective-permute-start(f32[2,1,512]{2,1,0:T(1,128)S(1)} %pad_maximum_fusion.10), channel_id=1, source_target_pairs={{0,8},{8,16},{16,24},{24,0},{1,9},{9,17},{17,25},{25,1},{2,10},{10... | collective-permute-start | bytes 12296 | tf_op jit(solution)/shard_map/ppermute | solution.py:15

commit v11 on v10

--- a/solution.py
+++ b/solution.py
@@ -132,14 +132,25 @@
         pieces.append(lax.ppermute(sent, "tile", pairs))
     pieces = jnp.stack(pieces)
     mine_tt = lax.dynamic_slice_in_dim(pieces, y * per_tile, per_tile, 2)
-    theirs_tt = lax.ppermute(
-        lax.dynamic_slice_in_dim(pieces, (1 - y) * per_tile, per_tile, 2), "tile", [(j, j ^ 1) for j in range(tiles)]
-    )
-    both_tt = jnp.stack([mine_tt, theirs_tt], axis=1)
-    both_tt = jnp.roll(jnp.roll(both_tt, z, axis=0), y, axis=1)
-    regrouped = both_tt.reshape((-1,) + both_tt.shape[3:])
-    view = gather_columns(regrouped, "freq", freqs)
-    view = jnp.moveaxis(view.reshape((freqs,) + regrouped.shape), 0, 2)
+    neighbour_tt = lax.dynamic_slice_in_dim(pieces, (1 - y) * per_tile, per_tile, 2)
+    outer = freqs // 2
+    same_core = [jnp.stack([mine_tt, lax.ppermute(neighbour_tt, "tile", swap)])]
+    for so in range(1, outer):
+        straight = [(i, (i - 2 * so) % freqs) for i in range(freqs)]
+        diagonal = [
+            (i * tiles + t, ((i - 2 * so) % freqs) * tiles + (t ^ 1)) for i in range(freqs) for t in range(tiles)
+        ]
+        same_core.append(
+            jnp.stack(
+                [lax.ppermute(mine_tt, "freq", straight), lax.ppermute(neighbour_tt, ("freq", "tile"), diagonal)]
+            )
+        )
+    same_core = jnp.stack(same_core)
+    partner = lax.ppermute(same_core, "freq", [(i, i ^ 1) for i in range(freqs)])
+    view = jnp.stack([same_core, partner], axis=1)
+    view = jnp.transpose(view, (3, 2, 4, 5, 0, 1, 6))
+    view = jnp.roll(jnp.roll(view, z, axis=0), y, axis=1)
+    view = view.reshape((-1,) + view.shape[3:4] + (freqs,) + view.shape[6:])
     elements, row_count, _, width = view.shape
     voxels = row_count * freqs * width
 

time: 45.9 us -> 48.7 us (1.061)
  waiting for transfers between devices: 15 us -> 16.3 us
  other arithmetic: 7.94 us -> 8.75 us
    convert_element_type x0 -> x1, other arithmetic: none -> 4.16 us  [body(): field_imag = (-jnp.sin(angle)).astype(jnp.bfloat16)]
    another operation x3, other arithmetic: 3.91 us -> 0.15 us  [the longest x1 0.11 us: body(): view = jnp.stack([same_core, partner], axis=1)]
    ppermute x3, waiting for transfers between devices: 5.63 us -> 7.73 us  [body(): pieces.append(lax.ppermute(sent, 'tile', pairs))]
    ppermute x4, waiting for transfers between devices: 6.25 us -> 4.73 us  [the longest x1 3.08 us: body(): same_core = [jnp.stack([mine_tt, lax.ppermute(neighbour_tt, 'tile', swap)])]]
    another operation x2 -> x1, local copies, waits for them, and re-layouts: 0.07 us -> 1.47 us  [body(): pieces = jnp.stack(pieces)]
    dynamic_slice x3 -> x1, local copies, waits for them, and re-layouts: 1.5 us -> 0.24 us  [body(): mine_tt = lax.dynamic_slice_in_dim(pieces, y * per_tile, per_tile, 2)]
    ppermute x3, waiting for transfers between devices: 0.01 us -> 1 us  [body(): cap_row.append(lax.ppermute(capture[0], 'tile', pairs))]
    convert_element_type x1 -> x3, local copies, waits for them, and re-layouts: 0.2 us -> 0.94 us  [body(): field_imag = (-jnp.sin(angle)).astype(jnp.bfloat16)]
  transfers between devices with their start and end apart: 15 -> 15, of which waited for: 6 -> 7; matrix products, arithmetic and copies ran while one was open for 19% -> 21% of each run, Pallas kernels for 0% -> 0%
where the time goes in v11:
time: 48.7 us; the launch traced here: 48.5 us
  starting transfers between devices  16.7 us (34%)
  waiting for transfers between devices  16.3 us (33%)
  other arithmetic  8.75 us (18%)
  local copies, waits for them, and re-layouts  3.84 us (8%)
  matrix products  1.76 us (4%)
  between operations  1.14 us (2%)
    ppermute x3, waiting for transfers between devices, body(): pieces.append(lax.ppermute(sent, 'tile', pairs))  7.73 us
    convert_element_type x1, other arithmetic, body(): field_imag = (-jnp.sin(angle)).astype(jnp.bfloat16)  4.16 us
    ppermute x3, starting transfers between devices, body(): pieces.append(lax.ppermute(sent, 'tile', pairs))  3.99 us
    ppermute x3, starting transfers between devices, body(): cap_row.append(lax.ppermute(capture[0], 'tile', pairs))  3.83 us
    ppermute x1, waiting for transfers between devices, body(): same_core = [jnp.stack([mine_tt, lax.ppermute(neighbour_tt, 'tile', swap)])]  3.08 us
    ppermute x3, waiting for transfers between devices, gather_shifted(): pieces.append(lax.ppermute(block, axis_name, pairs))  2.86 us
    ppermute x1, starting transfers between devices, body(): other = (own_swapped, lax.ppermute(jnp.stack(row[1:]), 'tile', swap))  1.97 us
    ppermute x3, starting transfers between devices, gather_shifted(): pieces.append(lax.ppermute(block, axis_name, pairs))  1.77 us
  transfers between devices with their start and end apart: 15, of which 7 were waited for; matrix products, arithmetic and copies ran while one was open for 21% of the time, Pallas kernels for 0%

profile of v11, /device:TPU:16, one launch (start us, length us, event | category | flops | bytes accessed | tf_op | source)
XLA Modules:
  0.0 48.5 jit_solution(15740145811220651673)
XLA Ops:
  0.0 1.5 %dynamic-slice_bitcast_fusion.4 = (f32[1,64,2,128]{3,2,1,0:T(2,128)S(1)}, f32[64,2,128]{2,1,0:T(2,128)S(1)}, f32[64,2,128]{2,1,0:T(2,128)S(1)}, f32[64,2,128]{2,1,0:T(2,128)S(1)}) fusion(f32[64,8,128]{2,1,0:T(8,128)} %param.7, s32[]{:T(128)S(6)} %select_n.138, s32[]{:T(128)S(6)} %select_n.140, s32[]{:T(128)S(6)} %select_n.144, s32[]{:T(128)S(6)} %select_n.142), kind=kLoop, calls=%fused_computation.58 | loop fusion | bytes 524304 | tf_op jit(solution)/shard_map/stack | solution.py:133
  1.5 0.5 %collective-permute-start = (f32[64,2,128]{2,1,0:T(2,128)S(1)}, f32[64,2,128]{2,1,0:T(2,128)S(1)}, u32[]{:S(2)}, u32[]{:S(2)}) collective-permute-start(f32[64,2,128]{2,1,0:T(2,128)S(1)} %get-tuple-element.41), channel_id=1, source_target_pairs={{0,6},{1,7},{2,0},{3,1},{4,2},{5,3},{6,4},{7,5},{8,14},{9,15},{10,... | collective-permute-start | bytes 196616 | tf_op jit(solution)/shard_map/ppermute | solution.py:132
  2.0 3.5 %collective-permute-start.1 = (f32[64,2,128]{2,1,0:T(2,128)S(1)}, f32[64,2,128]{2,1,0:T(2,128)S(1)}, u32[]{:S(2)}, u32[]{:S(2)}) collective-permute-start(f32[64,2,128]{2,1,0:T(2,128)S(1)} %get-tuple-element.43), channel_id=1, source_target_pairs={{0,4},{1,5},{2,6},{3,7},{4,0},{5,1},{6,2},{7,3},{8,12},{9,13},{10,... | collective-permute-start | bytes 196616 | tf_op jit(solution)/shard_map/ppermute | solution.py:132
  5.5 2.0 %collective-permute-start.7 = (bf16[2,64,512]{2,1,0:T(8,128)(2,1)}, bf16[2,64,512]{2,1,0:T(8,128)(2,1)S(1)}, u32[]{:S(2)}, u32[]{:S(2)}) collective-permute-start(bf16[2,64,512]{2,1,0:T(8,128)(2,1)} %bitcast.21), channel_id=1, source_target_pairs={{0,6},{1,7},{2,0},{3,1},{4,2},{5,3},{6,4},{7,5},{8,14},{9,15},{10,... | collective-permute-start | bytes 393224 | tf_op jit(solution)/shard_map/ppermute | solution.py:123
  7.5 1.8 %collective-permute-start.8 = (bf16[2,64,512]{2,1,0:T(8,128)(2,1)}, bf16[2,64,512]{2,1,0:T(8,128)(2,1)S(1)}, u32[]{:S(2)}, u32[]{:S(2)}) collective-permute-start(bf16[2,64,512]{2,1,0:T(8,128)(2,1)} %bitcast.21), channel_id=1, source_target_pairs={{0,4},{1,5},{2,6},{3,7},{4,0},{5,1},{6,2},{7,3},{8,12},{9,13},{10,... | collective-permute-start | bytes 393224 | tf_op jit(solution)/shard_map/ppermute | solution.py:123
  9.3 0.1 collective-permute-done.1
  9.4 7.6 %collective-permute-done.2 = f32[64,2,128]{2,1,0:T(2,128)S(1)} collective-permute-done((f32[64,2,128]{2,1,0:T(2,128)S(1)}, f32[64,2,128]{2,1,0:T(2,128)S(1)}, u32[]{:S(2)}, u32[]{:S(2)}) %collective-permute-start.2) | collective-permute-done | bytes 65568 | tf_op jit(solution)/shard_map/ppermute | solution.py:132
  17.0 0.1 pad_maximum_fusion.7
  17.1 0.2 constant_dynamic-slice_fusion.5
  17.4 1.6 %collective-permute-start.3 = (f32[4,64,1,128]{3,1,0,2:T(8,128)S(1)}, f32[4,64,1,128]{3,1,0,2:T(8,128)S(1)}, u32[]{:S(2)}, u32[]{:S(2)}) collective-permute-start(f32[4,64,1,128]{3,1,0,2:T(8,128)S(1)} %bitcast.103), channel_id=1, source_target_pairs={{0,1},{1,0},{2,3},{3,2},{4,5},{5,4},{6,7},{7,6},{8,9},{9,8},{10,11... | collective-permute-start | bytes 393224 | tf_op jit(solution)/shard_map/ppermute | solution.py:137
  19.0 1.4 %collective-permute-start.5 = (f32[4,64,1,128]{3,2,1,0:T(1,128)S(1)}, f32[4,64,1,128]{3,2,1,0:T(1,128)S(1)}, u32[]{:S(2)}, u32[]{:S(2)}) collective-permute-start(f32[4,64,1,128]{3,2,1,0:T(1,128)S(1)} %get-tuple-element.39), channel_id=1, source_target_pairs={{0,17},{1,16},{2,19},{3,18},{4,21},{5,20},{6,23},{7,22},{8,25},{9,... | collective-permute-start | bytes 393224 | tf_op jit(solution)/shard_map/ppermute | solution.py:145
  20.4 0.5 %collective-permute-start.4 = (f32[4,64,1,128]{3,1,0,2:T(8,128)S(1)}, f32[4,64,1,128]{3,1,0,2:T(8,128)S(1)}, u32[]{:S(2)}, u32[]{:S(2)}) collective-permute-start(f32[4,64,1,128]{3,1,0,2:T(8,128)S(1)} %bitcast.95), channel_id=1, source_target_pairs={{0,16},{8,24},{16,0},{24,8},{1,17},{9,25},{17,1},{25,9},{2,18},{10... | collective-permute-start | bytes 393224 | tf_op jit(solution)/shard_map/ppermute | solution.py:145
  21.0 0.1 select_reduce_fusion.1
  21.1 3.1 %collective-permute-done.3 = f32[4,64,1,128]{3,1,0,2:T(8,128)S(1)} collective-permute-done((f32[4,64,1,128]{3,1,0,2:T(8,128)S(1)}, f32[4,64,1,128]{3,1,0,2:T(8,128)S(1)}, u32[]{:S(2)}, u32[]{:S(2)}) %collective-permute-start.3) | collective-permute-done | bytes 131104 | tf_op jit(solution)/shard_map/ppermute | solution.py:137
  24.2 1.6 %collective-permute-done.4 = f32[4,64,1,128]{3,1,0,2:T(8,128)S(1)} collective-permute-done((f32[4,64,1,128]{3,1,0,2:T(8,128)S(1)}, f32[4,64,1,128]{3,1,0,2:T(8,128)S(1)}, u32[]{:S(2)}, u32[]{:S(2)}) %collective-permute-start.4) | collective-permute-done | bytes 131104 | tf_op jit(solution)/shard_map/ppermute | solution.py:145
  25.8 1.5 %collective-permute-start.10 = (bf16[2,64,512]{2,1,0:T(8,128)(2,1)}, bf16[2,64,512]{2,1,0:T(8,128)(2,1)}, u32[]{:S(2)}, u32[]{:S(2)}) collective-permute-start(bf16[2,64,512]{2,1,0:T(8,128)(2,1)} %bitcast.21), channel_id=1, source_target_pairs={{0,1},{1,0},{2,3},{3,2},{4,5},{5,4},{6,7},{7,6},{8,9},{9,8},{10,11... | collective-permute-start | bytes 393224 | tf_op jit(solution)/shard_map/ppermute | solution.py:124
  27.3 0.1 fusion.26
  27.4 0.1 collective-permute-start.6
  28.3 1.0 %collective-permute-done.9 = bf16[2,64,512]{2,1,0:T(8,128)(2,1)S(1)} collective-permute-done((bf16[2,64,512]{2,1,0:T(8,128)(2,1)}, bf16[2,64,512]{2,1,0:T(8,128)(2,1)S(1)}, u32[]{:S(2)}, u32[]{:S(2)}) %collective-permute-start.9) | collective-permute-done | bytes 131104 | tf_op jit(solution)/shard_map/ppermute | solution.py:123
  29.4 2.0 %collective-permute-start.11 = (bf16[3,2,64,512]{3,2,1,0:T(8,128)(2,1)S(1)}, bf16[3,2,64,512]{3,2,1,0:T(8,128)(2,1)}, u32[]{:S(2)}, u32[]{:S(2)}) collective-permute-start(bf16[3,2,64,512]{3,2,1,0:T(8,128)(2,1)S(1)} %pad_maximum_fusion.5), channel_id=1, source_target_pairs={{0,1},{1,0},{2,3},{3,2},{4,5},{5,4},{6,7},{7,6},{8,9},{9,8},{10,11... | collective-permute-start | bytes 1179656 | tf_op jit(solution)/shard_map/ppermute | solution.py:165
  31.3 1.0 %pad_maximum_fusion.4 = bf16[4,2,64,512]{3,2,1,0:T(8,128)(2,1)S(1)} fusion(bf16[1,2,64,512]{3,2,1,0:T(8,128)(2,1)S(1)} %bitcast.102, bf16[1,2,64,512]{3,2,1,0:T(8,128)(2,1)S(1)} %bitcast.100, bf16[1,2,64,512]{3,2,1,0:T(8,128)(2,1)S(1)} %bitcast.98, bf16[1,2,64,512]{3,2,1,0:T(8,128)(2,1)} %param.11), kind=kLoop, calls=%fused_computation.32 | loop fusion | flops 786432 | bytes 1048576 | tf_op jit(solution)/shard_map/stack | solution.py:166
  32.4 0.1 maximum_bitcast_fusion
  32.5 0.2 fusion.2
  32.7 4.2 %negate_convert_fusion = (bf16[4,2,64,1,2,2,128]{6,2,0,1,4,3,5:T(8,128)(2,1)S(1)}, bf16[4,2,64,1,2,2,128]{6,2,0,1,4,3,5:T(8,128)(2,1)S(1)}) fusion(s32[]{:T(128)S(6)} %select_n.151, f32[4,2,64,1,2,2,128]{6,2,0,1,4,3,5:T(8,128)S(1)} %fusion.2, f32[]{:T(128)} %bitcast.4), kind=kLoop, calls=%fused_computation.11 | loop fusion | flops 1835008 | bytes 2097160 | tf_op jit(solution)/shard_map/convert_element_type | solution.py:160
  36.9 0.5 %copy.16 = bf16[4,2,64,1,2,2,128]{6,5,4,2,1,0,3:T(2,128)(2,1)S(1)} copy(bf16[4,2,64,1,2,2,128]{6,2,0,1,4,3,5:T(8,128)(2,1)S(1)} %get-tuple-element.25) | data formatting | bytes 1048576 | tf_op jit(solution)/shard_map/convert_element_type | solution.py:159
  37.5 0.2 convert_element_type.44
  37.7 0.2 convert_element_type.47
  37.9 0.5 %copy.18 = bf16[4,2,64,1,2,2,128]{6,5,4,2,1,0,3:T(2,128)(2,1)S(1)} copy(bf16[4,2,64,1,2,2,128]{6,2,0,1,4,3,5:T(8,128)(2,1)S(1)} %get-tuple-element.24) | data formatting | bytes 1048576 | tf_op jit(solution)/shard_map/convert_element_type | solution.py:160
  38.4 0.2 convert_element_type.50
  38.6 0.2 convert_element_type.49
  38.8 0.1 dynamic-slice_bitcast_fusion
  38.9 0.1 fusion.15
  39.1 0.1 fusion.14
  39.2 0.2 fusion.27
  39.4 0.4 fusion.30
  39.9 0.4 convolution_add_fusion.1
  40.3 0.2 fusion.10
  40.5 0.1 fusion.12
  40.7 0.1 fusion.13
  40.8 1.1 %pad_maximum_fusion.6 = (bf16[4,1,64,512]{3,2,1,0:T(8,128)(2,1)S(1)}, bf16[4,1,64,512]{3,2,1,0:T(8,128)(2,1)S(1)}) fusion(bf16[3,2,64,512]{3,2,1,0:T(8,128)(2,1)} %collective-permute-done.11, bf16[1,2,64,512]{3,2,1,0:T(8,128)(2,1)} %bitcast.35), kind=kLoop, calls=%fused_computation.47 | loop fusion | flops 262144 | bytes 1048576 | tf_op jit(solution)/shard_map/concatenate | solution.py:191
  41.9 0.5 fusion.31
  42.4 0.4 convolution_add_fusion
  42.8 0.2 fusion.6
  43.2 1.6 %collective-permute-start.13 = (f32[2,1,512]{2,1,0:T(1,128)S(1)}, f32[2,1,512]{2,1,0:T(1,128)S(1)}, u32[]{:S(2)}, u32[]{:S(2)}) collective-permute-start(f32[2,1,512]{2,1,0:T(1,128)S(1)} %pad_maximum_fusion.8), channel_id=1, source_target_pairs={{0,16},{8,24},{16,0},{24,8},{1,17},{9,25},{17,1},{25,9},{2,18},{10... | collective-permute-start | bytes 12296 | tf_op jit(solution)/shard_map/ppermute | solution.py:15
  44.8 0.2 collective-permute-start.14
  45.0 1.9 %collective-permute-done.13 = f32[2,1,512]{2,1,0:T(1,128)S(1)} collective-permute-done((f32[2,1,512]{2,1,0:T(1,128)S(1)}, f32[2,1,512]{2,1,0:T(1,128)S(1)}, u32[]{:S(2)}, u32[]{:S(2)}) %collective-permute-start.13) | collective-permute-done | bytes 4128 | tf_op jit(solution)/shard_map/ppermute | solution.py:15
  46.9 0.9 %collective-permute-done.14 = f32[2,1,512]{2,1,0:T(1,128)S(1)} collective-permute-done((f32[2,1,512]{2,1,0:T(1,128)S(1)}, f32[2,1,512]{2,1,0:T(1,128)S(1)}, u32[]{:S(2)}, u32[]{:S(2)}) %collective-permute-start.14) | collective-permute-done | bytes 4128 | tf_op jit(solution)/shard_map/ppermute | solution.py:15
  47.9 0.6 %fusion.23 = f32[2,1,512]{2,1,0:T(1,128)} fusion(f32[8,2,1,512]{3,2,1,0:T(1,128)S(1)} %constant_dynamic-update-slice_fusion.2, s32[]{:T(128)S(6)} %add.214, s32[]{:T(128)S(6)} %add.213, s32[]{:T(128)S(6)} %add.212, s32[]{:T(128)S(6)} %select_n.159), kind=kLoop, calls=%fused_computation.92 | loop fusion | flops 3072 | bytes 20496 | tf_op jit(solution)/shard_map/add | solution.py:96
  (37 shorter events, 0.4 us)
Async XLA Ops:
  0.0 19.0 %copy-start.1 = (f32[1,2,64]{2,1,0:T(2,128)S(1)}, f32[1,2,64]{2,1,0:T(2,128)}, u32[]{:S(2)}) copy-start(f32[1,2,64]{2,1,0:T(2,128)} %param.10) | copy-start | bytes 1540
  0.0 21.0 %copy-start = (s32[1,512]{1,0:T(1,128)S(1)}, s32[1,512]{1,0:T(1,128)}, u32[]{:S(2)}) copy-start(s32[1,512]{1,0:T(1,128)} %param.8) | copy-start | bytes 6148
  1.5 7.8 %collective-permute-start = (f32[64,2,128]{2,1,0:T(2,128)S(1)}, f32[64,2,128]{2,1,0:T(2,128)S(1)}, u32[]{:S(2)}, u32[]{:S(2)}) collective-permute-start(f32[64,2,128]{2,1,0:T(2,128)S(1)} %get-tuple-element.41), channel_id=1, source_target_pairs={{0,6},{1,7},{2,0},{3,1},{4,2},{5,3},{6,4},{7,5},{8,14},{9,15},{10,... | collective-permute-start | bytes 196616 | tf_op jit(solution)/shard_map/ppermute | solution.py:132
  2.0 7.4 %collective-permute-start.1 = (f32[64,2,128]{2,1,0:T(2,128)S(1)}, f32[64,2,128]{2,1,0:T(2,128)S(1)}, u32[]{:S(2)}, u32[]{:S(2)}) collective-permute-start(f32[64,2,128]{2,1,0:T(2,128)S(1)} %get-tuple-element.43), channel_id=1, source_target_pairs={{0,4},{1,5},{2,6},{3,7},{4,0},{5,1},{6,2},{7,3},{8,12},{9,13},{10,... | collective-permute-start | bytes 196616 | tf_op jit(solution)/shard_map/ppermute | solution.py:132
  5.5 11.6 %collective-permute-start.2 = (f32[64,2,128]{2,1,0:T(2,128)S(1)}, f32[64,2,128]{2,1,0:T(2,128)S(1)}, u32[]{:S(2)}, u32[]{:S(2)}) collective-permute-start(f32[64,2,128]{2,1,0:T(2,128)S(1)} %get-tuple-element.42), channel_id=1, source_target_pairs={{0,2},{1,3},{2,4},{3,5},{4,6},{5,7},{6,0},{7,1},{8,10},{9,11},{10,... | collective-permute-start | bytes 196616 | tf_op jit(solution)/shard_map/ppermute | solution.py:132
  5.5 22.8 %collective-permute-start.7 = (bf16[2,64,512]{2,1,0:T(8,128)(2,1)}, bf16[2,64,512]{2,1,0:T(8,128)(2,1)S(1)}, u32[]{:S(2)}, u32[]{:S(2)}) collective-permute-start(bf16[2,64,512]{2,1,0:T(8,128)(2,1)} %bitcast.21), channel_id=1, source_target_pairs={{0,6},{1,7},{2,0},{3,1},{4,2},{5,3},{6,4},{7,5},{8,14},{9,15},{10,... | collective-permute-start | bytes 393224 | tf_op jit(solution)/shard_map/ppermute | solution.py:123
  7.5 20.8 %collective-permute-start.8 = (bf16[2,64,512]{2,1,0:T(8,128)(2,1)}, bf16[2,64,512]{2,1,0:T(8,128)(2,1)S(1)}, u32[]{:S(2)}, u32[]{:S(2)}) collective-permute-start(bf16[2,64,512]{2,1,0:T(8,128)(2,1)} %bitcast.21), channel_id=1, source_target_pairs={{0,4},{1,5},{2,6},{3,7},{4,0},{5,1},{6,2},{7,3},{8,12},{9,13},{10,... | collective-permute-start | bytes 393224 | tf_op jit(solution)/shard_map/ppermute | solution.py:123
  17.4 6.8 %collective-permute-start.3 = (f32[4,64,1,128]{3,1,0,2:T(8,128)S(1)}, f32[4,64,1,128]{3,1,0,2:T(8,128)S(1)}, u32[]{:S(2)}, u32[]{:S(2)}) collective-permute-start(f32[4,64,1,128]{3,1,0,2:T(8,128)S(1)} %bitcast.103), channel_id=1, source_target_pairs={{0,1},{1,0},{2,3},{3,2},{4,5},{5,4},{6,7},{7,6},{8,9},{9,8},{10,11... | collective-permute-start | bytes 393224 | tf_op jit(solution)/shard_map/ppermute | solution.py:137
  19.0 8.3 %collective-permute-start.5 = (f32[4,64,1,128]{3,2,1,0:T(1,128)S(1)}, f32[4,64,1,128]{3,2,1,0:T(1,128)S(1)}, u32[]{:S(2)}, u32[]{:S(2)}) collective-permute-start(f32[4,64,1,128]{3,2,1,0:T(1,128)S(1)} %get-tuple-element.39), channel_id=1, source_target_pairs={{0,17},{1,16},{2,19},{3,18},{4,21},{5,20},{6,23},{7,22},{8,25},{9,... | collective-permute-start | bytes 393224 | tf_op jit(solution)/shard_map/ppermute | solution.py:145
  20.4 5.4 %collective-permute-start.4 = (f32[4,64,1,128]{3,1,0,2:T(8,128)S(1)}, f32[4,64,1,128]{3,1,0,2:T(8,128)S(1)}, u32[]{:S(2)}, u32[]{:S(2)}) collective-permute-start(f32[4,64,1,128]{3,1,0,2:T(8,128)S(1)} %bitcast.95), channel_id=1, source_target_pairs={{0,16},{8,24},{16,0},{24,8},{1,17},{9,25},{17,1},{25,9},{2,18},{10... | collective-permute-start | bytes 393224 | tf_op jit(solution)/shard_map/ppermute | solution.py:145
  24.1 5.2 %collective-permute-start.9 = (bf16[2,64,512]{2,1,0:T(8,128)(2,1)}, bf16[2,64,512]{2,1,0:T(8,128)(2,1)S(1)}, u32[]{:S(2)}, u32[]{:S(2)}) collective-permute-start(bf16[2,64,512]{2,1,0:T(8,128)(2,1)} %bitcast.21), channel_id=1, source_target_pairs={{0,2},{1,3},{2,4},{3,5},{4,6},{5,7},{6,0},{7,1},{8,10},{9,11},{10,... | collective-permute-start | bytes 393224 | tf_op jit(solution)/shard_map/ppermute | solution.py:123
  25.8 15.0 %collective-permute-start.10 = (bf16[2,64,512]{2,1,0:T(8,128)(2,1)}, bf16[2,64,512]{2,1,0:T(8,128)(2,1)}, u32[]{:S(2)}, u32[]{:S(2)}) collective-permute-start(bf16[2,64,512]{2,1,0:T(8,128)(2,1)} %bitcast.21), channel_id=1, source_target_pairs={{0,1},{1,0},{2,3},{3,2},{4,5},{5,4},{6,7},{7,6},{8,9},{9,8},{10,11... | collective-permute-start | bytes 393224 | tf_op jit(solution)/shard_map/ppermute | solution.py:124
  27.4 4.9 %collective-permute-start.6 = (f32[2,2,4,64,1,128]{5,3,2,1,4,0:T(8,128)S(1)}, f32[2,2,4,64,1,128]{5,3,2,1,4,0:T(8,128)S(1)}, u32[]{:S(2)}, u32[]{:S(2)}) collective-permute-start(f32[2,2,4,64,1,128]{5,3,2,1,4,0:T(8,128)S(1)} %get-tuple-element.37), channel_id=1, source_target_pairs={{0,8},{8,0},{16,24},{24,16},{1,9},{9,1},{17,25},{25,17},{2,10},{10... | collective-permute-start | bytes 1572872 | tf_op jit(solution)/shard_map/ppermute | solution.py:149
  29.4 11.4 %collective-permute-start.11 = (bf16[3,2,64,512]{3,2,1,0:T(8,128)(2,1)S(1)}, bf16[3,2,64,512]{3,2,1,0:T(8,128)(2,1)}, u32[]{:S(2)}, u32[]{:S(2)}) collective-permute-start(bf16[3,2,64,512]{3,2,1,0:T(8,128)(2,1)S(1)} %pad_maximum_fusion.5), channel_id=1, source_target_pairs={{0,1},{1,0},{2,3},{3,2},{4,5},{5,4},{6,7},{7,6},{8,9},{9,8},{10,11... | collective-permute-start | bytes 1179656 | tf_op jit(solution)/shard_map/ppermute | solution.py:165
  43.1 1.8 %collective-permute-start.12 = (f32[2,1,512]{2,1,0:T(1,128)S(1)}, f32[2,1,512]{2,1,0:T(1,128)S(1)}, u32[]{:S(2)}, u32[]{:S(2)}) collective-permute-start(f32[2,1,512]{2,1,0:T(1,128)S(1)} %pad_maximum_fusion.8), channel_id=1, source_target_pairs={{0,24},{8,0},{16,8},{24,16},{1,25},{9,1},{17,9},{25,17},{2,26},{10... | collective-permute-start | bytes 12296 | tf_op jit(solution)/shard_map/ppermute | solution.py:15
  43.2 3.7 %collective-permute-start.13 = (f32[2,1,512]{2,1,0:T(1,128)S(1)}, f32[2,1,512]{2,1,0:T(1,128)S(1)}, u32[]{:S(2)}, u32[]{:S(2)}) collective-permute-start(f32[2,1,512]{2,1,0:T(1,128)S(1)} %pad_maximum_fusion.8), channel_id=1, source_target_pairs={{0,16},{8,24},{16,0},{24,8},{1,17},{9,25},{17,1},{25,9},{2,18},{10... | collective-permute-start | bytes 12296 | tf_op jit(solution)/shard_map/ppermute | solution.py:15
  44.8 3.0 %collective-permute-start.14 = (f32[2,1,512]{2,1,0:T(1,128)S(1)}, f32[2,1,512]{2,1,0:T(1,128)S(1)}, u32[]{:S(2)}, u32[]{:S(2)}) collective-permute-start(f32[2,1,512]{2,1,0:T(1,128)S(1)} %pad_maximum_fusion.8), channel_id=1, source_target_pairs={{0,8},{8,16},{16,24},{24,0},{1,9},{9,17},{17,25},{25,1},{2,10},{10... | collective-permute-start | bytes 12296 | tf_op jit(solution)/shard_map/ppermute | solution.py:15

commit v12 on v10

--- a/solution.py
+++ b/solution.py
@@ -117,11 +117,12 @@
     y = k % 2
     swap = [(j, j ^ 1) for j in range(tiles)]
 
-    cap_row = [capture[0]]
+    local = jnp.transpose(capture[0], (1, 0, 2)).reshape(capture.shape[2], -1)
+    cap_row = [local]
     for s in range(1, positions):
         pairs = [(p * 2 + r, ((p - s) % positions) * 2 + r) for p in range(positions) for r in range(2)]
-        cap_row.append(lax.ppermute(capture[0], "tile", pairs))
-    own_swapped = lax.ppermute(capture[0], "tile", swap)
+        cap_row.append(lax.ppermute(local, "tile", pairs))
+    own_swapped = lax.ppermute(local, "tile", swap)
 
     per_tile = travel_time.shape[1] // tiles
     pieces = [lax.dynamic_slice_in_dim(travel_time, 2 * z * per_tile, 2 * per_tile, 1)]
@@ -147,12 +148,13 @@
     angle = scaled * view.reshape(elements, voxels)
     field_real = jnp.cos(angle).astype(jnp.bfloat16)
     field_imag = (-jnp.sin(angle)).astype(jnp.bfloat16)
-    left = jnp.concatenate([field_real, field_imag], axis=1)
-    right = jnp.concatenate([-field_imag, field_real], axis=1)
-
-    row = cap_row
-    other = (own_swapped, lax.ppermute(jnp.stack(row[1:]), "tile", swap))
-    row = jnp.stack(row)
+    fields = jnp.concatenate(
+        [jnp.concatenate([field_real, field_imag], axis=1), jnp.concatenate([-field_imag, field_real], axis=1)],
+        axis=0,
+    )
+
+    rest = lax.ppermute(jnp.stack(cap_row[1:]), "tile", swap)
+    row = jnp.stack(cap_row)
     own = capture.shape[2]
 
     def rows_of(field, which_row):
@@ -161,11 +163,7 @@
         return jnp.roll(picked, -z, axis=0).reshape(-1, voxels)
 
     def partial_focus(group, g_real, g_imag):
-        cap_real = group[:, 0].reshape(-1, group.shape[-1])
-        cap_imag = group[:, 1].reshape(-1, group.shape[-1])
-        product = jnp.dot(cap_real, left, preferred_element_type=jnp.float32) + jnp.dot(
-            cap_imag, right, preferred_element_type=jnp.float32
-        )
+        product = jnp.dot(group.reshape(-1, group.shape[-1]), fields, preferred_element_type=jnp.float32)
         w_real = product[:, :voxels]
         w_imag = product[:, voxels:]
         g_real = g_real.astype(jnp.float32)
@@ -174,12 +172,17 @@
         part_imag = jnp.sum(g_real * w_imag + g_imag * w_real, axis=0)
         return part_real, part_imag
 
+    theirs_real_rows = rows_of(field_real, 1 - y)
+    theirs_imag_rows = rows_of(field_imag, 1 - y)
     mine_real, mine_imag = partial_focus(row, rows_of(field_real, y), rows_of(field_imag, y))
-    theirs_rows = (rows_of(field_real, 1 - y), rows_of(field_imag, 1 - y))
-    mine_real, mine_imag, theirs_rows, other = lax.optimization_barrier((mine_real, mine_imag, theirs_rows, other))
-    theirs_real, theirs_imag = partial_focus(jnp.concatenate([other[0][None], other[1]]), *theirs_rows)
-    focus_real = mine_real + theirs_real
-    focus_imag = mine_imag + theirs_imag
+    first_real, first_imag = partial_focus(own_swapped, theirs_real_rows[:own], theirs_imag_rows[:own])
+    theirs_rows = (theirs_real_rows[own:], theirs_imag_rows[own:])
+    mine_real, mine_imag, first_real, first_imag, theirs_rows, rest = lax.optimization_barrier(
+        (mine_real, mine_imag, first_real, first_imag, theirs_rows, rest)
+    )
+    theirs_real, theirs_imag = partial_focus(rest, *theirs_rows)
+    focus_real = mine_real + (first_real + theirs_real)
+    focus_imag = mine_imag + (first_imag + theirs_imag)
 
     outer = freqs // 2
     focus = jnp.stack([focus_real, focus_imag]).reshape(2, row_count, outer, 2, width)

time: 45.9 us -> 47.3 us (1.031)
  waiting for transfers between devices: 15 us -> 10.2 us
  starting transfers between devices: 16.5 us -> 21 us
  matrix products: 1.87 us -> 4.25 us
  other arithmetic: 7.94 us -> 5.95 us
  local copies, waits for them, and re-layouts: 3.42 us -> 4.31 us
    ppermute x3, waiting for transfers between devices: 5.63 us -> 0.01 us  [body(): pieces.append(lax.ppermute(sent, 'tile', pairs))]
    ppermute x1, starting transfers between devices: 1.58 us -> 6.01 us  [body(): lax.ppermute(lax.dynamic_slice_in_dim(pieces, (1 - y) * per_tile, per_til...]
    dot_general x4 -> x3, matrix products: 1.87 us -> 4.25 us  [partial_focus(): jnp.dot(group.reshape(-1, group.shape[-1]), fields, preferred_element_typ...]
    ppermute x1, waiting for transfers between devices: 1.48 us -> 3.68 us  [gather_columns(): same_core.append(lax.ppermute(block, axis_name, pairs))]
    ppermute x2, waiting for transfers between devices: 1.44 us -> 0.01 us  [gather_columns(): partner = [lax.ppermute(piece, axis_name, swap) for piece in same_core]]
    concatenate x1 -> x0, other arithmetic: 1.11 us -> none  [body(): jnp.concatenate([other[0][None], other[1]])]
    another operation x3, other arithmetic: 4.86 us -> 3.96 us
    ppermute x5, waiting for transfers between devices: 0.01 us -> 0.69 us  [the longest x1 0.68 us: body(): rest = lax.ppermute(jnp.stack(cap_row[1:]), 'tile', swap)]
  transfers between devices with their start and end apart: 15 -> 15, of which waited for: 6 -> 5; matrix products, arithmetic and copies ran while one was open for 19% -> 22% of each run, Pallas kernels for 0% -> 0%
where the time goes in v12:
time: 47.3 us; the launch traced here: 46.9 us
  starting transfers between devices  21 us (44%)
  waiting for transfers between devices  10.2 us (22%)
  other arithmetic  5.95 us (13%)
  local copies, waits for them, and re-layouts  4.31 us (9%)
  matrix products  4.25 us (9%)
  between operations  1.19 us (3%)
    ppermute x1, starting transfers between devices, body(): lax.ppermute(lax.dynamic_slice_in_dim(pieces, (1 - y) * per_tile, per_til...  6.01 us
    dot_general x3, matrix products, partial_focus(): jnp.dot(group.reshape(-1, group.shape[-1]), fields, preferred_element_typ...  4.25 us
    ppermute x3, starting transfers between devices, body(): pieces.append(lax.ppermute(sent, 'tile', pairs))  3.99 us
    ppermute x3, starting transfers between devices, body(): cap_row.append(lax.ppermute(local, 'tile', pairs))  3.94 us
    another operation x1, other arithmetic  3.85 us
    ppermute x1, waiting for transfers between devices, gather_columns(): same_core.append(lax.ppermute(block, axis_name, pairs))  3.68 us
    ppermute x1, waiting for transfers between devices, body(): lax.ppermute(lax.dynamic_slice_in_dim(pieces, (1 - y) * per_tile, per_til...  2.94 us
    ppermute x3, waiting for transfers between devices, gather_shifted(): pieces.append(lax.ppermute(block, axis_name, pairs))  2.92 us
  transfers between devices with their start and end apart: 15, of which 5 were waited for; matrix products, arithmetic and copies ran while one was open for 22% of the time, Pallas kernels for 0%

profile of v12, /device:TPU:16, one launch (start us, length us, event | category | flops | bytes accessed | tf_op | source)
XLA Modules:
  0.0 46.9 jit_solution(16758133971188588402)
XLA Ops:
  0.0 1.5 %constant_dynamic-slice_fusion.14 = (f32[64,2,128]{2,1,0:T(2,128)S(1)}, f32[64,2,128]{2,1,0:T(2,128)S(1)}, f32[64,2,128]{2,1,0:T(2,128)S(1)}, f32[64,2,128]{2,1,0:T(2,128)S(1)}) fusion(f32[64,8,128]{2,1,0:T(8,128)} %param.7, s32[]{:T(128)S(6)} %select_n.138, s32[]{:T(128)S(6)} %select_n.142, s32[]{:T(128)S(6)} %select_n.140, s32[]{:T(128)S(6)} %select_n.144), kind=kLoop, calls=%fused_computation.89 | loop fusion | bytes 524304 | tf_op jit(solution)/shard_map/dynamic_slice | solution.py:128
  1.5 0.0 copy-start.4
  1.5 0.5 %collective-permute-start = (f32[64,2,128]{2,0,1:T(8,128)S(1)}, f32[64,2,128]{2,0,1:T(8,128)S(1)}, u32[]{:S(2)}, u32[]{:S(2)}) collective-permute-start(f32[64,2,128]{2,0,1:T(8,128)S(1)} %copy.32), channel_id=1, source_target_pairs={{0,6},{1,7},{2,0},{3,1},{4,2},{5,3},{6,4},{7,5},{8,14},{9,15},{10,... | collective-permute-start | bytes 196616 | tf_op jit(solution)/shard_map/ppermute | solution.py:133
  2.0 3.5 %collective-permute-start.1 = (f32[64,2,128]{2,0,1:T(8,128)S(1)}, f32[64,2,128]{2,0,1:T(8,128)S(1)}, u32[]{:S(2)}, u32[]{:S(2)}) collective-permute-start(f32[64,2,128]{2,0,1:T(8,128)S(1)} %copy.33), channel_id=1, source_target_pairs={{0,4},{1,5},{2,6},{3,7},{4,0},{5,1},{6,2},{7,3},{8,12},{9,13},{10,... | collective-permute-start | bytes 196616 | tf_op jit(solution)/shard_map/ppermute | solution.py:133
  5.5 0.7 %copy.35 = bf16[2,8,8,512]{3,2,0,1:T(8,128)(2,1)} copy(bf16[2,8,8,512]{3,2,1,0:T(8,128)(2,1)S(1)} %bitcast.120) | data formatting | bytes 262144 | tf_op jit(solution)/shard_map/reshape | solution.py:120
  6.2 1.5 %collective-permute-start.10 = (bf16[64,1024]{1,0:T(8,128)(2,1)}, bf16[64,1024]{1,0:T(8,128)(2,1)}, u32[]{:S(2)}, u32[]{:S(2)}) collective-permute-start(bf16[64,1024]{1,0:T(8,128)(2,1)} %bitcast.60), channel_id=1, source_target_pairs={{0,1},{1,0},{2,3},{3,2},{4,5},{5,4},{6,7},{7,6},{8,9},{9,8},{10,11... | collective-permute-start | bytes 393224 | tf_op jit(solution)/shard_map/ppermute | solution.py:125
  7.7 2.0 %collective-permute-start.7 = (bf16[64,1024]{1,0:T(8,128)(2,1)}, bf16[64,1024]{1,0:T(8,128)(2,1)S(1)}, u32[]{:S(2)}, u32[]{:S(2)}) collective-permute-start(bf16[64,1024]{1,0:T(8,128)(2,1)} %bitcast.60), channel_id=1, source_target_pairs={{0,6},{1,7},{2,0},{3,1},{4,2},{5,3},{6,4},{7,5},{8,14},{9,15},{10,... | collective-permute-start | bytes 393224 | tf_op jit(solution)/shard_map/ppermute | solution.py:124
  9.7 1.9 %collective-permute-start.8 = (bf16[64,1024]{1,0:T(8,128)(2,1)}, bf16[64,1024]{1,0:T(8,128)(2,1)S(1)}, u32[]{:S(2)}, u32[]{:S(2)}) collective-permute-start(bf16[64,1024]{1,0:T(8,128)(2,1)} %bitcast.60), channel_id=1, source_target_pairs={{0,4},{1,5},{2,6},{3,7},{4,0},{5,1},{6,2},{7,3},{8,12},{9,13},{10,... | collective-permute-start | bytes 393224 | tf_op jit(solution)/shard_map/ppermute | solution.py:124
  11.7 0.0 collective-permute-done.1
  11.7 0.0 copy-start.3
  11.8 6.0 %collective-permute-start.3 = (f32[4,64,1,128]{3,1,0,2:T(8,128)S(1)}, f32[4,64,1,128]{3,1,0,2:T(8,128)S(1)}, u32[]{:S(2)}, u32[]{:S(2)}) collective-permute-start(f32[4,64,1,128]{3,1,0,2:T(8,128)S(1)} %get-tuple-element.34), channel_id=1, source_target_pairs={{0,1},{1,0},{2,3},{3,2},{4,5},{5,4},{6,7},{7,6},{8,9},{9,8},{10,11... | collective-permute-start | bytes 393224 | tf_op jit(solution)/shard_map/ppermute | solution.py:136
  17.8 2.9 %collective-permute-done.3 = f32[4,64,1,128]{3,1,0,2:T(8,128)S(1)} collective-permute-done((f32[4,64,1,128]{3,1,0,2:T(8,128)S(1)}, f32[4,64,1,128]{3,1,0,2:T(8,128)S(1)}, u32[]{:S(2)}, u32[]{:S(2)}) %collective-permute-start.3) | collective-permute-done | bytes 131104 | tf_op jit(solution)/shard_map/ppermute | solution.py:136
  20.7 0.1 fusion.14
  20.8 0.1 fusion.12
  20.9 1.6 %collective-permute-start.4 = (f32[512,1,128]{2,0,1:T(8,128)S(1)}, f32[512,1,128]{2,0,1:T(8,128)S(1)}, u32[]{:S(2)}, u32[]{:S(2)}) collective-permute-start(f32[512,1,128]{2,0,1:T(8,128)S(1)} %bitcast.113), channel_id=1, source_target_pairs={{0,16},{8,24},{16,0},{24,8},{1,17},{9,25},{17,1},{25,9},{2,18},{10... | collective-permute-start | bytes 786440 | tf_op jit(solution)/shard_map/ppermute | solution.py:68
  22.4 0.1 select_reduce_fusion.1
  23.2 0.1 copy.26
  23.4 0.1 stack_reshape.7
  23.5 0.1 collective-permute-start.5
  23.6 3.7 %collective-permute-done.4 = f32[512,1,128]{2,0,1:T(8,128)S(1)} collective-permute-done((f32[512,1,128]{2,0,1:T(8,128)S(1)}, f32[512,1,128]{2,0,1:T(8,128)S(1)}, u32[]{:S(2)}, u32[]{:S(2)}) %collective-permute-start.4) | collective-permute-done | bytes 262176 | tf_op jit(solution)/shard_map/ppermute | solution.py:68
  27.4 2.1 %collective-permute-start.11 = (bf16[3,64,1024]{2,1,0:T(8,128)(2,1)S(1)}, bf16[3,64,1024]{2,1,0:T(8,128)(2,1)}, u32[]{:S(2)}, u32[]{:S(2)}) collective-permute-start(bf16[3,64,1024]{2,1,0:T(8,128)(2,1)S(1)} %pad_maximum_fusion.1), channel_id=1, source_target_pairs={{0,1},{1,0},{2,3},{3,2},{4,5},{5,4},{6,7},{7,6},{8,9},{9,8},{10,11... | collective-permute-start | bytes 1179656 | tf_op jit(solution)/shard_map/ppermute | solution.py:156
  29.4 0.1 pad_maximum_fusion
  29.6 3.8 %negate_convert_fusion = (bf16[2,2,512,1,128]{4,2,0,3,1:T(8,128)(2,1)S(1)}, bf16[2,2,512,1,128]{4,2,0,3,1:T(8,128)(2,1)S(1)}) fusion(f32[2,1,512,1,128]{4,2,0,3,1:T(8,128)S(1)} %maximum_bitcast_fusion.1, f32[2,1,512,1,128]{4,2,0,3,1:T(8,128)S(1)} %maximum_bitcast_fusion, f32[]{:T(128)} %bitcast.4), kind=kLoop, calls=%fused_computation.3 | loop fusion | flops 1310720 | bytes 2097156 | tf_op jit(solution)/shard_map/convert.5
  33.5 0.4 copy.31
  33.9 0.2 copy.30
  34.2 0.4 copy.25
  34.6 0.2 copy.28
  34.8 0.2 convert_element_type.56
  35.0 0.2 convert_element_type.61
  35.3 0.1 bitcast_negate_fusion
  35.3 0.1 dynamic-slice_bitcast_fusion
  35.4 0.1 fusion.8
  35.6 0.7 %fusion.29 = f32[256,1024]{1,0:T(8,128)S(1)} fusion(bf16[256,1024]{1,0:T(8,128)(2,1)S(1)} %bitcast.119, bf16[512,512]{0,1:T(8,128)(2,1)S(1)} %bitcast.116, bf16[512,512]{0,1:T(8,128)(2,1)S(1)} %bitcast_negate_fusion, bf16[512,512]{0,1:T(8,128)(2,1)S(1)} %bitcast.108), kind=kOutput, calls=%fused_computation.109 | convolution fusion | flops 545259520 | bytes 3145728 | tf_op jit(solution)/shard_map/dot_general | solution.py:166
  36.3 0.1 fusion.9
  36.4 0.1 fusion.11
  36.6 1.6 %convolution_bitcast_fusion = f32[64,1024]{1,0:T(8,128)S(1)} fusion(bf16[64,1024]{1,0:T(8,128)(2,1)} %collective-permute-done.10, bf16[512,512]{0,1:T(8,128)(2,1)S(1)} %bitcast.117, bf16[512,512]{0,1:T(8,128)(2,1)S(1)} %bitcast_negate_fusion, bf16[512,512]{0,1:T(8,128)(2,1)S(1)} %bitcast.109), kind=kOutput, calls=%fused_computation.1 | convolution fusion | flops 142606336 | bytes 1966080 | tf_op jit(solution)/shard_map/dot_general | solution.py:166
  38.2 0.1 fusion.10
  38.4 0.1 fusion.19
  38.4 0.2 fusion.3
  38.7 0.7 %collective-permute-done.11 = bf16[3,64,1024]{2,1,0:T(8,128)(2,1)} collective-permute-done((bf16[3,64,1024]{2,1,0:T(8,128)(2,1)S(1)}, bf16[3,64,1024]{2,1,0:T(8,128)(2,1)}, u32[]{:S(2)}, u32[]{:S(2)}) %collective-permute-start.11) | collective-permute-done | bytes 393248 | tf_op jit(solution)/shard_map/ppermute | solution.py:156
  39.3 1.9 %fusion.28 = f32[192,1024]{1,0:T(8,128)S(1)} fusion(bf16[192,1024]{1,0:T(8,128)(2,1)} %bitcast.48, bf16[512,512]{0,1:T(8,128)(2,1)S(1)} %bitcast.118, bf16[512,512]{0,1:T(8,128)(2,1)S(1)} %bitcast_negate_fusion, bf16[512,512]{0,1:T(8,128)(2,1)S(1)} %bitcast.110), kind=kOutput, calls=%fused_computation.108 | convolution fusion | flops 411041792 | bytes 2752512 | tf_op jit(solution)/shard_map/dot_general | solution.py:166
  41.2 0.2 fusion.7
  41.5 1.1 %collective-permute-start.12 = (f32[2,1,512]{2,1,0:T(1,128)S(1)}, f32[2,1,512]{2,1,0:T(1,128)S(1)}, u32[]{:S(2)}, u32[]{:S(2)}) collective-permute-start(f32[2,1,512]{2,1,0:T(1,128)S(1)} %pad_maximum_fusion.3), channel_id=1, source_target_pairs={{0,24},{8,0},{16,8},{24,16},{1,25},{9,1},{17,9},{25,17},{2,26},{10... | collective-permute-start | bytes 12296 | tf_op jit(solution)/shard_map/ppermute | solution.py:15
  42.6 0.6 %collective-permute-start.13 = (f32[2,1,512]{2,1,0:T(1,128)S(1)}, f32[2,1,512]{2,1,0:T(1,128)S(1)}, u32[]{:S(2)}, u32[]{:S(2)}) collective-permute-start(f32[2,1,512]{2,1,0:T(1,128)S(1)} %pad_maximum_fusion.3), channel_id=1, source_target_pairs={{0,16},{8,24},{16,0},{24,8},{1,17},{9,25},{17,1},{25,9},{2,18},{10... | collective-permute-start | bytes 12296 | tf_op jit(solution)/shard_map/ppermute | solution.py:15
  43.2 0.1 collective-permute-start.14
  43.3 0.6 %collective-permute-done.12 = f32[2,1,512]{2,1,0:T(1,128)S(1)} collective-permute-done((f32[2,1,512]{2,1,0:T(1,128)S(1)}, f32[2,1,512]{2,1,0:T(1,128)S(1)}, u32[]{:S(2)}, u32[]{:S(2)}) %collective-permute-start.12) | collective-permute-done | bytes 4128 | tf_op jit(solution)/shard_map/ppermute | solution.py:15
  43.9 2.3 %collective-permute-done.13 = f32[2,1,512]{2,1,0:T(1,128)S(1)} collective-permute-done((f32[2,1,512]{2,1,0:T(1,128)S(1)}, f32[2,1,512]{2,1,0:T(1,128)S(1)}, u32[]{:S(2)}, u32[]{:S(2)}) %collective-permute-start.13) | collective-permute-done | bytes 4128 | tf_op jit(solution)/shard_map/ppermute | solution.py:15
  46.3 0.6 %fusion.24 = f32[2,1,512]{2,1,0:T(1,128)} fusion(f32[8,2,1,512]{3,2,1,0:T(1,128)S(1)} %constant_dynamic-update-slice_fusion, s32[]{:T(128)S(6)} %add.218, s32[]{:T(128)S(6)} %add.217, s32[]{:T(128)S(6)} %add.216, s32[]{:T(128)S(6)} %select_n.159), kind=kLoop, calls=%fused_computation.94 | loop fusion | flops 3072 | bytes 20496 | tf_op jit(solution)/shard_map/add | solution.py:96
  (52 shorter events, 0.5 us)
Async XLA Ops:
  0.0 5.5 %copy-start.2 = (bf16[1,2,64,512]{3,2,1,0:T(8,128)(2,1)S(1)}, bf16[1,2,64,512]{3,2,1,0:T(8,128)(2,1)}, u32[]{:S(2)}) copy-start(bf16[1,2,64,512]{3,2,1,0:T(8,128)(2,1)} %param.11) | copy-start | bytes 393220
  1.5 16.3 %copy-start.4 = (f32[1,2,64]{2,1,0:T(2,128)S(1)}, f32[1,2,64]{2,1,0:T(2,128)}, u32[]{:S(2)}) copy-start(f32[1,2,64]{2,1,0:T(2,128)} %param.10) | copy-start | bytes 1540
  1.5 8.2 %collective-permute-start = (f32[64,2,128]{2,0,1:T(8,128)S(1)}, f32[64,2,128]{2,0,1:T(8,128)S(1)}, u32[]{:S(2)}, u32[]{:S(2)}) collective-permute-start(f32[64,2,128]{2,0,1:T(8,128)S(1)} %copy.32), channel_id=1, source_target_pairs={{0,6},{1,7},{2,0},{3,1},{4,2},{5,3},{6,4},{7,5},{8,14},{9,15},{10,... | collective-permute-start | bytes 196616 | tf_op jit(solution)/shard_map/ppermute | solution.py:133
  2.0 9.6 %collective-permute-start.1 = (f32[64,2,128]{2,0,1:T(8,128)S(1)}, f32[64,2,128]{2,0,1:T(8,128)S(1)}, u32[]{:S(2)}, u32[]{:S(2)}) collective-permute-start(f32[64,2,128]{2,0,1:T(8,128)S(1)} %copy.33), channel_id=1, source_target_pairs={{0,4},{1,5},{2,6},{3,7},{4,0},{5,1},{6,2},{7,3},{8,12},{9,13},{10,... | collective-permute-start | bytes 196616 | tf_op jit(solution)/shard_map/ppermute | solution.py:133
  5.5 6.2 %collective-permute-start.2 = (f32[64,2,128]{2,0,1:T(8,128)S(1)}, f32[64,2,128]{2,0,1:T(8,128)S(1)}, u32[]{:S(2)}, u32[]{:S(2)}) collective-permute-start(f32[64,2,128]{2,0,1:T(8,128)S(1)} %copy.34), channel_id=1, source_target_pairs={{0,2},{1,3},{2,4},{3,5},{4,6},{5,7},{6,0},{7,1},{8,10},{9,11},{10,... | collective-permute-start | bytes 196616 | tf_op jit(solution)/shard_map/ppermute | solution.py:133
  6.2 30.4 %collective-permute-start.10 = (bf16[64,1024]{1,0:T(8,128)(2,1)}, bf16[64,1024]{1,0:T(8,128)(2,1)}, u32[]{:S(2)}, u32[]{:S(2)}) collective-permute-start(bf16[64,1024]{1,0:T(8,128)(2,1)} %bitcast.60), channel_id=1, source_target_pairs={{0,1},{1,0},{2,3},{3,2},{4,5},{5,4},{6,7},{7,6},{8,9},{9,8},{10,11... | collective-permute-start | bytes 393224 | tf_op jit(solution)/shard_map/ppermute | solution.py:125
  7.7 15.8 %collective-permute-start.7 = (bf16[64,1024]{1,0:T(8,128)(2,1)}, bf16[64,1024]{1,0:T(8,128)(2,1)S(1)}, u32[]{:S(2)}, u32[]{:S(2)}) collective-permute-start(bf16[64,1024]{1,0:T(8,128)(2,1)} %bitcast.60), channel_id=1, source_target_pairs={{0,6},{1,7},{2,0},{3,1},{4,2},{5,3},{6,4},{7,5},{8,14},{9,15},{10,... | collective-permute-start | bytes 393224 | tf_op jit(solution)/shard_map/ppermute | solution.py:124
  9.7 17.6 %collective-permute-start.8 = (bf16[64,1024]{1,0:T(8,128)(2,1)}, bf16[64,1024]{1,0:T(8,128)(2,1)S(1)}, u32[]{:S(2)}, u32[]{:S(2)}) collective-permute-start(bf16[64,1024]{1,0:T(8,128)(2,1)} %bitcast.60), channel_id=1, source_target_pairs={{0,4},{1,5},{2,6},{3,7},{4,0},{5,1},{6,2},{7,3},{8,12},{9,13},{10,... | collective-permute-start | bytes 393224 | tf_op jit(solution)/shard_map/ppermute | solution.py:124
  11.7 15.6 %collective-permute-start.9 = (bf16[64,1024]{1,0:T(8,128)(2,1)}, bf16[64,1024]{1,0:T(8,128)(2,1)S(1)}, u32[]{:S(2)}, u32[]{:S(2)}) collective-permute-start(bf16[64,1024]{1,0:T(8,128)(2,1)} %bitcast.60), channel_id=1, source_target_pairs={{0,2},{1,3},{2,4},{3,5},{4,6},{5,7},{6,0},{7,1},{8,10},{9,11},{10,... | collective-permute-start | bytes 393224 | tf_op jit(solution)/shard_map/ppermute | solution.py:124
  11.7 10.7 %copy-start.3 = (s32[1,512]{1,0:T(1,128)S(1)}, s32[1,512]{1,0:T(1,128)}, u32[]{:S(2)}) copy-start(s32[1,512]{1,0:T(1,128)} %param.8) | copy-start | bytes 6148
  11.8 9.0 %collective-permute-start.3 = (f32[4,64,1,128]{3,1,0,2:T(8,128)S(1)}, f32[4,64,1,128]{3,1,0,2:T(8,128)S(1)}, u32[]{:S(2)}, u32[]{:S(2)}) collective-permute-start(f32[4,64,1,128]{3,1,0,2:T(8,128)S(1)} %get-tuple-element.34), channel_id=1, source_target_pairs={{0,1},{1,0},{2,3},{3,2},{4,5},{5,4},{6,7},{7,6},{8,9},{9,8},{10,11... | collective-permute-start | bytes 393224 | tf_op jit(solution)/shard_map/ppermute | solution.py:136
  20.9 6.4 %collective-permute-start.4 = (f32[512,1,128]{2,0,1:T(8,128)S(1)}, f32[512,1,128]{2,0,1:T(8,128)S(1)}, u32[]{:S(2)}, u32[]{:S(2)}) collective-permute-start(f32[512,1,128]{2,0,1:T(8,128)S(1)} %bitcast.113), channel_id=1, source_target_pairs={{0,16},{8,24},{16,0},{24,8},{1,17},{9,25},{17,1},{25,9},{2,18},{10... | collective-permute-start | bytes 786440 | tf_op jit(solution)/shard_map/ppermute | solution.py:68
  23.5 6.0 %collective-permute-start.5 = (f32[512,1,128]{2,0,1:T(8,128)S(1)}, f32[512,1,128]{2,0,1:T(8,128)S(1)}, u32[]{:S(2)}, u32[]{:S(2)}) collective-permute-start(f32[512,1,128]{2,0,1:T(8,128)S(1)} %bitcast.114), channel_id=1, source_target_pairs={{0,8},{8,0},{16,24},{24,16},{1,9},{9,1},{17,25},{25,17},{2,10},{10... | collective-permute-start | bytes 786440 | tf_op jit(solution)/shard_map/ppermute | solution.py:70
  27.3 2.3 %collective-permute-start.6 = (f32[512,1,128]{2,0,1:T(8,128)S(1)}, f32[512,1,128]{2,0,1:T(8,128)S(1)}, u32[]{:S(2)}, u32[]{:S(2)}) collective-permute-start(f32[512,1,128]{2,0,1:T(8,128)S(1)} %collective-permute-done.4), channel_id=1, source_target_pairs={{0,8},{8,0},{16,24},{24,16},{1,9},{9,1},{17,25},{25,17},{2,10},{10... | collective-permute-start | bytes 786440 | tf_op jit(solution)/shard_map/ppermute | solution.py:70
  27.4 12.0 %collective-permute-start.11 = (bf16[3,64,1024]{2,1,0:T(8,128)(2,1)S(1)}, bf16[3,64,1024]{2,1,0:T(8,128)(2,1)}, u32[]{:S(2)}, u32[]{:S(2)}) collective-permute-start(bf16[3,64,1024]{2,1,0:T(8,128)(2,1)S(1)} %pad_maximum_fusion.1), channel_id=1, source_target_pairs={{0,1},{1,0},{2,3},{3,2},{4,5},{5,4},{6,7},{7,6},{8,9},{9,8},{10,11... | collective-permute-start | bytes 1179656 | tf_op jit(solution)/shard_map/ppermute | solution.py:156
  35.6 2.8 %copy-start = (bf16[4,64,512]{2,1,0:T(8,128)(2,1)}, bf16[4,64,512]{2,1,0:T(8,128)(2,1)S(1)}, u32[]{:S(2)}) copy-start(bf16[4,64,512]{2,1,0:T(8,128)(2,1)S(1)} %fusion.8) | copy-start | bytes 786436
  36.4 1.9 %copy-start.1 = (bf16[4,64,512]{2,1,0:T(8,128)(2,1)}, bf16[4,64,512]{2,1,0:T(8,128)(2,1)S(1)}, u32[]{:S(2)}) copy-start(bf16[4,64,512]{2,1,0:T(8,128)(2,1)S(1)} %fusion.9) | copy-start | bytes 786436
  39.3 1.9 %slice-start = ((bf16[4,64,512]{2,1,0:T(8,128)(2,1)}), bf16[3,64,512]{2,1,0:T(8,128)(2,1)S(1)}, s32[]{:S(2)}) async-start(bf16[4,64,512]{2,1,0:T(8,128)(2,1)} %copy-done), calls=%async_computation | async-start | bytes 393216 | tf_op jit(solution)/shard_map/slice | solution.py:179
  39.3 1.9 %slice-start.1 = ((bf16[4,64,512]{2,1,0:T(8,128)(2,1)}), bf16[3,64,512]{2,1,0:T(8,128)(2,1)S(1)}, s32[]{:S(2)}) async-start(bf16[4,64,512]{2,1,0:T(8,128)(2,1)} %copy-done.1), calls=%async_computation.1 | async-start | bytes 393216 | tf_op jit(solution)/shard_map/slice | solution.py:179
  41.5 2.4 %collective-permute-start.12 = (f32[2,1,512]{2,1,0:T(1,128)S(1)}, f32[2,1,512]{2,1,0:T(1,128)S(1)}, u32[]{:S(2)}, u32[]{:S(2)}) collective-permute-start(f32[2,1,512]{2,1,0:T(1,128)S(1)} %pad_maximum_fusion.3), channel_id=1, source_target_pairs={{0,24},{8,0},{16,8},{24,16},{1,25},{9,1},{17,9},{25,17},{2,26},{10... | collective-permute-start | bytes 12296 | tf_op jit(solution)/shard_map/ppermute | solution.py:15
  42.6 3.6 %collective-permute-start.13 = (f32[2,1,512]{2,1,0:T(1,128)S(1)}, f32[2,1,512]{2,1,0:T(1,128)S(1)}, u32[]{:S(2)}, u32[]{:S(2)}) collective-permute-start(f32[2,1,512]{2,1,0:T(1,128)S(1)} %pad_maximum_fusion.3), channel_id=1, source_target_pairs={{0,16},{8,24},{16,0},{24,8},{1,17},{9,25},{17,1},{25,9},{2,18},{10... | collective-permute-start | bytes 12296 | tf_op jit(solution)/shard_map/ppermute | solution.py:15
  43.2 3.1 %collective-permute-start.14 = (f32[2,1,512]{2,1,0:T(1,128)S(1)}, f32[2,1,512]{2,1,0:T(1,128)S(1)}, u32[]{:S(2)}, u32[]{:S(2)}) collective-permute-start(f32[2,1,512]{2,1,0:T(1,128)S(1)} %pad_maximum_fusion.3), channel_id=1, source_target_pairs={{0,8},{8,16},{16,24},{24,0},{1,9},{9,17},{17,25},{25,1},{2,10},{10... | collective-permute-start | bytes 12296 | tf_op jit(solution)/shard_map/ppermute | solution.py:15

commit v13 on v10

--- a/solution.py
+++ b/solution.py
@@ -143,10 +143,18 @@
     elements, row_count, _, width = view.shape
     voxels = row_count * freqs * width
 
-    scaled = TWO_PI * bins[0].astype(jnp.float32)
-    angle = scaled * view.reshape(elements, voxels)
-    field_real = jnp.cos(angle).astype(jnp.bfloat16)
-    field_imag = (-jnp.sin(angle)).astype(jnp.bfloat16)
+    turns = bins[0].astype(jnp.float32) * view.reshape(elements, voxels)
+    turns = turns - jnp.round(turns)
+    quarter = jnp.round(4.0 * turns)
+    theta = TWO_PI * (turns - 0.25 * quarter)
+    theta2 = theta * theta
+    sine = theta * (1.0 + theta2 * (-1.0 / 6.0 + theta2 * (1.0 / 120.0 + theta2 * (-1.0 / 5040.0 + theta2 / 362880.0))))
+    cosine = 1.0 + theta2 * (-0.5 + theta2 * (1.0 / 24.0 + theta2 * (-1.0 / 720.0 + theta2 * (1.0 / 40320.0))))
+    q = quarter.astype(jnp.int32) % 4
+    cos_full = jnp.where(q == 0, cosine, jnp.where(q == 1, -sine, jnp.where(q == 2, -cosine, sine)))
+    sin_full = jnp.where(q == 0, sine, jnp.where(q == 1, cosine, jnp.where(q == 2, -sine, -cosine)))
+    field_real = cos_full.astype(jnp.bfloat16)
+    field_imag = (-sin_full).astype(jnp.bfloat16)
     left = jnp.concatenate([field_real, field_imag], axis=1)
     right = jnp.concatenate([-field_imag, field_real], axis=1)
 

time: 45.9 us -> 48.4 us (1.054)
  other arithmetic: 7.94 us -> 9.75 us
  local copies, waits for them, and re-layouts: 3.42 us -> 4.65 us
  waiting for transfers between devices: 15 us -> 14.5 us
    another operation x1 -> x0, other arithmetic: 3.84 us -> none
    convert_element_type x0 -> x2, other arithmetic: none -> 3.3 us  [body(): field_real = cos_full.astype(jnp.bfloat16)]
    neg x1, other arithmetic: 0.07 us -> 2.46 us  [body(): right = jnp.concatenate([-field_imag, field_real], axis=1)]
    mul x0 -> x4, local copies, waits for them, and re-layouts: none -> 1.5 us  [body(): turns = bins[0].astype(jnp.float32) * view.reshape(elements, voxels)]
    convert_element_type x4 -> x0, local copies, waits for them, and re-layouts: 1.02 us -> none  [the longest x3 0.82 us: body(): field_real = jnp.cos(angle).astype(jnp.bfloat16)]
    another operation x1, other arithmetic: 0.97 us -> 0.07 us  [body(): row = jnp.stack(row)]
    unnamed x12 -> x18, local copies, waits for them, and re-layouts: 0.06 us -> 0.92 us
    another operation x1, other arithmetic: 0.05 us -> 0.81 us  [body(): other = (own_swapped, lax.ppermute(jnp.stack(row[1:]), 'tile', swap))]
  transfers between devices with their start and end apart: 15 -> 15, of which waited for: 6 -> 6; matrix products, arithmetic and copies ran while one was open for 19% -> 23% of each run, Pallas kernels for 0% -> 0%
where the time goes in v13:
time: 48.4 us; the launch traced here: 48.2 us
  starting transfers between devices  16.4 us (34%)
  waiting for transfers between devices  14.5 us (30%)
  other arithmetic  9.75 us (20%)
  local copies, waits for them, and re-layouts  4.65 us (10%)
  matrix products  1.86 us (4%)
  between operations  1.01 us (2%)
    ppermute x3, waiting for transfers between devices, body(): pieces.append(lax.ppermute(sent, 'tile', pairs))  5.63 us
    ppermute x3, starting transfers between devices, body(): cap_row.append(lax.ppermute(capture[0], 'tile', pairs))  4.38 us
    ppermute x3, starting transfers between devices, body(): pieces.append(lax.ppermute(sent, 'tile', pairs))  3.99 us
    ppermute x1, waiting for transfers between devices, body(): lax.ppermute(lax.dynamic_slice_in_dim(pieces, (1 - y) * per_tile, per_til...  3.33 us
    convert_element_type x2, other arithmetic, body(): field_real = cos_full.astype(jnp.bfloat16)  3.3 us
    ppermute x3, waiting for transfers between devices, gather_shifted(): pieces.append(lax.ppermute(block, axis_name, pairs))  3.07 us
    neg x1, other arithmetic, body(): right = jnp.concatenate([-field_imag, field_real], axis=1)  2.46 us
    ppermute x3, starting transfers between devices, gather_shifted(): pieces.append(lax.ppermute(block, axis_name, pairs))  1.83 us
  transfers between devices with their start and end apart: 15, of which 6 were waited for; matrix products, arithmetic and copies ran while one was open for 23% of the time, Pallas kernels for 0%

profile of v13, /device:TPU:16, one launch (start us, length us, event | category | flops | bytes accessed | tf_op | source)
XLA Modules:
  0.0 48.2 jit_solution(5375082515187187023)
XLA Ops:
  0.0 1.4 %constant_dynamic-slice_fusion.14 = (f32[64,2,128]{2,1,0:T(2,128)S(1)}, f32[64,2,128]{2,1,0:T(2,128)S(1)}, f32[64,2,128]{2,1,0:T(2,128)S(1)}, f32[64,2,128]{2,1,0:T(2,128)S(1)}) fusion(f32[64,8,128]{2,1,0:T(8,128)} %param.7, s32[]{:T(128)S(6)} %select_n.185, s32[]{:T(128)S(6)} %select_n.189, s32[]{:T(128)S(6)} %select_n.187, s32[]{:T(128)S(6)} %select_n.191), kind=kLoop, calls=%fused_computation.135 | loop fusion | bytes 524304 | tf_op jit(solution)/shard_map/dynamic_slice | solution.py:127
  1.4 0.5 %collective-permute-start = (f32[64,2,128]{2,0,1:T(8,128)S(1)}, f32[64,2,128]{2,0,1:T(8,128)S(1)}, u32[]{:S(2)}, u32[]{:S(2)}) collective-permute-start(f32[64,2,128]{2,0,1:T(8,128)S(1)} %copy.27), channel_id=1, source_target_pairs={{0,6},{1,7},{2,0},{3,1},{4,2},{5,3},{6,4},{7,5},{8,14},{9,15},{10,... | collective-permute-start | bytes 196616 | tf_op jit(solution)/shard_map/ppermute | solution.py:132
  1.9 3.5 %collective-permute-start.1 = (f32[64,2,128]{2,0,1:T(8,128)S(1)}, f32[64,2,128]{2,0,1:T(8,128)S(1)}, u32[]{:S(2)}, u32[]{:S(2)}) collective-permute-start(f32[64,2,128]{2,0,1:T(8,128)S(1)} %copy.28), channel_id=1, source_target_pairs={{0,4},{1,5},{2,6},{3,7},{4,0},{5,1},{6,2},{7,3},{8,12},{9,13},{10,... | collective-permute-start | bytes 196616 | tf_op jit(solution)/shard_map/ppermute | solution.py:132
  5.4 2.0 %collective-permute-start.7 = (bf16[2,64,512]{2,1,0:T(8,128)(2,1)S(1)}, bf16[2,64,512]{2,1,0:T(8,128)(2,1)S(1)}, u32[]{:S(2)}, u32[]{:S(2)}) collective-permute-start(bf16[2,64,512]{2,1,0:T(8,128)(2,1)S(1)} %bitcast.139), channel_id=1, source_target_pairs={{0,6},{1,7},{2,0},{3,1},{4,2},{5,3},{6,4},{7,5},{8,14},{9,15},{10,... | collective-permute-start | bytes 393224 | tf_op jit(solution)/shard_map/ppermute | solution.py:123
  7.4 1.9 %collective-permute-start.8 = (bf16[2,64,512]{2,1,0:T(8,128)(2,1)S(1)}, bf16[2,64,512]{2,1,0:T(8,128)(2,1)S(1)}, u32[]{:S(2)}, u32[]{:S(2)}) collective-permute-start(bf16[2,64,512]{2,1,0:T(8,128)(2,1)S(1)} %bitcast.140), channel_id=1, source_target_pairs={{0,4},{1,5},{2,6},{3,7},{4,0},{5,1},{6,2},{7,3},{8,12},{9,13},{10,... | collective-permute-start | bytes 393224 | tf_op jit(solution)/shard_map/ppermute | solution.py:123
  9.3 0.5 %collective-permute-start.9 = (bf16[2,64,512]{2,1,0:T(8,128)(2,1)S(1)}, bf16[2,64,512]{2,1,0:T(8,128)(2,1)S(1)}, u32[]{:S(2)}, u32[]{:S(2)}) collective-permute-start(bf16[2,64,512]{2,1,0:T(8,128)(2,1)S(1)} %bitcast.141), channel_id=1, source_target_pairs={{0,2},{1,3},{2,4},{3,5},{4,6},{5,7},{6,0},{7,1},{8,10},{9,11},{10,... | collective-permute-start | bytes 393224 | tf_op jit(solution)/shard_map/ppermute | solution.py:123
  9.8 1.5 %collective-permute-start.10 = (bf16[2,64,512]{2,1,0:T(8,128)(2,1)S(1)}, bf16[2,64,512]{2,1,0:T(8,128)(2,1)}, u32[]{:S(2)}, u32[]{:S(2)}) collective-permute-start(bf16[2,64,512]{2,1,0:T(8,128)(2,1)S(1)} %bitcast.142), channel_id=1, source_target_pairs={{0,1},{1,0},{2,3},{3,2},{4,5},{5,4},{6,7},{7,6},{8,9},{9,8},{10,11... | collective-permute-start | bytes 393224 | tf_op jit(solution)/shard_map/ppermute | solution.py:124
  11.3 5.6 %collective-permute-done.2 = f32[64,2,128]{2,0,1:T(8,128)S(1)} collective-permute-done((f32[64,2,128]{2,0,1:T(8,128)S(1)}, f32[64,2,128]{2,0,1:T(8,128)S(1)}, u32[]{:S(2)}, u32[]{:S(2)}) %collective-permute-start.2) | collective-permute-done | bytes 65568 | tf_op jit(solution)/shard_map/ppermute | solution.py:132
  17.0 1.6 %collective-permute-start.3 = (f32[4,64,1,128]{3,1,0,2:T(8,128)S(1)}, f32[4,64,1,128]{3,1,0,2:T(8,128)S(1)}, u32[]{:S(2)}, u32[]{:S(2)}) collective-permute-start(f32[4,64,1,128]{3,1,0,2:T(8,128)S(1)} %get-tuple-element.36), channel_id=1, source_target_pairs={{0,1},{1,0},{2,3},{3,2},{4,5},{5,4},{6,7},{7,6},{8,9},{9,8},{10,11... | collective-permute-start | bytes 393224 | tf_op jit(solution)/shard_map/ppermute | solution.py:135
  18.6 0.1 select_reduce_fusion.1
  18.7 3.3 %collective-permute-done.3 = f32[4,64,1,128]{3,1,0,2:T(8,128)S(1)} collective-permute-done((f32[4,64,1,128]{3,1,0,2:T(8,128)S(1)}, f32[4,64,1,128]{3,1,0,2:T(8,128)S(1)}, u32[]{:S(2)}, u32[]{:S(2)}) %collective-permute-start.3) | collective-permute-done | bytes 131104 | tf_op jit(solution)/shard_map/ppermute | solution.py:135
  22.1 0.1 fusion.29
  22.1 1.6 %collective-permute-start.4 = (f32[512,1,128]{2,0,1:T(8,128)S(1)}, f32[512,1,128]{2,0,1:T(8,128)S(1)}, u32[]{:S(2)}, u32[]{:S(2)}) collective-permute-start(f32[512,1,128]{2,0,1:T(8,128)S(1)} %bitcast.119), channel_id=1, source_target_pairs={{0,16},{8,24},{16,0},{24,8},{1,17},{9,25},{17,1},{25,9},{2,18},{10... | collective-permute-start | bytes 786440 | tf_op jit(solution)/shard_map/ppermute | solution.py:68
  24.4 0.8 %pad_maximum_fusion.7 = bf16[3,2,64,512]{3,2,1,0:T(8,128)(2,1)} fusion(bf16[1,2,64,512]{3,2,1,0:T(8,128)(2,1)S(1)} %bitcast.130, bf16[1,2,64,512]{3,2,1,0:T(8,128)(2,1)S(1)} %bitcast.128, bf16[1,2,64,512]{3,2,1,0:T(8,128)(2,1)S(1)} %bitcast.126), kind=kLoop, calls=%fused_computation.92 | loop fusion | flops 393216 | bytes 786432 | tf_op jit(solution)/shard_map/stack | solution.py:162
  25.2 1.5 %collective-permute-start.11 = (bf16[3,2,64,512]{3,2,1,0:T(8,128)(2,1)}, bf16[3,2,64,512]{3,2,1,0:T(8,128)(2,1)}, u32[]{:S(2)}, u32[]{:S(2)}) collective-permute-start(bf16[3,2,64,512]{3,2,1,0:T(8,128)(2,1)} %pad_maximum_fusion.7), channel_id=1, source_target_pairs={{0,1},{1,0},{2,3},{3,2},{4,5},{5,4},{6,7},{7,6},{8,9},{9,8},{10,11... | collective-permute-start | bytes 1179656 | tf_op jit(solution)/shard_map/ppermute | solution.py:162
  26.7 0.1 pad_maximum_fusion.6
  26.8 0.1 collective-permute-start.5
  26.9 1.7 %collective-permute-done.4 = f32[512,1,128]{2,0,1:T(8,128)S(1)} collective-permute-done((f32[512,1,128]{2,0,1:T(8,128)S(1)}, f32[512,1,128]{2,0,1:T(8,128)S(1)}, u32[]{:S(2)}, u32[]{:S(2)}) %collective-permute-start.4) | collective-permute-done | bytes 262176 | tf_op jit(solution)/shard_map/ppermute | solution.py:68
  28.6 0.7 %fusion.46 = (bf16[4,1,64,512]{3,2,1,0:T(8,128)(2,1)S(1)}, bf16[4,1,64,512]{3,2,1,0:T(8,128)(2,1)}) fusion(bf16[4,2,64,512]{3,2,1,0:T(8,128)(2,1)S(1)} %pad_maximum_fusion.6), kind=kLoop, calls=%fused_computation.156 | loop fusion | bytes 1048576 | tf_op jit(solution)/shard_map/slice | solution.py:173
  29.4 0.7 %collective-permute-done.6 = f32[512,1,128]{2,0,1:T(8,128)S(1)} collective-permute-done((f32[512,1,128]{2,0,1:T(8,128)S(1)}, f32[512,1,128]{2,0,1:T(8,128)S(1)}, u32[]{:S(2)}, u32[]{:S(2)}) %collective-permute-start.6) | collective-permute-done | bytes 262176 | tf_op jit(solution)/shard_map/ppermute | solution.py:70
  30.1 0.1 maximum_bitcast_fusion.1
  30.2 0.1 maximum_multiply_fusion
  30.3 0.1 copy.24
  30.3 0.7 %copy.25 = f32[512,1,4,128]{3,2,0,1:T(4,128)S(1)} copy(f32[512,1,4,128]{3,0,2,1:T(8,128)S(1)} %bitcast.117) | data formatting | bytes 2097152 | tf_op jit(solution)/shard_map/mul | solution.py:146
  31.0 0.3 copy.26
  31.4 2.5 %fusion.45 = (bf16[512,512]{0,1:T(8,128)(2,1)S(1)}, bf16[512,512]{0,1:T(8,128)(2,1)}) fusion(f32[512,1,4,128]{0,3,2,1:T(8,128)S(1)} %copy.26), kind=kLoop, calls=%fused_computation.155 | loop fusion | flops 13107200 | bytes 2097152 | tf_op jit(solution)/shard_map/neg | solution.py:159
  33.8 1.6 %select_convert_fusion = bf16[512,512]{0,1:T(8,128)(2,1)S(1)} fusion(f32[512,1,4,128]{0,3,2,1:T(8,128)S(1)} %copy.26), kind=kLoop, calls=%fused_computation.17 | loop fusion | flops 12058624 | bytes 1572864 | tf_op jit(solution)/shard_map/convert_element_type | solution.py:156
  35.4 0.4 mul.297
  35.8 1.7 %select_convert_fusion.1 = (bf16[4,2,64,512]{3,2,1,0:T(8,128)(2,1)S(1)}, bf16[4,2,64,512]{3,2,1,0:T(8,128)(2,1)S(1)}) fusion(f32[4,2,64,512]{3,2,1,0:T(8,128)S(1)} %mul.297), kind=kLoop, calls=%fused_computation.33 | loop fusion | flops 13369344 | bytes 2097152 | tf_op jit(solution)/shard_map/convert_element_type | solution.py:156
  37.6 0.1 dynamic-slice_bitcast_fusion
  37.7 0.1 fusion.28
  37.8 0.1 fusion.27
  37.9 0.8 %copy-done = bf16[512,512]{0,1:T(8,128)(2,1)S(1)} copy-done((bf16[512,512]{0,1:T(8,128)(2,1)S(1)}, bf16[512,512]{0,1:T(8,128)(2,1)}, u32[]{:S(2)}) %copy-start) | copy-done | bytes 524312
  38.7 0.1 copy-done.1
  38.8 0.5 fusion.15
  39.3 0.5 convolution_add_fusion.1
  39.7 0.2 fusion.23
  40.0 0.1 fusion.25
  40.1 0.1 fusion.26
  40.2 1.1 %pad_maximum_fusion.8 = (bf16[4,1,64,512]{3,2,1,0:T(8,128)(2,1)S(1)}, bf16[4,1,64,512]{3,2,1,0:T(8,128)(2,1)S(1)}) fusion(bf16[3,2,64,512]{3,2,1,0:T(8,128)(2,1)} %collective-permute-done.11, bf16[1,2,64,512]{3,2,1,0:T(8,128)(2,1)} %bitcast.38), kind=kLoop, calls=%fused_computation.102 | loop fusion | flops 262144 | bytes 1048576 | tf_op jit(solution)/shard_map/concatenate | solution.py:188
  41.3 0.5 fusion.14
  41.8 0.5 convolution_add_fusion
  42.3 0.2 fusion.17
  42.6 1.3 %collective-permute-start.12 = (f32[2,1,512]{2,1,0:T(1,128)S(1)}, f32[2,1,512]{2,1,0:T(1,128)S(1)}, u32[]{:S(2)}, u32[]{:S(2)}) collective-permute-start(f32[2,1,512]{2,1,0:T(1,128)S(1)} %pad_maximum_fusion.10), channel_id=1, source_target_pairs={{0,24},{8,0},{16,8},{24,16},{1,25},{9,1},{17,9},{25,17},{2,26},{10... | collective-permute-start | bytes 12296 | tf_op jit(solution)/shard_map/ppermute | solution.py:15
  43.9 0.5 %collective-permute-start.13 = (f32[2,1,512]{2,1,0:T(1,128)S(1)}, f32[2,1,512]{2,1,0:T(1,128)S(1)}, u32[]{:S(2)}, u32[]{:S(2)}) collective-permute-start(f32[2,1,512]{2,1,0:T(1,128)S(1)} %pad_maximum_fusion.10), channel_id=1, source_target_pairs={{0,16},{8,24},{16,0},{24,8},{1,17},{9,25},{17,1},{25,9},{2,18},{10... | collective-permute-start | bytes 12296 | tf_op jit(solution)/shard_map/ppermute | solution.py:15
  44.4 0.8 %collective-permute-done.12 = f32[2,1,512]{2,1,0:T(1,128)S(1)} collective-permute-done((f32[2,1,512]{2,1,0:T(1,128)S(1)}, f32[2,1,512]{2,1,0:T(1,128)S(1)}, u32[]{:S(2)}, u32[]{:S(2)}) %collective-permute-start.12) | collective-permute-done | bytes 4128 | tf_op jit(solution)/shard_map/ppermute | solution.py:15
  45.2 2.3 %collective-permute-done.13 = f32[2,1,512]{2,1,0:T(1,128)S(1)} collective-permute-done((f32[2,1,512]{2,1,0:T(1,128)S(1)}, f32[2,1,512]{2,1,0:T(1,128)S(1)}, u32[]{:S(2)}, u32[]{:S(2)}) %collective-permute-start.13) | collective-permute-done | bytes 4128 | tf_op jit(solution)/shard_map/ppermute | solution.py:15
  47.6 0.6 %fusion.40 = f32[2,1,512]{2,1,0:T(1,128)} fusion(f32[8,2,1,512]{3,2,1,0:T(1,128)S(1)} %constant_dynamic-update-slice_fusion, s32[]{:T(128)S(6)} %add.340, s32[]{:T(128)S(6)} %add.339, s32[]{:T(128)S(6)} %add.338, s32[]{:T(128)S(6)} %select_n.220), kind=kLoop, calls=%fused_computation.144 | loop fusion | flops 3072 | bytes 20496 | tf_op jit(solution)/shard_map/add | solution.py:96
  (45 shorter events, 0.3 us)
Async XLA Ops:
  0.0 5.4 %copy-start.2 = (bf16[1,2,64,512]{3,2,1,0:T(8,128)(2,1)S(1)}, bf16[1,2,64,512]{3,2,1,0:T(8,128)(2,1)}, u32[]{:S(2)}) copy-start(bf16[1,2,64,512]{3,2,1,0:T(8,128)(2,1)} %param.11) | copy-start | bytes 393220
  0.0 18.6 %copy-start.4 = (f32[1,2,64]{2,1,0:T(2,128)S(1)}, f32[1,2,64]{2,1,0:T(2,128)}, u32[]{:S(2)}) copy-start(f32[1,2,64]{2,1,0:T(2,128)} %param.10) | copy-start | bytes 1540
  0.0 18.6 %copy-start.3 = (s32[1,512]{1,0:T(1,128)S(1)}, s32[1,512]{1,0:T(1,128)}, u32[]{:S(2)}) copy-start(s32[1,512]{1,0:T(1,128)} %param.8) | copy-start | bytes 6148
  1.4 7.9 %collective-permute-start = (f32[64,2,128]{2,0,1:T(8,128)S(1)}, f32[64,2,128]{2,0,1:T(8,128)S(1)}, u32[]{:S(2)}, u32[]{:S(2)}) collective-permute-start(f32[64,2,128]{2,0,1:T(8,128)S(1)} %copy.27), channel_id=1, source_target_pairs={{0,6},{1,7},{2,0},{3,1},{4,2},{5,3},{6,4},{7,5},{8,14},{9,15},{10,... | collective-permute-start | bytes 196616 | tf_op jit(solution)/shard_map/ppermute | solution.py:132
  1.9 7.9 %collective-permute-start.1 = (f32[64,2,128]{2,0,1:T(8,128)S(1)}, f32[64,2,128]{2,0,1:T(8,128)S(1)}, u32[]{:S(2)}, u32[]{:S(2)}) collective-permute-start(f32[64,2,128]{2,0,1:T(8,128)S(1)} %copy.28), channel_id=1, source_target_pairs={{0,4},{1,5},{2,6},{3,7},{4,0},{5,1},{6,2},{7,3},{8,12},{9,13},{10,... | collective-permute-start | bytes 196616 | tf_op jit(solution)/shard_map/ppermute | solution.py:132
  5.4 11.5 %collective-permute-start.2 = (f32[64,2,128]{2,0,1:T(8,128)S(1)}, f32[64,2,128]{2,0,1:T(8,128)S(1)}, u32[]{:S(2)}, u32[]{:S(2)}) collective-permute-start(f32[64,2,128]{2,0,1:T(8,128)S(1)} %copy.29), channel_id=1, source_target_pairs={{0,2},{1,3},{2,4},{3,5},{4,6},{5,7},{6,0},{7,1},{8,10},{9,11},{10,... | collective-permute-start | bytes 196616 | tf_op jit(solution)/shard_map/ppermute | solution.py:132
  5.4 19.0 %collective-permute-start.7 = (bf16[2,64,512]{2,1,0:T(8,128)(2,1)S(1)}, bf16[2,64,512]{2,1,0:T(8,128)(2,1)S(1)}, u32[]{:S(2)}, u32[]{:S(2)}) collective-permute-start(bf16[2,64,512]{2,1,0:T(8,128)(2,1)S(1)} %bitcast.139), channel_id=1, source_target_pairs={{0,6},{1,7},{2,0},{3,1},{4,2},{5,3},{6,4},{7,5},{8,14},{9,15},{10,... | collective-permute-start | bytes 393224 | tf_op jit(solution)/shard_map/ppermute | solution.py:123
  7.4 17.0 %collective-permute-start.8 = (bf16[2,64,512]{2,1,0:T(8,128)(2,1)S(1)}, bf16[2,64,512]{2,1,0:T(8,128)(2,1)S(1)}, u32[]{:S(2)}, u32[]{:S(2)}) collective-permute-start(bf16[2,64,512]{2,1,0:T(8,128)(2,1)S(1)} %bitcast.140), channel_id=1, source_target_pairs={{0,4},{1,5},{2,6},{3,7},{4,0},{5,1},{6,2},{7,3},{8,12},{9,13},{10,... | collective-permute-start | bytes 393224 | tf_op jit(solution)/shard_map/ppermute | solution.py:123
  9.3 15.1 %collective-permute-start.9 = (bf16[2,64,512]{2,1,0:T(8,128)(2,1)S(1)}, bf16[2,64,512]{2,1,0:T(8,128)(2,1)S(1)}, u32[]{:S(2)}, u32[]{:S(2)}) collective-permute-start(bf16[2,64,512]{2,1,0:T(8,128)(2,1)S(1)} %bitcast.141), channel_id=1, source_target_pairs={{0,2},{1,3},{2,4},{3,5},{4,6},{5,7},{6,0},{7,1},{8,10},{9,11},{10,... | collective-permute-start | bytes 393224 | tf_op jit(solution)/shard_map/ppermute | solution.py:123
  9.8 30.4 %collective-permute-start.10 = (bf16[2,64,512]{2,1,0:T(8,128)(2,1)S(1)}, bf16[2,64,512]{2,1,0:T(8,128)(2,1)}, u32[]{:S(2)}, u32[]{:S(2)}) collective-permute-start(bf16[2,64,512]{2,1,0:T(8,128)(2,1)S(1)} %bitcast.142), channel_id=1, source_target_pairs={{0,1},{1,0},{2,3},{3,2},{4,5},{5,4},{6,7},{7,6},{8,9},{9,8},{10,11... | collective-permute-start | bytes 393224 | tf_op jit(solution)/shard_map/ppermute | solution.py:124
  17.0 5.0 %collective-permute-start.3 = (f32[4,64,1,128]{3,1,0,2:T(8,128)S(1)}, f32[4,64,1,128]{3,1,0,2:T(8,128)S(1)}, u32[]{:S(2)}, u32[]{:S(2)}) collective-permute-start(f32[4,64,1,128]{3,1,0,2:T(8,128)S(1)} %get-tuple-element.36), channel_id=1, source_target_pairs={{0,1},{1,0},{2,3},{3,2},{4,5},{5,4},{6,7},{7,6},{8,9},{9,8},{10,11... | collective-permute-start | bytes 393224 | tf_op jit(solution)/shard_map/ppermute | solution.py:135
  22.1 6.4 %collective-permute-start.4 = (f32[512,1,128]{2,0,1:T(8,128)S(1)}, f32[512,1,128]{2,0,1:T(8,128)S(1)}, u32[]{:S(2)}, u32[]{:S(2)}) collective-permute-start(f32[512,1,128]{2,0,1:T(8,128)S(1)} %bitcast.119), channel_id=1, source_target_pairs={{0,16},{8,24},{16,0},{24,8},{1,17},{9,25},{17,1},{25,9},{2,18},{10... | collective-permute-start | bytes 786440 | tf_op jit(solution)/shard_map/ppermute | solution.py:68
  25.2 15.0 %collective-permute-start.11 = (bf16[3,2,64,512]{3,2,1,0:T(8,128)(2,1)}, bf16[3,2,64,512]{3,2,1,0:T(8,128)(2,1)}, u32[]{:S(2)}, u32[]{:S(2)}) collective-permute-start(bf16[3,2,64,512]{3,2,1,0:T(8,128)(2,1)} %pad_maximum_fusion.7), channel_id=1, source_target_pairs={{0,1},{1,0},{2,3},{3,2},{4,5},{5,4},{6,7},{7,6},{8,9},{9,8},{10,11... | collective-permute-start | bytes 1179656 | tf_op jit(solution)/shard_map/ppermute | solution.py:162
  26.8 2.6 %collective-permute-start.5 = (f32[512,1,128]{2,0,1:T(8,128)S(1)}, f32[512,1,128]{2,0,1:T(8,128)S(1)}, u32[]{:S(2)}, u32[]{:S(2)}) collective-permute-start(f32[512,1,128]{2,0,1:T(8,128)S(1)} %bitcast.120), channel_id=1, source_target_pairs={{0,8},{8,0},{16,24},{24,16},{1,9},{9,1},{17,25},{25,17},{2,10},{10... | collective-permute-start | bytes 786440 | tf_op jit(solution)/shard_map/ppermute | solution.py:70
  28.6 1.5 %collective-permute-start.6 = (f32[512,1,128]{2,0,1:T(8,128)S(1)}, f32[512,1,128]{2,0,1:T(8,128)S(1)}, u32[]{:S(2)}, u32[]{:S(2)}) collective-permute-start(f32[512,1,128]{2,0,1:T(8,128)S(1)} %collective-permute-done.4), channel_id=1, source_target_pairs={{0,8},{8,0},{16,24},{24,16},{1,9},{9,1},{17,25},{25,17},{2,10},{10... | collective-permute-start | bytes 786440 | tf_op jit(solution)/shard_map/ppermute | solution.py:70
  37.7 1.0 %copy-start = (bf16[512,512]{0,1:T(8,128)(2,1)S(1)}, bf16[512,512]{0,1:T(8,128)(2,1)}, u32[]{:S(2)}) copy-start(bf16[512,512]{0,1:T(8,128)(2,1)} %get-tuple-element.25) | copy-start | bytes 1572868
  37.7 1.1 %copy-start.1 = (bf16[4,1,64,512]{3,2,1,0:T(8,128)(2,1)S(1)}, bf16[4,1,64,512]{3,2,1,0:T(8,128)(2,1)}, u32[]{:S(2)}) copy-start(bf16[4,1,64,512]{3,2,1,0:T(8,128)(2,1)} %get-tuple-element.35) | copy-start | bytes 786436
  42.6 2.6 %collective-permute-start.12 = (f32[2,1,512]{2,1,0:T(1,128)S(1)}, f32[2,1,512]{2,1,0:T(1,128)S(1)}, u32[]{:S(2)}, u32[]{:S(2)}) collective-permute-start(f32[2,1,512]{2,1,0:T(1,128)S(1)} %pad_maximum_fusion.10), channel_id=1, source_target_pairs={{0,24},{8,0},{16,8},{24,16},{1,25},{9,1},{17,9},{25,17},{2,26},{10... | collective-permute-start | bytes 12296 | tf_op jit(solution)/shard_map/ppermute | solution.py:15
  43.9 3.6 %collective-permute-start.13 = (f32[2,1,512]{2,1,0:T(1,128)S(1)}, f32[2,1,512]{2,1,0:T(1,128)S(1)}, u32[]{:S(2)}, u32[]{:S(2)}) collective-permute-start(f32[2,1,512]{2,1,0:T(1,128)S(1)} %pad_maximum_fusion.10), channel_id=1, source_target_pairs={{0,16},{8,24},{16,0},{24,8},{1,17},{9,25},{17,1},{25,9},{2,18},{10... | collective-permute-start | bytes 12296 | tf_op jit(solution)/shard_map/ppermute | solution.py:15
  44.4 3.1 %collective-permute-start.14 = (f32[2,1,512]{2,1,0:T(1,128)S(1)}, f32[2,1,512]{2,1,0:T(1,128)S(1)}, u32[]{:S(2)}, u32[]{:S(2)}) collective-permute-start(f32[2,1,512]{2,1,0:T(1,128)S(1)} %pad_maximum_fusion.10), channel_id=1, source_target_pairs={{0,8},{8,16},{16,24},{24,0},{1,9},{9,17},{17,25},{25,1},{2,10},{10... | collective-permute-start | bytes 12296 | tf_op jit(solution)/shard_map/ppermute | solution.py:15

commit v14 on v10

--- a/solution.py
+++ b/solution.py
@@ -147,8 +147,6 @@
     angle = scaled * view.reshape(elements, voxels)
     field_real = jnp.cos(angle).astype(jnp.bfloat16)
     field_imag = (-jnp.sin(angle)).astype(jnp.bfloat16)
-    left = jnp.concatenate([field_real, field_imag], axis=1)
-    right = jnp.concatenate([-field_imag, field_real], axis=1)
 
     row = cap_row
     other = (own_swapped, lax.ppermute(jnp.stack(row[1:]), "tile", swap))
@@ -163,11 +161,12 @@
     def partial_focus(group, g_real, g_imag):
         cap_real = group[:, 0].reshape(-1, group.shape[-1])
         cap_imag = group[:, 1].reshape(-1, group.shape[-1])
-        product = jnp.dot(cap_real, left, preferred_element_type=jnp.float32) + jnp.dot(
-            cap_imag, right, preferred_element_type=jnp.float32
+        w_real = jnp.dot(cap_real, field_real, preferred_element_type=jnp.float32) - jnp.dot(
+            cap_imag, field_imag, preferred_element_type=jnp.float32
         )
-        w_real = product[:, :voxels]
-        w_imag = product[:, voxels:]
+        w_imag = jnp.dot(cap_real, field_imag, preferred_element_type=jnp.float32) + jnp.dot(
+            cap_imag, field_real, preferred_element_type=jnp.float32
+        )
         g_real = g_real.astype(jnp.float32)
         g_imag = g_imag.astype(jnp.float32)
         part_real = jnp.sum(g_real * w_real - g_imag * w_imag, axis=0)

time: 45.9 us -> 46.6 us (1.015)
  matrix products: 1.87 us -> 2.76 us
  waiting for transfers between devices: 15 us -> 14.3 us
  local copies, waits for them, and re-layouts: 3.42 us -> 4.1 us
    dot_general x4 -> x8, matrix products: 1.87 us -> 2.76 us  [the longest x2 0.79 us: partial_focus(): jnp.dot(cap_imag, field_real, preferred_element_type=jnp.float32)]
    unnamed x12, local copies, waits for them, and re-layouts: 0.06 us -> 0.74 us
    ppermute x1, waiting for transfers between devices: 3.33 us -> 2.66 us  [body(): lax.ppermute(lax.dynamic_slice_in_dim(pieces, (1 - y) * per_tile, per_til...]
where the time goes in v14:
time: 46.6 us; the launch traced here: 46.4 us
  starting transfers between devices  16.5 us (35%)
  waiting for transfers between devices  14.3 us (31%)
  other arithmetic  7.64 us (16%)
  local copies, waits for them, and re-layouts  4.1 us (9%)
  matrix products  2.76 us (6%)
  between operations  1.05 us (2%)
    ppermute x3, waiting for transfers between devices, body(): pieces.append(lax.ppermute(sent, 'tile', pairs))  5.63 us
    ppermute x3, starting transfers between devices, body(): cap_row.append(lax.ppermute(capture[0], 'tile', pairs))  4.39 us
    ppermute x3, starting transfers between devices, body(): pieces.append(lax.ppermute(sent, 'tile', pairs))  3.99 us
    another operation x1, other arithmetic  3.84 us
    ppermute x3, waiting for transfers between devices, gather_shifted(): pieces.append(lax.ppermute(block, axis_name, pairs))  3.07 us
    ppermute x1, waiting for transfers between devices, body(): lax.ppermute(lax.dynamic_slice_in_dim(pieces, (1 - y) * per_tile, per_til...  2.66 us
    ppermute x3, starting transfers between devices, gather_shifted(): pieces.append(lax.ppermute(block, axis_name, pairs))  1.83 us
    ppermute x1, starting transfers between devices, body(): lax.ppermute(lax.dynamic_slice_in_dim(pieces, (1 - y) * per_tile, per_til...  1.58 us
  transfers between devices with their start and end apart: 15, of which 6 were waited for; matrix products, arithmetic and copies ran while one was open for 19% of the time, Pallas kernels for 0%

profile of v14, /device:TPU:16, one launch (start us, length us, event | category | flops | bytes accessed | tf_op | source)
XLA Modules:
  0.0 46.4 jit_solution(4940399213455476361)
XLA Ops:
  0.0 1.5 %constant_dynamic-slice_fusion.14 = (f32[64,2,128]{2,1,0:T(2,128)S(1)}, f32[64,2,128]{2,1,0:T(2,128)S(1)}, f32[64,2,128]{2,1,0:T(2,128)S(1)}, f32[64,2,128]{2,1,0:T(2,128)S(1)}) fusion(f32[64,8,128]{2,1,0:T(8,128)} %param.7, s32[]{:T(128)S(6)} %select_n.138, s32[]{:T(128)S(6)} %select_n.142, s32[]{:T(128)S(6)} %select_n.140, s32[]{:T(128)S(6)} %select_n.144), kind=kLoop, calls=%fused_computation.85 | loop fusion | bytes 524304 | tf_op jit(solution)/shard_map/dynamic_slice | solution.py:127
  1.5 0.5 %collective-permute-start = (f32[64,2,128]{2,0,1:T(8,128)S(1)}, f32[64,2,128]{2,0,1:T(8,128)S(1)}, u32[]{:S(2)}, u32[]{:S(2)}) collective-permute-start(f32[64,2,128]{2,0,1:T(8,128)S(1)} %copy.28), channel_id=1, source_target_pairs={{0,6},{1,7},{2,0},{3,1},{4,2},{5,3},{6,4},{7,5},{8,14},{9,15},{10,... | collective-permute-start | bytes 196616 | tf_op jit(solution)/shard_map/ppermute | solution.py:132
  2.0 3.5 %collective-permute-start.1 = (f32[64,2,128]{2,0,1:T(8,128)S(1)}, f32[64,2,128]{2,0,1:T(8,128)S(1)}, u32[]{:S(2)}, u32[]{:S(2)}) collective-permute-start(f32[64,2,128]{2,0,1:T(8,128)S(1)} %copy.29), channel_id=1, source_target_pairs={{0,4},{1,5},{2,6},{3,7},{4,0},{5,1},{6,2},{7,3},{8,12},{9,13},{10,... | collective-permute-start | bytes 196616 | tf_op jit(solution)/shard_map/ppermute | solution.py:132
  5.5 2.0 %collective-permute-start.7 = (bf16[2,64,512]{2,1,0:T(8,128)(2,1)}, bf16[2,64,512]{2,1,0:T(8,128)(2,1)S(1)}, u32[]{:S(2)}, u32[]{:S(2)}) collective-permute-start(bf16[2,64,512]{2,1,0:T(8,128)(2,1)} %bitcast.22), channel_id=1, source_target_pairs={{0,6},{1,7},{2,0},{3,1},{4,2},{5,3},{6,4},{7,5},{8,14},{9,15},{10,... | collective-permute-start | bytes 393224 | tf_op jit(solution)/shard_map/ppermute | solution.py:123
  7.5 1.9 %collective-permute-start.8 = (bf16[2,64,512]{2,1,0:T(8,128)(2,1)}, bf16[2,64,512]{2,1,0:T(8,128)(2,1)S(1)}, u32[]{:S(2)}, u32[]{:S(2)}) collective-permute-start(bf16[2,64,512]{2,1,0:T(8,128)(2,1)} %bitcast.22), channel_id=1, source_target_pairs={{0,4},{1,5},{2,6},{3,7},{4,0},{5,1},{6,2},{7,3},{8,12},{9,13},{10,... | collective-permute-start | bytes 393224 | tf_op jit(solution)/shard_map/ppermute | solution.py:123
  9.4 0.5 %collective-permute-start.9 = (bf16[2,64,512]{2,1,0:T(8,128)(2,1)}, bf16[2,64,512]{2,1,0:T(8,128)(2,1)S(1)}, u32[]{:S(2)}, u32[]{:S(2)}) collective-permute-start(bf16[2,64,512]{2,1,0:T(8,128)(2,1)} %bitcast.22), channel_id=1, source_target_pairs={{0,2},{1,3},{2,4},{3,5},{4,6},{5,7},{6,0},{7,1},{8,10},{9,11},{10,... | collective-permute-start | bytes 393224 | tf_op jit(solution)/shard_map/ppermute | solution.py:123
  9.9 1.5 %collective-permute-start.10 = (bf16[2,64,512]{2,1,0:T(8,128)(2,1)}, bf16[2,64,512]{2,1,0:T(8,128)(2,1)}, u32[]{:S(2)}, u32[]{:S(2)}) collective-permute-start(bf16[2,64,512]{2,1,0:T(8,128)(2,1)} %bitcast.22), channel_id=1, source_target_pairs={{0,1},{1,0},{2,3},{3,2},{4,5},{5,4},{6,7},{7,6},{8,9},{9,8},{10,11... | collective-permute-start | bytes 393224 | tf_op jit(solution)/shard_map/ppermute | solution.py:124
  11.4 5.6 %collective-permute-done.2 = f32[64,2,128]{2,0,1:T(8,128)S(1)} collective-permute-done((f32[64,2,128]{2,0,1:T(8,128)S(1)}, f32[64,2,128]{2,0,1:T(8,128)S(1)}, u32[]{:S(2)}, u32[]{:S(2)}) %collective-permute-start.2) | collective-permute-done | bytes 65568 | tf_op jit(solution)/shard_map/ppermute | solution.py:132
  17.1 0.0 copy-start.1
  17.1 1.6 %collective-permute-start.3 = (f32[4,64,1,128]{3,1,0,2:T(8,128)S(1)}, f32[4,64,1,128]{3,1,0,2:T(8,128)S(1)}, u32[]{:S(2)}, u32[]{:S(2)}) collective-permute-start(f32[4,64,1,128]{3,1,0,2:T(8,128)S(1)} %get-tuple-element.34), channel_id=1, source_target_pairs={{0,1},{1,0},{2,3},{3,2},{4,5},{5,4},{6,7},{7,6},{8,9},{9,8},{10,11... | collective-permute-start | bytes 393224 | tf_op jit(solution)/shard_map/ppermute | solution.py:135
  18.7 0.7 %copy-done = s32[1,512]{1,0:T(1,128)S(1)} copy-done((s32[1,512]{1,0:T(1,128)S(1)}, s32[1,512]{1,0:T(1,128)}, u32[]{:S(2)}) %copy-start) | copy-done | bytes 2072
  19.4 0.1 select_reduce_fusion.1
  19.5 2.7 %collective-permute-done.3 = f32[4,64,1,128]{3,1,0,2:T(8,128)S(1)} collective-permute-done((f32[4,64,1,128]{3,1,0,2:T(8,128)S(1)}, f32[4,64,1,128]{3,1,0,2:T(8,128)S(1)}, u32[]{:S(2)}, u32[]{:S(2)}) %collective-permute-start.3) | collective-permute-done | bytes 131104 | tf_op jit(solution)/shard_map/ppermute | solution.py:135
  22.1 0.1 fusion.15
  22.2 0.1 fusion.13
  22.3 1.6 %collective-permute-start.4 = (f32[512,1,128]{2,0,1:T(8,128)S(1)}, f32[512,1,128]{2,0,1:T(8,128)S(1)}, u32[]{:S(2)}, u32[]{:S(2)}) collective-permute-start(f32[512,1,128]{2,0,1:T(8,128)S(1)} %bitcast.119), channel_id=1, source_target_pairs={{0,16},{8,24},{16,0},{24,8},{1,17},{9,25},{17,1},{25,9},{2,18},{10... | collective-permute-start | bytes 786440 | tf_op jit(solution)/shard_map/ppermute | solution.py:68
  24.6 1.6 %collective-permute-start.11 = (bf16[3,2,64,512]{3,2,1,0:T(8,128)(2,1)S(1)}, bf16[3,2,64,512]{3,2,1,0:T(8,128)(2,1)}, u32[]{:S(2)}, u32[]{:S(2)}) collective-permute-start(bf16[3,2,64,512]{3,2,1,0:T(8,128)(2,1)S(1)} %pad_maximum_fusion.1), channel_id=1, source_target_pairs={{0,1},{1,0},{2,3},{3,2},{4,5},{5,4},{6,7},{7,6},{8,9},{9,8},{10,11... | collective-permute-start | bytes 1179656 | tf_op jit(solution)/shard_map/ppermute | solution.py:152
  26.2 1.0 %pad_maximum_fusion = bf16[4,2,64,512]{3,2,1,0:T(8,128)(2,1)S(1)} fusion(bf16[1,2,64,512]{3,2,1,0:T(8,128)(2,1)S(1)} %bitcast.129, bf16[1,2,64,512]{3,2,1,0:T(8,128)(2,1)S(1)} %bitcast.127, bf16[1,2,64,512]{3,2,1,0:T(8,128)(2,1)S(1)} %bitcast.125, bf16[1,2,64,512]{3,2,1,0:T(8,128)(2,1)} %param.11), kind=kLoop, calls=%fused_computation.33 | loop fusion | flops 786432 | bytes 1048576 | tf_op jit(solution)/shard_map/stack | solution.py:153
  27.1 0.1 collective-permute-start.5
  27.2 1.5 %collective-permute-done.4 = f32[512,1,128]{2,0,1:T(8,128)S(1)} collective-permute-done((f32[512,1,128]{2,0,1:T(8,128)S(1)}, f32[512,1,128]{2,0,1:T(8,128)S(1)}, u32[]{:S(2)}, u32[]{:S(2)}) %collective-permute-start.4) | collective-permute-done | bytes 262176 | tf_op jit(solution)/shard_map/ppermute | solution.py:68
  28.8 1.4 %collective-permute-done.6 = f32[512,1,128]{2,0,1:T(8,128)S(1)} collective-permute-done((f32[512,1,128]{2,0,1:T(8,128)S(1)}, f32[512,1,128]{2,0,1:T(8,128)S(1)}, u32[]{:S(2)}, u32[]{:S(2)}) %collective-permute-start.6) | collective-permute-done | bytes 262176 | tf_op jit(solution)/shard_map/ppermute | solution.py:70
  30.3 3.8 %cosine_convert_fusion = (bf16[2,2,512,1,128]{4,2,0,3,1:T(8,128)(2,1)S(1)}, bf16[2,2,512,1,128]{4,2,0,3,1:T(8,128)(2,1)S(1)}) fusion(f32[2,1,512,1,128]{4,2,0,3,1:T(8,128)S(1)} %maximum_bitcast_fusion.1, f32[2,1,512,1,128]{4,2,0,3,1:T(8,128)S(1)} %maximum_bitcast_fusion, f32[]{:T(128)} %bitcast.4), kind=kLoop, calls=%fused_computation.6 | loop fusion | flops 1310720 | bytes 2097156 | tf_op jit(solution)/shard_map/convert.5
  34.2 0.4 copy.23
  34.6 0.2 copy.24
  34.9 0.4 copy.27
  35.3 0.2 copy.26
  35.5 0.2 convert_element_type.50
  35.7 0.2 convert_element_type.55
  35.9 0.1 dynamic-slice_bitcast_fusion
  36.0 0.1 fusion.12
  36.1 0.1 fusion.11
  36.2 0.3 fusion.27
  36.6 0.3 fusion.28
  36.9 0.3 convolution_subtract_fusion.1
  37.3 0.5 fusion.7
  37.7 0.1 fusion.9
  37.8 0.1 fusion.10
  38.0 1.1 %pad_maximum_fusion.2 = (bf16[4,1,64,512]{3,2,1,0:T(8,128)(2,1)S(1)}, bf16[4,1,64,512]{3,2,1,0:T(8,128)(2,1)S(1)}) fusion(bf16[3,2,64,512]{3,2,1,0:T(8,128)(2,1)} %collective-permute-done.11, bf16[1,2,64,512]{3,2,1,0:T(8,128)(2,1)} %bitcast.42), kind=kLoop, calls=%fused_computation.52 | loop fusion | flops 262144 | bytes 1048576 | tf_op jit(solution)/shard_map/concatenate | solution.py:179
  39.1 0.3 fusion.29
  39.4 0.3 fusion.30
  39.8 0.3 convolution_subtract_fusion
  40.1 0.3 convolution_add_fusion
  40.4 0.2 fusion.3
  40.8 1.3 %collective-permute-start.12 = (f32[2,1,512]{2,1,0:T(1,128)S(1)}, f32[2,1,512]{2,1,0:T(1,128)S(1)}, u32[]{:S(2)}, u32[]{:S(2)}) collective-permute-start(f32[2,1,512]{2,1,0:T(1,128)S(1)} %pad_maximum_fusion.4), channel_id=1, source_target_pairs={{0,24},{8,0},{16,8},{24,16},{1,25},{9,1},{17,9},{25,17},{2,26},{10... | collective-permute-start | bytes 12296 | tf_op jit(solution)/shard_map/ppermute | solution.py:15
  42.1 0.5 %collective-permute-start.13 = (f32[2,1,512]{2,1,0:T(1,128)S(1)}, f32[2,1,512]{2,1,0:T(1,128)S(1)}, u32[]{:S(2)}, u32[]{:S(2)}) collective-permute-start(f32[2,1,512]{2,1,0:T(1,128)S(1)} %pad_maximum_fusion.4), channel_id=1, source_target_pairs={{0,16},{8,24},{16,0},{24,8},{1,17},{9,25},{17,1},{25,9},{2,18},{10... | collective-permute-start | bytes 12296 | tf_op jit(solution)/shard_map/ppermute | solution.py:15
  42.6 0.8 %collective-permute-done.12 = f32[2,1,512]{2,1,0:T(1,128)S(1)} collective-permute-done((f32[2,1,512]{2,1,0:T(1,128)S(1)}, f32[2,1,512]{2,1,0:T(1,128)S(1)}, u32[]{:S(2)}, u32[]{:S(2)}) %collective-permute-start.12) | collective-permute-done | bytes 4128 | tf_op jit(solution)/shard_map/ppermute | solution.py:15
  43.4 2.3 %collective-permute-done.13 = f32[2,1,512]{2,1,0:T(1,128)S(1)} collective-permute-done((f32[2,1,512]{2,1,0:T(1,128)S(1)}, f32[2,1,512]{2,1,0:T(1,128)S(1)}, u32[]{:S(2)}, u32[]{:S(2)}) %collective-permute-start.13) | collective-permute-done | bytes 4128 | tf_op jit(solution)/shard_map/ppermute | solution.py:15
  45.7 0.6 %fusion.21 = f32[2,1,512]{2,1,0:T(1,128)} fusion(f32[8,2,1,512]{3,2,1,0:T(1,128)S(1)} %constant_dynamic-update-slice_fusion, s32[]{:T(128)S(6)} %add.214, s32[]{:T(128)S(6)} %add.213, s32[]{:T(128)S(6)} %add.212, s32[]{:T(128)S(6)} %select_n.159), kind=kLoop, calls=%fused_computation.90 | loop fusion | flops 3072 | bytes 20496 | tf_op jit(solution)/shard_map/add | solution.py:96
  (43 shorter events, 0.5 us)
Async XLA Ops:
  1.5 7.9 %collective-permute-start = (f32[64,2,128]{2,0,1:T(8,128)S(1)}, f32[64,2,128]{2,0,1:T(8,128)S(1)}, u32[]{:S(2)}, u32[]{:S(2)}) collective-permute-start(f32[64,2,128]{2,0,1:T(8,128)S(1)} %copy.28), channel_id=1, source_target_pairs={{0,6},{1,7},{2,0},{3,1},{4,2},{5,3},{6,4},{7,5},{8,14},{9,15},{10,... | collective-permute-start | bytes 196616 | tf_op jit(solution)/shard_map/ppermute | solution.py:132
  2.0 7.9 %collective-permute-start.1 = (f32[64,2,128]{2,0,1:T(8,128)S(1)}, f32[64,2,128]{2,0,1:T(8,128)S(1)}, u32[]{:S(2)}, u32[]{:S(2)}) collective-permute-start(f32[64,2,128]{2,0,1:T(8,128)S(1)} %copy.29), channel_id=1, source_target_pairs={{0,4},{1,5},{2,6},{3,7},{4,0},{5,1},{6,2},{7,3},{8,12},{9,13},{10,... | collective-permute-start | bytes 196616 | tf_op jit(solution)/shard_map/ppermute | solution.py:132
  5.5 11.5 %collective-permute-start.2 = (f32[64,2,128]{2,0,1:T(8,128)S(1)}, f32[64,2,128]{2,0,1:T(8,128)S(1)}, u32[]{:S(2)}, u32[]{:S(2)}) collective-permute-start(f32[64,2,128]{2,0,1:T(8,128)S(1)} %copy.30), channel_id=1, source_target_pairs={{0,2},{1,3},{2,4},{3,5},{4,6},{5,7},{6,0},{7,1},{8,10},{9,11},{10,... | collective-permute-start | bytes 196616 | tf_op jit(solution)/shard_map/ppermute | solution.py:132
  5.5 19.0 %collective-permute-start.7 = (bf16[2,64,512]{2,1,0:T(8,128)(2,1)}, bf16[2,64,512]{2,1,0:T(8,128)(2,1)S(1)}, u32[]{:S(2)}, u32[]{:S(2)}) collective-permute-start(bf16[2,64,512]{2,1,0:T(8,128)(2,1)} %bitcast.22), channel_id=1, source_target_pairs={{0,6},{1,7},{2,0},{3,1},{4,2},{5,3},{6,4},{7,5},{8,14},{9,15},{10,... | collective-permute-start | bytes 393224 | tf_op jit(solution)/shard_map/ppermute | solution.py:123
  7.5 17.0 %collective-permute-start.8 = (bf16[2,64,512]{2,1,0:T(8,128)(2,1)}, bf16[2,64,512]{2,1,0:T(8,128)(2,1)S(1)}, u32[]{:S(2)}, u32[]{:S(2)}) collective-permute-start(bf16[2,64,512]{2,1,0:T(8,128)(2,1)} %bitcast.22), channel_id=1, source_target_pairs={{0,4},{1,5},{2,6},{3,7},{4,0},{5,1},{6,2},{7,3},{8,12},{9,13},{10,... | collective-permute-start | bytes 393224 | tf_op jit(solution)/shard_map/ppermute | solution.py:123
  9.4 15.1 %collective-permute-start.9 = (bf16[2,64,512]{2,1,0:T(8,128)(2,1)}, bf16[2,64,512]{2,1,0:T(8,128)(2,1)S(1)}, u32[]{:S(2)}, u32[]{:S(2)}) collective-permute-start(bf16[2,64,512]{2,1,0:T(8,128)(2,1)} %bitcast.22), channel_id=1, source_target_pairs={{0,2},{1,3},{2,4},{3,5},{4,6},{5,7},{6,0},{7,1},{8,10},{9,11},{10,... | collective-permute-start | bytes 393224 | tf_op jit(solution)/shard_map/ppermute | solution.py:123
  9.9 28.1 %collective-permute-start.10 = (bf16[2,64,512]{2,1,0:T(8,128)(2,1)}, bf16[2,64,512]{2,1,0:T(8,128)(2,1)}, u32[]{:S(2)}, u32[]{:S(2)}) collective-permute-start(bf16[2,64,512]{2,1,0:T(8,128)(2,1)} %bitcast.22), channel_id=1, source_target_pairs={{0,1},{1,0},{2,3},{3,2},{4,5},{5,4},{6,7},{7,6},{8,9},{9,8},{10,11... | collective-permute-start | bytes 393224 | tf_op jit(solution)/shard_map/ppermute | solution.py:124
  17.1 1.6 %copy-start.1 = (f32[1,2,64]{2,1,0:T(2,128)S(1)}, f32[1,2,64]{2,1,0:T(2,128)}, u32[]{:S(2)}) copy-start(f32[1,2,64]{2,1,0:T(2,128)} %param.10) | copy-start | bytes 1540
  17.1 5.0 %collective-permute-start.3 = (f32[4,64,1,128]{3,1,0,2:T(8,128)S(1)}, f32[4,64,1,128]{3,1,0,2:T(8,128)S(1)}, u32[]{:S(2)}, u32[]{:S(2)}) collective-permute-start(f32[4,64,1,128]{3,1,0,2:T(8,128)S(1)} %get-tuple-element.34), channel_id=1, source_target_pairs={{0,1},{1,0},{2,3},{3,2},{4,5},{5,4},{6,7},{7,6},{8,9},{9,8},{10,11... | collective-permute-start | bytes 393224 | tf_op jit(solution)/shard_map/ppermute | solution.py:135
  18.7 0.7 %copy-start = (s32[1,512]{1,0:T(1,128)S(1)}, s32[1,512]{1,0:T(1,128)}, u32[]{:S(2)}) copy-start(s32[1,512]{1,0:T(1,128)} %param.8) | copy-start | bytes 6148
  22.3 6.4 %collective-permute-start.4 = (f32[512,1,128]{2,0,1:T(8,128)S(1)}, f32[512,1,128]{2,0,1:T(8,128)S(1)}, u32[]{:S(2)}, u32[]{:S(2)}) collective-permute-start(f32[512,1,128]{2,0,1:T(8,128)S(1)} %bitcast.119), channel_id=1, source_target_pairs={{0,16},{8,24},{16,0},{24,8},{1,17},{9,25},{17,1},{25,9},{2,18},{10... | collective-permute-start | bytes 786440 | tf_op jit(solution)/shard_map/ppermute | solution.py:68
  24.6 13.4 %collective-permute-start.11 = (bf16[3,2,64,512]{3,2,1,0:T(8,128)(2,1)S(1)}, bf16[3,2,64,512]{3,2,1,0:T(8,128)(2,1)}, u32[]{:S(2)}, u32[]{:S(2)}) collective-permute-start(bf16[3,2,64,512]{3,2,1,0:T(8,128)(2,1)S(1)} %pad_maximum_fusion.1), channel_id=1, source_target_pairs={{0,1},{1,0},{2,3},{3,2},{4,5},{5,4},{6,7},{7,6},{8,9},{9,8},{10,11... | collective-permute-start | bytes 1179656 | tf_op jit(solution)/shard_map/ppermute | solution.py:152
  27.1 1.7 %collective-permute-start.5 = (f32[512,1,128]{2,0,1:T(8,128)S(1)}, f32[512,1,128]{2,0,1:T(8,128)S(1)}, u32[]{:S(2)}, u32[]{:S(2)}) collective-permute-start(f32[512,1,128]{2,0,1:T(8,128)S(1)} %bitcast.120), channel_id=1, source_target_pairs={{0,8},{8,0},{16,24},{24,16},{1,9},{9,1},{17,25},{25,17},{2,10},{10... | collective-permute-start | bytes 786440 | tf_op jit(solution)/shard_map/ppermute | solution.py:70
  28.7 1.5 %collective-permute-start.6 = (f32[512,1,128]{2,0,1:T(8,128)S(1)}, f32[512,1,128]{2,0,1:T(8,128)S(1)}, u32[]{:S(2)}, u32[]{:S(2)}) collective-permute-start(f32[512,1,128]{2,0,1:T(8,128)S(1)} %collective-permute-done.4), channel_id=1, source_target_pairs={{0,8},{8,0},{16,24},{24,16},{1,9},{9,1},{17,25},{25,17},{2,10},{10... | collective-permute-start | bytes 786440 | tf_op jit(solution)/shard_map/ppermute | solution.py:70
  40.8 2.6 %collective-permute-start.12 = (f32[2,1,512]{2,1,0:T(1,128)S(1)}, f32[2,1,512]{2,1,0:T(1,128)S(1)}, u32[]{:S(2)}, u32[]{:S(2)}) collective-permute-start(f32[2,1,512]{2,1,0:T(1,128)S(1)} %pad_maximum_fusion.4), channel_id=1, source_target_pairs={{0,24},{8,0},{16,8},{24,16},{1,25},{9,1},{17,9},{25,17},{2,26},{10... | collective-permute-start | bytes 12296 | tf_op jit(solution)/shard_map/ppermute | solution.py:15
  42.1 3.6 %collective-permute-start.13 = (f32[2,1,512]{2,1,0:T(1,128)S(1)}, f32[2,1,512]{2,1,0:T(1,128)S(1)}, u32[]{:S(2)}, u32[]{:S(2)}) collective-permute-start(f32[2,1,512]{2,1,0:T(1,128)S(1)} %pad_maximum_fusion.4), channel_id=1, source_target_pairs={{0,16},{8,24},{16,0},{24,8},{1,17},{9,25},{17,1},{25,9},{2,18},{10... | collective-permute-start | bytes 12296 | tf_op jit(solution)/shard_map/ppermute | solution.py:15
  42.6 3.1 %collective-permute-start.14 = (f32[2,1,512]{2,1,0:T(1,128)S(1)}, f32[2,1,512]{2,1,0:T(1,128)S(1)}, u32[]{:S(2)}, u32[]{:S(2)}) collective-permute-start(f32[2,1,512]{2,1,0:T(1,128)S(1)} %pad_maximum_fusion.4), channel_id=1, source_target_pairs={{0,8},{8,16},{16,24},{24,0},{1,9},{9,17},{17,25},{25,1},{2,10},{10... | collective-permute-start | bytes 12296 | tf_op jit(solution)/shard_map/ppermute | solution.py:15

commit v15 on v10

--- a/solution.py
+++ b/solution.py
@@ -124,13 +124,14 @@
     own_swapped = lax.ppermute(capture[0], "tile", swap)
 
     per_tile = travel_time.shape[1] // tiles
-    pieces = [lax.dynamic_slice_in_dim(travel_time, 2 * z * per_tile, 2 * per_tile, 1)]
+    by_row = jnp.transpose(travel_time, (1, 0, 2))
+    pieces = [lax.dynamic_slice_in_dim(by_row, 2 * z * per_tile, 2 * per_tile, 0)]
     for s in range(1, positions):
         target = (z - s) % positions
-        sent = lax.dynamic_slice_in_dim(travel_time, 2 * target * per_tile, 2 * per_tile, 1)
+        sent = lax.dynamic_slice_in_dim(by_row, 2 * target * per_tile, 2 * per_tile, 0)
         pairs = [(p * 2 + r, ((p - s) % positions) * 2 + r) for p in range(positions) for r in range(2)]
         pieces.append(lax.ppermute(sent, "tile", pairs))
-    pieces = jnp.stack(pieces)
+    pieces = jnp.moveaxis(jnp.stack(pieces), 2, 1)
     mine_tt = lax.dynamic_slice_in_dim(pieces, y * per_tile, per_tile, 2)
     theirs_tt = lax.ppermute(
         lax.dynamic_slice_in_dim(pieces, (1 - y) * per_tile, per_tile, 2), "tile", [(j, j ^ 1) for j in range(tiles)]

time: 45.9 us -> 46.9 us (1.022)
  waiting for transfers between devices: 15 us -> 17.2 us
  other arithmetic: 7.94 us -> 7.14 us
  starting transfers between devices: 16.5 us -> 15.8 us
    another operation x2 -> x4, local copies, waits for them, and re-layouts: 0.07 us -> 1.78 us  [the longest x1 1.47 us: body(): pieces = jnp.moveaxis(jnp.stack(pieces), 2, 1)]
    dynamic_slice x3 -> x0, local copies, waits for them, and re-layouts: 1.5 us -> none  [the longest x2 1.47 us: body(): lax.dynamic_slice_in_dim(travel_time, 2 * z * per_tile, 2 * per_tile, 1)]
    ppermute x3, starting transfers between devices: 4.39 us -> 5.73 us  [body(): cap_row.append(lax.ppermute(capture[0], 'tile', pairs))]
    ppermute x1, waiting for transfers between devices: 1.48 us -> 2.56 us  [gather_columns(): same_core.append(lax.ppermute(block, axis_name, pairs))]
    ppermute x1, starting transfers between devices: 1.58 us -> 0.57 us  [body(): lax.ppermute(lax.dynamic_slice_in_dim(pieces, (1 - y) * per_tile, per_til...]
    ppermute x1, waiting for transfers between devices: 3.33 us -> 4.3 us  [body(): lax.ppermute(lax.dynamic_slice_in_dim(pieces, (1 - y) * per_tile, per_til...]
    another operation x1, other arithmetic: 0.97 us -> 0.07 us  [body(): row = jnp.stack(row)]
    ppermute x3, starting transfers between devices: 3.99 us -> 3.1 us  [body(): pieces.append(lax.ppermute(sent, 'tile', pairs))]
  transfers between devices with their start and end apart: 15 -> 15, of which waited for: 6 -> 6; matrix products, arithmetic and copies ran while one was open for 19% -> 17% of each run, Pallas kernels for 0% -> 0%
where the time goes in v15:
time: 46.9 us; the launch traced here: 46.7 us
  waiting for transfers between devices  17.2 us (37%)
  starting transfers between devices  15.8 us (34%)
  other arithmetic  7.14 us (15%)
  local copies, waits for them, and re-layouts  3.62 us (8%)
  matrix products  1.86 us (4%)
  between operations  1.07 us (2%)
    ppermute x3, waiting for transfers between devices, body(): pieces.append(lax.ppermute(sent, 'tile', pairs))  5.86 us
    ppermute x3, starting transfers between devices, body(): cap_row.append(lax.ppermute(capture[0], 'tile', pairs))  5.73 us
    ppermute x1, waiting for transfers between devices, body(): lax.ppermute(lax.dynamic_slice_in_dim(pieces, (1 - y) * per_tile, per_til...  4.3 us
    another operation x1, other arithmetic  3.84 us
    ppermute x3, starting transfers between devices, body(): pieces.append(lax.ppermute(sent, 'tile', pairs))  3.1 us
    ppermute x3, waiting for transfers between devices, gather_shifted(): pieces.append(lax.ppermute(block, axis_name, pairs))  3.07 us
    ppermute x1, waiting for transfers between devices, gather_columns(): same_core.append(lax.ppermute(block, axis_name, pairs))  2.56 us
    ppermute x3, starting transfers between devices, gather_shifted(): pieces.append(lax.ppermute(block, axis_name, pairs))  1.83 us
  transfers between devices with their start and end apart: 15, of which 6 were waited for; matrix products, arithmetic and copies ran while one was open for 17% of the time, Pallas kernels for 0%

profile of v15, /device:TPU:16, one launch (start us, length us, event | category | flops | bytes accessed | tf_op | source)
XLA Modules:
  0.0 46.7 jit_solution(6888644239758295590)
XLA Ops:
  0.0 1.5 %dynamic-slice_bitcast_fusion.7 = (f32[1,2,64,128]{3,1,2,0:T(2,128)S(1)}, f32[2,64,128]{2,0,1:T(2,128)S(1)}, f32[2,64,128]{2,0,1:T(2,128)S(1)}, f32[2,64,128]{2,0,1:T(2,128)S(1)}) fusion(f32[64,8,128]{2,1,0:T(8,128)} %param.7, s32[]{:T(128)S(6)} %select_n.138, s32[]{:T(128)S(6)} %select_n.140, s32[]{:T(128)S(6)} %select_n.144, s32[]{:T(128)S(6)} %select_n.142), kind=kLoop, calls=%fused_computation.66 | loop fusion | bytes 524304 | tf_op jit(solution)/shard_map/stack | solution.py:134
  1.5 0.1 collective-permute-start.1
  1.6 1.9 %collective-permute-start.2 = (f32[2,64,128]{2,0,1:T(2,128)S(1)}, f32[2,64,128]{2,0,1:T(2,128)S(1)}, u32[]{:S(2)}, u32[]{:S(2)}) collective-permute-start(f32[2,64,128]{2,0,1:T(2,128)S(1)} %get-tuple-element.38), channel_id=1, source_target_pairs={{0,2},{1,3},{2,4},{3,5},{4,6},{5,7},{6,0},{7,1},{8,10},{9,11},{10,... | collective-permute-start | bytes 196616 | tf_op jit(solution)/shard_map/ppermute | solution.py:133
  3.5 1.1 %collective-permute-start = (f32[2,64,128]{2,0,1:T(2,128)S(1)}, f32[2,64,128]{2,0,1:T(2,128)S(1)}, u32[]{:S(2)}, u32[]{:S(2)}) collective-permute-start(f32[2,64,128]{2,0,1:T(2,128)S(1)} %get-tuple-element.37), channel_id=1, source_target_pairs={{0,6},{1,7},{2,0},{3,1},{4,2},{5,3},{6,4},{7,5},{8,14},{9,15},{10,... | collective-permute-start | bytes 196616 | tf_op jit(solution)/shard_map/ppermute | solution.py:133
  4.6 2.0 %collective-permute-start.7 = (bf16[2,64,512]{2,1,0:T(8,128)(2,1)}, bf16[2,64,512]{2,1,0:T(8,128)(2,1)S(1)}, u32[]{:S(2)}, u32[]{:S(2)}) collective-permute-start(bf16[2,64,512]{2,1,0:T(8,128)(2,1)} %bitcast.126), channel_id=1, source_target_pairs={{0,6},{1,7},{2,0},{3,1},{4,2},{5,3},{6,4},{7,5},{8,14},{9,15},{10,... | collective-permute-start | bytes 393224 | tf_op jit(solution)/shard_map/ppermute | solution.py:123
  6.6 1.7 %collective-permute-start.8 = (bf16[2,64,512]{2,1,0:T(8,128)(2,1)}, bf16[2,64,512]{2,1,0:T(8,128)(2,1)S(1)}, u32[]{:S(2)}, u32[]{:S(2)}) collective-permute-start(bf16[2,64,512]{2,1,0:T(8,128)(2,1)} %bitcast.127), channel_id=1, source_target_pairs={{0,4},{1,5},{2,6},{3,7},{4,0},{5,1},{6,2},{7,3},{8,12},{9,13},{10,... | collective-permute-start | bytes 393224 | tf_op jit(solution)/shard_map/ppermute | solution.py:123
  8.3 2.0 %collective-permute-start.9 = (bf16[2,64,512]{2,1,0:T(8,128)(2,1)}, bf16[2,64,512]{2,1,0:T(8,128)(2,1)S(1)}, u32[]{:S(2)}, u32[]{:S(2)}) collective-permute-start(bf16[2,64,512]{2,1,0:T(8,128)(2,1)} %bitcast.128), channel_id=1, source_target_pairs={{0,2},{1,3},{2,4},{3,5},{4,6},{5,7},{6,0},{7,1},{8,10},{9,11},{10,... | collective-permute-start | bytes 393224 | tf_op jit(solution)/shard_map/ppermute | solution.py:123
  10.3 5.9 %collective-permute-done.2 = f32[2,64,128]{2,0,1:T(2,128)S(1)} collective-permute-done((f32[2,64,128]{2,0,1:T(2,128)S(1)}, f32[2,64,128]{2,0,1:T(2,128)S(1)}, u32[]{:S(2)}, u32[]{:S(2)}) %collective-permute-start.2) | collective-permute-done | bytes 65568 | tf_op jit(solution)/shard_map/ppermute | solution.py:133
  16.2 1.5 %collective-permute-start.10 = (bf16[2,64,512]{2,1,0:T(8,128)(2,1)}, bf16[2,64,512]{2,1,0:T(8,128)(2,1)}, u32[]{:S(2)}, u32[]{:S(2)}) collective-permute-start(bf16[2,64,512]{2,1,0:T(8,128)(2,1)} %bitcast.129), channel_id=1, source_target_pairs={{0,1},{1,0},{2,3},{3,2},{4,5},{5,4},{6,7},{7,6},{8,9},{9,8},{10,11... | collective-permute-start | bytes 393224 | tf_op jit(solution)/shard_map/ppermute | solution.py:124
  17.7 0.1 pad_maximum_fusion.9
  17.8 0.2 constant_dynamic-slice_fusion.10
  18.1 0.6 %collective-permute-start.3 = (f32[4,64,1,128]{3,1,0,2:T(8,128)S(1)}, f32[4,64,1,128]{3,1,0,2:T(8,128)S(1)}, u32[]{:S(2)}, u32[]{:S(2)}) collective-permute-start(f32[4,64,1,128]{3,1,0,2:T(8,128)S(1)} %bitcast.125), channel_id=1, source_target_pairs={{0,1},{1,0},{2,3},{3,2},{4,5},{5,4},{6,7},{7,6},{8,9},{9,8},{10,11... | collective-permute-start | bytes 393224 | tf_op jit(solution)/shard_map/ppermute | solution.py:136
  18.7 0.1 select_reduce_fusion.1
  18.8 4.3 %collective-permute-done.3 = f32[4,64,1,128]{3,1,0,2:T(8,128)S(1)} collective-permute-done((f32[4,64,1,128]{3,1,0,2:T(8,128)S(1)}, f32[4,64,1,128]{3,1,0,2:T(8,128)S(1)}, u32[]{:S(2)}, u32[]{:S(2)}) %collective-permute-start.3) | collective-permute-done | bytes 131104 | tf_op jit(solution)/shard_map/ppermute | solution.py:136
  23.1 0.1 fusion.17
  23.2 0.1 fusion.15
  23.2 1.6 %collective-permute-start.4 = (f32[512,1,128]{2,0,1:T(8,128)S(1)}, f32[512,1,128]{2,0,1:T(8,128)S(1)}, u32[]{:S(2)}, u32[]{:S(2)}) collective-permute-start(f32[512,1,128]{2,0,1:T(8,128)S(1)} %bitcast.105), channel_id=1, source_target_pairs={{0,16},{8,24},{16,0},{24,8},{1,17},{9,25},{17,1},{25,9},{2,18},{10... | collective-permute-start | bytes 786440 | tf_op jit(solution)/shard_map/ppermute | solution.py:68
  25.5 0.0 collective-permute-done.7
  25.6 1.4 %collective-permute-start.11 = (bf16[3,2,64,512]{3,2,1,0:T(8,128)(2,1)S(1)}, bf16[3,2,64,512]{3,2,1,0:T(8,128)(2,1)}, u32[]{:S(2)}, u32[]{:S(2)}) collective-permute-start(bf16[3,2,64,512]{3,2,1,0:T(8,128)(2,1)S(1)} %pad_maximum_fusion.7), channel_id=1, source_target_pairs={{0,1},{1,0},{2,3},{3,2},{4,5},{5,4},{6,7},{7,6},{8,9},{9,8},{10,11... | collective-permute-start | bytes 1179656 | tf_op jit(solution)/shard_map/ppermute | solution.py:155
  27.0 0.1 pad_maximum_fusion.6
  27.0 0.1 collective-permute-start.5
  27.1 2.6 %collective-permute-done.4 = f32[512,1,128]{2,0,1:T(8,128)S(1)} collective-permute-done((f32[512,1,128]{2,0,1:T(8,128)S(1)}, f32[512,1,128]{2,0,1:T(8,128)S(1)}, u32[]{:S(2)}, u32[]{:S(2)}) %collective-permute-start.4) | collective-permute-done | bytes 262176 | tf_op jit(solution)/shard_map/ppermute | solution.py:68
  29.8 1.4 %collective-permute-done.6 = f32[512,1,128]{2,0,1:T(8,128)S(1)} collective-permute-done((f32[512,1,128]{2,0,1:T(8,128)S(1)}, f32[512,1,128]{2,0,1:T(8,128)S(1)}, u32[]{:S(2)}, u32[]{:S(2)}) %collective-permute-start.6) | collective-permute-done | bytes 262176 | tf_op jit(solution)/shard_map/ppermute | solution.py:70
  31.2 3.8 %cosine_convert_fusion = (bf16[2,2,512,1,128]{4,2,0,3,1:T(8,128)(2,1)S(1)}, bf16[2,2,512,1,128]{4,2,0,3,1:T(8,128)(2,1)S(1)}) fusion(f32[2,1,512,1,128]{4,2,0,3,1:T(8,128)S(1)} %maximum_bitcast_fusion.1, f32[2,1,512,1,128]{4,2,0,3,1:T(8,128)S(1)} %maximum_bitcast_fusion, f32[]{:T(128)} %bitcast.4), kind=kLoop, calls=%fused_computation.6 | loop fusion | flops 1310720 | bytes 2097156 | tf_op jit(solution)/shard_map/convert.5
  35.1 0.4 copy.15
  35.6 0.2 copy.16
  35.8 0.4 copy.19
  36.2 0.2 copy.18
  36.5 0.2 convert_element_type.44
  36.7 0.2 convert_element_type.49
  36.9 0.1 dynamic-slice_bitcast_fusion
  37.0 0.1 fusion.14
  37.1 0.1 fusion.13
  37.2 0.1 bitcast_negate_fusion
  37.3 0.5 fusion.1
  37.8 0.5 %convolution_add_fusion.1 = f32[256,1024]{1,0:T(8,128)S(1)} fusion(f32[256,1024]{1,0:T(8,128)S(1)} %fusion.1, bf16[256,512]{1,0:T(8,128)(2,1)S(1)} %bitcast.110, bf16[512,512]{0,1:T(8,128)(2,1)S(1)} %bitcast.100, bf16[512,512]{0,1:T(8,128)(2,1)S(1)} %bitcast_negate_fusion), kind=kOutput, calls=%fused_computation.1 | convolution fusion | flops 270794752 | bytes 3407872 | tf_op jit(solution)/shard_map/dot_general | solution.py:167
  38.2 0.2 fusion.9
  38.5 0.1 fusion.11
  38.6 0.1 fusion.12
  38.7 1.1 %pad_maximum_fusion.8 = (bf16[4,1,64,512]{3,2,1,0:T(8,128)(2,1)S(1)}, bf16[4,1,64,512]{3,2,1,0:T(8,128)(2,1)S(1)}) fusion(bf16[3,2,64,512]{3,2,1,0:T(8,128)(2,1)} %collective-permute-done.11, bf16[1,2,64,512]{3,2,1,0:T(8,128)(2,1)} %bitcast.47), kind=kLoop, calls=%fused_computation.54 | loop fusion | flops 262144 | bytes 1048576 | tf_op jit(solution)/shard_map/concatenate | solution.py:181
  39.9 0.5 fusion
  40.3 0.5 %convolution_add_fusion = f32[256,1024]{1,0:T(8,128)S(1)} fusion(f32[256,1024]{1,0:T(8,128)S(1)} %fusion, bf16[256,512]{1,0:T(8,128)(2,1)S(1)} %bitcast.111, bf16[512,512]{0,1:T(8,128)(2,1)S(1)} %bitcast.102, bf16[512,512]{0,1:T(8,128)(2,1)S(1)} %bitcast_negate_fusion), kind=kOutput, calls=%fused_computation | convolution fusion | flops 270794752 | bytes 3407872 | tf_op jit(solution)/shard_map/dot_general | solution.py:167
  40.8 0.2 fusion.5
  41.1 1.3 %collective-permute-start.12 = (f32[2,1,512]{2,1,0:T(1,128)S(1)}, f32[2,1,512]{2,1,0:T(1,128)S(1)}, u32[]{:S(2)}, u32[]{:S(2)}) collective-permute-start(f32[2,1,512]{2,1,0:T(1,128)S(1)} %pad_maximum_fusion.10), channel_id=1, source_target_pairs={{0,24},{8,0},{16,8},{24,16},{1,25},{9,1},{17,9},{25,17},{2,26},{10... | collective-permute-start | bytes 12296 | tf_op jit(solution)/shard_map/ppermute | solution.py:15
  42.4 0.5 %collective-permute-start.13 = (f32[2,1,512]{2,1,0:T(1,128)S(1)}, f32[2,1,512]{2,1,0:T(1,128)S(1)}, u32[]{:S(2)}, u32[]{:S(2)}) collective-permute-start(f32[2,1,512]{2,1,0:T(1,128)S(1)} %pad_maximum_fusion.10), channel_id=1, source_target_pairs={{0,16},{8,24},{16,0},{24,8},{1,17},{9,25},{17,1},{25,9},{2,18},{10... | collective-permute-start | bytes 12296 | tf_op jit(solution)/shard_map/ppermute | solution.py:15
  43.0 0.8 %collective-permute-done.12 = f32[2,1,512]{2,1,0:T(1,128)S(1)} collective-permute-done((f32[2,1,512]{2,1,0:T(1,128)S(1)}, f32[2,1,512]{2,1,0:T(1,128)S(1)}, u32[]{:S(2)}, u32[]{:S(2)}) %collective-permute-start.12) | collective-permute-done | bytes 4128 | tf_op jit(solution)/shard_map/ppermute | solution.py:15
  43.7 2.3 %collective-permute-done.13 = f32[2,1,512]{2,1,0:T(1,128)S(1)} collective-permute-done((f32[2,1,512]{2,1,0:T(1,128)S(1)}, f32[2,1,512]{2,1,0:T(1,128)S(1)}, u32[]{:S(2)}, u32[]{:S(2)}) %collective-permute-start.13) | collective-permute-done | bytes 4128 | tf_op jit(solution)/shard_map/ppermute | solution.py:15
  46.1 0.6 %fusion.23 = f32[2,1,512]{2,1,0:T(1,128)} fusion(f32[8,2,1,512]{3,2,1,0:T(1,128)S(1)} %constant_dynamic-update-slice_fusion, s32[]{:T(128)S(6)} %add.214, s32[]{:T(128)S(6)} %add.213, s32[]{:T(128)S(6)} %add.212, s32[]{:T(128)S(6)} %select_n.159), kind=kLoop, calls=%fused_computation.91 | loop fusion | flops 3072 | bytes 20496 | tf_op jit(solution)/shard_map/add | solution.py:96
  (39 shorter events, 0.4 us)
Async XLA Ops:
  0.0 18.6 %copy-start.2 = (f32[1,2,64]{2,1,0:T(2,128)S(1)}, f32[1,2,64]{2,1,0:T(2,128)}, u32[]{:S(2)}) copy-start(f32[1,2,64]{2,1,0:T(2,128)} %param.10) | copy-start | bytes 1540
  0.0 18.7 %copy-start.1 = (s32[1,512]{1,0:T(1,128)S(1)}, s32[1,512]{1,0:T(1,128)}, u32[]{:S(2)}) copy-start(s32[1,512]{1,0:T(1,128)} %param.8) | copy-start | bytes 6148
  1.5 6.9 %collective-permute-start.1 = (f32[2,64,128]{2,0,1:T(2,128)S(1)}, f32[2,64,128]{2,0,1:T(2,128)S(1)}, u32[]{:S(2)}, u32[]{:S(2)}) collective-permute-start(f32[2,64,128]{2,0,1:T(2,128)S(1)} %get-tuple-element.39), channel_id=1, source_target_pairs={{0,4},{1,5},{2,6},{3,7},{4,0},{5,1},{6,2},{7,3},{8,12},{9,13},{10,... | collective-permute-start | bytes 196616 | tf_op jit(solution)/shard_map/ppermute | solution.py:133
  1.6 14.6 %collective-permute-start.2 = (f32[2,64,128]{2,0,1:T(2,128)S(1)}, f32[2,64,128]{2,0,1:T(2,128)S(1)}, u32[]{:S(2)}, u32[]{:S(2)}) collective-permute-start(f32[2,64,128]{2,0,1:T(2,128)S(1)} %get-tuple-element.38), channel_id=1, source_target_pairs={{0,2},{1,3},{2,4},{3,5},{4,6},{5,7},{6,0},{7,1},{8,10},{9,11},{10,... | collective-permute-start | bytes 196616 | tf_op jit(solution)/shard_map/ppermute | solution.py:133
  3.5 14.2 %collective-permute-start = (f32[2,64,128]{2,0,1:T(2,128)S(1)}, f32[2,64,128]{2,0,1:T(2,128)S(1)}, u32[]{:S(2)}, u32[]{:S(2)}) collective-permute-start(f32[2,64,128]{2,0,1:T(2,128)S(1)} %get-tuple-element.37), channel_id=1, source_target_pairs={{0,6},{1,7},{2,0},{3,1},{4,2},{5,3},{6,4},{7,5},{8,14},{9,15},{10,... | collective-permute-start | bytes 196616 | tf_op jit(solution)/shard_map/ppermute | solution.py:133
  4.6 20.9 %collective-permute-start.7 = (bf16[2,64,512]{2,1,0:T(8,128)(2,1)}, bf16[2,64,512]{2,1,0:T(8,128)(2,1)S(1)}, u32[]{:S(2)}, u32[]{:S(2)}) collective-permute-start(bf16[2,64,512]{2,1,0:T(8,128)(2,1)} %bitcast.126), channel_id=1, source_target_pairs={{0,6},{1,7},{2,0},{3,1},{4,2},{5,3},{6,4},{7,5},{8,14},{9,15},{10,... | collective-permute-start | bytes 393224 | tf_op jit(solution)/shard_map/ppermute | solution.py:123
  6.6 18.9 %collective-permute-start.8 = (bf16[2,64,512]{2,1,0:T(8,128)(2,1)}, bf16[2,64,512]{2,1,0:T(8,128)(2,1)S(1)}, u32[]{:S(2)}, u32[]{:S(2)}) collective-permute-start(bf16[2,64,512]{2,1,0:T(8,128)(2,1)} %bitcast.127), channel_id=1, source_target_pairs={{0,4},{1,5},{2,6},{3,7},{4,0},{5,1},{6,2},{7,3},{8,12},{9,13},{10,... | collective-permute-start | bytes 393224 | tf_op jit(solution)/shard_map/ppermute | solution.py:123
  8.3 17.2 %collective-permute-start.9 = (bf16[2,64,512]{2,1,0:T(8,128)(2,1)}, bf16[2,64,512]{2,1,0:T(8,128)(2,1)S(1)}, u32[]{:S(2)}, u32[]{:S(2)}) collective-permute-start(bf16[2,64,512]{2,1,0:T(8,128)(2,1)} %bitcast.128), channel_id=1, source_target_pairs={{0,2},{1,3},{2,4},{3,5},{4,6},{5,7},{6,0},{7,1},{8,10},{9,11},{10,... | collective-permute-start | bytes 393224 | tf_op jit(solution)/shard_map/ppermute | solution.py:123
  16.2 22.5 %collective-permute-start.10 = (bf16[2,64,512]{2,1,0:T(8,128)(2,1)}, bf16[2,64,512]{2,1,0:T(8,128)(2,1)}, u32[]{:S(2)}, u32[]{:S(2)}) collective-permute-start(bf16[2,64,512]{2,1,0:T(8,128)(2,1)} %bitcast.129), channel_id=1, source_target_pairs={{0,1},{1,0},{2,3},{3,2},{4,5},{5,4},{6,7},{7,6},{8,9},{9,8},{10,11... | collective-permute-start | bytes 393224 | tf_op jit(solution)/shard_map/ppermute | solution.py:124
  18.1 5.0 %collective-permute-start.3 = (f32[4,64,1,128]{3,1,0,2:T(8,128)S(1)}, f32[4,64,1,128]{3,1,0,2:T(8,128)S(1)}, u32[]{:S(2)}, u32[]{:S(2)}) collective-permute-start(f32[4,64,1,128]{3,1,0,2:T(8,128)S(1)} %bitcast.125), channel_id=1, source_target_pairs={{0,1},{1,0},{2,3},{3,2},{4,5},{5,4},{6,7},{7,6},{8,9},{9,8},{10,11... | collective-permute-start | bytes 393224 | tf_op jit(solution)/shard_map/ppermute | solution.py:136
  18.6 8.3 %copy-start = (bf16[1,2,64,512]{3,2,1,0:T(8,128)(2,1)S(1)}, bf16[1,2,64,512]{3,2,1,0:T(8,128)(2,1)}, u32[]{:S(2)}) copy-start(bf16[1,2,64,512]{3,2,1,0:T(8,128)(2,1)} %param.11) | copy-start | bytes 393220
  23.2 6.4 %collective-permute-start.4 = (f32[512,1,128]{2,0,1:T(8,128)S(1)}, f32[512,1,128]{2,0,1:T(8,128)S(1)}, u32[]{:S(2)}, u32[]{:S(2)}) collective-permute-start(f32[512,1,128]{2,0,1:T(8,128)S(1)} %bitcast.105), channel_id=1, source_target_pairs={{0,16},{8,24},{16,0},{24,8},{1,17},{9,25},{17,1},{25,9},{2,18},{10... | collective-permute-start | bytes 786440 | tf_op jit(solution)/shard_map/ppermute | solution.py:68
  25.6 13.2 %collective-permute-start.11 = (bf16[3,2,64,512]{3,2,1,0:T(8,128)(2,1)S(1)}, bf16[3,2,64,512]{3,2,1,0:T(8,128)(2,1)}, u32[]{:S(2)}, u32[]{:S(2)}) collective-permute-start(bf16[3,2,64,512]{3,2,1,0:T(8,128)(2,1)S(1)} %pad_maximum_fusion.7), channel_id=1, source_target_pairs={{0,1},{1,0},{2,3},{3,2},{4,5},{5,4},{6,7},{7,6},{8,9},{9,8},{10,11... | collective-permute-start | bytes 1179656 | tf_op jit(solution)/shard_map/ppermute | solution.py:155
  27.0 2.7 %collective-permute-start.5 = (f32[512,1,128]{2,0,1:T(8,128)S(1)}, f32[512,1,128]{2,0,1:T(8,128)S(1)}, u32[]{:S(2)}, u32[]{:S(2)}) collective-permute-start(f32[512,1,128]{2,0,1:T(8,128)S(1)} %bitcast.106), channel_id=1, source_target_pairs={{0,8},{8,0},{16,24},{24,16},{1,9},{9,1},{17,25},{25,17},{2,10},{10... | collective-permute-start | bytes 786440 | tf_op jit(solution)/shard_map/ppermute | solution.py:70
  29.7 1.5 %collective-permute-start.6 = (f32[512,1,128]{2,0,1:T(8,128)S(1)}, f32[512,1,128]{2,0,1:T(8,128)S(1)}, u32[]{:S(2)}, u32[]{:S(2)}) collective-permute-start(f32[512,1,128]{2,0,1:T(8,128)S(1)} %collective-permute-done.4), channel_id=1, source_target_pairs={{0,8},{8,0},{16,24},{24,16},{1,9},{9,1},{17,25},{25,17},{2,10},{10... | collective-permute-start | bytes 786440 | tf_op jit(solution)/shard_map/ppermute | solution.py:70
  41.1 2.6 %collective-permute-start.12 = (f32[2,1,512]{2,1,0:T(1,128)S(1)}, f32[2,1,512]{2,1,0:T(1,128)S(1)}, u32[]{:S(2)}, u32[]{:S(2)}) collective-permute-start(f32[2,1,512]{2,1,0:T(1,128)S(1)} %pad_maximum_fusion.10), channel_id=1, source_target_pairs={{0,24},{8,0},{16,8},{24,16},{1,25},{9,1},{17,9},{25,17},{2,26},{10... | collective-permute-start | bytes 12296 | tf_op jit(solution)/shard_map/ppermute | solution.py:15
  42.4 3.6 %collective-permute-start.13 = (f32[2,1,512]{2,1,0:T(1,128)S(1)}, f32[2,1,512]{2,1,0:T(1,128)S(1)}, u32[]{:S(2)}, u32[]{:S(2)}) collective-permute-start(f32[2,1,512]{2,1,0:T(1,128)S(1)} %pad_maximum_fusion.10), channel_id=1, source_target_pairs={{0,16},{8,24},{16,0},{24,8},{1,17},{9,25},{17,1},{25,9},{2,18},{10... | collective-permute-start | bytes 12296 | tf_op jit(solution)/shard_map/ppermute | solution.py:15
  43.0 3.1 %collective-permute-start.14 = (f32[2,1,512]{2,1,0:T(1,128)S(1)}, f32[2,1,512]{2,1,0:T(1,128)S(1)}, u32[]{:S(2)}, u32[]{:S(2)}) collective-permute-start(f32[2,1,512]{2,1,0:T(1,128)S(1)} %pad_maximum_fusion.10), channel_id=1, source_target_pairs={{0,8},{8,16},{16,24},{24,0},{1,9},{9,17},{17,25},{25,1},{2,10},{10... | collective-permute-start | bytes 12296 | tf_op jit(solution)/shard_map/ppermute | solution.py:15

commit v16 on v10

--- a/solution.py
+++ b/solution.py
@@ -121,7 +121,6 @@
     for s in range(1, positions):
         pairs = [(p * 2 + r, ((p - s) % positions) * 2 + r) for p in range(positions) for r in range(2)]
         cap_row.append(lax.ppermute(capture[0], "tile", pairs))
-    own_swapped = lax.ppermute(capture[0], "tile", swap)
 
     per_tile = travel_time.shape[1] // tiles
     pieces = [lax.dynamic_slice_in_dim(travel_time, 2 * z * per_tile, 2 * per_tile, 1)]
@@ -135,6 +134,8 @@
     theirs_tt = lax.ppermute(
         lax.dynamic_slice_in_dim(pieces, (1 - y) * per_tile, per_tile, 2), "tile", [(j, j ^ 1) for j in range(tiles)]
     )
+    cap_own, theirs_tt = lax.optimization_barrier((capture[0], theirs_tt))
+    own_swapped = lax.ppermute(cap_own, "tile", swap)
     both_tt = jnp.stack([mine_tt, theirs_tt], axis=1)
     both_tt = jnp.roll(jnp.roll(both_tt, z, axis=0), y, axis=1)
     regrouped = both_tt.reshape((-1,) + both_tt.shape[3:])

time: 45.9 us -> 46.2 us (level)
    ppermute x3, waiting for transfers between devices: 5.63 us -> 7.15 us  [body(): pieces.append(lax.ppermute(sent, 'tile', pairs))]
    ppermute x2, waiting for transfers between devices: 1.44 us -> 0.01 us  [gather_columns(): partner = [lax.ppermute(piece, axis_name, swap) for piece in same_core]]
  transfers between devices with their start and end apart: 15 -> 15, of which waited for: 6 -> 5; matrix products, arithmetic and copies ran while one was open for 19% -> 19% of each run, Pallas kernels for 0% -> 0%
where the time goes in v16:
time: 46.2 us; the launch traced here: 46 us
  starting transfers between devices  16.7 us (36%)
  waiting for transfers between devices  15 us (32%)
  other arithmetic  7.94 us (17%)
  local copies, waits for them, and re-layouts  3.42 us (7%)
  matrix products  1.86 us (4%)
  between operations  1.04 us (2%)
    ppermute x3, waiting for transfers between devices, body(): pieces.append(lax.ppermute(sent, 'tile', pairs))  7.15 us
    ppermute x3, starting transfers between devices, body(): cap_row.append(lax.ppermute(capture[0], 'tile', pairs))  4.39 us
    ppermute x3, starting transfers between devices, body(): pieces.append(lax.ppermute(sent, 'tile', pairs))  3.99 us
    another operation x1, other arithmetic  3.84 us
    ppermute x1, waiting for transfers between devices, body(): lax.ppermute(lax.dynamic_slice_in_dim(pieces, (1 - y) * per_tile, per_til...  3.33 us
    ppermute x3, waiting for transfers between devices, gather_shifted(): pieces.append(lax.ppermute(block, axis_name, pairs))  3.07 us
    ppermute x3, starting transfers between devices, gather_shifted(): pieces.append(lax.ppermute(block, axis_name, pairs))  1.91 us
    ppermute x1, starting transfers between devices, body(): lax.ppermute(lax.dynamic_slice_in_dim(pieces, (1 - y) * per_tile, per_til...  1.58 us
  transfers between devices with their start and end apart: 15, of which 5 were waited for; matrix products, arithmetic and copies ran while one was open for 19% of the time, Pallas kernels for 0%

profile of v16, /device:TPU:16, one launch (start us, length us, event | category | flops | bytes accessed | tf_op | source)
XLA Modules:
  0.0 46.0 jit_solution(15957549835801529448)
XLA Ops:
  0.0 1.5 %constant_dynamic-slice_fusion.14 = (f32[64,2,128]{2,1,0:T(2,128)S(1)}, f32[64,2,128]{2,1,0:T(2,128)S(1)}, f32[64,2,128]{2,1,0:T(2,128)S(1)}, f32[64,2,128]{2,1,0:T(2,128)S(1)}) fusion(f32[64,8,128]{2,1,0:T(8,128)} %param.7, s32[]{:T(128)S(6)} %select_n.138, s32[]{:T(128)S(6)} %select_n.142, s32[]{:T(128)S(6)} %select_n.140, s32[]{:T(128)S(6)} %select_n.144), kind=kLoop, calls=%fused_computation.87 | loop fusion | bytes 524304 | tf_op jit(solution)/shard_map/dynamic_slice | solution.py:126
  1.5 0.5 %collective-permute-start = (f32[64,2,128]{2,0,1:T(8,128)S(1)}, f32[64,2,128]{2,0,1:T(8,128)S(1)}, u32[]{:S(2)}, u32[]{:S(2)}) collective-permute-start(f32[64,2,128]{2,0,1:T(8,128)S(1)} %copy.28), channel_id=1, source_target_pairs={{0,6},{1,7},{2,0},{3,1},{4,2},{5,3},{6,4},{7,5},{8,14},{9,15},{10,... | collective-permute-start | bytes 196616 | tf_op jit(solution)/shard_map/ppermute | solution.py:131
  2.0 3.5 %collective-permute-start.1 = (f32[64,2,128]{2,0,1:T(8,128)S(1)}, f32[64,2,128]{2,0,1:T(8,128)S(1)}, u32[]{:S(2)}, u32[]{:S(2)}) collective-permute-start(f32[64,2,128]{2,0,1:T(8,128)S(1)} %copy.29), channel_id=1, source_target_pairs={{0,4},{1,5},{2,6},{3,7},{4,0},{5,1},{6,2},{7,3},{8,12},{9,13},{10,... | collective-permute-start | bytes 196616 | tf_op jit(solution)/shard_map/ppermute | solution.py:131
  5.5 0.0 collective-permute-start.2
  5.5 2.0 %collective-permute-start.7 = (bf16[2,64,512]{2,1,0:T(8,128)(2,1)}, bf16[2,64,512]{2,1,0:T(8,128)(2,1)S(1)}, u32[]{:S(2)}, u32[]{:S(2)}) collective-permute-start(bf16[2,64,512]{2,1,0:T(8,128)(2,1)} %bitcast.10), channel_id=1, source_target_pairs={{0,6},{1,7},{2,0},{3,1},{4,2},{5,3},{6,4},{7,5},{8,14},{9,15},{10,... | collective-permute-start | bytes 393224 | tf_op jit(solution)/shard_map/ppermute | solution.py:123
  7.5 1.9 %collective-permute-start.8 = (bf16[2,64,512]{2,1,0:T(8,128)(2,1)}, bf16[2,64,512]{2,1,0:T(8,128)(2,1)S(1)}, u32[]{:S(2)}, u32[]{:S(2)}) collective-permute-start(bf16[2,64,512]{2,1,0:T(8,128)(2,1)} %bitcast.10), channel_id=1, source_target_pairs={{0,4},{1,5},{2,6},{3,7},{4,0},{5,1},{6,2},{7,3},{8,12},{9,13},{10,... | collective-permute-start | bytes 393224 | tf_op jit(solution)/shard_map/ppermute | solution.py:123
  9.4 0.5 %collective-permute-start.9 = (bf16[2,64,512]{2,1,0:T(8,128)(2,1)}, bf16[2,64,512]{2,1,0:T(8,128)(2,1)S(1)}, u32[]{:S(2)}, u32[]{:S(2)}) collective-permute-start(bf16[2,64,512]{2,1,0:T(8,128)(2,1)} %bitcast.10), channel_id=1, source_target_pairs={{0,2},{1,3},{2,4},{3,5},{4,6},{5,7},{6,0},{7,1},{8,10},{9,11},{10,... | collective-permute-start | bytes 393224 | tf_op jit(solution)/shard_map/ppermute | solution.py:123
  9.9 7.1 %collective-permute-done.2 = f32[64,2,128]{2,0,1:T(8,128)S(1)} collective-permute-done((f32[64,2,128]{2,0,1:T(8,128)S(1)}, f32[64,2,128]{2,0,1:T(8,128)S(1)}, u32[]{:S(2)}, u32[]{:S(2)}) %collective-permute-start.2) | collective-permute-done | bytes 65568 | tf_op jit(solution)/shard_map/ppermute | solution.py:131
  17.1 1.6 %collective-permute-start.3 = (f32[4,64,1,128]{3,1,0,2:T(8,128)S(1)}, f32[4,64,1,128]{3,1,0,2:T(8,128)S(1)}, u32[]{:S(2)}, u32[]{:S(2)}) collective-permute-start(f32[4,64,1,128]{3,1,0,2:T(8,128)S(1)} %get-tuple-element.38), channel_id=1, source_target_pairs={{0,1},{1,0},{2,3},{3,2},{4,5},{5,4},{6,7},{7,6},{8,9},{9,8},{10,11... | collective-permute-start | bytes 393224 | tf_op jit(solution)/shard_map/ppermute | solution.py:134
  18.7 0.1 select_reduce_fusion.1
  18.8 3.3 %collective-permute-done.3 = f32[4,64,1,128]{3,1,0,2:T(8,128)S(1)} collective-permute-done((f32[4,64,1,128]{3,1,0,2:T(8,128)S(1)}, f32[4,64,1,128]{3,1,0,2:T(8,128)S(1)}, u32[]{:S(2)}, u32[]{:S(2)}) %collective-permute-start.3) | collective-permute-done | bytes 131104 | tf_op jit(solution)/shard_map/ppermute | solution.py:134
  22.1 0.1 fusion.17
  22.2 0.1 fusion.15
  22.3 1.6 %collective-permute-start.4 = (f32[512,1,128]{2,0,1:T(8,128)S(1)}, f32[512,1,128]{2,0,1:T(8,128)S(1)}, u32[]{:S(2)}, u32[]{:S(2)}) collective-permute-start(f32[512,1,128]{2,0,1:T(8,128)S(1)} %bitcast.98), channel_id=1, source_target_pairs={{0,16},{8,24},{16,0},{24,8},{1,17},{9,25},{17,1},{25,9},{2,18},{10... | collective-permute-start | bytes 786440 | tf_op jit(solution)/shard_map/ppermute | solution.py:68
  24.5 0.0 collective-permute-done.9
  24.6 1.6 %collective-permute-start.11 = (bf16[3,2,64,512]{3,2,1,0:T(8,128)(2,1)S(1)}, bf16[3,2,64,512]{3,2,1,0:T(8,128)(2,1)}, u32[]{:S(2)}, u32[]{:S(2)}) collective-permute-start(bf16[3,2,64,512]{3,2,1,0:T(8,128)(2,1)S(1)} %pad_maximum_fusion.7), channel_id=1, source_target_pairs={{0,1},{1,0},{2,3},{3,2},{4,5},{5,4},{6,7},{7,6},{8,9},{9,8},{10,11... | collective-permute-start | bytes 1179656 | tf_op jit(solution)/shard_map/ppermute | solution.py:155
  26.2 1.0 %pad_maximum_fusion.6 = bf16[4,2,64,512]{3,2,1,0:T(8,128)(2,1)S(1)} fusion(bf16[1,2,64,512]{3,2,1,0:T(8,128)(2,1)S(1)} %bitcast.110, bf16[1,2,64,512]{3,2,1,0:T(8,128)(2,1)S(1)} %bitcast.108, bf16[1,2,64,512]{3,2,1,0:T(8,128)(2,1)S(1)} %bitcast.106, bf16[1,2,64,512]{3,2,1,0:T(8,128)(2,1)} %param.11), kind=kLoop, calls=%fused_computation.35 | loop fusion | flops 786432 | bytes 1048576 | tf_op jit(solution)/shard_map/stack | solution.py:156
  27.1 0.1 collective-permute-start.5
  27.2 1.5 %collective-permute-done.4 = f32[512,1,128]{2,0,1:T(8,128)S(1)} collective-permute-done((f32[512,1,128]{2,0,1:T(8,128)S(1)}, f32[512,1,128]{2,0,1:T(8,128)S(1)}, u32[]{:S(2)}, u32[]{:S(2)}) %collective-permute-start.4) | collective-permute-done | bytes 262176 | tf_op jit(solution)/shard_map/ppermute | solution.py:68
  28.7 0.0 collective-permute-start.6
  28.7 1.6 %collective-permute-start.10 = (bf16[2,64,512]{2,1,0:T(8,128)(2,1)}, bf16[2,64,512]{2,1,0:T(8,128)(2,1)}, u32[]{:S(2)}, u32[]{:S(2)}) collective-permute-start(bf16[2,64,512]{2,1,0:T(8,128)(2,1)} %bitcast.10), channel_id=1, source_target_pairs={{0,1},{1,0},{2,3},{3,2},{4,5},{5,4},{6,7},{7,6},{8,9},{9,8},{10,11... | collective-permute-start | bytes 393224 | tf_op jit(solution)/shard_map/ppermute | solution.py:138
  30.4 0.0 collective-permute-done.6
  30.4 3.8 %cosine_convert_fusion = (bf16[2,2,512,1,128]{4,2,0,3,1:T(8,128)(2,1)S(1)}, bf16[2,2,512,1,128]{4,2,0,3,1:T(8,128)(2,1)S(1)}) fusion(f32[2,1,512,1,128]{4,2,0,3,1:T(8,128)S(1)} %maximum_bitcast_fusion.1, f32[2,1,512,1,128]{4,2,0,3,1:T(8,128)S(1)} %maximum_bitcast_fusion, f32[]{:T(128)} %bitcast.4), kind=kLoop, calls=%fused_computation.6 | loop fusion | flops 1310720 | bytes 2097156 | tf_op jit(solution)/shard_map/convert.5
  34.3 0.4 copy.23
  34.7 0.2 copy.24
  35.0 0.4 copy.27
  35.4 0.2 copy.26
  35.6 0.2 convert_element_type.44
  35.8 0.2 convert_element_type.49
  36.0 0.1 dynamic-slice_bitcast_fusion
  36.2 0.1 fusion.14
  36.3 0.1 fusion.13
  36.4 0.1 bitcast_negate_fusion
  36.5 0.5 %fusion.1 = f32[256,1024]{1,0:T(8,128)S(1)} fusion(bf16[256,512]{1,0:T(8,128)(2,1)S(1)} %bitcast.112, bf16[512,512]{0,1:T(8,128)(2,1)S(1)} %bitcast.96, bf16[512,512]{0,1:T(8,128)(2,1)S(1)} %bitcast.92), kind=kOutput, calls=%fused_computation.8 | convolution fusion | flops 270532608 | bytes 2359296 | tf_op jit(solution)/shard_map/dot_general | solution.py:167
  36.9 0.5 %convolution_add_fusion.1 = f32[256,1024]{1,0:T(8,128)S(1)} fusion(f32[256,1024]{1,0:T(8,128)S(1)} %fusion.1, bf16[256,512]{1,0:T(8,128)(2,1)S(1)} %bitcast.103, bf16[512,512]{0,1:T(8,128)(2,1)S(1)} %bitcast.93, bf16[512,512]{0,1:T(8,128)(2,1)S(1)} %bitcast_negate_fusion), kind=kOutput, calls=%fused_computation.1 | convolution fusion | flops 270794752 | bytes 3407872 | tf_op jit(solution)/shard_map/dot_general | solution.py:167
  37.4 0.2 fusion.9
  37.7 0.1 fusion.11
  37.8 0.1 fusion.12
  37.9 0.0 collective-permute-done.10
  37.9 1.1 %pad_maximum_fusion.8 = (bf16[4,1,64,512]{3,2,1,0:T(8,128)(2,1)S(1)}, bf16[4,1,64,512]{3,2,1,0:T(8,128)(2,1)S(1)}) fusion(bf16[3,2,64,512]{3,2,1,0:T(8,128)(2,1)} %collective-permute-done.11, bf16[1,2,64,512]{3,2,1,0:T(8,128)(2,1)} %bitcast.42), kind=kLoop, calls=%fused_computation.54 | loop fusion | flops 262144 | bytes 1048576 | tf_op jit(solution)/shard_map/concatenate | solution.py:181
  39.0 0.5 %fusion = f32[256,1024]{1,0:T(8,128)S(1)} fusion(bf16[256,512]{1,0:T(8,128)(2,1)S(1)} %bitcast.115, bf16[512,512]{0,1:T(8,128)(2,1)S(1)} %bitcast.97, bf16[512,512]{0,1:T(8,128)(2,1)S(1)} %bitcast.94), kind=kOutput, calls=%fused_computation.7 | convolution fusion | flops 270532608 | bytes 2359296 | tf_op jit(solution)/shard_map/dot_general | solution.py:167
  39.5 0.5 %convolution_add_fusion = f32[256,1024]{1,0:T(8,128)S(1)} fusion(f32[256,1024]{1,0:T(8,128)S(1)} %fusion, bf16[256,512]{1,0:T(8,128)(2,1)S(1)} %bitcast.104, bf16[512,512]{0,1:T(8,128)(2,1)S(1)} %bitcast.95, bf16[512,512]{0,1:T(8,128)(2,1)S(1)} %bitcast_negate_fusion), kind=kOutput, calls=%fused_computation | convolution fusion | flops 270794752 | bytes 3407872 | tf_op jit(solution)/shard_map/dot_general | solution.py:167
  40.0 0.2 fusion.5
  40.3 1.4 %collective-permute-start.12 = (f32[2,1,512]{2,1,0:T(1,128)S(1)}, f32[2,1,512]{2,1,0:T(1,128)S(1)}, u32[]{:S(2)}, u32[]{:S(2)}) collective-permute-start(f32[2,1,512]{2,1,0:T(1,128)S(1)} %pad_maximum_fusion.10), channel_id=1, source_target_pairs={{0,24},{8,0},{16,8},{24,16},{1,25},{9,1},{17,9},{25,17},{2,26},{10... | collective-permute-start | bytes 12296 | tf_op jit(solution)/shard_map/ppermute | solution.py:15
  41.7 0.5 %collective-permute-start.13 = (f32[2,1,512]{2,1,0:T(1,128)S(1)}, f32[2,1,512]{2,1,0:T(1,128)S(1)}, u32[]{:S(2)}, u32[]{:S(2)}) collective-permute-start(f32[2,1,512]{2,1,0:T(1,128)S(1)} %pad_maximum_fusion.10), channel_id=1, source_target_pairs={{0,16},{8,24},{16,0},{24,8},{1,17},{9,25},{17,1},{25,9},{2,18},{10... | collective-permute-start | bytes 12296 | tf_op jit(solution)/shard_map/ppermute | solution.py:15
  42.2 0.8 %collective-permute-done.12 = f32[2,1,512]{2,1,0:T(1,128)S(1)} collective-permute-done((f32[2,1,512]{2,1,0:T(1,128)S(1)}, f32[2,1,512]{2,1,0:T(1,128)S(1)}, u32[]{:S(2)}, u32[]{:S(2)}) %collective-permute-start.12) | collective-permute-done | bytes 4128 | tf_op jit(solution)/shard_map/ppermute | solution.py:15
  43.0 2.3 %collective-permute-done.13 = f32[2,1,512]{2,1,0:T(1,128)S(1)} collective-permute-done((f32[2,1,512]{2,1,0:T(1,128)S(1)}, f32[2,1,512]{2,1,0:T(1,128)S(1)}, u32[]{:S(2)}, u32[]{:S(2)}) %collective-permute-start.13) | collective-permute-done | bytes 4128 | tf_op jit(solution)/shard_map/ppermute | solution.py:15
  45.4 0.6 %fusion.23 = f32[2,1,512]{2,1,0:T(1,128)} fusion(f32[8,2,1,512]{3,2,1,0:T(1,128)S(1)} %constant_dynamic-update-slice_fusion, s32[]{:T(128)S(6)} %add.214, s32[]{:T(128)S(6)} %add.213, s32[]{:T(128)S(6)} %add.212, s32[]{:T(128)S(6)} %select_n.159), kind=kLoop, calls=%fused_computation.92 | loop fusion | flops 3072 | bytes 20496 | tf_op jit(solution)/shard_map/add | solution.py:96
  (41 shorter events, 0.5 us)
Async XLA Ops:
  0.0 18.7 %copy-start.1 = (f32[1,2,64]{2,1,0:T(2,128)S(1)}, f32[1,2,64]{2,1,0:T(2,128)}, u32[]{:S(2)}) copy-start(f32[1,2,64]{2,1,0:T(2,128)} %param.10) | copy-start | bytes 1540
  0.0 18.7 %copy-start = (s32[1,512]{1,0:T(1,128)S(1)}, s32[1,512]{1,0:T(1,128)}, u32[]{:S(2)}) copy-start(s32[1,512]{1,0:T(1,128)} %param.8) | copy-start | bytes 6148
  1.5 7.9 %collective-permute-start = (f32[64,2,128]{2,0,1:T(8,128)S(1)}, f32[64,2,128]{2,0,1:T(8,128)S(1)}, u32[]{:S(2)}, u32[]{:S(2)}) collective-permute-start(f32[64,2,128]{2,0,1:T(8,128)S(1)} %copy.28), channel_id=1, source_target_pairs={{0,6},{1,7},{2,0},{3,1},{4,2},{5,3},{6,4},{7,5},{8,14},{9,15},{10,... | collective-permute-start | bytes 196616 | tf_op jit(solution)/shard_map/ppermute | solution.py:131
  2.0 7.9 %collective-permute-start.1 = (f32[64,2,128]{2,0,1:T(8,128)S(1)}, f32[64,2,128]{2,0,1:T(8,128)S(1)}, u32[]{:S(2)}, u32[]{:S(2)}) collective-permute-start(f32[64,2,128]{2,0,1:T(8,128)S(1)} %copy.29), channel_id=1, source_target_pairs={{0,4},{1,5},{2,6},{3,7},{4,0},{5,1},{6,2},{7,3},{8,12},{9,13},{10,... | collective-permute-start | bytes 196616 | tf_op jit(solution)/shard_map/ppermute | solution.py:131
  5.5 11.5 %collective-permute-start.2 = (f32[64,2,128]{2,0,1:T(8,128)S(1)}, f32[64,2,128]{2,0,1:T(8,128)S(1)}, u32[]{:S(2)}, u32[]{:S(2)}) collective-permute-start(f32[64,2,128]{2,0,1:T(8,128)S(1)} %copy.30), channel_id=1, source_target_pairs={{0,2},{1,3},{2,4},{3,5},{4,6},{5,7},{6,0},{7,1},{8,10},{9,11},{10,... | collective-permute-start | bytes 196616 | tf_op jit(solution)/shard_map/ppermute | solution.py:131
  5.5 19.0 %collective-permute-start.7 = (bf16[2,64,512]{2,1,0:T(8,128)(2,1)}, bf16[2,64,512]{2,1,0:T(8,128)(2,1)S(1)}, u32[]{:S(2)}, u32[]{:S(2)}) collective-permute-start(bf16[2,64,512]{2,1,0:T(8,128)(2,1)} %bitcast.10), channel_id=1, source_target_pairs={{0,6},{1,7},{2,0},{3,1},{4,2},{5,3},{6,4},{7,5},{8,14},{9,15},{10,... | collective-permute-start | bytes 393224 | tf_op jit(solution)/shard_map/ppermute | solution.py:123
  7.5 17.0 %collective-permute-start.8 = (bf16[2,64,512]{2,1,0:T(8,128)(2,1)}, bf16[2,64,512]{2,1,0:T(8,128)(2,1)S(1)}, u32[]{:S(2)}, u32[]{:S(2)}) collective-permute-start(bf16[2,64,512]{2,1,0:T(8,128)(2,1)} %bitcast.10), channel_id=1, source_target_pairs={{0,4},{1,5},{2,6},{3,7},{4,0},{5,1},{6,2},{7,3},{8,12},{9,13},{10,... | collective-permute-start | bytes 393224 | tf_op jit(solution)/shard_map/ppermute | solution.py:123
  9.4 15.1 %collective-permute-start.9 = (bf16[2,64,512]{2,1,0:T(8,128)(2,1)}, bf16[2,64,512]{2,1,0:T(8,128)(2,1)S(1)}, u32[]{:S(2)}, u32[]{:S(2)}) collective-permute-start(bf16[2,64,512]{2,1,0:T(8,128)(2,1)} %bitcast.10), channel_id=1, source_target_pairs={{0,2},{1,3},{2,4},{3,5},{4,6},{5,7},{6,0},{7,1},{8,10},{9,11},{10,... | collective-permute-start | bytes 393224 | tf_op jit(solution)/shard_map/ppermute | solution.py:123
  17.1 5.0 %collective-permute-start.3 = (f32[4,64,1,128]{3,1,0,2:T(8,128)S(1)}, f32[4,64,1,128]{3,1,0,2:T(8,128)S(1)}, u32[]{:S(2)}, u32[]{:S(2)}) collective-permute-start(f32[4,64,1,128]{3,1,0,2:T(8,128)S(1)} %get-tuple-element.38), channel_id=1, source_target_pairs={{0,1},{1,0},{2,3},{3,2},{4,5},{5,4},{6,7},{7,6},{8,9},{9,8},{10,11... | collective-permute-start | bytes 393224 | tf_op jit(solution)/shard_map/ppermute | solution.py:134
  22.3 6.4 %collective-permute-start.4 = (f32[512,1,128]{2,0,1:T(8,128)S(1)}, f32[512,1,128]{2,0,1:T(8,128)S(1)}, u32[]{:S(2)}, u32[]{:S(2)}) collective-permute-start(f32[512,1,128]{2,0,1:T(8,128)S(1)} %bitcast.98), channel_id=1, source_target_pairs={{0,16},{8,24},{16,0},{24,8},{1,17},{9,25},{17,1},{25,9},{2,18},{10... | collective-permute-start | bytes 786440 | tf_op jit(solution)/shard_map/ppermute | solution.py:68
  24.6 13.3 %collective-permute-start.11 = (bf16[3,2,64,512]{3,2,1,0:T(8,128)(2,1)S(1)}, bf16[3,2,64,512]{3,2,1,0:T(8,128)(2,1)}, u32[]{:S(2)}, u32[]{:S(2)}) collective-permute-start(bf16[3,2,64,512]{3,2,1,0:T(8,128)(2,1)S(1)} %pad_maximum_fusion.7), channel_id=1, source_target_pairs={{0,1},{1,0},{2,3},{3,2},{4,5},{5,4},{6,7},{7,6},{8,9},{9,8},{10,11... | collective-permute-start | bytes 1179656 | tf_op jit(solution)/shard_map/ppermute | solution.py:155
  27.1 3.2 %collective-permute-start.5 = (f32[512,1,128]{2,0,1:T(8,128)S(1)}, f32[512,1,128]{2,0,1:T(8,128)S(1)}, u32[]{:S(2)}, u32[]{:S(2)}) collective-permute-start(f32[512,1,128]{2,0,1:T(8,128)S(1)} %bitcast.99), channel_id=1, source_target_pairs={{0,8},{8,0},{16,24},{24,16},{1,9},{9,1},{17,25},{25,17},{2,10},{10... | collective-permute-start | bytes 786440 | tf_op jit(solution)/shard_map/ppermute | solution.py:70
  28.7 1.7 %collective-permute-start.6 = (f32[512,1,128]{2,0,1:T(8,128)S(1)}, f32[512,1,128]{2,0,1:T(8,128)S(1)}, u32[]{:S(2)}, u32[]{:S(2)}) collective-permute-start(f32[512,1,128]{2,0,1:T(8,128)S(1)} %collective-permute-done.4), channel_id=1, source_target_pairs={{0,8},{8,0},{16,24},{24,16},{1,9},{9,1},{17,25},{25,17},{2,10},{10... | collective-permute-start | bytes 786440 | tf_op jit(solution)/shard_map/ppermute | solution.py:70
  28.7 9.2 %collective-permute-start.10 = (bf16[2,64,512]{2,1,0:T(8,128)(2,1)}, bf16[2,64,512]{2,1,0:T(8,128)(2,1)}, u32[]{:S(2)}, u32[]{:S(2)}) collective-permute-start(bf16[2,64,512]{2,1,0:T(8,128)(2,1)} %bitcast.10), channel_id=1, source_target_pairs={{0,1},{1,0},{2,3},{3,2},{4,5},{5,4},{6,7},{7,6},{8,9},{9,8},{10,11... | collective-permute-start | bytes 393224 | tf_op jit(solution)/shard_map/ppermute | solution.py:138
  40.3 2.7 %collective-permute-start.12 = (f32[2,1,512]{2,1,0:T(1,128)S(1)}, f32[2,1,512]{2,1,0:T(1,128)S(1)}, u32[]{:S(2)}, u32[]{:S(2)}) collective-permute-start(f32[2,1,512]{2,1,0:T(1,128)S(1)} %pad_maximum_fusion.10), channel_id=1, source_target_pairs={{0,24},{8,0},{16,8},{24,16},{1,25},{9,1},{17,9},{25,17},{2,26},{10... | collective-permute-start | bytes 12296 | tf_op jit(solution)/shard_map/ppermute | solution.py:15
  41.7 3.6 %collective-permute-start.13 = (f32[2,1,512]{2,1,0:T(1,128)S(1)}, f32[2,1,512]{2,1,0:T(1,128)S(1)}, u32[]{:S(2)}, u32[]{:S(2)}) collective-permute-start(f32[2,1,512]{2,1,0:T(1,128)S(1)} %pad_maximum_fusion.10), channel_id=1, source_target_pairs={{0,16},{8,24},{16,0},{24,8},{1,17},{9,25},{17,1},{25,9},{2,18},{10... | collective-permute-start | bytes 12296 | tf_op jit(solution)/shard_map/ppermute | solution.py:15
  42.2 3.1 %collective-permute-start.14 = (f32[2,1,512]{2,1,0:T(1,128)S(1)}, f32[2,1,512]{2,1,0:T(1,128)S(1)}, u32[]{:S(2)}, u32[]{:S(2)}) collective-permute-start(f32[2,1,512]{2,1,0:T(1,128)S(1)} %pad_maximum_fusion.10), channel_id=1, source_target_pairs={{0,8},{8,16},{16,24},{24,0},{1,9},{9,17},{17,25},{25,1},{2,10},{10... | collective-permute-start | bytes 12296 | tf_op jit(solution)/shard_map/ppermute | solution.py:15

commit v17 on v10

--- a/solution.py
+++ b/solution.py
@@ -135,10 +135,22 @@
     theirs_tt = lax.ppermute(
         lax.dynamic_slice_in_dim(pieces, (1 - y) * per_tile, per_tile, 2), "tile", [(j, j ^ 1) for j in range(tiles)]
     )
-    both_tt = jnp.stack([mine_tt, theirs_tt], axis=1)
-    both_tt = jnp.roll(jnp.roll(both_tt, z, axis=0), y, axis=1)
-    regrouped = both_tt.reshape((-1,) + both_tt.shape[3:])
-    view = gather_columns(regrouped, "freq", freqs)
+
+    def regroup(mine_part, their_part):
+        both = jnp.stack([mine_part, their_part], axis=1)
+        both = jnp.roll(jnp.roll(both, z, axis=0), y, axis=1)
+        return both.reshape((-1,) + both.shape[3:])
+
+    blocks = [regroup(mine_tt, theirs_tt)]
+    for so in range(1, freqs // 2):
+        straight = [(i, (i - 2 * so) % freqs) for i in range(freqs)]
+        blocks.append(
+            regroup(lax.ppermute(mine_tt, "freq", straight), lax.ppermute(theirs_tt, "freq", straight))
+        )
+    core_swap = [(i, i ^ 1) for i in range(freqs)]
+    partner = [lax.ppermute(piece, "freq", core_swap) for piece in blocks]
+    regrouped = blocks[0]
+    view = jnp.stack([jnp.stack(blocks), jnp.stack(partner)], axis=1)
     view = jnp.moveaxis(view.reshape((freqs,) + regrouped.shape), 0, 2)
     elements, row_count, _, width = view.shape
     voxels = row_count * freqs * width

time: 45.9 us -> 54 us (1.18)
  the two profiles are of different devices: /device:TPU:16 before, /device:TPU:0 now
where the time goes in v17:
time: 54 us; the launch traced here: 53.8 us
  starting transfers between devices  27.2 us (50%)
  waiting for transfers between devices  12 us (22%)
  other arithmetic  8.06 us (15%)
  local copies, waits for them, and re-layouts  3.44 us (6%)
  matrix products  1.86 us (3%)
  between operations  1.21 us (2%)
    ppermute x3, starting transfers between devices, body(): cap_row.append(lax.ppermute(capture[0], 'tile', pairs))  13.6 us
    ppermute x3, starting transfers between devices, body(): pieces.append(lax.ppermute(sent, 'tile', pairs))  5 us
    another operation x1, other arithmetic  3.84 us
    ppermute x1, waiting for transfers between devices, body(): lax.ppermute(theirs_tt, 'freq', straight)  3.26 us
    ppermute x1, waiting for transfers between devices, body(): lax.ppermute(lax.dynamic_slice_in_dim(pieces, (1 - y) * per_tile, per_til...  3.19 us
    ppermute x3, waiting for transfers between devices, gather_shifted(): pieces.append(lax.ppermute(block, axis_name, pairs))  3.07 us
    ppermute x3, starting transfers between devices, gather_shifted(): pieces.append(lax.ppermute(block, axis_name, pairs))  1.82 us
    ppermute x1, starting transfers between devices, body(): other = (own_swapped, lax.ppermute(jnp.stack(row[1:]), 'tile', swap))  1.58 us
  transfers between devices with their start and end apart: 16, of which 7 were waited for; matrix products, arithmetic and copies ran while one was open for 19% of the time, Pallas kernels for 0%

profile of v17, /device:TPU:0, one launch (start us, length us, event | category | flops | bytes accessed | tf_op | source)
XLA Modules:
  0.0 53.8 jit_solution(15723216373544991015)
XLA Ops:
  0.0 5.0 %collective-permute-start.8 = (bf16[2,64,512]{2,1,0:T(8,128)(2,1)}, bf16[2,64,512]{2,1,0:T(8,128)(2,1)S(1)}, u32[]{:S(2)}, u32[]{:S(2)}) collective-permute-start(bf16[2,64,512]{2,1,0:T(8,128)(2,1)} %bitcast.25), channel_id=1, source_target_pairs={{0,6},{1,7},{2,0},{3,1},{4,2},{5,3},{6,4},{7,5},{8,14},{9,15},{10,... | collective-permute-start | bytes 393224 | tf_op jit(solution)/shard_map/ppermute | solution.py:123
  5.1 1.5 %constant_dynamic-slice_fusion.15 = (f32[64,2,128]{2,1,0:T(2,128)S(1)}, f32[64,2,128]{2,1,0:T(2,128)S(1)}, f32[64,2,128]{2,1,0:T(2,128)S(1)}, f32[64,2,128]{2,1,0:T(2,128)S(1)}) fusion(f32[64,8,128]{2,1,0:T(8,128)} %param.11, s32[]{:T(128)S(6)} %select_n.132, s32[]{:T(128)S(6)} %select_n.136, s32[]{:T(128)S(6)} %select_n.134, s32[]{:T(128)S(6)} %select_n.138), kind=kLoop, calls=%fused_computation.97 | loop fusion | bytes 524304 | tf_op jit(solution)/shard_map/dynamic_slice | solution.py:127
  6.5 0.5 collective-permute-start
  7.0 2.6 %collective-permute-start.1 = (f32[64,2,128]{2,0,1:T(8,128)S(1)}, f32[64,2,128]{2,0,1:T(8,128)S(1)}, u32[]{:S(2)}, u32[]{:S(2)}) collective-permute-start(f32[64,2,128]{2,0,1:T(8,128)S(1)} %copy.32), channel_id=1, source_target_pairs={{0,4},{1,5},{2,6},{3,7},{4,0},{5,1},{6,2},{7,3},{8,12},{9,13},{10,... | collective-permute-start | bytes 196616 | tf_op jit(solution)/shard_map/ppermute | solution.py:132
  9.6 1.9 %collective-permute-start.2 = (f32[64,2,128]{2,0,1:T(8,128)S(1)}, f32[64,2,128]{2,0,1:T(8,128)S(1)}, u32[]{:S(2)}, u32[]{:S(2)}) collective-permute-start(f32[64,2,128]{2,0,1:T(8,128)S(1)} %copy.33), channel_id=1, source_target_pairs={{0,2},{1,3},{2,4},{3,5},{4,6},{5,7},{6,0},{7,1},{8,10},{9,11},{10,... | collective-permute-start | bytes 196616 | tf_op jit(solution)/shard_map/ppermute | solution.py:132
  11.6 0.1 select_reduce_fusion.1
  12.5 0.9 %collective-permute-done = f32[64,2,128]{2,0,1:T(8,128)S(1)} collective-permute-done((f32[64,2,128]{2,0,1:T(8,128)S(1)}, f32[64,2,128]{2,0,1:T(8,128)S(1)}, u32[]{:S(2)}, u32[]{:S(2)}) %collective-permute-start) | collective-permute-done | bytes 65568 | tf_op jit(solution)/shard_map/ppermute | solution.py:132
  13.4 8.6 %collective-permute-start.10 = (bf16[2,64,512]{2,1,0:T(8,128)(2,1)}, bf16[2,64,512]{2,1,0:T(8,128)(2,1)S(1)}, u32[]{:S(2)}, u32[]{:S(2)}) collective-permute-start(bf16[2,64,512]{2,1,0:T(8,128)(2,1)} %bitcast.25), channel_id=1, source_target_pairs={{0,2},{1,3},{2,4},{3,5},{4,6},{5,7},{6,0},{7,1},{8,10},{9,11},{10,... | collective-permute-start | bytes 393224 | tf_op jit(solution)/shard_map/ppermute | solution.py:123
  21.9 0.1 collective-permute-done.1
  22.1 1.5 %collective-permute-start.11 = (bf16[2,64,512]{2,1,0:T(8,128)(2,1)}, bf16[2,64,512]{2,1,0:T(8,128)(2,1)}, u32[]{:S(2)}, u32[]{:S(2)}) collective-permute-start(bf16[2,64,512]{2,1,0:T(8,128)(2,1)} %bitcast.25), channel_id=1, source_target_pairs={{0,1},{1,0},{2,3},{3,2},{4,5},{5,4},{6,7},{7,6},{8,9},{9,8},{10,11... | collective-permute-start | bytes 393224 | tf_op jit(solution)/shard_map/ppermute | solution.py:124
  23.7 0.6 %collective-permute-start.3 = (f32[4,64,1,128]{3,1,0,2:T(8,128)S(1)}, f32[4,64,1,128]{3,1,0,2:T(8,128)S(1)}, u32[]{:S(2)}, u32[]{:S(2)}) collective-permute-start(f32[4,64,1,128]{3,1,0,2:T(8,128)S(1)} %get-tuple-element.36), channel_id=1, source_target_pairs={{0,1},{1,0},{2,3},{3,2},{4,5},{5,4},{6,7},{7,6},{8,9},{9,8},{10,11... | collective-permute-start | bytes 393224 | tf_op jit(solution)/shard_map/ppermute | solution.py:135
  24.2 1.5 %collective-permute-start.4 = (f32[4,64,1,128]{3,1,0,2:T(8,128)S(1)}, f32[4,64,1,128]{3,1,0,2:T(8,128)S(1)}, u32[]{:S(2)}, u32[]{:S(2)}) collective-permute-start(f32[4,64,1,128]{3,1,0,2:T(8,128)S(1)} %get-tuple-element.37), channel_id=1, source_target_pairs={{0,16},{8,24},{16,0},{24,8},{1,17},{9,25},{17,1},{25,9},{2,18},{10... | collective-permute-start | bytes 393224 | tf_op jit(solution)/shard_map/ppermute | solution.py:148
  25.8 1.6 %collective-permute-start.12 = (bf16[3,2,64,512]{3,2,1,0:T(8,128)(2,1)S(1)}, bf16[3,2,64,512]{3,2,1,0:T(8,128)(2,1)}, u32[]{:S(2)}, u32[]{:S(2)}) collective-permute-start(bf16[3,2,64,512]{3,2,1,0:T(8,128)(2,1)S(1)} %pad_maximum_fusion.7), channel_id=1, source_target_pairs={{0,1},{1,0},{2,3},{3,2},{4,5},{5,4},{6,7},{7,6},{8,9},{9,8},{10,11... | collective-permute-start | bytes 1179656 | tf_op jit(solution)/shard_map/ppermute | solution.py:166
  27.4 1.0 %pad_maximum_fusion.6 = bf16[4,2,64,512]{3,2,1,0:T(8,128)(2,1)S(1)} fusion(bf16[1,2,64,512]{3,2,1,0:T(8,128)(2,1)S(1)} %bitcast.114, bf16[1,2,64,512]{3,2,1,0:T(8,128)(2,1)S(1)} %bitcast.112, bf16[1,2,64,512]{3,2,1,0:T(8,128)(2,1)S(1)} %bitcast.110, bf16[1,2,64,512]{3,2,1,0:T(8,128)(2,1)} %param.15), kind=kLoop, calls=%fused_computation.41 | loop fusion | flops 786432 | bytes 1048576 | tf_op jit(solution)/shard_map/stack | solution.py:167
  28.4 3.2 %collective-permute-done.3 = f32[4,64,1,128]{3,1,0,2:T(8,128)S(1)} collective-permute-done((f32[4,64,1,128]{3,1,0,2:T(8,128)S(1)}, f32[4,64,1,128]{3,1,0,2:T(8,128)S(1)}, u32[]{:S(2)}, u32[]{:S(2)}) %collective-permute-start.3) | collective-permute-done | bytes 131104 | tf_op jit(solution)/shard_map/ppermute | solution.py:135
  31.5 1.5 %collective-permute-start.5 = (f32[4,64,1,128]{3,1,0,2:T(8,128)S(1)}, f32[4,64,1,128]{3,1,0,2:T(8,128)S(1)}, u32[]{:S(2)}, u32[]{:S(2)}) collective-permute-start(f32[4,64,1,128]{3,1,0,2:T(8,128)S(1)} %collective-permute-done.3), channel_id=1, source_target_pairs={{0,16},{8,24},{16,0},{24,8},{1,17},{9,25},{17,1},{25,9},{2,18},{10... | collective-permute-start | bytes 393224 | tf_op jit(solution)/shard_map/ppermute | solution.py:148
  33.1 0.1 fusion.19
  33.2 0.1 collective-permute-start.6
  33.3 3.3 %collective-permute-done.5 = f32[4,64,1,128]{3,1,0,2:T(8,128)S(1)} collective-permute-done((f32[4,64,1,128]{3,1,0,2:T(8,128)S(1)}, f32[4,64,1,128]{3,1,0,2:T(8,128)S(1)}, u32[]{:S(2)}, u32[]{:S(2)}) %collective-permute-start.5) | collective-permute-done | bytes 131104 | tf_op jit(solution)/shard_map/ppermute | solution.py:148
  36.5 0.1 fusion.17
  36.6 0.1 fusion.15
  36.7 0.1 collective-permute-start.7
  36.8 1.4 %collective-permute-done.7 = f32[512,1,128]{2,0,1:T(8,128)S(1)} collective-permute-done((f32[512,1,128]{2,0,1:T(8,128)S(1)}, f32[512,1,128]{2,0,1:T(8,128)S(1)}, u32[]{:S(2)}, u32[]{:S(2)}) %collective-permute-start.7) | collective-permute-done | bytes 262176 | tf_op jit(solution)/shard_map/ppermute | solution.py:151
  38.3 3.8 %cosine_convert_fusion = (bf16[2,2,512,1,128]{4,2,0,3,1:T(8,128)(2,1)S(1)}, bf16[2,2,512,1,128]{4,2,0,3,1:T(8,128)(2,1)S(1)}) fusion(f32[2,1,512,1,128]{4,2,0,3,1:T(8,128)S(1)} %maximum_bitcast_fusion.1, f32[2,1,512,1,128]{4,2,0,3,1:T(8,128)S(1)} %maximum_bitcast_fusion, f32[]{:T(128)} %bitcast.4), kind=kLoop, calls=%fused_computation.6 | loop fusion | flops 1310720 | bytes 2097156 | tf_op jit(solution)/shard_map/convert.5
  42.2 0.4 copy.26
  42.6 0.2 copy.27
  42.9 0.4 copy.30
  43.3 0.2 copy.29
  43.5 0.2 convert_element_type.44
  43.7 0.2 convert_element_type.49
  43.9 0.1 dynamic-slice_bitcast_fusion
  44.0 0.1 fusion.14
  44.2 0.1 fusion.13
  44.3 0.1 bitcast_negate_fusion
  44.4 0.5 fusion.1
  44.8 0.5 convolution_add_fusion.1
  45.3 0.2 fusion.9
  45.5 0.1 fusion.11
  45.7 0.1 fusion.12
  45.8 1.1 %pad_maximum_fusion.8 = (bf16[4,1,64,512]{3,2,1,0:T(8,128)(2,1)S(1)}, bf16[4,1,64,512]{3,2,1,0:T(8,128)(2,1)S(1)}) fusion(bf16[3,2,64,512]{3,2,1,0:T(8,128)(2,1)} %collective-permute-done.12, bf16[1,2,64,512]{3,2,1,0:T(8,128)(2,1)} %bitcast.45), kind=kLoop, calls=%fused_computation.64 | loop fusion | flops 262144 | bytes 1048576 | tf_op jit(solution)/shard_map/concatenate | solution.py:192
  46.9 0.5 fusion
  47.4 0.5 convolution_add_fusion
  47.9 0.2 fusion.3
  48.2 1.3 %collective-permute-start.13 = (f32[2,1,512]{2,1,0:T(1,128)S(1)}, f32[2,1,512]{2,1,0:T(1,128)S(1)}, u32[]{:S(2)}, u32[]{:S(2)}) collective-permute-start(f32[2,1,512]{2,1,0:T(1,128)S(1)} %pad_maximum_fusion.10), channel_id=1, source_target_pairs={{0,24},{8,0},{16,8},{24,16},{1,25},{9,1},{17,9},{25,17},{2,26},{10... | collective-permute-start | bytes 12296 | tf_op jit(solution)/shard_map/ppermute | solution.py:15
  49.5 0.5 collective-permute-start.14
  50.0 0.8 %collective-permute-done.13 = f32[2,1,512]{2,1,0:T(1,128)S(1)} collective-permute-done((f32[2,1,512]{2,1,0:T(1,128)S(1)}, f32[2,1,512]{2,1,0:T(1,128)S(1)}, u32[]{:S(2)}, u32[]{:S(2)}) %collective-permute-start.13) | collective-permute-done | bytes 4128 | tf_op jit(solution)/shard_map/ppermute | solution.py:15
  50.8 2.3 %collective-permute-done.14 = f32[2,1,512]{2,1,0:T(1,128)S(1)} collective-permute-done((f32[2,1,512]{2,1,0:T(1,128)S(1)}, f32[2,1,512]{2,1,0:T(1,128)S(1)}, u32[]{:S(2)}, u32[]{:S(2)}) %collective-permute-start.14) | collective-permute-done | bytes 4128 | tf_op jit(solution)/shard_map/ppermute | solution.py:15
  53.2 0.6 %fusion.27 = f32[2,1,512]{2,1,0:T(1,128)} fusion(f32[8,2,1,512]{3,2,1,0:T(1,128)S(1)} %constant_dynamic-update-slice_fusion, s32[]{:T(128)S(6)} %add.218, s32[]{:T(128)S(6)} %add.217, s32[]{:T(128)S(6)} %add.216, s32[]{:T(128)S(6)} %select_n.149), kind=kLoop, calls=%fused_computation.102 | loop fusion | flops 3072 | bytes 20496 | tf_op jit(solution)/shard_map/add | solution.py:96
  (46 shorter events, 0.5 us)
Async XLA Ops:
  0.0 11.6 %copy-start.1 = (f32[1,2,64]{2,1,0:T(2,128)S(1)}, f32[1,2,64]{2,1,0:T(2,128)}, u32[]{:S(2)}) copy-start(f32[1,2,64]{2,1,0:T(2,128)} %param.14) | copy-start | bytes 1540
  0.0 11.6 %copy-start = (s32[1,512]{1,0:T(1,128)S(1)}, s32[1,512]{1,0:T(1,128)}, u32[]{:S(2)}) copy-start(s32[1,512]{1,0:T(1,128)} %param.12) | copy-start | bytes 6148
  0.0 24.2 %collective-permute-start.8 = (bf16[2,64,512]{2,1,0:T(8,128)(2,1)}, bf16[2,64,512]{2,1,0:T(8,128)(2,1)S(1)}, u32[]{:S(2)}, u32[]{:S(2)}) collective-permute-start(bf16[2,64,512]{2,1,0:T(8,128)(2,1)} %bitcast.25), channel_id=1, source_target_pairs={{0,6},{1,7},{2,0},{3,1},{4,2},{5,3},{6,4},{7,5},{8,14},{9,15},{10,... | collective-permute-start | bytes 393224 | tf_op jit(solution)/shard_map/ppermute | solution.py:123
  5.1 20.7 %collective-permute-start.9 = (bf16[2,64,512]{2,1,0:T(8,128)(2,1)}, bf16[2,64,512]{2,1,0:T(8,128)(2,1)S(1)}, u32[]{:S(2)}, u32[]{:S(2)}) collective-permute-start(bf16[2,64,512]{2,1,0:T(8,128)(2,1)} %bitcast.25), channel_id=1, source_target_pairs={{0,4},{1,5},{2,6},{3,7},{4,0},{5,1},{6,2},{7,3},{8,12},{9,13},{10,... | collective-permute-start | bytes 393224 | tf_op jit(solution)/shard_map/ppermute | solution.py:123
  6.5 6.8 %collective-permute-start = (f32[64,2,128]{2,0,1:T(8,128)S(1)}, f32[64,2,128]{2,0,1:T(8,128)S(1)}, u32[]{:S(2)}, u32[]{:S(2)}) collective-permute-start(f32[64,2,128]{2,0,1:T(8,128)S(1)} %copy.31), channel_id=1, source_target_pairs={{0,6},{1,7},{2,0},{3,1},{4,2},{5,3},{6,4},{7,5},{8,14},{9,15},{10,... | collective-permute-start | bytes 196616 | tf_op jit(solution)/shard_map/ppermute | solution.py:132
  7.0 15.0 %collective-permute-start.1 = (f32[64,2,128]{2,0,1:T(8,128)S(1)}, f32[64,2,128]{2,0,1:T(8,128)S(1)}, u32[]{:S(2)}, u32[]{:S(2)}) collective-permute-start(f32[64,2,128]{2,0,1:T(8,128)S(1)} %copy.32), channel_id=1, source_target_pairs={{0,4},{1,5},{2,6},{3,7},{4,0},{5,1},{6,2},{7,3},{8,12},{9,13},{10,... | collective-permute-start | bytes 196616 | tf_op jit(solution)/shard_map/ppermute | solution.py:132
  9.6 14.0 %collective-permute-start.2 = (f32[64,2,128]{2,0,1:T(8,128)S(1)}, f32[64,2,128]{2,0,1:T(8,128)S(1)}, u32[]{:S(2)}, u32[]{:S(2)}) collective-permute-start(f32[64,2,128]{2,0,1:T(8,128)S(1)} %copy.33), channel_id=1, source_target_pairs={{0,2},{1,3},{2,4},{3,5},{4,6},{5,7},{6,0},{7,1},{8,10},{9,11},{10,... | collective-permute-start | bytes 196616 | tf_op jit(solution)/shard_map/ppermute | solution.py:132
  13.4 12.4 %collective-permute-start.10 = (bf16[2,64,512]{2,1,0:T(8,128)(2,1)}, bf16[2,64,512]{2,1,0:T(8,128)(2,1)S(1)}, u32[]{:S(2)}, u32[]{:S(2)}) collective-permute-start(bf16[2,64,512]{2,1,0:T(8,128)(2,1)} %bitcast.25), channel_id=1, source_target_pairs={{0,2},{1,3},{2,4},{3,5},{4,6},{5,7},{6,0},{7,1},{8,10},{9,11},{10,... | collective-permute-start | bytes 393224 | tf_op jit(solution)/shard_map/ppermute | solution.py:123
  22.1 23.7 %collective-permute-start.11 = (bf16[2,64,512]{2,1,0:T(8,128)(2,1)}, bf16[2,64,512]{2,1,0:T(8,128)(2,1)}, u32[]{:S(2)}, u32[]{:S(2)}) collective-permute-start(bf16[2,64,512]{2,1,0:T(8,128)(2,1)} %bitcast.25), channel_id=1, source_target_pairs={{0,1},{1,0},{2,3},{3,2},{4,5},{5,4},{6,7},{7,6},{8,9},{9,8},{10,11... | collective-permute-start | bytes 393224 | tf_op jit(solution)/shard_map/ppermute | solution.py:124
  23.7 7.9 %collective-permute-start.3 = (f32[4,64,1,128]{3,1,0,2:T(8,128)S(1)}, f32[4,64,1,128]{3,1,0,2:T(8,128)S(1)}, u32[]{:S(2)}, u32[]{:S(2)}) collective-permute-start(f32[4,64,1,128]{3,1,0,2:T(8,128)S(1)} %get-tuple-element.36), channel_id=1, source_target_pairs={{0,1},{1,0},{2,3},{3,2},{4,5},{5,4},{6,7},{7,6},{8,9},{9,8},{10,11... | collective-permute-start | bytes 393224 | tf_op jit(solution)/shard_map/ppermute | solution.py:135
  24.2 9.0 %collective-permute-start.4 = (f32[4,64,1,128]{3,1,0,2:T(8,128)S(1)}, f32[4,64,1,128]{3,1,0,2:T(8,128)S(1)}, u32[]{:S(2)}, u32[]{:S(2)}) collective-permute-start(f32[4,64,1,128]{3,1,0,2:T(8,128)S(1)} %get-tuple-element.37), channel_id=1, source_target_pairs={{0,16},{8,24},{16,0},{24,8},{1,17},{9,25},{17,1},{25,9},{2,18},{10... | collective-permute-start | bytes 393224 | tf_op jit(solution)/shard_map/ppermute | solution.py:148
  25.8 20.0 %collective-permute-start.12 = (bf16[3,2,64,512]{3,2,1,0:T(8,128)(2,1)S(1)}, bf16[3,2,64,512]{3,2,1,0:T(8,128)(2,1)}, u32[]{:S(2)}, u32[]{:S(2)}) collective-permute-start(bf16[3,2,64,512]{3,2,1,0:T(8,128)(2,1)S(1)} %pad_maximum_fusion.7), channel_id=1, source_target_pairs={{0,1},{1,0},{2,3},{3,2},{4,5},{5,4},{6,7},{7,6},{8,9},{9,8},{10,11... | collective-permute-start | bytes 1179656 | tf_op jit(solution)/shard_map/ppermute | solution.py:166
  31.5 5.0 %collective-permute-start.5 = (f32[4,64,1,128]{3,1,0,2:T(8,128)S(1)}, f32[4,64,1,128]{3,1,0,2:T(8,128)S(1)}, u32[]{:S(2)}, u32[]{:S(2)}) collective-permute-start(f32[4,64,1,128]{3,1,0,2:T(8,128)S(1)} %collective-permute-done.3), channel_id=1, source_target_pairs={{0,16},{8,24},{16,0},{24,8},{1,17},{9,25},{17,1},{25,9},{2,18},{10... | collective-permute-start | bytes 393224 | tf_op jit(solution)/shard_map/ppermute | solution.py:148
  33.2 3.7 %collective-permute-start.6 = (f32[512,1,128]{2,0,1:T(8,128)S(1)}, f32[512,1,128]{2,0,1:T(8,128)S(1)}, u32[]{:S(2)}, u32[]{:S(2)}) collective-permute-start(f32[512,1,128]{2,0,1:T(8,128)S(1)} %bitcast.100), channel_id=1, source_target_pairs={{0,8},{8,0},{16,24},{24,16},{1,9},{9,1},{17,25},{25,17},{2,10},{10... | collective-permute-start | bytes 786440 | tf_op jit(solution)/shard_map/ppermute | solution.py:151
  36.7 1.6 %collective-permute-start.7 = (f32[512,1,128]{2,0,1:T(8,128)S(1)}, f32[512,1,128]{2,0,1:T(8,128)S(1)}, u32[]{:S(2)}, u32[]{:S(2)}) collective-permute-start(f32[512,1,128]{2,0,1:T(8,128)S(1)} %bitcast.104), channel_id=1, source_target_pairs={{0,8},{8,0},{16,24},{24,16},{1,9},{9,1},{17,25},{25,17},{2,10},{10... | collective-permute-start | bytes 786440 | tf_op jit(solution)/shard_map/ppermute | solution.py:151
  48.2 2.6 %collective-permute-start.13 = (f32[2,1,512]{2,1,0:T(1,128)S(1)}, f32[2,1,512]{2,1,0:T(1,128)S(1)}, u32[]{:S(2)}, u32[]{:S(2)}) collective-permute-start(f32[2,1,512]{2,1,0:T(1,128)S(1)} %pad_maximum_fusion.10), channel_id=1, source_target_pairs={{0,24},{8,0},{16,8},{24,16},{1,25},{9,1},{17,9},{25,17},{2,26},{10... | collective-permute-start | bytes 12296 | tf_op jit(solution)/shard_map/ppermute | solution.py:15
  49.5 3.6 %collective-permute-start.14 = (f32[2,1,512]{2,1,0:T(1,128)S(1)}, f32[2,1,512]{2,1,0:T(1,128)S(1)}, u32[]{:S(2)}, u32[]{:S(2)}) collective-permute-start(f32[2,1,512]{2,1,0:T(1,128)S(1)} %pad_maximum_fusion.10), channel_id=1, source_target_pairs={{0,16},{8,24},{16,0},{24,8},{1,17},{9,25},{17,1},{25,9},{2,18},{10... | collective-permute-start | bytes 12296 | tf_op jit(solution)/shard_map/ppermute | solution.py:15
  50.0 3.1 %collective-permute-start.15 = (f32[2,1,512]{2,1,0:T(1,128)S(1)}, f32[2,1,512]{2,1,0:T(1,128)S(1)}, u32[]{:S(2)}, u32[]{:S(2)}) collective-permute-start(f32[2,1,512]{2,1,0:T(1,128)S(1)} %pad_maximum_fusion.10), channel_id=1, source_target_pairs={{0,8},{8,16},{16,24},{24,0},{1,9},{9,17},{17,25},{25,1},{2,10},{10... | collective-permute-start | bytes 12296 | tf_op jit(solution)/shard_map/ppermute | solution.py:15

commit v18 on v10

--- a/solution.py
+++ b/solution.py
@@ -143,8 +143,8 @@
     elements, row_count, _, width = view.shape
     voxels = row_count * freqs * width
 
-    scaled = TWO_PI * bins[0].astype(jnp.float32)
-    angle = scaled * view.reshape(elements, voxels)
+    turns = bins[0].astype(jnp.float32) * view.reshape(elements, voxels)
+    angle = TWO_PI * (turns - jnp.round(turns))
     field_real = jnp.cos(angle).astype(jnp.bfloat16)
     field_imag = (-jnp.sin(angle)).astype(jnp.bfloat16)
     left = jnp.concatenate([field_real, field_imag], axis=1)

time: 45.9 us -> 54.7 us (1.19)
  other arithmetic: 7.94 us -> 16.1 us
  local copies, waits for them, and re-layouts: 3.42 us -> 4.66 us
    convert_element_type x0 -> x2, other arithmetic: none -> 7.64 us  [body(): field_real = jnp.cos(angle).astype(jnp.bfloat16)]
    neg x1, other arithmetic: 0.07 us -> 4.42 us  [body(): right = jnp.concatenate([-field_imag, field_real], axis=1)]
    another operation x1 -> x0, other arithmetic: 3.84 us -> none
    mul x0 -> x4, local copies, waits for them, and re-layouts: none -> 1.5 us  [body(): turns = bins[0].astype(jnp.float32) * view.reshape(elements, voxels)]
    convert_element_type x4 -> x0, local copies, waits for them, and re-layouts: 1.02 us -> none  [the longest x3 0.82 us: body(): field_real = jnp.cos(angle).astype(jnp.bfloat16)]
    another operation x1, other arithmetic: 0.97 us -> 0.07 us  [body(): row = jnp.stack(row)]
    unnamed x12 -> x18, local copies, waits for them, and re-layouts: 0.06 us -> 0.92 us
    another operation x1, other arithmetic: 0.05 us -> 0.81 us  [body(): other = (own_swapped, lax.ppermute(jnp.stack(row[1:]), 'tile', swap))]
  transfers between devices with their start and end apart: 15 -> 15, of which waited for: 6 -> 6; matrix products, arithmetic and copies ran while one was open for 19% -> 32% of each run, Pallas kernels for 0% -> 0%
where the time goes in v18:
time: 54.7 us; the launch traced here: 54.5 us
  starting transfers between devices  16.4 us (30%)
  other arithmetic  16.1 us (29%)
  waiting for transfers between devices  14.5 us (27%)
  local copies, waits for them, and re-layouts  4.66 us (9%)
  matrix products  1.86 us (3%)
  between operations  1.02 us (2%)
    convert_element_type x2, other arithmetic, body(): field_real = jnp.cos(angle).astype(jnp.bfloat16)  7.64 us
    ppermute x3, waiting for transfers between devices, body(): pieces.append(lax.ppermute(sent, 'tile', pairs))  5.63 us
    neg x1, other arithmetic, body(): right = jnp.concatenate([-field_imag, field_real], axis=1)  4.42 us
    ppermute x3, starting transfers between devices, body(): cap_row.append(lax.ppermute(capture[0], 'tile', pairs))  4.38 us
    ppermute x3, starting transfers between devices, body(): pieces.append(lax.ppermute(sent, 'tile', pairs))  3.99 us
    ppermute x1, waiting for transfers between devices, body(): lax.ppermute(lax.dynamic_slice_in_dim(pieces, (1 - y) * per_tile, per_til...  3.33 us
    ppermute x3, waiting for transfers between devices, gather_shifted(): pieces.append(lax.ppermute(block, axis_name, pairs))  3.07 us
    ppermute x3, starting transfers between devices, gather_shifted(): pieces.append(lax.ppermute(block, axis_name, pairs))  1.82 us
  transfers between devices with their start and end apart: 15, of which 6 were waited for; matrix products, arithmetic and copies ran while one was open for 32% of the time, Pallas kernels for 0%

profile of v18, /device:TPU:16, one launch (start us, length us, event | category | flops | bytes accessed | tf_op | source)
XLA Modules:
  0.0 54.5 jit_solution(16260555920959645174)
XLA Ops:
  0.0 1.4 %constant_dynamic-slice_fusion.14 = (f32[64,2,128]{2,1,0:T(2,128)S(1)}, f32[64,2,128]{2,1,0:T(2,128)S(1)}, f32[64,2,128]{2,1,0:T(2,128)S(1)}, f32[64,2,128]{2,1,0:T(2,128)S(1)}) fusion(f32[64,8,128]{2,1,0:T(8,128)} %param.7, s32[]{:T(128)S(6)} %select_n.138, s32[]{:T(128)S(6)} %select_n.142, s32[]{:T(128)S(6)} %select_n.140, s32[]{:T(128)S(6)} %select_n.144), kind=kLoop, calls=%fused_computation.93 | loop fusion | bytes 524304 | tf_op jit(solution)/shard_map/dynamic_slice | solution.py:127
  1.4 0.5 collective-permute-start
  1.9 3.5 %collective-permute-start.1 = (f32[64,2,128]{2,0,1:T(8,128)S(1)}, f32[64,2,128]{2,0,1:T(8,128)S(1)}, u32[]{:S(2)}, u32[]{:S(2)}) collective-permute-start(f32[64,2,128]{2,0,1:T(8,128)S(1)} %copy.28), channel_id=1, source_target_pairs={{0,4},{1,5},{2,6},{3,7},{4,0},{5,1},{6,2},{7,3},{8,12},{9,13},{10,... | collective-permute-start | bytes 196616 | tf_op jit(solution)/shard_map/ppermute | solution.py:132
  5.4 2.0 %collective-permute-start.7 = (bf16[2,64,512]{2,1,0:T(8,128)(2,1)S(1)}, bf16[2,64,512]{2,1,0:T(8,128)(2,1)S(1)}, u32[]{:S(2)}, u32[]{:S(2)}) collective-permute-start(bf16[2,64,512]{2,1,0:T(8,128)(2,1)S(1)} %bitcast.109), channel_id=1, source_target_pairs={{0,6},{1,7},{2,0},{3,1},{4,2},{5,3},{6,4},{7,5},{8,14},{9,15},{10,... | collective-permute-start | bytes 393224 | tf_op jit(solution)/shard_map/ppermute | solution.py:123
  7.4 1.9 %collective-permute-start.8 = (bf16[2,64,512]{2,1,0:T(8,128)(2,1)S(1)}, bf16[2,64,512]{2,1,0:T(8,128)(2,1)S(1)}, u32[]{:S(2)}, u32[]{:S(2)}) collective-permute-start(bf16[2,64,512]{2,1,0:T(8,128)(2,1)S(1)} %bitcast.110), channel_id=1, source_target_pairs={{0,4},{1,5},{2,6},{3,7},{4,0},{5,1},{6,2},{7,3},{8,12},{9,13},{10,... | collective-permute-start | bytes 393224 | tf_op jit(solution)/shard_map/ppermute | solution.py:123
  9.3 0.5 collective-permute-start.9
  9.8 1.5 %collective-permute-start.10 = (bf16[2,64,512]{2,1,0:T(8,128)(2,1)S(1)}, bf16[2,64,512]{2,1,0:T(8,128)(2,1)}, u32[]{:S(2)}, u32[]{:S(2)}) collective-permute-start(bf16[2,64,512]{2,1,0:T(8,128)(2,1)S(1)} %bitcast.112), channel_id=1, source_target_pairs={{0,1},{1,0},{2,3},{3,2},{4,5},{5,4},{6,7},{7,6},{8,9},{9,8},{10,11... | collective-permute-start | bytes 393224 | tf_op jit(solution)/shard_map/ppermute | solution.py:124
  11.3 5.6 %collective-permute-done.2 = f32[64,2,128]{2,0,1:T(8,128)S(1)} collective-permute-done((f32[64,2,128]{2,0,1:T(8,128)S(1)}, f32[64,2,128]{2,0,1:T(8,128)S(1)}, u32[]{:S(2)}, u32[]{:S(2)}) %collective-permute-start.2) | collective-permute-done | bytes 65568 | tf_op jit(solution)/shard_map/ppermute | solution.py:132
  17.0 1.6 %collective-permute-start.3 = (f32[4,64,1,128]{3,1,0,2:T(8,128)S(1)}, f32[4,64,1,128]{3,1,0,2:T(8,128)S(1)}, u32[]{:S(2)}, u32[]{:S(2)}) collective-permute-start(f32[4,64,1,128]{3,1,0,2:T(8,128)S(1)} %get-tuple-element.36), channel_id=1, source_target_pairs={{0,1},{1,0},{2,3},{3,2},{4,5},{5,4},{6,7},{7,6},{8,9},{9,8},{10,11... | collective-permute-start | bytes 393224 | tf_op jit(solution)/shard_map/ppermute | solution.py:135
  18.6 0.1 select_reduce_fusion.1
  18.7 3.3 %collective-permute-done.3 = f32[4,64,1,128]{3,1,0,2:T(8,128)S(1)} collective-permute-done((f32[4,64,1,128]{3,1,0,2:T(8,128)S(1)}, f32[4,64,1,128]{3,1,0,2:T(8,128)S(1)}, u32[]{:S(2)}, u32[]{:S(2)}) %collective-permute-start.3) | collective-permute-done | bytes 131104 | tf_op jit(solution)/shard_map/ppermute | solution.py:135
  22.1 0.1 fusion.17
  22.1 1.6 %collective-permute-start.4 = (f32[512,1,128]{2,0,1:T(8,128)S(1)}, f32[512,1,128]{2,0,1:T(8,128)S(1)}, u32[]{:S(2)}, u32[]{:S(2)}) collective-permute-start(f32[512,1,128]{2,0,1:T(8,128)S(1)} %bitcast.89), channel_id=1, source_target_pairs={{0,16},{8,24},{16,0},{24,8},{1,17},{9,25},{17,1},{25,9},{2,18},{10... | collective-permute-start | bytes 786440 | tf_op jit(solution)/shard_map/ppermute | solution.py:68
  24.4 0.8 %pad_maximum_fusion.7 = bf16[3,2,64,512]{3,2,1,0:T(8,128)(2,1)} fusion(bf16[1,2,64,512]{3,2,1,0:T(8,128)(2,1)S(1)} %bitcast.100, bf16[1,2,64,512]{3,2,1,0:T(8,128)(2,1)S(1)} %bitcast.98, bf16[1,2,64,512]{3,2,1,0:T(8,128)(2,1)S(1)} %bitcast.96), kind=kLoop, calls=%fused_computation.50 | loop fusion | flops 393216 | bytes 786432 | tf_op jit(solution)/shard_map/stack | solution.py:154
  25.2 1.5 %collective-permute-start.11 = (bf16[3,2,64,512]{3,2,1,0:T(8,128)(2,1)}, bf16[3,2,64,512]{3,2,1,0:T(8,128)(2,1)}, u32[]{:S(2)}, u32[]{:S(2)}) collective-permute-start(bf16[3,2,64,512]{3,2,1,0:T(8,128)(2,1)} %pad_maximum_fusion.7), channel_id=1, source_target_pairs={{0,1},{1,0},{2,3},{3,2},{4,5},{5,4},{6,7},{7,6},{8,9},{9,8},{10,11... | collective-permute-start | bytes 1179656 | tf_op jit(solution)/shard_map/ppermute | solution.py:154
  26.7 0.1 pad_maximum_fusion.6
  26.8 0.1 collective-permute-start.5
  26.9 1.7 %collective-permute-done.4 = f32[512,1,128]{2,0,1:T(8,128)S(1)} collective-permute-done((f32[512,1,128]{2,0,1:T(8,128)S(1)}, f32[512,1,128]{2,0,1:T(8,128)S(1)}, u32[]{:S(2)}, u32[]{:S(2)}) %collective-permute-start.4) | collective-permute-done | bytes 262176 | tf_op jit(solution)/shard_map/ppermute | solution.py:68
  28.6 0.7 %fusion.34 = (bf16[4,1,64,512]{3,2,1,0:T(8,128)(2,1)S(1)}, bf16[4,1,64,512]{3,2,1,0:T(8,128)(2,1)}) fusion(bf16[4,2,64,512]{3,2,1,0:T(8,128)(2,1)S(1)} %pad_maximum_fusion.6), kind=kLoop, calls=%fused_computation.114 | loop fusion | bytes 1048576 | tf_op jit(solution)/shard_map/slice | solution.py:165
  29.4 0.7 %collective-permute-done.6 = f32[512,1,128]{2,0,1:T(8,128)S(1)} collective-permute-done((f32[512,1,128]{2,0,1:T(8,128)S(1)}, f32[512,1,128]{2,0,1:T(8,128)S(1)}, u32[]{:S(2)}, u32[]{:S(2)}) %collective-permute-start.6) | collective-permute-done | bytes 262176 | tf_op jit(solution)/shard_map/ppermute | solution.py:70
  30.1 0.1 maximum_bitcast_fusion.1
  30.2 0.1 maximum_multiply_fusion
  30.3 0.1 copy.24
  30.3 0.7 %copy.25 = f32[512,1,4,128]{3,2,0,1:T(4,128)S(1)} copy(f32[512,1,4,128]{3,0,2,1:T(8,128)S(1)} %bitcast.87) | data formatting | bytes 2097152 | tf_op jit(solution)/shard_map/mul | solution.py:146
  31.0 0.3 copy.26
  31.4 4.4 %fusion.33 = (bf16[512,512]{0,1:T(8,128)(2,1)S(1)}, bf16[512,512]{0,1:T(8,128)(2,1)}) fusion(f32[512,1,4,128]{0,3,2,1:T(8,128)S(1)} %copy.26), kind=kLoop, calls=%fused_computation.113 | loop fusion | flops 2097152 | bytes 2097152 | tf_op jit(solution)/shard_map/neg | solution.py:151
  35.8 3.7 %cosine_convert_fusion = bf16[512,512]{0,1:T(8,128)(2,1)S(1)} fusion(f32[512,1,4,128]{0,3,2,1:T(8,128)S(1)} %copy.26), kind=kLoop, calls=%fused_computation.11 | loop fusion | flops 1048576 | bytes 1572864 | tf_op jit(solution)/shard_map/convert_element_type | solution.py:148
  39.5 0.4 mul.205
  39.9 4.0 %cosine_convert_fusion.1 = (bf16[4,2,64,512]{3,2,1,0:T(8,128)(2,1)S(1)}, bf16[4,2,64,512]{3,2,1,0:T(8,128)(2,1)S(1)}) fusion(f32[4,2,64,512]{3,2,1,0:T(8,128)S(1)} %mul.205), kind=kLoop, calls=%fused_computation.12 | loop fusion | flops 1572864 | bytes 2097152 | tf_op jit(solution)/shard_map/convert_element_type | solution.py:148
  43.9 0.1 dynamic-slice_bitcast_fusion
  44.0 0.1 fusion.16
  44.1 0.1 fusion.15
  44.2 0.8 %copy-done = bf16[512,512]{0,1:T(8,128)(2,1)S(1)} copy-done((bf16[512,512]{0,1:T(8,128)(2,1)S(1)}, bf16[512,512]{0,1:T(8,128)(2,1)}, u32[]{:S(2)}) %copy-start) | copy-done | bytes 524312
  45.0 0.1 copy-done.1
  45.1 0.5 fusion.3
  45.6 0.5 convolution_add_fusion.1
  46.0 0.2 fusion.11
  46.3 0.1 fusion.13
  46.4 0.1 fusion.14
  46.5 1.1 %pad_maximum_fusion.8 = (bf16[4,1,64,512]{3,2,1,0:T(8,128)(2,1)S(1)}, bf16[4,1,64,512]{3,2,1,0:T(8,128)(2,1)S(1)}) fusion(bf16[3,2,64,512]{3,2,1,0:T(8,128)(2,1)} %collective-permute-done.11, bf16[1,2,64,512]{3,2,1,0:T(8,128)(2,1)} %bitcast.38), kind=kLoop, calls=%fused_computation.60 | loop fusion | flops 262144 | bytes 1048576 | tf_op jit(solution)/shard_map/concatenate | solution.py:180
  47.7 0.5 fusion.2
  48.1 0.5 convolution_add_fusion
  48.6 0.2 fusion.7
  48.9 1.3 %collective-permute-start.12 = (f32[2,1,512]{2,1,0:T(1,128)S(1)}, f32[2,1,512]{2,1,0:T(1,128)S(1)}, u32[]{:S(2)}, u32[]{:S(2)}) collective-permute-start(f32[2,1,512]{2,1,0:T(1,128)S(1)} %pad_maximum_fusion.10), channel_id=1, source_target_pairs={{0,24},{8,0},{16,8},{24,16},{1,25},{9,1},{17,9},{25,17},{2,26},{10... | collective-permute-start | bytes 12296 | tf_op jit(solution)/shard_map/ppermute | solution.py:15
  50.2 0.5 collective-permute-start.13
  50.8 0.8 %collective-permute-done.12 = f32[2,1,512]{2,1,0:T(1,128)S(1)} collective-permute-done((f32[2,1,512]{2,1,0:T(1,128)S(1)}, f32[2,1,512]{2,1,0:T(1,128)S(1)}, u32[]{:S(2)}, u32[]{:S(2)}) %collective-permute-start.12) | collective-permute-done | bytes 4128 | tf_op jit(solution)/shard_map/ppermute | solution.py:15
  51.5 2.3 %collective-permute-done.13 = f32[2,1,512]{2,1,0:T(1,128)S(1)} collective-permute-done((f32[2,1,512]{2,1,0:T(1,128)S(1)}, f32[2,1,512]{2,1,0:T(1,128)S(1)}, u32[]{:S(2)}, u32[]{:S(2)}) %collective-permute-start.13) | collective-permute-done | bytes 4128 | tf_op jit(solution)/shard_map/ppermute | solution.py:15
  53.9 0.6 %fusion.25 = f32[2,1,512]{2,1,0:T(1,128)} fusion(f32[8,2,1,512]{3,2,1,0:T(1,128)S(1)} %constant_dynamic-update-slice_fusion, s32[]{:T(128)S(6)} %add.214, s32[]{:T(128)S(6)} %add.213, s32[]{:T(128)S(6)} %add.212, s32[]{:T(128)S(6)} %select_n.159), kind=kLoop, calls=%fused_computation.98 | loop fusion | flops 3072 | bytes 20496 | tf_op jit(solution)/shard_map/add | solution.py:96
  (45 shorter events, 0.3 us)
Async XLA Ops:
  0.0 5.4 %copy-start.2 = (bf16[1,2,64,512]{3,2,1,0:T(8,128)(2,1)S(1)}, bf16[1,2,64,512]{3,2,1,0:T(8,128)(2,1)}, u32[]{:S(2)}) copy-start(bf16[1,2,64,512]{3,2,1,0:T(8,128)(2,1)} %param.11) | copy-start | bytes 393220
  0.0 18.6 %copy-start.4 = (f32[1,2,64]{2,1,0:T(2,128)S(1)}, f32[1,2,64]{2,1,0:T(2,128)}, u32[]{:S(2)}) copy-start(f32[1,2,64]{2,1,0:T(2,128)} %param.10) | copy-start | bytes 1540
  0.0 18.6 %copy-start.3 = (s32[1,512]{1,0:T(1,128)S(1)}, s32[1,512]{1,0:T(1,128)}, u32[]{:S(2)}) copy-start(s32[1,512]{1,0:T(1,128)} %param.8) | copy-start | bytes 6148
  1.4 7.9 %collective-permute-start = (f32[64,2,128]{2,0,1:T(8,128)S(1)}, f32[64,2,128]{2,0,1:T(8,128)S(1)}, u32[]{:S(2)}, u32[]{:S(2)}) collective-permute-start(f32[64,2,128]{2,0,1:T(8,128)S(1)} %copy.27), channel_id=1, source_target_pairs={{0,6},{1,7},{2,0},{3,1},{4,2},{5,3},{6,4},{7,5},{8,14},{9,15},{10,... | collective-permute-start | bytes 196616 | tf_op jit(solution)/shard_map/ppermute | solution.py:132
  1.9 7.9 %collective-permute-start.1 = (f32[64,2,128]{2,0,1:T(8,128)S(1)}, f32[64,2,128]{2,0,1:T(8,128)S(1)}, u32[]{:S(2)}, u32[]{:S(2)}) collective-permute-start(f32[64,2,128]{2,0,1:T(8,128)S(1)} %copy.28), channel_id=1, source_target_pairs={{0,4},{1,5},{2,6},{3,7},{4,0},{5,1},{6,2},{7,3},{8,12},{9,13},{10,... | collective-permute-start | bytes 196616 | tf_op jit(solution)/shard_map/ppermute | solution.py:132
  5.4 11.5 %collective-permute-start.2 = (f32[64,2,128]{2,0,1:T(8,128)S(1)}, f32[64,2,128]{2,0,1:T(8,128)S(1)}, u32[]{:S(2)}, u32[]{:S(2)}) collective-permute-start(f32[64,2,128]{2,0,1:T(8,128)S(1)} %copy.29), channel_id=1, source_target_pairs={{0,2},{1,3},{2,4},{3,5},{4,6},{5,7},{6,0},{7,1},{8,10},{9,11},{10,... | collective-permute-start | bytes 196616 | tf_op jit(solution)/shard_map/ppermute | solution.py:132
  5.4 19.0 %collective-permute-start.7 = (bf16[2,64,512]{2,1,0:T(8,128)(2,1)S(1)}, bf16[2,64,512]{2,1,0:T(8,128)(2,1)S(1)}, u32[]{:S(2)}, u32[]{:S(2)}) collective-permute-start(bf16[2,64,512]{2,1,0:T(8,128)(2,1)S(1)} %bitcast.109), channel_id=1, source_target_pairs={{0,6},{1,7},{2,0},{3,1},{4,2},{5,3},{6,4},{7,5},{8,14},{9,15},{10,... | collective-permute-start | bytes 393224 | tf_op jit(solution)/shard_map/ppermute | solution.py:123
  7.4 17.0 %collective-permute-start.8 = (bf16[2,64,512]{2,1,0:T(8,128)(2,1)S(1)}, bf16[2,64,512]{2,1,0:T(8,128)(2,1)S(1)}, u32[]{:S(2)}, u32[]{:S(2)}) collective-permute-start(bf16[2,64,512]{2,1,0:T(8,128)(2,1)S(1)} %bitcast.110), channel_id=1, source_target_pairs={{0,4},{1,5},{2,6},{3,7},{4,0},{5,1},{6,2},{7,3},{8,12},{9,13},{10,... | collective-permute-start | bytes 393224 | tf_op jit(solution)/shard_map/ppermute | solution.py:123
  9.3 15.1 %collective-permute-start.9 = (bf16[2,64,512]{2,1,0:T(8,128)(2,1)S(1)}, bf16[2,64,512]{2,1,0:T(8,128)(2,1)S(1)}, u32[]{:S(2)}, u32[]{:S(2)}) collective-permute-start(bf16[2,64,512]{2,1,0:T(8,128)(2,1)S(1)} %bitcast.111), channel_id=1, source_target_pairs={{0,2},{1,3},{2,4},{3,5},{4,6},{5,7},{6,0},{7,1},{8,10},{9,11},{10,... | collective-permute-start | bytes 393224 | tf_op jit(solution)/shard_map/ppermute | solution.py:123
  9.8 36.7 %collective-permute-start.10 = (bf16[2,64,512]{2,1,0:T(8,128)(2,1)S(1)}, bf16[2,64,512]{2,1,0:T(8,128)(2,1)}, u32[]{:S(2)}, u32[]{:S(2)}) collective-permute-start(bf16[2,64,512]{2,1,0:T(8,128)(2,1)S(1)} %bitcast.112), channel_id=1, source_target_pairs={{0,1},{1,0},{2,3},{3,2},{4,5},{5,4},{6,7},{7,6},{8,9},{9,8},{10,11... | collective-permute-start | bytes 393224 | tf_op jit(solution)/shard_map/ppermute | solution.py:124
  17.0 5.0 %collective-permute-start.3 = (f32[4,64,1,128]{3,1,0,2:T(8,128)S(1)}, f32[4,64,1,128]{3,1,0,2:T(8,128)S(1)}, u32[]{:S(2)}, u32[]{:S(2)}) collective-permute-start(f32[4,64,1,128]{3,1,0,2:T(8,128)S(1)} %get-tuple-element.36), channel_id=1, source_target_pairs={{0,1},{1,0},{2,3},{3,2},{4,5},{5,4},{6,7},{7,6},{8,9},{9,8},{10,11... | collective-permute-start | bytes 393224 | tf_op jit(solution)/shard_map/ppermute | solution.py:135
  22.1 6.4 %collective-permute-start.4 = (f32[512,1,128]{2,0,1:T(8,128)S(1)}, f32[512,1,128]{2,0,1:T(8,128)S(1)}, u32[]{:S(2)}, u32[]{:S(2)}) collective-permute-start(f32[512,1,128]{2,0,1:T(8,128)S(1)} %bitcast.89), channel_id=1, source_target_pairs={{0,16},{8,24},{16,0},{24,8},{1,17},{9,25},{17,1},{25,9},{2,18},{10... | collective-permute-start | bytes 786440 | tf_op jit(solution)/shard_map/ppermute | solution.py:68
  25.2 21.3 %collective-permute-start.11 = (bf16[3,2,64,512]{3,2,1,0:T(8,128)(2,1)}, bf16[3,2,64,512]{3,2,1,0:T(8,128)(2,1)}, u32[]{:S(2)}, u32[]{:S(2)}) collective-permute-start(bf16[3,2,64,512]{3,2,1,0:T(8,128)(2,1)} %pad_maximum_fusion.7), channel_id=1, source_target_pairs={{0,1},{1,0},{2,3},{3,2},{4,5},{5,4},{6,7},{7,6},{8,9},{9,8},{10,11... | collective-permute-start | bytes 1179656 | tf_op jit(solution)/shard_map/ppermute | solution.py:154
  26.8 2.6 %collective-permute-start.5 = (f32[512,1,128]{2,0,1:T(8,128)S(1)}, f32[512,1,128]{2,0,1:T(8,128)S(1)}, u32[]{:S(2)}, u32[]{:S(2)}) collective-permute-start(f32[512,1,128]{2,0,1:T(8,128)S(1)} %bitcast.90), channel_id=1, source_target_pairs={{0,8},{8,0},{16,24},{24,16},{1,9},{9,1},{17,25},{25,17},{2,10},{10... | collective-permute-start | bytes 786440 | tf_op jit(solution)/shard_map/ppermute | solution.py:70
  28.6 1.5 %collective-permute-start.6 = (f32[512,1,128]{2,0,1:T(8,128)S(1)}, f32[512,1,128]{2,0,1:T(8,128)S(1)}, u32[]{:S(2)}, u32[]{:S(2)}) collective-permute-start(f32[512,1,128]{2,0,1:T(8,128)S(1)} %collective-permute-done.4), channel_id=1, source_target_pairs={{0,8},{8,0},{16,24},{24,16},{1,9},{9,1},{17,25},{25,17},{2,10},{10... | collective-permute-start | bytes 786440 | tf_op jit(solution)/shard_map/ppermute | solution.py:70
  44.0 1.0 %copy-start = (bf16[512,512]{0,1:T(8,128)(2,1)S(1)}, bf16[512,512]{0,1:T(8,128)(2,1)}, u32[]{:S(2)}) copy-start(bf16[512,512]{0,1:T(8,128)(2,1)} %get-tuple-element.25) | copy-start | bytes 1572868
  44.0 1.1 %copy-start.1 = (bf16[4,1,64,512]{3,2,1,0:T(8,128)(2,1)S(1)}, bf16[4,1,64,512]{3,2,1,0:T(8,128)(2,1)}, u32[]{:S(2)}) copy-start(bf16[4,1,64,512]{3,2,1,0:T(8,128)(2,1)} %get-tuple-element.35) | copy-start | bytes 786436
  48.9 2.6 %collective-permute-start.12 = (f32[2,1,512]{2,1,0:T(1,128)S(1)}, f32[2,1,512]{2,1,0:T(1,128)S(1)}, u32[]{:S(2)}, u32[]{:S(2)}) collective-permute-start(f32[2,1,512]{2,1,0:T(1,128)S(1)} %pad_maximum_fusion.10), channel_id=1, source_target_pairs={{0,24},{8,0},{16,8},{24,16},{1,25},{9,1},{17,9},{25,17},{2,26},{10... | collective-permute-start | bytes 12296 | tf_op jit(solution)/shard_map/ppermute | solution.py:15
  50.2 3.6 %collective-permute-start.13 = (f32[2,1,512]{2,1,0:T(1,128)S(1)}, f32[2,1,512]{2,1,0:T(1,128)S(1)}, u32[]{:S(2)}, u32[]{:S(2)}) collective-permute-start(f32[2,1,512]{2,1,0:T(1,128)S(1)} %pad_maximum_fusion.10), channel_id=1, source_target_pairs={{0,16},{8,24},{16,0},{24,8},{1,17},{9,25},{17,1},{25,9},{2,18},{10... | collective-permute-start | bytes 12296 | tf_op jit(solution)/shard_map/ppermute | solution.py:15
  50.7 3.1 %collective-permute-start.14 = (f32[2,1,512]{2,1,0:T(1,128)S(1)}, f32[2,1,512]{2,1,0:T(1,128)S(1)}, u32[]{:S(2)}, u32[]{:S(2)}) collective-permute-start(f32[2,1,512]{2,1,0:T(1,128)S(1)} %pad_maximum_fusion.10), channel_id=1, source_target_pairs={{0,8},{8,16},{16,24},{24,0},{1,9},{9,17},{17,25},{25,1},{2,10},{10... | collective-permute-start | bytes 12296 | tf_op jit(solution)/shard_map/ppermute | solution.py:15

commit v19 on v10

--- a/solution.py
+++ b/solution.py
@@ -175,11 +175,16 @@
         return part_real, part_imag
 
     mine_real, mine_imag = partial_focus(row, rows_of(field_real, y), rows_of(field_imag, y))
-    theirs_rows = (rows_of(field_real, 1 - y), rows_of(field_imag, 1 - y))
-    mine_real, mine_imag, theirs_rows, other = lax.optimization_barrier((mine_real, mine_imag, theirs_rows, other))
-    theirs_real, theirs_imag = partial_focus(jnp.concatenate([other[0][None], other[1]]), *theirs_rows)
-    focus_real = mine_real + theirs_real
-    focus_imag = mine_imag + theirs_imag
+    theirs_real_rows = rows_of(field_real, 1 - y)
+    theirs_imag_rows = rows_of(field_imag, 1 - y)
+    first_real, first_imag = partial_focus(other[0][None], theirs_real_rows[:own], theirs_imag_rows[:own])
+    theirs_rows = (theirs_real_rows[own:], theirs_imag_rows[own:])
+    mine_real, mine_imag, first_real, first_imag, theirs_rows, rest = lax.optimization_barrier(
+        (mine_real, mine_imag, first_real, first_imag, theirs_rows, other[1])
+    )
+    theirs_real, theirs_imag = partial_focus(rest, *theirs_rows)
+    focus_real = mine_real + (first_real + theirs_real)
+    focus_imag = mine_imag + (first_imag + theirs_imag)
 
     outer = freqs // 2
     focus = jnp.stack([focus_real, focus_imag]).reshape(2, row_count, outer, 2, width)

time: 45.9 us -> 47.9 us (1.044); the launches traced: 45.7 us -> 47.1 us
  waiting for transfers between devices: 15 us -> 11.8 us
  matrix products: 1.87 us -> 4.49 us
  starting transfers between devices: 16.5 us -> 18.2 us
  local copies, waits for them, and re-layouts: 3.42 us -> 3.99 us
    ppermute x3, waiting for transfers between devices: 5.63 us -> 4.27 us  [body(): pieces.append(lax.ppermute(sent, 'tile', pairs))]
    dot_general x2 -> x3, matrix products: 0.93 us -> 2.25 us  [partial_focus(): jnp.dot(cap_real, left, preferred_element_type=jnp.float32)]
    dot_general x2 -> x3, matrix products: 0.94 us -> 2.25 us  [partial_focus(): jnp.dot(cap_imag, right, preferred_element_type=jnp.float32)]
    ppermute x1, waiting for transfers between devices: 1.48 us -> 0.31 us  [gather_columns(): same_core.append(lax.ppermute(block, axis_name, pairs))]
    concatenate x1 -> x0, other arithmetic: 1.11 us -> none  [body(): jnp.concatenate([other[0][None], other[1]])]
    ppermute x1, starting transfers between devices: 1.58 us -> 2.59 us  [body(): lax.ppermute(lax.dynamic_slice_in_dim(pieces, (1 - y) * per_tile, per_til...]
    another operation x1, other arithmetic: 0.05 us -> 0.79 us  [body(): other = (own_swapped, lax.ppermute(jnp.stack(row[1:]), 'tile', swap))]
    slice x0 -> x4, local copies, waits for them, and re-layouts: none -> 0.5 us  [body(): theirs_rows = (theirs_real_rows[own:], theirs_imag_rows[own:])]
  transfers between devices with their start and end apart: 15 -> 15, of which waited for: 6 -> 7; matrix products, arithmetic and copies ran while one was open for 19% -> 26% of each run, Pallas kernels for 0% -> 0%
where the time goes in v19:
time: 47.9 us; the launch traced here: 47.1 us
  starting transfers between devices  18.2 us (38%)
  waiting for transfers between devices  11.8 us (25%)
  other arithmetic  7.58 us (16%)
  matrix products  4.49 us (9%)
  local copies, waits for them, and re-layouts  3.99 us (8%)
  between operations  1.05 us (2%)
    ppermute x3, starting transfers between devices, body(): cap_row.append(lax.ppermute(capture[0], 'tile', pairs))  4.38 us
    ppermute x3, waiting for transfers between devices, body(): pieces.append(lax.ppermute(sent, 'tile', pairs))  4.27 us
    ppermute x3, starting transfers between devices, body(): pieces.append(lax.ppermute(sent, 'tile', pairs))  3.99 us
    another operation x1, other arithmetic  3.84 us
    ppermute x3, waiting for transfers between devices, gather_shifted(): pieces.append(lax.ppermute(block, axis_name, pairs))  3.05 us
    ppermute x1, waiting for transfers between devices, body(): lax.ppermute(lax.dynamic_slice_in_dim(pieces, (1 - y) * per_tile, per_til...  2.83 us
    ppermute x1, starting transfers between devices, body(): lax.ppermute(lax.dynamic_slice_in_dim(pieces, (1 - y) * per_tile, per_til...  2.59 us
    dot_general x3, matrix products, partial_focus(): jnp.dot(cap_real, left, preferred_element_type=jnp.float32)  2.25 us
  transfers between devices with their start and end apart: 15, of which 7 were waited for; matrix products, arithmetic and copies ran while one was open for 26% of the time, Pallas kernels for 0%

profile of v19, /device:TPU:16, one launch (start us, length us, event | category | flops | bytes accessed | tf_op | source)
XLA Modules:
  0.0 47.1 jit_solution(2209451256510563703)
XLA Ops:
  0.0 1.5 %constant_dynamic-slice_fusion.14 = (f32[64,2,128]{2,1,0:T(2,128)S(1)}, f32[64,2,128]{2,1,0:T(2,128)S(1)}, f32[64,2,128]{2,1,0:T(2,128)S(1)}, f32[64,2,128]{2,1,0:T(2,128)S(1)}) fusion(f32[64,8,128]{2,1,0:T(8,128)} %param.7, s32[]{:T(128)S(6)} %select_n.138, s32[]{:T(128)S(6)} %select_n.142, s32[]{:T(128)S(6)} %select_n.140, s32[]{:T(128)S(6)} %select_n.144), kind=kLoop, calls=%fused_computation.98 | loop fusion | bytes 524304 | tf_op jit(solution)/shard_map/dynamic_slice | solution.py:127
  1.5 0.5 %collective-permute-start = (f32[64,2,128]{2,0,1:T(8,128)S(1)}, f32[64,2,128]{2,0,1:T(8,128)S(1)}, u32[]{:S(2)}, u32[]{:S(2)}) collective-permute-start(f32[64,2,128]{2,0,1:T(8,128)S(1)} %copy.28), channel_id=1, source_target_pairs={{0,6},{1,7},{2,0},{3,1},{4,2},{5,3},{6,4},{7,5},{8,14},{9,15},{10,... | collective-permute-start | bytes 196616 | tf_op jit(solution)/shard_map/ppermute | solution.py:132
  2.0 3.5 %collective-permute-start.1 = (f32[64,2,128]{2,0,1:T(8,128)S(1)}, f32[64,2,128]{2,0,1:T(8,128)S(1)}, u32[]{:S(2)}, u32[]{:S(2)}) collective-permute-start(f32[64,2,128]{2,0,1:T(8,128)S(1)} %copy.29), channel_id=1, source_target_pairs={{0,4},{1,5},{2,6},{3,7},{4,0},{5,1},{6,2},{7,3},{8,12},{9,13},{10,... | collective-permute-start | bytes 196616 | tf_op jit(solution)/shard_map/ppermute | solution.py:132
  5.5 1.6 %collective-permute-start.10 = (bf16[2,64,512]{2,1,0:T(8,128)(2,1)}, bf16[2,64,512]{2,1,0:T(8,128)(2,1)}, u32[]{:S(2)}, u32[]{:S(2)}) collective-permute-start(bf16[2,64,512]{2,1,0:T(8,128)(2,1)} %bitcast.22), channel_id=1, source_target_pairs={{0,1},{1,0},{2,3},{3,2},{4,5},{5,4},{6,7},{7,6},{8,9},{9,8},{10,11... | collective-permute-start | bytes 393224 | tf_op jit(solution)/shard_map/ppermute | solution.py:124
  7.1 2.0 %collective-permute-start.7 = (bf16[2,64,512]{2,1,0:T(8,128)(2,1)}, bf16[2,64,512]{2,1,0:T(8,128)(2,1)S(1)}, u32[]{:S(2)}, u32[]{:S(2)}) collective-permute-start(bf16[2,64,512]{2,1,0:T(8,128)(2,1)} %bitcast.22), channel_id=1, source_target_pairs={{0,6},{1,7},{2,0},{3,1},{4,2},{5,3},{6,4},{7,5},{8,14},{9,15},{10,... | collective-permute-start | bytes 393224 | tf_op jit(solution)/shard_map/ppermute | solution.py:123
  9.1 1.9 %collective-permute-start.8 = (bf16[2,64,512]{2,1,0:T(8,128)(2,1)}, bf16[2,64,512]{2,1,0:T(8,128)(2,1)S(1)}, u32[]{:S(2)}, u32[]{:S(2)}) collective-permute-start(bf16[2,64,512]{2,1,0:T(8,128)(2,1)} %bitcast.22), channel_id=1, source_target_pairs={{0,4},{1,5},{2,6},{3,7},{4,0},{5,1},{6,2},{7,3},{8,12},{9,13},{10,... | collective-permute-start | bytes 393224 | tf_op jit(solution)/shard_map/ppermute | solution.py:123
  11.0 0.5 %collective-permute-start.9 = (bf16[2,64,512]{2,1,0:T(8,128)(2,1)}, bf16[2,64,512]{2,1,0:T(8,128)(2,1)S(1)}, u32[]{:S(2)}, u32[]{:S(2)}) collective-permute-start(bf16[2,64,512]{2,1,0:T(8,128)(2,1)} %bitcast.22), channel_id=1, source_target_pairs={{0,2},{1,3},{2,4},{3,5},{4,6},{5,7},{6,0},{7,1},{8,10},{9,11},{10,... | collective-permute-start | bytes 393224 | tf_op jit(solution)/shard_map/ppermute | solution.py:123
  11.5 4.3 %collective-permute-done.2 = f32[64,2,128]{2,0,1:T(8,128)S(1)} collective-permute-done((f32[64,2,128]{2,0,1:T(8,128)S(1)}, f32[64,2,128]{2,0,1:T(8,128)S(1)}, u32[]{:S(2)}, u32[]{:S(2)}) %collective-permute-start.2) | collective-permute-done | bytes 65568 | tf_op jit(solution)/shard_map/ppermute | solution.py:132
  15.8 2.6 %collective-permute-start.3 = (f32[4,64,1,128]{3,1,0,2:T(8,128)S(1)}, f32[4,64,1,128]{3,1,0,2:T(8,128)S(1)}, u32[]{:S(2)}, u32[]{:S(2)}) collective-permute-start(f32[4,64,1,128]{3,1,0,2:T(8,128)S(1)} %get-tuple-element.38), channel_id=1, source_target_pairs={{0,1},{1,0},{2,3},{3,2},{4,5},{5,4},{6,7},{7,6},{8,9},{9,8},{10,11... | collective-permute-start | bytes 393224 | tf_op jit(solution)/shard_map/ppermute | solution.py:135
  18.4 0.1 select_reduce_fusion.1
  18.5 2.8 %collective-permute-done.3 = f32[4,64,1,128]{3,1,0,2:T(8,128)S(1)} collective-permute-done((f32[4,64,1,128]{3,1,0,2:T(8,128)S(1)}, f32[4,64,1,128]{3,1,0,2:T(8,128)S(1)}, u32[]{:S(2)}, u32[]{:S(2)}) %collective-permute-start.3) | collective-permute-done | bytes 131104 | tf_op jit(solution)/shard_map/ppermute | solution.py:135
  21.5 1.6 %collective-permute-start.4 = (f32[512,1,128]{2,0,1:T(8,128)S(1)}, f32[512,1,128]{2,0,1:T(8,128)S(1)}, u32[]{:S(2)}, u32[]{:S(2)}) collective-permute-start(f32[512,1,128]{2,0,1:T(8,128)S(1)} %bitcast.125), channel_id=1, source_target_pairs={{0,16},{8,24},{16,0},{24,8},{1,17},{9,25},{17,1},{25,9},{2,18},{10... | collective-permute-start | bytes 786440 | tf_op jit(solution)/shard_map/ppermute | solution.py:68
  23.8 0.8 %pad_maximum_fusion.3 = bf16[3,2,64,512]{3,2,1,0:T(8,128)(2,1)} fusion(bf16[1,2,64,512]{3,2,1,0:T(8,128)(2,1)S(1)} %bitcast.134, bf16[1,2,64,512]{3,2,1,0:T(8,128)(2,1)S(1)} %bitcast.132, bf16[1,2,64,512]{3,2,1,0:T(8,128)(2,1)S(1)} %bitcast.130), kind=kLoop, calls=%fused_computation.42 | loop fusion | flops 393216 | bytes 786432 | tf_op jit(solution)/shard_map/stack | solution.py:154
  24.6 2.0 %collective-permute-start.11 = (bf16[3,2,64,512]{3,2,1,0:T(8,128)(2,1)}, bf16[3,2,64,512]{3,2,1,0:T(8,128)(2,1)S(1)}, u32[]{:S(2)}, u32[]{:S(2)}) collective-permute-start(bf16[3,2,64,512]{3,2,1,0:T(8,128)(2,1)} %pad_maximum_fusion.3), channel_id=1, source_target_pairs={{0,1},{1,0},{2,3},{3,2},{4,5},{5,4},{6,7},{7,6},{8,9},{9,8},{10,11... | collective-permute-start | bytes 1179656 | tf_op jit(solution)/shard_map/ppermute | solution.py:154
  26.6 1.0 %pad_maximum_fusion.2 = bf16[4,2,64,512]{3,2,1,0:T(8,128)(2,1)S(1)} fusion(bf16[1,2,64,512]{3,2,1,0:T(8,128)(2,1)S(1)} %bitcast.135, bf16[1,2,64,512]{3,2,1,0:T(8,128)(2,1)S(1)} %bitcast.133, bf16[1,2,64,512]{3,2,1,0:T(8,128)(2,1)S(1)} %bitcast.131, bf16[1,2,64,512]{3,2,1,0:T(8,128)(2,1)} %param.11), kind=kLoop, calls=%fused_computation.27 | loop fusion | flops 786432 | bytes 1048576 | tf_op jit(solution)/shard_map/stack | solution.py:155
  27.5 0.1 collective-permute-start.5
  27.6 0.3 collective-permute-done.4
  27.9 0.2 collective-permute-start.6
  28.2 0.9 %collective-permute-done.5 = f32[512,1,128]{2,0,1:T(8,128)S(1)} collective-permute-done((f32[512,1,128]{2,0,1:T(8,128)S(1)}, f32[512,1,128]{2,0,1:T(8,128)S(1)}, u32[]{:S(2)}, u32[]{:S(2)}) %collective-permute-start.5) | collective-permute-done | bytes 262176 | tf_op jit(solution)/shard_map/ppermute | solution.py:70
  29.1 0.4 collective-permute-done.6
  29.6 3.8 %cosine_convert_fusion = (bf16[2,2,512,1,128]{4,2,0,3,1:T(8,128)(2,1)S(1)}, bf16[2,2,512,1,128]{4,2,0,3,1:T(8,128)(2,1)S(1)}) fusion(f32[2,1,512,1,128]{4,2,0,3,1:T(8,128)S(1)} %maximum_bitcast_fusion.1, f32[2,1,512,1,128]{4,2,0,3,1:T(8,128)S(1)} %maximum_bitcast_fusion, f32[]{:T(128)} %bitcast.4), kind=kLoop, calls=%fused_computation.8 | loop fusion | flops 1310720 | bytes 2097156 | tf_op jit(solution)/shard_map/convert.7
  33.5 0.4 copy.27
  33.9 0.2 copy.26
  34.1 0.4 copy.23
  34.6 0.2 copy.24
  34.8 0.2 convert_element_type.56
  35.0 0.2 convert_element_type.61
  35.2 0.1 dynamic-slice_bitcast_fusion
  35.3 0.1 fusion.12
  35.4 0.1 fusion.13
  35.5 0.1 bitcast_negate_fusion
  35.6 1.3 %fusion.9 = f32[1024,64]{0,1:T(8,128)S(1)} fusion(bf16[512,512]{0,1:T(8,128)(2,1)S(1)} %bitcast.114, bf16[512,512]{0,1:T(8,128)(2,1)S(1)} %bitcast_negate_fusion, bf16[1,2,64,512]{3,2,1,0:T(8,128)(2,1)} %bitcast.40), kind=kOutput, calls=%fused_computation.43 | convolution fusion | flops 69206016 | bytes 1376256 | tf_op jit(solution)/shard_map/dot_general | solution.py:166
  36.9 1.3 %fusion = f32[64,1024]{1,0:T(8,128)S(1)} fusion(f32[1024,64]{0,1:T(8,128)S(1)} %fusion.9, bf16[512,512]{0,1:T(8,128)(2,1)S(1)} %bitcast.120, bf16[512,512]{0,1:T(8,128)(2,1)S(1)} %bitcast.115, bf16[1,2,64,512]{3,2,1,0:T(8,128)(2,1)} %bitcast.40), kind=kOutput, calls=%fused_computation.3 | convolution fusion | flops 69271552 | bytes 1638400 | tf_op jit(solution)/shard_map/dot_general | solution.py:166
  38.3 0.1 fusion.15
  38.4 0.1 fusion.14
  38.5 0.5 fusion.11
  39.0 0.5 convolution_add_fusion
  39.5 0.2 fusion.4
  39.8 0.5 %fusion.10 = f32[192,1024]{1,0:T(8,128)S(1)} fusion(bf16[192,512]{1,0:T(8,128)(2,1)S(1)} %bitcast.141, bf16[512,512]{0,1:T(8,128)(2,1)S(1)} %bitcast.122, bf16[512,512]{0,1:T(8,128)(2,1)S(1)} %bitcast.118), kind=kOutput, calls=%fused_computation.44 | convolution fusion | flops 203423744 | bytes 2031616 | tf_op jit(solution)/shard_map/dot_general | solution.py:166
  40.3 0.5 %convolution_add_fusion.1 = f32[192,1024]{1,0:T(8,128)S(1)} fusion(f32[192,1024]{1,0:T(8,128)S(1)} %fusion.10, bf16[192,512]{1,0:T(8,128)(2,1)S(1)} %bitcast.129, bf16[512,512]{0,1:T(8,128)(2,1)S(1)} %bitcast.119, bf16[512,512]{0,1:T(8,128)(2,1)S(1)} %bitcast_negate_fusion), kind=kOutput, calls=%fused_computation.1 | convolution fusion | flops 203620352 | bytes 2818048 | tf_op jit(solution)/shard_map/dot_general | solution.py:166
  40.8 0.4 slice-done
  41.2 0.1 slice-done.1
  41.3 0.1 fusion.8
  41.6 1.2 %collective-permute-start.12 = (f32[2,1,512]{2,1,0:T(1,128)S(1)}, f32[2,1,512]{2,1,0:T(1,128)S(1)}, u32[]{:S(2)}, u32[]{:S(2)}) collective-permute-start(f32[2,1,512]{2,1,0:T(1,128)S(1)} %pad_maximum_fusion.11), channel_id=1, source_target_pairs={{0,24},{8,0},{16,8},{24,16},{1,25},{9,1},{17,9},{25,17},{2,26},{10... | collective-permute-start | bytes 12296 | tf_op jit(solution)/shard_map/ppermute | solution.py:15
  42.8 0.6 %collective-permute-start.13 = (f32[2,1,512]{2,1,0:T(1,128)S(1)}, f32[2,1,512]{2,1,0:T(1,128)S(1)}, u32[]{:S(2)}, u32[]{:S(2)}) collective-permute-start(f32[2,1,512]{2,1,0:T(1,128)S(1)} %pad_maximum_fusion.11), channel_id=1, source_target_pairs={{0,16},{8,24},{16,0},{24,8},{1,17},{9,25},{17,1},{25,9},{2,18},{10... | collective-permute-start | bytes 12296 | tf_op jit(solution)/shard_map/ppermute | solution.py:15
  43.4 0.7 %collective-permute-done.12 = f32[2,1,512]{2,1,0:T(1,128)S(1)} collective-permute-done((f32[2,1,512]{2,1,0:T(1,128)S(1)}, f32[2,1,512]{2,1,0:T(1,128)S(1)}, u32[]{:S(2)}, u32[]{:S(2)}) %collective-permute-start.12) | collective-permute-done | bytes 4128 | tf_op jit(solution)/shard_map/ppermute | solution.py:15
  44.1 2.3 %collective-permute-done.13 = f32[2,1,512]{2,1,0:T(1,128)S(1)} collective-permute-done((f32[2,1,512]{2,1,0:T(1,128)S(1)}, f32[2,1,512]{2,1,0:T(1,128)S(1)}, u32[]{:S(2)}, u32[]{:S(2)}) %collective-permute-start.13) | collective-permute-done | bytes 4128 | tf_op jit(solution)/shard_map/ppermute | solution.py:15
  46.5 0.6 %fusion.28 = f32[2,1,512]{2,1,0:T(1,128)} fusion(f32[8,2,1,512]{3,2,1,0:T(1,128)S(1)} %constant_dynamic-update-slice_fusion, s32[]{:T(128)S(6)} %add.234, s32[]{:T(128)S(6)} %add.233, s32[]{:T(128)S(6)} %add.232, s32[]{:T(128)S(6)} %select_n.159), kind=kLoop, calls=%fused_computation.103 | loop fusion | flops 3072 | bytes 20496 | tf_op jit(solution)/shard_map/add | solution.py:96
  (52 shorter events, 0.6 us)
Async XLA Ops:
  0.0 18.4 %copy-start.3 = (f32[1,2,64]{2,1,0:T(2,128)S(1)}, f32[1,2,64]{2,1,0:T(2,128)}, u32[]{:S(2)}) copy-start(f32[1,2,64]{2,1,0:T(2,128)} %param.10) | copy-start | bytes 1540
  0.0 18.4 %copy-start.2 = (s32[1,512]{1,0:T(1,128)S(1)}, s32[1,512]{1,0:T(1,128)}, u32[]{:S(2)}) copy-start(s32[1,512]{1,0:T(1,128)} %param.8) | copy-start | bytes 6148
  1.5 7.6 %collective-permute-start = (f32[64,2,128]{2,0,1:T(8,128)S(1)}, f32[64,2,128]{2,0,1:T(8,128)S(1)}, u32[]{:S(2)}, u32[]{:S(2)}) collective-permute-start(f32[64,2,128]{2,0,1:T(8,128)S(1)} %copy.28), channel_id=1, source_target_pairs={{0,6},{1,7},{2,0},{3,1},{4,2},{5,3},{6,4},{7,5},{8,14},{9,15},{10,... | collective-permute-start | bytes 196616 | tf_op jit(solution)/shard_map/ppermute | solution.py:132
  2.0 9.0 %collective-permute-start.1 = (f32[64,2,128]{2,0,1:T(8,128)S(1)}, f32[64,2,128]{2,0,1:T(8,128)S(1)}, u32[]{:S(2)}, u32[]{:S(2)}) collective-permute-start(f32[64,2,128]{2,0,1:T(8,128)S(1)} %copy.29), channel_id=1, source_target_pairs={{0,4},{1,5},{2,6},{3,7},{4,0},{5,1},{6,2},{7,3},{8,12},{9,13},{10,... | collective-permute-start | bytes 196616 | tf_op jit(solution)/shard_map/ppermute | solution.py:132
  5.5 10.3 %collective-permute-start.2 = (f32[64,2,128]{2,0,1:T(8,128)S(1)}, f32[64,2,128]{2,0,1:T(8,128)S(1)}, u32[]{:S(2)}, u32[]{:S(2)}) collective-permute-start(f32[64,2,128]{2,0,1:T(8,128)S(1)} %copy.30), channel_id=1, source_target_pairs={{0,2},{1,3},{2,4},{3,5},{4,6},{5,7},{6,0},{7,1},{8,10},{9,11},{10,... | collective-permute-start | bytes 196616 | tf_op jit(solution)/shard_map/ppermute | solution.py:132
  5.5 30.1 %collective-permute-start.10 = (bf16[2,64,512]{2,1,0:T(8,128)(2,1)}, bf16[2,64,512]{2,1,0:T(8,128)(2,1)}, u32[]{:S(2)}, u32[]{:S(2)}) collective-permute-start(bf16[2,64,512]{2,1,0:T(8,128)(2,1)} %bitcast.22), channel_id=1, source_target_pairs={{0,1},{1,0},{2,3},{3,2},{4,5},{5,4},{6,7},{7,6},{8,9},{9,8},{10,11... | collective-permute-start | bytes 393224 | tf_op jit(solution)/shard_map/ppermute | solution.py:124
  7.1 16.6 %collective-permute-start.7 = (bf16[2,64,512]{2,1,0:T(8,128)(2,1)}, bf16[2,64,512]{2,1,0:T(8,128)(2,1)S(1)}, u32[]{:S(2)}, u32[]{:S(2)}) collective-permute-start(bf16[2,64,512]{2,1,0:T(8,128)(2,1)} %bitcast.22), channel_id=1, source_target_pairs={{0,6},{1,7},{2,0},{3,1},{4,2},{5,3},{6,4},{7,5},{8,14},{9,15},{10,... | collective-permute-start | bytes 393224 | tf_op jit(solution)/shard_map/ppermute | solution.py:123
  9.1 14.7 %collective-permute-start.8 = (bf16[2,64,512]{2,1,0:T(8,128)(2,1)}, bf16[2,64,512]{2,1,0:T(8,128)(2,1)S(1)}, u32[]{:S(2)}, u32[]{:S(2)}) collective-permute-start(bf16[2,64,512]{2,1,0:T(8,128)(2,1)} %bitcast.22), channel_id=1, source_target_pairs={{0,4},{1,5},{2,6},{3,7},{4,0},{5,1},{6,2},{7,3},{8,12},{9,13},{10,... | collective-permute-start | bytes 393224 | tf_op jit(solution)/shard_map/ppermute | solution.py:123
  11.0 12.7 %collective-permute-start.9 = (bf16[2,64,512]{2,1,0:T(8,128)(2,1)}, bf16[2,64,512]{2,1,0:T(8,128)(2,1)S(1)}, u32[]{:S(2)}, u32[]{:S(2)}) collective-permute-start(bf16[2,64,512]{2,1,0:T(8,128)(2,1)} %bitcast.22), channel_id=1, source_target_pairs={{0,2},{1,3},{2,4},{3,5},{4,6},{5,7},{6,0},{7,1},{8,10},{9,11},{10,... | collective-permute-start | bytes 393224 | tf_op jit(solution)/shard_map/ppermute | solution.py:123
  15.8 5.5 %collective-permute-start.3 = (f32[4,64,1,128]{3,1,0,2:T(8,128)S(1)}, f32[4,64,1,128]{3,1,0,2:T(8,128)S(1)}, u32[]{:S(2)}, u32[]{:S(2)}) collective-permute-start(f32[4,64,1,128]{3,1,0,2:T(8,128)S(1)} %get-tuple-element.38), channel_id=1, source_target_pairs={{0,1},{1,0},{2,3},{3,2},{4,5},{5,4},{6,7},{7,6},{8,9},{9,8},{10,11... | collective-permute-start | bytes 393224 | tf_op jit(solution)/shard_map/ppermute | solution.py:135
  21.5 6.4 %collective-permute-start.4 = (f32[512,1,128]{2,0,1:T(8,128)S(1)}, f32[512,1,128]{2,0,1:T(8,128)S(1)}, u32[]{:S(2)}, u32[]{:S(2)}) collective-permute-start(f32[512,1,128]{2,0,1:T(8,128)S(1)} %bitcast.125), channel_id=1, source_target_pairs={{0,16},{8,24},{16,0},{24,8},{1,17},{9,25},{17,1},{25,9},{2,18},{10... | collective-permute-start | bytes 786440 | tf_op jit(solution)/shard_map/ppermute | solution.py:68
  24.6 15.2 %collective-permute-start.11 = (bf16[3,2,64,512]{3,2,1,0:T(8,128)(2,1)}, bf16[3,2,64,512]{3,2,1,0:T(8,128)(2,1)S(1)}, u32[]{:S(2)}, u32[]{:S(2)}) collective-permute-start(bf16[3,2,64,512]{3,2,1,0:T(8,128)(2,1)} %pad_maximum_fusion.3), channel_id=1, source_target_pairs={{0,1},{1,0},{2,3},{3,2},{4,5},{5,4},{6,7},{7,6},{8,9},{9,8},{10,11... | collective-permute-start | bytes 1179656 | tf_op jit(solution)/shard_map/ppermute | solution.py:154
  27.5 1.6 %collective-permute-start.5 = (f32[512,1,128]{2,0,1:T(8,128)S(1)}, f32[512,1,128]{2,0,1:T(8,128)S(1)}, u32[]{:S(2)}, u32[]{:S(2)}) collective-permute-start(f32[512,1,128]{2,0,1:T(8,128)S(1)} %bitcast.126), channel_id=1, source_target_pairs={{0,8},{8,0},{16,24},{24,16},{1,9},{9,1},{17,25},{25,17},{2,10},{10... | collective-permute-start | bytes 786440 | tf_op jit(solution)/shard_map/ppermute | solution.py:70
  27.9 1.6 %collective-permute-start.6 = (f32[512,1,128]{2,0,1:T(8,128)S(1)}, f32[512,1,128]{2,0,1:T(8,128)S(1)}, u32[]{:S(2)}, u32[]{:S(2)}) collective-permute-start(f32[512,1,128]{2,0,1:T(8,128)S(1)} %collective-permute-done.4), channel_id=1, source_target_pairs={{0,8},{8,0},{16,24},{24,16},{1,9},{9,1},{17,25},{25,17},{2,10},{10... | collective-permute-start | bytes 786440 | tf_op jit(solution)/shard_map/ppermute | solution.py:70
  35.4 2.8 %copy-start = (bf16[4,64,512]{2,1,0:T(8,128)(2,1)}, bf16[4,64,512]{2,1,0:T(8,128)(2,1)S(1)}, u32[]{:S(2)}) copy-start(bf16[4,64,512]{2,1,0:T(8,128)(2,1)S(1)} %fusion.12) | copy-start | bytes 786436
  35.5 2.7 %copy-start.1 = (bf16[4,64,512]{2,1,0:T(8,128)(2,1)}, bf16[4,64,512]{2,1,0:T(8,128)(2,1)S(1)}, u32[]{:S(2)}) copy-start(bf16[4,64,512]{2,1,0:T(8,128)(2,1)S(1)} %fusion.13) | copy-start | bytes 786436
  40.3 0.9 %slice-start = ((bf16[4,64,512]{2,1,0:T(8,128)(2,1)}), bf16[3,64,512]{2,1,0:T(8,128)(2,1)S(1)}, s32[]{:S(2)}) async-start(bf16[4,64,512]{2,1,0:T(8,128)(2,1)} %copy-done), calls=%async_computation | async-start | bytes 393216 | tf_op jit(solution)/shard_map/slice | solution.py:181
  40.3 1.0 %slice-start.1 = ((bf16[4,64,512]{2,1,0:T(8,128)(2,1)}), bf16[3,64,512]{2,1,0:T(8,128)(2,1)S(1)}, s32[]{:S(2)}) async-start(bf16[4,64,512]{2,1,0:T(8,128)(2,1)} %copy-done.1), calls=%async_computation.1 | async-start | bytes 393216 | tf_op jit(solution)/shard_map/slice | solution.py:181
  41.6 2.6 %collective-permute-start.12 = (f32[2,1,512]{2,1,0:T(1,128)S(1)}, f32[2,1,512]{2,1,0:T(1,128)S(1)}, u32[]{:S(2)}, u32[]{:S(2)}) collective-permute-start(f32[2,1,512]{2,1,0:T(1,128)S(1)} %pad_maximum_fusion.11), channel_id=1, source_target_pairs={{0,24},{8,0},{16,8},{24,16},{1,25},{9,1},{17,9},{25,17},{2,26},{10... | collective-permute-start | bytes 12296 | tf_op jit(solution)/shard_map/ppermute | solution.py:15
  42.8 3.6 %collective-permute-start.13 = (f32[2,1,512]{2,1,0:T(1,128)S(1)}, f32[2,1,512]{2,1,0:T(1,128)S(1)}, u32[]{:S(2)}, u32[]{:S(2)}) collective-permute-start(f32[2,1,512]{2,1,0:T(1,128)S(1)} %pad_maximum_fusion.11), channel_id=1, source_target_pairs={{0,16},{8,24},{16,0},{24,8},{1,17},{9,25},{17,1},{25,9},{2,18},{10... | collective-permute-start | bytes 12296 | tf_op jit(solution)/shard_map/ppermute | solution.py:15
  43.4 3.1 %collective-permute-start.14 = (f32[2,1,512]{2,1,0:T(1,128)S(1)}, f32[2,1,512]{2,1,0:T(1,128)S(1)}, u32[]{:S(2)}, u32[]{:S(2)}) collective-permute-start(f32[2,1,512]{2,1,0:T(1,128)S(1)} %pad_maximum_fusion.11), channel_id=1, source_target_pairs={{0,8},{8,16},{16,24},{24,0},{1,9},{9,17},{17,25},{25,1},{2,10},{10... | collective-permute-start | bytes 12296 | tf_op jit(solution)/shard_map/ppermute | solution.py:15

commit v20 on v10

--- a/solution.py
+++ b/solution.py
@@ -197,7 +197,7 @@
     part_real = square_real * focus_real - square_imag * focus_imag
     part_imag = square_real * focus_imag + square_imag * focus_real
     partial_image = jnp.stack([part_real, part_imag])
-    return all_sum_once(partial_image, "freq", freqs)
+    return all_sum(partial_image, "freq", freqs)
 
 
 def solution(mesh):

time: 45.9 us -> 45.8 us (level)
    ppermute x3 -> x2, waiting for transfers between devices: 3.07 us -> 3.15 us  [all_sum(): value = value + lax.ppermute(value, axis_name, pairs)]
    ppermute x3 -> x2, starting transfers between devices: 1.82 us -> 1.75 us  [all_sum(): value = value + lax.ppermute(value, axis_name, pairs)]
  transfers between devices with their start and end apart: 15 -> 14, of which waited for: 6 -> 6; matrix products, arithmetic and copies ran while one was open for 19% -> 19% of each run, Pallas kernels for 0% -> 0%
where the time goes in v20:
time: 45.8 us; the launch traced here: 45.7 us
  starting transfers between devices  16.4 us (36%)
  waiting for transfers between devices  15.1 us (33%)
  other arithmetic  7.91 us (17%)
  local copies, waits for them, and re-layouts  3.37 us (7%)
  matrix products  1.87 us (4%)
  between operations  1.01 us (2%)
    ppermute x3, waiting for transfers between devices, body(): pieces.append(lax.ppermute(sent, 'tile', pairs))  5.63 us
    ppermute x3, starting transfers between devices, body(): cap_row.append(lax.ppermute(capture[0], 'tile', pairs))  4.39 us
    ppermute x3, starting transfers between devices, body(): pieces.append(lax.ppermute(sent, 'tile', pairs))  3.99 us
    another operation x1, other arithmetic  3.84 us
    ppermute x1, waiting for transfers between devices, body(): lax.ppermute(lax.dynamic_slice_in_dim(pieces, (1 - y) * per_tile, per_til...  3.33 us
    ppermute x2, waiting for transfers between devices, all_sum(): value = value + lax.ppermute(value, axis_name, pairs)  3.15 us
    ppermute x2, starting transfers between devices, all_sum(): value = value + lax.ppermute(value, axis_name, pairs)  1.75 us
    ppermute x1, starting transfers between devices, body(): lax.ppermute(lax.dynamic_slice_in_dim(pieces, (1 - y) * per_tile, per_til...  1.58 us
  transfers between devices with their start and end apart: 14, of which 6 were waited for; matrix products, arithmetic and copies ran while one was open for 19% of the time, Pallas kernels for 0%

profile of v20, /device:TPU:16, one launch (start us, length us, event | category | flops | bytes accessed | tf_op | source)
XLA Modules:
  0.0 45.7 jit_solution(1858034862971560721)
XLA Ops:
  0.0 1.5 %constant_dynamic-slice_fusion.4 = (f32[64,2,128]{2,1,0:T(2,128)S(1)}, f32[64,2,128]{2,1,0:T(2,128)S(1)}, f32[64,2,128]{2,1,0:T(2,128)S(1)}, f32[64,2,128]{2,1,0:T(2,128)S(1)}) fusion(f32[64,8,128]{2,1,0:T(8,128)} %param.7, s32[]{:T(128)S(6)} %select_n.128, s32[]{:T(128)S(6)} %select_n.132, s32[]{:T(128)S(6)} %select_n.130, s32[]{:T(128)S(6)} %select_n.134), kind=kLoop, calls=%fused_computation.75 | loop fusion | bytes 524304 | tf_op jit(solution)/shard_map/dynamic_slice | solution.py:127
  1.5 0.5 %collective-permute-start = (f32[64,2,128]{2,0,1:T(8,128)S(1)}, f32[64,2,128]{2,0,1:T(8,128)S(1)}, u32[]{:S(2)}, u32[]{:S(2)}) collective-permute-start(f32[64,2,128]{2,0,1:T(8,128)S(1)} %copy.28), channel_id=1, source_target_pairs={{0,6},{1,7},{2,0},{3,1},{4,2},{5,3},{6,4},{7,5},{8,14},{9,15},{10,... | collective-permute-start | bytes 196616 | tf_op jit(solution)/shard_map/ppermute | solution.py:132
  2.0 3.5 %collective-permute-start.1 = (f32[64,2,128]{2,0,1:T(8,128)S(1)}, f32[64,2,128]{2,0,1:T(8,128)S(1)}, u32[]{:S(2)}, u32[]{:S(2)}) collective-permute-start(f32[64,2,128]{2,0,1:T(8,128)S(1)} %copy.29), channel_id=1, source_target_pairs={{0,4},{1,5},{2,6},{3,7},{4,0},{5,1},{6,2},{7,3},{8,12},{9,13},{10,... | collective-permute-start | bytes 196616 | tf_op jit(solution)/shard_map/ppermute | solution.py:132
  5.5 2.0 %collective-permute-start.7 = (bf16[2,64,512]{2,1,0:T(8,128)(2,1)}, bf16[2,64,512]{2,1,0:T(8,128)(2,1)S(1)}, u32[]{:S(2)}, u32[]{:S(2)}) collective-permute-start(bf16[2,64,512]{2,1,0:T(8,128)(2,1)} %bitcast.22), channel_id=1, source_target_pairs={{0,6},{1,7},{2,0},{3,1},{4,2},{5,3},{6,4},{7,5},{8,14},{9,15},{10,... | collective-permute-start | bytes 393224 | tf_op jit(solution)/shard_map/ppermute | solution.py:123
  7.5 1.9 %collective-permute-start.8 = (bf16[2,64,512]{2,1,0:T(8,128)(2,1)}, bf16[2,64,512]{2,1,0:T(8,128)(2,1)S(1)}, u32[]{:S(2)}, u32[]{:S(2)}) collective-permute-start(bf16[2,64,512]{2,1,0:T(8,128)(2,1)} %bitcast.22), channel_id=1, source_target_pairs={{0,4},{1,5},{2,6},{3,7},{4,0},{5,1},{6,2},{7,3},{8,12},{9,13},{10,... | collective-permute-start | bytes 393224 | tf_op jit(solution)/shard_map/ppermute | solution.py:123
  9.4 0.0 collective-permute-done
  9.4 0.5 %collective-permute-start.9 = (bf16[2,64,512]{2,1,0:T(8,128)(2,1)}, bf16[2,64,512]{2,1,0:T(8,128)(2,1)S(1)}, u32[]{:S(2)}, u32[]{:S(2)}) collective-permute-start(bf16[2,64,512]{2,1,0:T(8,128)(2,1)} %bitcast.22), channel_id=1, source_target_pairs={{0,2},{1,3},{2,4},{3,5},{4,6},{5,7},{6,0},{7,1},{8,10},{9,11},{10,... | collective-permute-start | bytes 393224 | tf_op jit(solution)/shard_map/ppermute | solution.py:123
  9.9 0.0 collective-permute-done.1
  9.9 1.5 %collective-permute-start.10 = (bf16[2,64,512]{2,1,0:T(8,128)(2,1)}, bf16[2,64,512]{2,1,0:T(8,128)(2,1)}, u32[]{:S(2)}, u32[]{:S(2)}) collective-permute-start(bf16[2,64,512]{2,1,0:T(8,128)(2,1)} %bitcast.22), channel_id=1, source_target_pairs={{0,1},{1,0},{2,3},{3,2},{4,5},{5,4},{6,7},{7,6},{8,9},{9,8},{10,11... | collective-permute-start | bytes 393224 | tf_op jit(solution)/shard_map/ppermute | solution.py:124
  11.4 5.6 %collective-permute-done.2 = f32[64,2,128]{2,0,1:T(8,128)S(1)} collective-permute-done((f32[64,2,128]{2,0,1:T(8,128)S(1)}, f32[64,2,128]{2,0,1:T(8,128)S(1)}, u32[]{:S(2)}, u32[]{:S(2)}) %collective-permute-start.2) | collective-permute-done | bytes 65568 | tf_op jit(solution)/shard_map/ppermute | solution.py:132
  17.1 1.6 %collective-permute-start.3 = (f32[4,64,1,128]{3,1,0,2:T(8,128)S(1)}, f32[4,64,1,128]{3,1,0,2:T(8,128)S(1)}, u32[]{:S(2)}, u32[]{:S(2)}) collective-permute-start(f32[4,64,1,128]{3,1,0,2:T(8,128)S(1)} %get-tuple-element.34), channel_id=1, source_target_pairs={{0,1},{1,0},{2,3},{3,2},{4,5},{5,4},{6,7},{7,6},{8,9},{9,8},{10,11... | collective-permute-start | bytes 393224 | tf_op jit(solution)/shard_map/ppermute | solution.py:135
  18.7 0.1 select_reduce_fusion.1
  18.8 3.3 %collective-permute-done.3 = f32[4,64,1,128]{3,1,0,2:T(8,128)S(1)} collective-permute-done((f32[4,64,1,128]{3,1,0,2:T(8,128)S(1)}, f32[4,64,1,128]{3,1,0,2:T(8,128)S(1)}, u32[]{:S(2)}, u32[]{:S(2)}) %collective-permute-start.3) | collective-permute-done | bytes 131104 | tf_op jit(solution)/shard_map/ppermute | solution.py:135
  22.1 0.1 fusion.17
  22.2 0.1 fusion.15
  22.3 1.6 %collective-permute-start.4 = (f32[512,1,128]{2,0,1:T(8,128)S(1)}, f32[512,1,128]{2,0,1:T(8,128)S(1)}, u32[]{:S(2)}, u32[]{:S(2)}) collective-permute-start(f32[512,1,128]{2,0,1:T(8,128)S(1)} %bitcast.84), channel_id=1, source_target_pairs={{0,16},{8,24},{16,0},{24,8},{1,17},{9,25},{17,1},{25,9},{2,18},{10... | collective-permute-start | bytes 786440 | tf_op jit(solution)/shard_map/ppermute | solution.py:68
  24.5 0.0 collective-permute-done.9
  24.6 1.6 %collective-permute-start.11 = (bf16[3,2,64,512]{3,2,1,0:T(8,128)(2,1)S(1)}, bf16[3,2,64,512]{3,2,1,0:T(8,128)(2,1)}, u32[]{:S(2)}, u32[]{:S(2)}) collective-permute-start(bf16[3,2,64,512]{3,2,1,0:T(8,128)(2,1)S(1)} %pad_maximum_fusion.7), channel_id=1, source_target_pairs={{0,1},{1,0},{2,3},{3,2},{4,5},{5,4},{6,7},{7,6},{8,9},{9,8},{10,11... | collective-permute-start | bytes 1179656 | tf_op jit(solution)/shard_map/ppermute | solution.py:154
  26.2 1.0 %pad_maximum_fusion.6 = bf16[4,2,64,512]{3,2,1,0:T(8,128)(2,1)S(1)} fusion(bf16[1,2,64,512]{3,2,1,0:T(8,128)(2,1)S(1)} %bitcast.96, bf16[1,2,64,512]{3,2,1,0:T(8,128)(2,1)S(1)} %bitcast.94, bf16[1,2,64,512]{3,2,1,0:T(8,128)(2,1)S(1)} %bitcast.92, bf16[1,2,64,512]{3,2,1,0:T(8,128)(2,1)} %param.11), kind=kLoop, calls=%fused_computation.35 | loop fusion | flops 786432 | bytes 1048576 | tf_op jit(solution)/shard_map/stack | solution.py:155
  27.1 0.1 collective-permute-start.5
  27.2 1.5 %collective-permute-done.4 = f32[512,1,128]{2,0,1:T(8,128)S(1)} collective-permute-done((f32[512,1,128]{2,0,1:T(8,128)S(1)}, f32[512,1,128]{2,0,1:T(8,128)S(1)}, u32[]{:S(2)}, u32[]{:S(2)}) %collective-permute-start.4) | collective-permute-done | bytes 262176 | tf_op jit(solution)/shard_map/ppermute | solution.py:68
  28.8 0.0 collective-permute-done.5
  28.8 1.4 %collective-permute-done.6 = f32[512,1,128]{2,0,1:T(8,128)S(1)} collective-permute-done((f32[512,1,128]{2,0,1:T(8,128)S(1)}, f32[512,1,128]{2,0,1:T(8,128)S(1)}, u32[]{:S(2)}, u32[]{:S(2)}) %collective-permute-start.6) | collective-permute-done | bytes 262176 | tf_op jit(solution)/shard_map/ppermute | solution.py:70
  30.3 3.8 %cosine_convert_fusion = (bf16[2,2,512,1,128]{4,2,0,3,1:T(8,128)(2,1)S(1)}, bf16[2,2,512,1,128]{4,2,0,3,1:T(8,128)(2,1)S(1)}) fusion(f32[2,1,512,1,128]{4,2,0,3,1:T(8,128)S(1)} %maximum_bitcast_fusion.1, f32[2,1,512,1,128]{4,2,0,3,1:T(8,128)S(1)} %maximum_bitcast_fusion, f32[]{:T(128)} %bitcast.4), kind=kLoop, calls=%fused_computation.6 | loop fusion | flops 1310720 | bytes 2097156 | tf_op jit(solution)/shard_map/convert.5
  34.2 0.4 copy.23
  34.6 0.2 copy.24
  34.8 0.4 copy.27
  35.3 0.2 copy.26
  35.5 0.2 convert_element_type.44
  35.7 0.2 convert_element_type.49
  35.9 0.1 dynamic-slice_bitcast_fusion
  36.0 0.1 fusion.14
  36.1 0.1 fusion.13
  36.2 0.1 bitcast_negate_fusion
  36.3 0.5 %fusion.1 = f32[256,1024]{1,0:T(8,128)S(1)} fusion(bf16[256,512]{1,0:T(8,128)(2,1)S(1)} %bitcast.98, bf16[512,512]{0,1:T(8,128)(2,1)S(1)} %bitcast.82, bf16[512,512]{0,1:T(8,128)(2,1)S(1)} %bitcast.78), kind=kOutput, calls=%fused_computation.8 | convolution fusion | flops 270532608 | bytes 2359296 | tf_op jit(solution)/shard_map/dot_general | solution.py:166
  36.8 0.5 %convolution_add_fusion.1 = f32[256,1024]{1,0:T(8,128)S(1)} fusion(f32[256,1024]{1,0:T(8,128)S(1)} %fusion.1, bf16[256,512]{1,0:T(8,128)(2,1)S(1)} %bitcast.89, bf16[512,512]{0,1:T(8,128)(2,1)S(1)} %bitcast.79, bf16[512,512]{0,1:T(8,128)(2,1)S(1)} %bitcast_negate_fusion), kind=kOutput, calls=%fused_computation.1 | convolution fusion | flops 270794752 | bytes 3407872 | tf_op jit(solution)/shard_map/dot_general | solution.py:166
  37.3 0.2 fusion.9
  37.5 0.1 fusion.11
  37.6 0.1 fusion.12
  37.8 1.1 %pad_maximum_fusion.8 = (bf16[4,1,64,512]{3,2,1,0:T(8,128)(2,1)S(1)}, bf16[4,1,64,512]{3,2,1,0:T(8,128)(2,1)S(1)}) fusion(bf16[3,2,64,512]{3,2,1,0:T(8,128)(2,1)} %collective-permute-done.11, bf16[1,2,64,512]{3,2,1,0:T(8,128)(2,1)} %bitcast.42), kind=kLoop, calls=%fused_computation.54 | loop fusion | flops 262144 | bytes 1048576 | tf_op jit(solution)/shard_map/concatenate | solution.py:180
  38.9 0.5 %fusion = f32[256,1024]{1,0:T(8,128)S(1)} fusion(bf16[256,512]{1,0:T(8,128)(2,1)S(1)} %bitcast.101, bf16[512,512]{0,1:T(8,128)(2,1)S(1)} %bitcast.83, bf16[512,512]{0,1:T(8,128)(2,1)S(1)} %bitcast.80), kind=kOutput, calls=%fused_computation.7 | convolution fusion | flops 270532608 | bytes 2359296 | tf_op jit(solution)/shard_map/dot_general | solution.py:166
  39.4 0.5 %convolution_add_fusion = f32[256,1024]{1,0:T(8,128)S(1)} fusion(f32[256,1024]{1,0:T(8,128)S(1)} %fusion, bf16[256,512]{1,0:T(8,128)(2,1)S(1)} %bitcast.90, bf16[512,512]{0,1:T(8,128)(2,1)S(1)} %bitcast.81, bf16[512,512]{0,1:T(8,128)(2,1)S(1)} %bitcast_negate_fusion), kind=kOutput, calls=%fused_computation | convolution fusion | flops 270794752 | bytes 3407872 | tf_op jit(solution)/shard_map/dot_general | solution.py:166
  39.8 0.2 fusion.5
  40.2 0.2 collective-permute-start.12
  40.3 1.0 %collective-permute-done.12 = f32[2,1,512]{2,1,0:T(1,128)S(1)} collective-permute-done((f32[2,1,512]{2,1,0:T(1,128)S(1)}, f32[2,1,512]{2,1,0:T(1,128)S(1)}, u32[]{:S(2)}, u32[]{:S(2)}) %collective-permute-start.12) | collective-permute-done | bytes 4128 | tf_op jit(solution)/shard_map/ppermute | solution.py:104
  41.4 1.5 %collective-permute-start.13 = (f32[2,1,512]{2,1,0:T(1,128)S(1)}, f32[2,1,512]{2,1,0:T(1,128)S(1)}, u32[]{:S(2)}, u32[]{:S(2)}) collective-permute-start(f32[2,1,512]{2,1,0:T(1,128)S(1)} %fusion.27), channel_id=1, source_target_pairs={{0,16},{8,24},{16,0},{24,8},{1,17},{9,25},{17,1},{25,9},{2,18},{10... | collective-permute-start | bytes 12296 | tf_op jit(solution)/shard_map/ppermute | solution.py:104
  42.9 2.1 %collective-permute-done.13 = f32[2,1,512]{2,1,0:T(1,128)S(1)} collective-permute-done((f32[2,1,512]{2,1,0:T(1,128)S(1)}, f32[2,1,512]{2,1,0:T(1,128)S(1)}, u32[]{:S(2)}, u32[]{:S(2)}) %collective-permute-start.13) | collective-permute-done | bytes 4128 | tf_op jit(solution)/shard_map/ppermute | solution.py:104
  45.1 0.6 %fusion.34 = f32[2,1,512]{2,1,0:T(1,128)} fusion(f32[2,1,512]{2,1,0:T(1,128)S(1)} %collective-permute-done.13, f32[2,1,512]{2,1,0:T(1,128)S(1)} %collective-permute-done.12, f32[1,1,512]{2,1,0:T(1,128)S(1)} %get-tuple-element.41, f32[1,1,512]{2,1,0:T(1,128)S(1)} %get-tuple-element.40), kind=kLoop, calls=%fused_computation.95 | loop fusion | flops 3072 | bytes 16384 | tf_op jit(solution)/shard_map/add | solution.py:104
  (32 shorter events, 0.4 us)
Async XLA Ops:
  0.0 18.7 %copy-start.1 = (f32[1,2,64]{2,1,0:T(2,128)S(1)}, f32[1,2,64]{2,1,0:T(2,128)}, u32[]{:S(2)}) copy-start(f32[1,2,64]{2,1,0:T(2,128)} %param.10) | copy-start | bytes 1540
  0.0 18.7 %copy-start = (s32[1,512]{1,0:T(1,128)S(1)}, s32[1,512]{1,0:T(1,128)}, u32[]{:S(2)}) copy-start(s32[1,512]{1,0:T(1,128)} %param.8) | copy-start | bytes 6148
  1.5 7.9 %collective-permute-start = (f32[64,2,128]{2,0,1:T(8,128)S(1)}, f32[64,2,128]{2,0,1:T(8,128)S(1)}, u32[]{:S(2)}, u32[]{:S(2)}) collective-permute-start(f32[64,2,128]{2,0,1:T(8,128)S(1)} %copy.28), channel_id=1, source_target_pairs={{0,6},{1,7},{2,0},{3,1},{4,2},{5,3},{6,4},{7,5},{8,14},{9,15},{10,... | collective-permute-start | bytes 196616 | tf_op jit(solution)/shard_map/ppermute | solution.py:132
  2.0 7.9 %collective-permute-start.1 = (f32[64,2,128]{2,0,1:T(8,128)S(1)}, f32[64,2,128]{2,0,1:T(8,128)S(1)}, u32[]{:S(2)}, u32[]{:S(2)}) collective-permute-start(f32[64,2,128]{2,0,1:T(8,128)S(1)} %copy.29), channel_id=1, source_target_pairs={{0,4},{1,5},{2,6},{3,7},{4,0},{5,1},{6,2},{7,3},{8,12},{9,13},{10,... | collective-permute-start | bytes 196616 | tf_op jit(solution)/shard_map/ppermute | solution.py:132
  5.5 11.5 %collective-permute-start.2 = (f32[64,2,128]{2,0,1:T(8,128)S(1)}, f32[64,2,128]{2,0,1:T(8,128)S(1)}, u32[]{:S(2)}, u32[]{:S(2)}) collective-permute-start(f32[64,2,128]{2,0,1:T(8,128)S(1)} %copy.30), channel_id=1, source_target_pairs={{0,2},{1,3},{2,4},{3,5},{4,6},{5,7},{6,0},{7,1},{8,10},{9,11},{10,... | collective-permute-start | bytes 196616 | tf_op jit(solution)/shard_map/ppermute | solution.py:132
  5.5 19.0 %collective-permute-start.7 = (bf16[2,64,512]{2,1,0:T(8,128)(2,1)}, bf16[2,64,512]{2,1,0:T(8,128)(2,1)S(1)}, u32[]{:S(2)}, u32[]{:S(2)}) collective-permute-start(bf16[2,64,512]{2,1,0:T(8,128)(2,1)} %bitcast.22), channel_id=1, source_target_pairs={{0,6},{1,7},{2,0},{3,1},{4,2},{5,3},{6,4},{7,5},{8,14},{9,15},{10,... | collective-permute-start | bytes 393224 | tf_op jit(solution)/shard_map/ppermute | solution.py:123
  7.5 17.0 %collective-permute-start.8 = (bf16[2,64,512]{2,1,0:T(8,128)(2,1)}, bf16[2,64,512]{2,1,0:T(8,128)(2,1)S(1)}, u32[]{:S(2)}, u32[]{:S(2)}) collective-permute-start(bf16[2,64,512]{2,1,0:T(8,128)(2,1)} %bitcast.22), channel_id=1, source_target_pairs={{0,4},{1,5},{2,6},{3,7},{4,0},{5,1},{6,2},{7,3},{8,12},{9,13},{10,... | collective-permute-start | bytes 393224 | tf_op jit(solution)/shard_map/ppermute | solution.py:123
  9.4 15.1 %collective-permute-start.9 = (bf16[2,64,512]{2,1,0:T(8,128)(2,1)}, bf16[2,64,512]{2,1,0:T(8,128)(2,1)S(1)}, u32[]{:S(2)}, u32[]{:S(2)}) collective-permute-start(bf16[2,64,512]{2,1,0:T(8,128)(2,1)} %bitcast.22), channel_id=1, source_target_pairs={{0,2},{1,3},{2,4},{3,5},{4,6},{5,7},{6,0},{7,1},{8,10},{9,11},{10,... | collective-permute-start | bytes 393224 | tf_op jit(solution)/shard_map/ppermute | solution.py:123
  9.9 27.8 %collective-permute-start.10 = (bf16[2,64,512]{2,1,0:T(8,128)(2,1)}, bf16[2,64,512]{2,1,0:T(8,128)(2,1)}, u32[]{:S(2)}, u32[]{:S(2)}) collective-permute-start(bf16[2,64,512]{2,1,0:T(8,128)(2,1)} %bitcast.22), channel_id=1, source_target_pairs={{0,1},{1,0},{2,3},{3,2},{4,5},{5,4},{6,7},{7,6},{8,9},{9,8},{10,11... | collective-permute-start | bytes 393224 | tf_op jit(solution)/shard_map/ppermute | solution.py:124
  17.1 5.0 %collective-permute-start.3 = (f32[4,64,1,128]{3,1,0,2:T(8,128)S(1)}, f32[4,64,1,128]{3,1,0,2:T(8,128)S(1)}, u32[]{:S(2)}, u32[]{:S(2)}) collective-permute-start(f32[4,64,1,128]{3,1,0,2:T(8,128)S(1)} %get-tuple-element.34), channel_id=1, source_target_pairs={{0,1},{1,0},{2,3},{3,2},{4,5},{5,4},{6,7},{7,6},{8,9},{9,8},{10,11... | collective-permute-start | bytes 393224 | tf_op jit(solution)/shard_map/ppermute | solution.py:135
  22.3 6.4 %collective-permute-start.4 = (f32[512,1,128]{2,0,1:T(8,128)S(1)}, f32[512,1,128]{2,0,1:T(8,128)S(1)}, u32[]{:S(2)}, u32[]{:S(2)}) collective-permute-start(f32[512,1,128]{2,0,1:T(8,128)S(1)} %bitcast.84), channel_id=1, source_target_pairs={{0,16},{8,24},{16,0},{24,8},{1,17},{9,25},{17,1},{25,9},{2,18},{10... | collective-permute-start | bytes 786440 | tf_op jit(solution)/shard_map/ppermute | solution.py:68
  24.6 13.2 %collective-permute-start.11 = (bf16[3,2,64,512]{3,2,1,0:T(8,128)(2,1)S(1)}, bf16[3,2,64,512]{3,2,1,0:T(8,128)(2,1)}, u32[]{:S(2)}, u32[]{:S(2)}) collective-permute-start(bf16[3,2,64,512]{3,2,1,0:T(8,128)(2,1)S(1)} %pad_maximum_fusion.7), channel_id=1, source_target_pairs={{0,1},{1,0},{2,3},{3,2},{4,5},{5,4},{6,7},{7,6},{8,9},{9,8},{10,11... | collective-permute-start | bytes 1179656 | tf_op jit(solution)/shard_map/ppermute | solution.py:154
  27.1 1.7 %collective-permute-start.5 = (f32[512,1,128]{2,0,1:T(8,128)S(1)}, f32[512,1,128]{2,0,1:T(8,128)S(1)}, u32[]{:S(2)}, u32[]{:S(2)}) collective-permute-start(f32[512,1,128]{2,0,1:T(8,128)S(1)} %bitcast.85), channel_id=1, source_target_pairs={{0,8},{8,0},{16,24},{24,16},{1,9},{9,1},{17,25},{25,17},{2,10},{10... | collective-permute-start | bytes 786440 | tf_op jit(solution)/shard_map/ppermute | solution.py:70
  28.7 1.5 %collective-permute-start.6 = (f32[512,1,128]{2,0,1:T(8,128)S(1)}, f32[512,1,128]{2,0,1:T(8,128)S(1)}, u32[]{:S(2)}, u32[]{:S(2)}) collective-permute-start(f32[512,1,128]{2,0,1:T(8,128)S(1)} %collective-permute-done.4), channel_id=1, source_target_pairs={{0,8},{8,0},{16,24},{24,16},{1,9},{9,1},{17,25},{25,17},{2,10},{10... | collective-permute-start | bytes 786440 | tf_op jit(solution)/shard_map/ppermute | solution.py:70
  40.2 1.2 %collective-permute-start.12 = (f32[2,1,512]{2,1,0:T(1,128)S(1)}, f32[2,1,512]{2,1,0:T(1,128)S(1)}, u32[]{:S(2)}, u32[]{:S(2)}) collective-permute-start(f32[2,1,512]{2,1,0:T(1,128)S(1)} %pad_maximum_fusion.10), channel_id=1, source_target_pairs={{0,8},{8,0},{16,24},{24,16},{1,9},{9,1},{17,25},{25,17},{2,10},{10... | collective-permute-start | bytes 12296 | tf_op jit(solution)/shard_map/ppermute | solution.py:104
  41.4 3.7 %collective-permute-start.13 = (f32[2,1,512]{2,1,0:T(1,128)S(1)}, f32[2,1,512]{2,1,0:T(1,128)S(1)}, u32[]{:S(2)}, u32[]{:S(2)}) collective-permute-start(f32[2,1,512]{2,1,0:T(1,128)S(1)} %fusion.27), channel_id=1, source_target_pairs={{0,16},{8,24},{16,0},{24,8},{1,17},{9,25},{17,1},{25,9},{2,18},{10... | collective-permute-start | bytes 12296 | tf_op jit(solution)/shard_map/ppermute | solution.py:104
